TPU v7x, 32 devices: a whole 2x2x4 slice. The times are simulated.
32 devices in a mesh: rep: 4 (over y, core), seq: 4 (over z), fsdp: 2 (over x).
Axes of the slice: x: 2, y: 2, z: 4, core: 2. Of those that a mesh axis runs over, the one named last changes fastest.
Arguments:
- tokens: bfloat16 [4096, 4096], P(('rep', 'seq')), may hold values from -6 to 6
- cotangent: bfloat16 [4096, 4096], P(('rep', 'seq')), may hold values from -3 to 3
- norm_gain: float32 [4096], replicated, may hold values from 0.1 to 1.9
- gate_weight: bfloat16 [4096, 12288], P(None, ('seq', 'fsdp')), may hold values from -0.09375 to 0.09375
- up_weight: bfloat16 [4096, 12288], P(None, ('seq', 'fsdp')), may hold values from -0.09375 to 0.09375
- down_weight: bfloat16 [12288, 4096], P(('seq', 'fsdp')), may hold values from -0.0546875 to 0.0546875
- depths: int32 [4096], P(('rep', 'seq')), may hold values from 0 to 4, as said below
Outputs:
- branch_grad: bfloat16 [4096, 4096], P(('rep', 'seq', 'fsdp'))
- gate_grad: float32 [4096, 12288], P('rep', ('seq', 'fsdp'))
- up_grad: float32 [4096, 12288], P('rep', ('seq', 'fsdp'))
- down_grad: float32 [12288, 4096], P(('seq', 'fsdp'), 'rep')
Inputs may be any that keep to these rules, and one draw needn't show every extreme that they name: `depths`: within each aligned block of 256 rows (the tokens of one seq shard) at most 8 and at least 4 tokens have a depth greater than 1, and some block has exactly 8.
All inputs are finite; a program needn't handle non-finite values.
Results may differ from a plain program's by a relative error of at most 0.019.
Values may be sent and summed in bfloat16 or wider, within the bound.
No kernel may reach another device: no remote copies, remote signals or barrier semaphores. Data moves between devices by JAX's collectives and lax.ppermute only.
A program may use at most 192 MiB of HBM per device.

v0:
```python
from functools import partial

import jax
import jax.numpy as jnp
from jax import lax
from jax.sharding import PartitionSpec as P

REC = 1
MAXACT = 8


EPSILON = 1e-05


def normalize(widened, norm_gain):
    factor = lax.rsqrt(jnp.mean(widened * widened, axis=-1, keepdims=True) + EPSILON)
    return widened * factor * norm_gain


def contract_first(left, right):
    return lax.dot_general(
        left, right, (((0,), (0,)), ((), ())), preferred_element_type=jnp.float32
    )


def contract_last(left, right):
    return lax.dot_general(
        left, right, (((1,), (1,)), ((), ())), preferred_element_type=jnp.float32
    )


def local(tokens, cotangent, norm_gain, gate_weight, up_weight, down_weight, depths):
    parts = lax.axis_size("fsdp")
    place = lax.axis_index("fsdp")
    rows_here = tokens.shape[0]
    own_rows = rows_here // parts
    active = depths > REC
    widened = tokens.astype(jnp.float32)
    normed = normalize(widened, norm_gain).astype(jnp.bfloat16)
    masked = jnp.where(active[:, None], cotangent, jnp.zeros_like(cotangent))
    ordinal = jnp.cumsum(active.astype(jnp.int32)) - 1
    selector = (ordinal[None, :] == jnp.arange(MAXACT, dtype=jnp.int32)[:, None]) & active[None, :]
    picker = selector.astype(jnp.bfloat16)
    send_normed = jnp.dot(picker, normed, preferred_element_type=jnp.float32).astype(jnp.bfloat16)
    send_masked = jnp.dot(picker, masked, preferred_element_type=jnp.float32).astype(jnp.bfloat16)
    source = jnp.dot(selector.astype(jnp.float32), widened, precision=lax.Precision.HIGHEST)
    all_normed, all_masked = (
        lax.all_gather(send_normed, "seq", axis=0, tiled=True),
        lax.all_gather(send_masked, "seq", axis=0, tiled=True),
    )
    gate = jnp.dot(all_normed, gate_weight, preferred_element_type=jnp.float32)
    up = jnp.dot(all_normed, up_weight, preferred_element_type=jnp.float32)
    sigmoid_gate = jax.nn.sigmoid(gate)
    swished = gate * sigmoid_gate
    hidden = (swished * up).astype(jnp.bfloat16)
    hidden_grad = contract_last(all_masked, down_weight)
    gate_rows = (hidden_grad * up * sigmoid_gate * (1.0 + gate * (1.0 - sigmoid_gate))).astype(
        jnp.bfloat16
    )
    up_rows = (hidden_grad * swished).astype(jnp.bfloat16)
    gate_term = contract_first(all_normed, gate_rows)
    up_term = contract_first(all_normed, up_rows)
    down_term = contract_first(hidden, all_masked)
    grads = (
        lax.psum_scatter(
            gate_term.astype(jnp.bfloat16), "rep", scatter_dimension=0, tiled=True
        ).astype(jnp.float32),
        lax.psum_scatter(
            up_term.astype(jnp.bfloat16), "rep", scatter_dimension=0, tiled=True
        ).astype(jnp.float32),
        lax.psum_scatter(
            down_term.astype(jnp.bfloat16), "rep", scatter_dimension=1, tiled=True
        ).astype(jnp.float32),
    )
    slot_count = send_normed.shape[0]
    share = slot_count // parts
    feature_grad = lax.psum_scatter(
        contract_last(gate_rows, gate_weight) + contract_last(up_rows, up_weight),
        ("seq", "fsdp"),
        scatter_dimension=0,
        tiled=True,
    )
    mine = lax.dynamic_slice_in_dim(source, place * share, share, 0)
    _, pullback = jax.vjp(partial(normalize, norm_gain=norm_gain), mine)
    slot_grad = pullback(feature_grad)[0].astype(jnp.bfloat16)
    every_slot = lax.all_gather(slot_grad, "fsdp", axis=0, tiled=True)
    own_columns = lax.dynamic_slice_in_dim(picker, place * own_rows, own_rows, 1)
    branch_grad = contract_first(own_columns, every_slot).astype(jnp.bfloat16)
    return (branch_grad, grads[0], grads[1], grads[2])


def solution(mesh):
    in_specs = (
        P(("rep", "seq"), None),
        P(("rep", "seq"), None),
        P(),
        P(None, ("seq", "fsdp")),
        P(None, ("seq", "fsdp")),
        P(("seq", "fsdp"), None),
        P(("rep", "seq")),
    )
    out_specs = (
        P(("rep", "seq", "fsdp"), None),
        P("rep", ("seq", "fsdp")),
        P("rep", ("seq", "fsdp")),
        P(("seq", "fsdp"), "rep"),
    )
    return jax.shard_map(local, mesh=mesh, in_specs=in_specs, out_specs=out_specs, check_vma=False)
```

profile of v0, /device:TPU:0, one launch (start us, length us, event | category | flops | bytes accessed | tf_op | source)
XLA Modules:
  0.0 399.6 jit_solution(12583813852467027454)
XLA Ops:
  8.0 2.1 fusion
  10.1 0.7 convert_bitcast_fusion
  10.8 0.3 reduce-window.9
  11.4 2.0 convolution_convert_fusion.5
  13.5 2.4 convolution_convert_fusion.4
  15.9 15.6 %all_gather.10 = bf16[32,4096]{1,0:T(8,128)(2,1)S(1)} all-gather(bf16[8,4096]{1,0:T(8,128)(2,1)S(1)} %convolution_convert_fusion.4), channel_id=1, replica_groups=mesh['rep'=4,'seq'=4,'fsdp'=2] {'seq'}, dimensions={0}, use_global_device_ids=true | all-gather | bytes 327680 | tf_op jit(solution)/shard_map/all_gather | solution.py:48
  31.5 6.9 %fusion.24 = f32[32,1536]{1,0:T(8,128)S(1)} fusion(bf16[32,4096]{1,0:T(8,128)(2,1)S(1)} %all_gather.10, bf16[4096,1536]{1,0:T(8,128)(2,1)} %param.10), kind=kOutput, calls=%fused_computation.44 | convolution fusion | flops 402653184 | bytes 13041664 | tf_op jit(solution)/shard_map/dot_general | solution.py:51
  38.4 0.1 slice-done.5
  38.6 2.2 fusion.23
  40.7 14.6 %all_gather.9 = bf16[32,4096]{1,0:T(8,128)(2,1)S(1)} all-gather(bf16[8,4096]{1,0:T(8,128)(2,1)S(1)} %convolution_convert_fusion.5), channel_id=1, replica_groups=mesh['rep'=4,'seq'=4,'fsdp'=2] {'seq'}, dimensions={0}, use_global_device_ids=true | all-gather | bytes 327680 | tf_op jit(solution)/shard_map/all_gather | solution.py:49
  55.3 8.6 %multiply_convert_fusion.1 = (bf16[32,1536]{1,0:T(8,128)(2,1)S(1)}, bf16[32,1536]{1,0:T(8,128)(2,1)S(1)}) fusion(f32[32,1536]{1,0:T(8,128)S(1)} %fusion.24, f32[32,1536]{1,0:T(8,128)S(1)} %fusion.23, bf16[32,4096]{1,0:T(8,128)(2,1)S(1)} %all_gather.9, bf16[1536,4096]{1,0:T(8,128)(2,1)} %param.12), kind=kOutput, calls=%fused_computation.18 | convolution fusion | flops 403292160 | bytes 13434880 | tf_op jit(solution)/shard_map/dot_general | solution.py:27
  63.9 3.7 fusion.25
  67.6 9.1 %convolution_add_fusion = f32[32,4096]{1,0:T(8,128)} fusion(f32[32,4096]{1,0:T(8,128)S(1)} %fusion.25, bf16[32,1536]{1,0:T(8,128)(2,1)S(1)} %get-tuple-element.8, bf16[4096,1536]{1,0:T(8,128)(2,1)} %param.11), kind=kOutput, calls=%fused_computation.6 | convolution fusion | flops 402784256 | bytes 13729792 | tf_op jit(solution)/shard_map/dot_general | solution.py:27
  76.8 6.5 %convolution_convert_fusion = bf16[1536,4096]{1,0:T(8,128)(2,1)} fusion(bf16[32,4096]{1,0:T(8,128)(2,1)S(1)} %all_gather.9, f32[32,1536]{1,0:T(8,128)S(1)} %fusion.23, f32[32,1536]{1,0:T(8,128)S(1)} %fusion.24), kind=kOutput, calls=%fused_computation | convolution fusion | flops 409239552 | bytes 13238272 | tf_op jit(solution)/shard_map/dot_general | solution.py:21
  83.4 0.2 reduce-scatter.6.cloned.1.call-start
  83.6 6.5 %convolution_convert_fusion.1 = bf16[4096,1536]{1,0:T(8,128)(2,1)} fusion(bf16[32,4096]{1,0:T(8,128)(2,1)S(1)} %all_gather.10, bf16[32,1536]{1,0:T(8,128)(2,1)S(1)} %get-tuple-element.8), kind=kOutput, calls=%fused_computation.1 | convolution fusion | flops 408944640 | bytes 12943360 | tf_op jit(solution)/shard_map/dot_general | solution.py:21
  90.2 9.4 %convolution_convert_fusion.2 = bf16[4096,1536]{1,0:T(8,128)(2,1)} fusion(bf16[32,4096]{1,0:T(8,128)(2,1)S(1)} %all_gather.10, bf16[32,1536]{1,0:T(8,128)(2,1)S(1)} %get-tuple-element.9), kind=kOutput, calls=%fused_computation.2 | convolution fusion | flops 408944640 | bytes 12943360 | tf_op jit(solution)/shard_map/dot_general | solution.py:21
  99.6 0.6 copy-done.2
  100.2 0.6 dynamic-slice
  101.6 0.2 copy-done
  101.8 0.4 fusion.19
  102.2 48.1 %all-reduce.3.cloned.1.call-done = f32[32,4096]{1,0:T(8,128)} async-done(((f32[32,4096]{1,0:T(8,128)}), f32[32,4096]{1,0:T(8,128)}) %all-reduce.3.cloned.1.call-update) | async-done | bytes 524304
  150.3 1.1 multiply_reduce_fusion.1
  151.4 1.0 fusion.12
  152.4 4.6 %all-gather = bf16[2,4,4096]{2,1,0:T(4,128)(2,1)S(1)} all-gather(bf16[1,4,4096]{2,1,0:T(4,128)(2,1)S(1)} %fusion.12), channel_id=1, replica_groups=mesh['rep'=4,'seq'=4,'fsdp'=2] {'fsdp'}, dimensions={0}, use_global_device_ids=true | all-gather | bytes 98304 | tf_op jit(solution)/shard_map/all_gather | solution.py:86
  157.1 1.5 convolution_convert_fusion.3
  158.5 24.9 %reduce-scatter.8.cloned.1.call-done = bf16[1536,1024]{1,0:T(8,128)(2,1)} async-done(((bf16[1536,4096]{1,0:T(8,128)(2,1)}), bf16[1536,1024]{1,0:T(8,128)(2,1)}) %reduce-scatter.8.cloned.1.call-update) | async-done | bytes 3145744 | tf_op jit(solution)/shard_map/reduce_scatter | solution.py:71
  183.4 5.3 %convert_element_type.62 = f32[1536,1024]{1,0:T(8,128)} convert(bf16[1536,1024]{1,0:T(8,128)(2,1)} %reduce-scatter.8.cloned.1.call-done) | non-fusion elementwise | flops 1572864 | bytes 9437184 | tf_op jit(solution)/shard_map/convert_element_type | solution.py:73
  188.8 96.2 %reduce-scatter.6.cloned.1.call-done = bf16[1024,1536]{1,0:T(8,128)(2,1)} async-done(((bf16[4096,1536]{1,0:T(8,128)(2,1)}), bf16[1024,1536]{1,0:T(8,128)(2,1)}) %reduce-scatter.6.cloned.1.call-update) | async-done | bytes 3145744 | tf_op jit(solution)/shard_map/reduce_scatter | solution.py:68
  285.0 5.5 %convert_element_type.59 = f32[1024,1536]{1,0:T(8,128)} convert(bf16[1024,1536]{1,0:T(8,128)(2,1)} %reduce-scatter.6.cloned.1.call-done) | non-fusion elementwise | flops 1572864 | bytes 9437184 | tf_op jit(solution)/shard_map/convert_element_type | solution.py:70
  290.4 96.1 %reduce-scatter.4.cloned.1.call-done = bf16[1024,1536]{1,0:T(8,128)(2,1)} async-done(((bf16[4096,1536]{1,0:T(8,128)(2,1)}), bf16[1024,1536]{1,0:T(8,128)(2,1)}) %reduce-scatter.4.cloned.1.call-update) | async-done | bytes 3145744 | tf_op jit(solution)/shard_map/reduce_scatter | solution.py:65
  386.5 5.5 %convert_element_type.57 = f32[1024,1536]{1,0:T(8,128)} convert(bf16[1024,1536]{1,0:T(8,128)(2,1)} %reduce-scatter.4.cloned.1.call-done) | non-fusion elementwise | flops 1572864 | bytes 9437184 | tf_op jit(solution)/shard_map/convert_element_type | solution.py:67
  (32 shorter events, 0.6 us)
Async XLA Ops:
  8.0 142.3 %all-reduce.3.cloned.1.call-start = ((), (), s32[]{:S(2)}) async-start(), calls=%async_computation.6 | async-start | bytes 1048576
  13.5 24.9 %slice-start.3 = ((s8[12582912]{0:T(1024)(128)(4,1)}), s8[4194304]{0:T(1024)(128)(4,1)S(1)}, s32[]{:S(2)}) async-start(s8[12582912]{0:T(1024)(128)(4,1)} %bitcast.26), calls=%async_computation.10 | async-start | bytes 8388608
  31.5 6.9 %slice-start.4 = ((s8[12582912]{0:T(1024)(128)(4,1)}), s8[4194304]{0:T(1024)(128)(4,1)S(1)}, s32[]{:S(2)}) async-start(s8[12582912]{0:T(1024)(128)(4,1)} %bitcast.26), calls=%async_computation.11 | async-start | bytes 8388608
  31.5 7.0 %slice-start.5 = ((s8[12582912]{0:T(1024)(128)(4,1)}), s8[4194304]{0:T(1024)(128)(4,1)S(1)}, s32[]{:S(2)}) async-start(s8[12582912]{0:T(1024)(128)(4,1)} %bitcast.26), calls=%async_computation.12 | async-start | bytes 8388608
  38.6 25.3 %slice-start = ((s8[12582912]{0:T(1024)(128)(4,1)}), s8[4194304]{0:T(1024)(128)(4,1)S(1)}, s32[]{:S(2)}) async-start(s8[12582912]{0:T(1024)(128)(4,1)} %bitcast.24), calls=%async_computation.7 | async-start | bytes 8388608
  38.6 25.3 %slice-start.1 = ((s8[12582912]{0:T(1024)(128)(4,1)}), s8[4194304]{0:T(1024)(128)(4,1)S(1)}, s32[]{:S(2)}) async-start(s8[12582912]{0:T(1024)(128)(4,1)} %bitcast.24), calls=%async_computation.8 | async-start | bytes 8388608
  55.3 8.6 %slice-start.2 = ((s8[12582912]{0:T(1024)(128)(4,1)}), s8[4194304]{0:T(1024)(128)(4,1)S(1)}, s32[]{:S(2)}) async-start(s8[12582912]{0:T(1024)(128)(4,1)} %bitcast.24), calls=%async_computation.9 | async-start | bytes 8388608
  76.8 106.6 %reduce-scatter.8.cloned.1.call-start = ((), (), s32[]{:S(2)}) async-start(), calls=%async_computation.5 | async-start | bytes 15728640 | tf_op jit(solution)/shard_map/reduce_scatter | solution.py:71
  83.4 201.6 %reduce-scatter.6.cloned.1.call-start = ((), (), s32[]{:S(2)}) async-start(), calls=%async_computation.4 | async-start | bytes 15728640 | tf_op jit(solution)/shard_map/reduce_scatter | solution.py:68
  90.2 296.4 %reduce-scatter.4.cloned.1.call-start = ((), (), s32[]{:S(2)}) async-start(), calls=%async_computation.3 | async-start | bytes 15728640 | tf_op jit(solution)/shard_map/reduce_scatter | solution.py:65
  99.6 0.7 copy-start.2
  99.6 2.3 copy-start
  99.6 50.7 %copy-start.1 = (f32[4096]{0:T(1024)S(1)}, f32[4096]{0:T(1024)}, u32[]{:S(2)}) copy-start(f32[4096]{0:T(1024)} %param.9) | copy-start | bytes 49156
Sparse Core Ops, SparseCore 0:
  76.9 73.3 all-reduce.2
Sparse Core Ops, SparseCore 1:
  83.5 99.9 reduce-scatter.7
  186.1 98.9 reduce-scatter.5
  287.6 98.9 reduce-scatter.3
where the time goes:
time: 400 us
  waiting for transfers between devices  265 us (66%)
  matrix products  59.1 us (15%)
  blocking collectives  34.8 us (9%)
  other arithmetic  21.6 us (5%)
  between operations  16.5 us (4%)
    reduce_scatter x1, waiting for transfers between devices, local(): lax.psum_scatter(up_term.astype(jnp.bfloat16), 'rep', scatter_dimension=0...  96.2 us
    reduce_scatter x1, waiting for transfers between devices, local(): lax.psum_scatter(gate_term.astype(jnp.bfloat16), 'rep', scatter_dimension...  96.1 us
    unnamed x5, waiting for transfers between devices  48.2 us
    reduce_scatter x1, waiting for transfers between devices, local(): lax.psum_scatter(down_term.astype(jnp.bfloat16), 'rep', scatter_dimension...  24.9 us
    dot_general x4, matrix products, contract_first(): lax.dot_general(left, right, (((0,), (0,)), ((), ())), preferred_element_...  23.8 us
    dot_general x3, matrix products, contract_last(): lax.dot_general(left, right, (((1,), (1,)), ((), ())), preferred_element_...  21.4 us
    convert_element_type x3, other arithmetic, local(): grads = (lax.psum_scatter(gate_term.astype(jnp.bfloat16), 'rep', scatter_...  16.3 us
    all_gather x1, blocking collectives, local(): lax.all_gather(send_normed, 'seq', axis=0, tiled=True)  15.6 us
  transfers between devices with their start and end apart: 4, of which 4 were waited for; matrix products, arithmetic and copies ran while one was open for 9% of the time, Pallas kernels for 0%

commit v1 on v0

v1 whole, which is shorter than its diff:
```python
from functools import partial

import jax
import jax.numpy as jnp
from jax import lax
from jax.sharding import PartitionSpec as P

REC = 1
MAXACT = 8


EPSILON = 1e-05


def normalize(widened, norm_gain):
    factor = lax.rsqrt(jnp.mean(widened * widened, axis=-1, keepdims=True) + EPSILON)
    return widened * factor * norm_gain


def contract_first(left, right):
    return lax.dot_general(
        left, right, (((0,), (0,)), ((), ())), preferred_element_type=jnp.float32
    )


def contract_last(left, right):
    return lax.dot_general(
        left, right, (((1,), (1,)), ((), ())), preferred_element_type=jnp.float32
    )


def local(tokens, cotangent, norm_gain, gate_weight, up_weight, down_weight, depths):
    parts = lax.axis_size("fsdp")
    place = lax.axis_index("fsdp")
    replicas = lax.axis_size("rep")
    replica = lax.axis_index("rep")
    features = tokens.shape[1]
    feature_share = features // replicas
    rows_here = tokens.shape[0]
    own_rows = rows_here // parts
    active = depths > REC
    ordinal = jnp.cumsum(active.astype(jnp.int32)) - 1
    selector = (ordinal[None, :] == jnp.arange(MAXACT, dtype=jnp.int32)[:, None]) & active[None, :]
    picker = selector.astype(jnp.bfloat16)
    source = jnp.dot(picker, tokens, preferred_element_type=jnp.float32)
    send_masked = jnp.dot(picker, cotangent, preferred_element_type=jnp.float32).astype(jnp.bfloat16)
    send_normed = normalize(source, norm_gain).astype(jnp.bfloat16)
    all_normed = lax.all_gather(send_normed, ("rep", "seq"), axis=0, tiled=True)
    all_masked = lax.all_gather(send_masked, ("rep", "seq"), axis=0, tiled=True)
    gate = jnp.dot(all_normed, gate_weight, preferred_element_type=jnp.float32)
    up = jnp.dot(all_normed, up_weight, preferred_element_type=jnp.float32)
    sigmoid_gate = jax.nn.sigmoid(gate)
    swished = gate * sigmoid_gate
    hidden = (swished * up).astype(jnp.bfloat16)
    hidden_grad = contract_last(all_masked, down_weight)
    gate_rows = (hidden_grad * up * sigmoid_gate * (1.0 + gate * (1.0 - sigmoid_gate))).astype(
        jnp.bfloat16
    )
    up_rows = (hidden_grad * swished).astype(jnp.bfloat16)
    normed_cols = lax.dynamic_slice_in_dim(all_normed, replica * feature_share, feature_share, 1)
    masked_cols = lax.dynamic_slice_in_dim(all_masked, replica * feature_share, feature_share, 1)
    gate_grad = contract_first(normed_cols, gate_rows)
    up_grad = contract_first(normed_cols, up_rows)
    down_grad = contract_first(hidden, masked_cols)
    window = all_normed.shape[0] // replicas
    window_gate = lax.dynamic_slice_in_dim(gate_rows, replica * window, window, 0)
    window_up = lax.dynamic_slice_in_dim(up_rows, replica * window, window, 0)
    partial_features = contract_last(window_gate, gate_weight) + contract_last(window_up, up_weight)
    slot_count = send_normed.shape[0]
    share = slot_count // parts
    feature_grad = lax.psum_scatter(
        partial_features.astype(jnp.bfloat16),
        ("seq", "fsdp"),
        scatter_dimension=0,
        tiled=True,
    ).astype(jnp.float32)
    mine = lax.dynamic_slice_in_dim(source, place * share, share, 0)
    _, pullback = jax.vjp(partial(normalize, norm_gain=norm_gain), mine)
    slot_grad = pullback(feature_grad)[0].astype(jnp.bfloat16)
    every_slot = lax.all_gather(slot_grad, "fsdp", axis=0, tiled=True)
    own_columns = lax.dynamic_slice_in_dim(picker, place * own_rows, own_rows, 1)
    branch_grad = contract_first(own_columns, every_slot).astype(jnp.bfloat16)
    return (branch_grad, gate_grad, up_grad, down_grad)


def solution(mesh):
    in_specs = (
        P(("rep", "seq"), None),
        P(("rep", "seq"), None),
        P(),
        P(None, ("seq", "fsdp")),
        P(None, ("seq", "fsdp")),
        P(("seq", "fsdp"), None),
        P(("rep", "seq")),
    )
    out_specs = (
        P(("rep", "seq", "fsdp"), None),
        P("rep", ("seq", "fsdp")),
        P("rep", ("seq", "fsdp")),
        P(("seq", "fsdp"), "rep"),
    )
    return jax.shard_map(local, mesh=mesh, in_specs=in_specs, out_specs=out_specs, check_vma=False)
```

time: 400 us -> 199 us (0.50)
  waiting for transfers between devices: 265 us -> 119 us
  blocking collectives: 34.8 us -> 4.59 us
  other arithmetic: 21.6 us -> 4.69 us
  matrix products: 59.1 us -> 53.3 us
    reduce_scatter x3 -> x0, waiting for transfers between devices: 217 us -> none  [the longest x1 96.2 us: local(): lax.psum_scatter(up_term.astype(jnp.bfloat16), 'rep', scatter_dimension=0...]
    all_gather x0 -> x2, waiting for transfers between devices: none -> 62.3 us  [the longest x1 36.2 us: local(): all_normed = lax.all_gather(send_normed, ('rep', 'seq'), axis=0, tiled=True)]
    all_gather x2 -> x0, blocking collectives: 30.2 us -> none  [the longest x1 15.6 us: local(): lax.all_gather(send_normed, 'seq', axis=0, tiled=True)]
    convert_element_type x3 -> x1, other arithmetic: 16.3 us -> 1.43 us  [local(): send_normed = normalize(source, norm_gain).astype(jnp.bfloat16)]
    dot_general x4, matrix products: 23.8 us -> 14.2 us  [contract_first(): lax.dot_general(left, right, (((0,), (0,)), ((), ())), preferred_element_...]
    unnamed x5 -> x4, waiting for transfers between devices: 48.2 us -> 56.9 us
    dot_general x1, matrix products: 2.16 us -> 6.74 us  [local(): up = jnp.dot(all_normed, up_weight, preferred_element_type=jnp.float32)]
  transfers between devices with their start and end apart: 4 -> 3, of which waited for: 4 -> 3; matrix products, arithmetic and copies ran while one was open for 9% -> 15% of each run, Pallas kernels for 0% -> 0%
where the time goes in v1:
time: 199 us; the launch traced here: 198 us
  waiting for transfers between devices  119 us (60%)
  matrix products  53.3 us (27%)
  between operations  14.6 us (7%)
  other arithmetic  4.69 us (2%)
  blocking collectives  4.59 us (2%)
    unnamed x4, waiting for transfers between devices  56.9 us
    all_gather x1, waiting for transfers between devices, local(): all_normed = lax.all_gather(send_normed, ('rep', 'seq'), axis=0, tiled=True)  36.2 us
    all_gather x1, waiting for transfers between devices, local(): all_masked = lax.all_gather(send_masked, ('rep', 'seq'), axis=0, tiled=True)  26.1 us
    dot_general x3, matrix products, contract_last(): lax.dot_general(left, right, (((1,), (1,)), ((), ())), preferred_element_...  22.5 us
    dot_general x4, matrix products, contract_first(): lax.dot_general(left, right, (((0,), (0,)), ((), ())), preferred_element_...  14.2 us
    dot_general x1, matrix products, local(): gate = jnp.dot(all_normed, gate_weight, preferred_element_type=jnp.float32)  6.77 us
    dot_general x1, matrix products, local(): up = jnp.dot(all_normed, up_weight, preferred_element_type=jnp.float32)  6.74 us
    all_gather x1, blocking collectives, local(): every_slot = lax.all_gather(slot_grad, 'fsdp', axis=0, tiled=True)  4.59 us
  transfers between devices with their start and end apart: 3, of which 3 were waited for; matrix products, arithmetic and copies ran while one was open for 15% of the time, Pallas kernels for 0%

profile of v1, /device:TPU:0, one launch (start us, length us, event | category | flops | bytes accessed | tf_op | source)
XLA Modules:
  0.0 198.2 jit_solution(12777274194914511911)
XLA Ops:
  7.2 0.0 copy-start
  7.2 0.0 all-gather.6.cloned.1.call-start
  7.2 0.8 convert_bitcast_fusion
  8.1 0.3 reduce-window.9
  8.4 0.1 slice.7
  8.5 0.1 slice_reduce_fusion
  8.6 0.1 add_bitcast_fusion
  8.7 0.1 copy-done
  8.8 0.5 multiply_reduce_fusion
  9.3 1.4 multiply_convert_fusion.4
  10.7 0.0 all-gather.6.cloned.1.call-update
  10.7 0.0 all-gather.4.cloned.1.call-start
  10.8 2.6 %convolution_convert_fusion.1 = bf16[8,4096]{1,0:T(8,128)(2,1)} fusion(bf16[256,4096]{1,0:T(8,128)(2,1)} %param.8, s32[256]{0:T(256)S(1)} %add_bitcast_fusion, pred[256]{0:T(512)(128)(4,1)S(1)} %get-tuple-element.7), kind=kOutput, calls=%fused_computation.3 | convolution fusion | flops 16814080 | bytes 2163968 | tf_op jit(solution)/shard_map/dot_general | solution.py:46
  13.4 0.0 all-gather.4.cloned.1.call-update
  13.4 0.0 all-reduce.3.cloned.1.call-start
  13.5 1.2 dynamic-slice
  15.4 36.2 %all-gather.6.cloned.1.call-done = bf16[128,4096]{1,0:T(8,128)(2,1)} async-done(((bf16[8,4096]{1,0:T(8,128)(2,1)}), bf16[128,4096]{1,0:T(8,128)(2,1)}) %all-gather.6.cloned.1.call-update) | async-done | bytes 1048592 | tf_op jit(solution)/shard_map/all_gather | solution.py:48
  51.6 6.8 %fusion.28 = f32[128,1536]{1,0:T(8,128)S(1)} fusion(bf16[128,4096]{1,0:T(8,128)(2,1)} %all-gather.6.cloned.1.call-done, bf16[4096,1536]{1,0:T(8,128)(2,1)} %param.10), kind=kOutput, calls=%fused_computation.46 | convolution fusion | flops 1610612736 | bytes 14417920 | tf_op jit(solution)/shard_map/dot_general | solution.py:50
  58.4 6.7 %fusion.27 = f32[128,1536]{1,0:T(8,128)S(1)} fusion(bf16[128,4096]{1,0:T(8,128)(2,1)S(1)} %copy-done.2, bf16[4096,1536]{1,0:T(8,128)(2,1)} %param.11), kind=kOutput, calls=%fused_computation.45 | convolution fusion | flops 1610612736 | bytes 14417920 | tf_op jit(solution)/shard_map/dot_general | solution.py:51
  65.1 26.1 %all-gather.4.cloned.1.call-done = bf16[128,4096]{1,0:T(8,128)(2,1)} async-done(((bf16[8,4096]{1,0:T(8,128)(2,1)}), bf16[128,4096]{1,0:T(8,128)(2,1)}) %all-gather.4.cloned.1.call-update) | async-done | bytes 1048592 | tf_op jit(solution)/shard_map/all_gather | solution.py:49
  91.3 9.4 %multiply_convert_fusion.1 = (bf16[128,1536]{1,0:T(8,128)(2,1)S(1)}, bf16[128,1536]{1,0:T(8,128)(2,1)S(1)}) fusion(f32[128,1536]{1,0:T(8,128)S(1)} %fusion.28, f32[128,1536]{1,0:T(8,128)S(1)} %fusion.27, bf16[128,4096]{1,0:T(8,128)(2,1)} %all-gather.4.cloned.1.call-done, bf16[1536,4096]{1,0:T(8,128)(2,1)} %param.12), kind=kOutput, calls=%fused_computation.5 | convolution fusion | flops 1613168640 | bytes 15990784 | tf_op jit(solution)/shard_map/dot_general | solution.py:27
  100.8 8.6 %fusion.10 = f32[32,4096]{1,0:T(8,128)S(1)} fusion(bf16[4096,1536]{1,0:T(8,128)(2,1)} %param.10, bf16[128,1536]{1,0:T(8,128)(2,1)S(1)} %get-tuple-element.9, s32[]{:T(128)S(6)} %select_n.15), kind=kOutput, calls=%fused_computation.19 | convolution fusion | flops 402653184 | bytes 13205508 | tf_op jit(solution)/shard_map/dot_general | solution.py:27
  109.4 4.5 %fusion = bf16[32,4096]{1,0:T(8,128)(2,1)} fusion(f32[32,4096]{1,0:T(8,128)S(1)} %fusion.10, bf16[4096,1536]{1,0:T(8,128)(2,1)S(1)} %bitcast.21, bf16[128,1536]{1,0:T(8,128)(2,1)S(1)} %get-tuple-element.8, s32[]{:T(128)S(6)} %select_n.15), kind=kOutput, calls=%fused_computation.2 | convolution fusion | flops 402915328 | bytes 13467652 | tf_op jit(solution)/shard_map/dot_general | solution.py:27
  113.9 0.0 all-reduce.3.cloned.1.call-update
  114.0 5.3 %fusion.2 = f32[1536,1024]{1,0:T(8,128)} fusion(f32[128,1536]{1,0:T(8,128)} %copy-done.4, bf16[128,4096]{1,0:T(8,128)(2,1)} %all-gather.4.cloned.1.call-done, s32[]{:T(128)S(6)} %select_n.17, f32[128,1536]{1,0:T(8,128)} %copy-done.3), kind=kOutput, calls=%fused_computation.9 | convolution fusion | flops 403832832 | bytes 8126468 | tf_op jit(solution)/shard_map/dot_general | solution.py:21
  119.3 3.7 %fusion.4 = f32[1024,1536]{1,0:T(8,128)} fusion(bf16[128,1536]{1,0:T(8,128)(2,1)S(1)} %copy-done.8, bf16[128,4096]{1,0:T(8,128)(2,1)S(1)} %copy-done.2, s32[]{:T(128)S(6)} %select_n.17), kind=kOutput, calls=%fused_computation.11 | convolution fusion | flops 402653184 | bytes 6946820 | tf_op jit(solution)/shard_map/dot_general | solution.py:21
  123.0 3.7 %fusion.6 = f32[1024,1536]{1,0:T(8,128)} fusion(bf16[128,1536]{1,0:T(8,128)(2,1)S(1)} %copy-done.6, bf16[128,4096]{1,0:T(8,128)(2,1)S(1)} %copy-done.2, s32[]{:T(128)S(6)} %select_n.17), kind=kOutput, calls=%fused_computation.13 | convolution fusion | flops 402653184 | bytes 6946820 | tf_op jit(solution)/shard_map/dot_general | solution.py:21
  126.7 56.8 %all-reduce.3.cloned.1.call-done = bf16[32,4096]{1,0:T(8,128)(2,1)} async-done(((bf16[32,4096]{1,0:T(8,128)(2,1)}), bf16[32,4096]{1,0:T(8,128)(2,1)}) %all-reduce.3.cloned.1.call-update) | async-done | bytes 262160
  183.6 1.0 multiply_reduce_fusion.2
  184.6 0.9 fusion.13
  185.6 4.6 %all-gather = bf16[2,4,4096]{2,1,0:T(4,128)(2,1)S(1)} all-gather(bf16[1,4,4096]{2,1,0:T(4,128)(2,1)S(1)} %fusion.13), channel_id=1, replica_groups=mesh['rep'=4,'seq'=4,'fsdp'=2] {'fsdp'}, dimensions={0}, use_global_device_ids=true | all-gather | bytes 98304 | tf_op jit(solution)/shard_map/all_gather | solution.py:80
  190.2 1.5 convolution_convert_fusion
  (30 shorter events, 0.2 us)
Async XLA Ops:
  7.2 1.6 copy-start
  7.2 44.4 %all-gather.6.cloned.1.call-start = ((), (), s32[]{:S(2)}) async-start(), calls=%async_computation.1 | async-start | bytes 1114112 | tf_op jit(solution)/shard_map/all_gather | solution.py:48
  10.7 80.5 %all-gather.4.cloned.1.call-start = ((), (), s32[]{:S(2)}) async-start(), calls=%async_computation | async-start | bytes 1114112 | tf_op jit(solution)/shard_map/all_gather | solution.py:49
  13.4 170.2 %all-reduce.3.cloned.1.call-start = ((), (), s32[]{:S(2)}) async-start(), calls=%async_computation.2 | async-start | bytes 524288
  51.6 6.8 %copy-start.2 = (bf16[128,4096]{1,0:T(8,128)(2,1)S(1)}, bf16[128,4096]{1,0:T(8,128)(2,1)}, u32[]{:S(2)}) copy-start(bf16[128,4096]{1,0:T(8,128)(2,1)} %all-gather.6.cloned.1.call-done) | copy-start | bytes 3145732
  58.4 42.3 %copy-start.3 = (f32[128,1536]{1,0:T(8,128)}, f32[128,1536]{1,0:T(8,128)S(1)}, u32[]{:S(2)}) copy-start(f32[128,1536]{1,0:T(8,128)S(1)} %fusion.28) | copy-start | bytes 2359300
  65.1 44.2 %copy-start.4 = (f32[128,1536]{1,0:T(8,128)}, f32[128,1536]{1,0:T(8,128)S(1)}, u32[]{:S(2)}) copy-start(f32[128,1536]{1,0:T(8,128)S(1)} %fusion.27) | copy-start | bytes 2359300
  91.3 18.1 %slice-start = ((s8[12582912]{0:T(1024)(128)(4,1)}), s8[4194304]{0:T(1024)(128)(4,1)S(1)}, s32[]{:S(2)}) async-start(s8[12582912]{0:T(1024)(128)(4,1)} %bitcast.20), calls=%async_computation.3 | async-start | bytes 8388608
  91.3 18.2 %slice-start.1 = ((s8[12582912]{0:T(1024)(128)(4,1)}), s8[4194304]{0:T(1024)(128)(4,1)S(1)}, s32[]{:S(2)}) async-start(s8[12582912]{0:T(1024)(128)(4,1)} %bitcast.20), calls=%async_computation.4 | async-start | bytes 8388608
  100.7 8.7 %copy-start.5 = (bf16[128,1536]{1,0:T(8,128)(2,1)}, bf16[128,1536]{1,0:T(8,128)(2,1)S(1)}, u32[]{:S(2)}) copy-start(bf16[128,1536]{1,0:T(8,128)(2,1)S(1)} %get-tuple-element.9) | copy-start | bytes 1179652
  100.7 8.7 %copy-start.7 = (bf16[128,1536]{1,0:T(8,128)(2,1)}, bf16[128,1536]{1,0:T(8,128)(2,1)S(1)}, u32[]{:S(2)}) copy-start(bf16[128,1536]{1,0:T(8,128)(2,1)S(1)} %get-tuple-element.8) | copy-start | bytes 1179652
  100.7 8.7 %slice-start.2 = ((s8[12582912]{0:T(1024)(128)(4,1)}), s8[4194304]{0:T(1024)(128)(4,1)S(1)}, s32[]{:S(2)}) async-start(s8[12582912]{0:T(1024)(128)(4,1)} %bitcast.20), calls=%async_computation.5 | async-start | bytes 8388608
  113.9 5.4 %copy-start.8 = (bf16[128,1536]{1,0:T(8,128)(2,1)S(1)}, bf16[128,1536]{1,0:T(8,128)(2,1)}, u32[]{:S(2)}) copy-start(bf16[128,1536]{1,0:T(8,128)(2,1)} %copy-done.7) | copy-start | bytes 1179652
  113.9 9.1 %copy-start.6 = (bf16[128,1536]{1,0:T(8,128)(2,1)S(1)}, bf16[128,1536]{1,0:T(8,128)(2,1)}, u32[]{:S(2)}) copy-start(bf16[128,1536]{1,0:T(8,128)(2,1)} %copy-done.5) | copy-start | bytes 1179652
  114.0 77.7 %copy-start.1 = (bf16[256,4096]{1,0:T(8,128)(2,1)S(1)}, bf16[256,4096]{1,0:T(8,128)(2,1)}, u32[]{:S(2)}) copy-start(bf16[256,4096]{1,0:T(8,128)(2,1)} %param.7) | copy-start | bytes 6291460
  119.3 64.3 %copy-start.9 = (f32[4096]{0:T(1024)S(1)}, f32[4096]{0:T(1024)}, u32[]{:S(2)}) copy-start(f32[4096]{0:T(1024)} %param.9) | copy-start | bytes 49156
Sparse Core Ops, SparseCore 0:
  10.9 40.6 all-gather.5
  54.4 36.8 all-gather.3
  114.1 69.4 all-reduce.2

commit v2 on v1

v2 whole, which is shorter than its diff:
```python
from functools import partial

import jax
import jax.numpy as jnp
from jax import lax
from jax.sharding import PartitionSpec as P

REC = 1
MAXACT = 8


EPSILON = 1e-05


def normalize(widened, norm_gain):
    factor = lax.rsqrt(jnp.mean(widened * widened, axis=-1, keepdims=True) + EPSILON)
    return widened * factor * norm_gain


def contract_first(left, right):
    return lax.dot_general(
        left, right, (((0,), (0,)), ((), ())), preferred_element_type=jnp.float32
    )


def contract_last(left, right):
    return lax.dot_general(
        left, right, (((1,), (1,)), ((), ())), preferred_element_type=jnp.float32
    )


def local(tokens, cotangent, norm_gain, gate_weight, up_weight, down_weight, depths):
    parts = lax.axis_size("fsdp")
    place = lax.axis_index("fsdp")
    replicas = lax.axis_size("rep")
    shards = lax.axis_size("seq")
    features = tokens.shape[1]
    feature_share = features // replicas
    rows_here = tokens.shape[0]
    own_rows = rows_here // parts
    active = depths > REC
    ordinal = jnp.cumsum(active.astype(jnp.int32)) - 1
    selector = (ordinal[None, :] == jnp.arange(MAXACT, dtype=jnp.int32)[:, None]) & active[None, :]
    picker = selector.astype(jnp.bfloat16)
    source = jnp.dot(picker, tokens, preferred_element_type=jnp.float32)
    send_masked = jnp.dot(picker, cotangent, preferred_element_type=jnp.float32).astype(jnp.bfloat16)
    send_normed = normalize(source, norm_gain).astype(jnp.bfloat16)
    packed = lax.all_gather(
        jnp.concatenate([send_normed, send_masked], axis=0), "seq", axis=0, tiled=False
    )
    window_normed = packed[:, :MAXACT].reshape(shards * MAXACT, features)
    window_masked = packed[:, MAXACT:].reshape(shards * MAXACT, features)
    window = window_normed.shape[0]
    gate = jnp.dot(window_normed, gate_weight, preferred_element_type=jnp.float32)
    up = jnp.dot(window_normed, up_weight, preferred_element_type=jnp.float32)
    sigmoid_gate = jax.nn.sigmoid(gate)
    swished = gate * sigmoid_gate
    hidden = (swished * up).astype(jnp.bfloat16)
    hidden_grad = contract_last(window_masked, down_weight)
    gate_rows = (hidden_grad * up * sigmoid_gate * (1.0 + gate * (1.0 - sigmoid_gate))).astype(
        jnp.bfloat16
    )
    up_rows = (hidden_grad * swished).astype(jnp.bfloat16)
    partial_features = contract_last(gate_rows, gate_weight) + contract_last(up_rows, up_weight)
    outgoing = jnp.broadcast_to(
        partial_features.astype(jnp.bfloat16).reshape(shards, 1, MAXACT, features),
        (shards, parts, MAXACT, features),
    ).reshape(shards * parts, MAXACT, features)
    incoming = lax.all_to_all(outgoing, ("seq", "fsdp"), 0, 0, tiled=True)
    feature_grad = jnp.sum(incoming.astype(jnp.float32), axis=0)
    factors = lax.all_gather(
        jnp.concatenate([gate_rows, up_rows, hidden], axis=0), "rep", axis=0, tiled=False
    )
    every_gate = factors[:, :window].reshape(replicas * window, -1)
    every_up = factors[:, window : 2 * window].reshape(replicas * window, -1)
    every_hidden = factors[:, 2 * window :].reshape(replicas * window, -1)
    columns = jnp.concatenate([window_normed, window_masked], axis=0)
    columns = columns.reshape(2 * window, replicas, feature_share).transpose(1, 0, 2)
    columns = lax.all_to_all(columns, "rep", 0, 0, tiled=True)
    normed_cols = columns[:, :window].reshape(replicas * window, feature_share)
    masked_cols = columns[:, window:].reshape(replicas * window, feature_share)
    gate_grad = contract_first(normed_cols, every_gate)
    up_grad = contract_first(normed_cols, every_up)
    down_grad = contract_first(every_hidden, masked_cols)
    _, pullback = jax.vjp(partial(normalize, norm_gain=norm_gain), source)
    slot_grad = pullback(feature_grad)[0].astype(jnp.bfloat16)
    own_columns = lax.dynamic_slice_in_dim(picker, place * own_rows, own_rows, 1)
    branch_grad = contract_first(own_columns, slot_grad).astype(jnp.bfloat16)
    return (branch_grad, gate_grad, up_grad, down_grad)


def solution(mesh):
    in_specs = (
        P(("rep", "seq"), None),
        P(("rep", "seq"), None),
        P(),
        P(None, ("seq", "fsdp")),
        P(None, ("seq", "fsdp")),
        P(("seq", "fsdp"), None),
        P(("rep", "seq")),
    )
    out_specs = (
        P(("rep", "seq", "fsdp"), None),
        P("rep", ("seq", "fsdp")),
        P("rep", ("seq", "fsdp")),
        P(("seq", "fsdp"), "rep"),
    )
    return jax.shard_map(local, mesh=mesh, in_specs=in_specs, out_specs=out_specs, check_vma=False)
```

time: 199 us -> 112 us (0.56)
  waiting for transfers between devices: 119 us -> 16.4 us
  blocking collectives: 4.59 us -> 17.4 us
  starting transfers between devices: 0.12 us -> 9.98 us
  matrix products: 53.3 us -> 45.9 us
  local copies, waits for them, and re-layouts: 1.65 us -> 4.14 us
    all_gather x2 -> x1, waiting for transfers between devices: 62.3 us -> 0.01 us  [local(): lax.all_gather(jnp.concatenate([gate_rows, up_rows, hidden], axis=0), 're...]
    unnamed x4 -> x1, waiting for transfers between devices: 56.9 us -> 0.02 us
    all_to_all x0 -> x2, waiting for transfers between devices: none -> 16.4 us  [the longest x1 9.44 us: local(): incoming = lax.all_to_all(outgoing, ('seq', 'fsdp'), 0, 0, tiled=True)]
    all_gather x1, blocking collectives: 4.59 us -> 17.4 us  [local(): lax.all_gather(jnp.concatenate([send_normed, send_masked], axis=0), 'seq'...]
    all_to_all x0 -> x2, starting transfers between devices: none -> 9.94 us  [the longest x1 6.29 us: local(): incoming = lax.all_to_all(outgoing, ('seq', 'fsdp'), 0, 0, tiled=True)]
    dot_general x2, matrix products: 13.5 us -> 4.35 us  [the longest x1 2.19 us: local(): up = jnp.dot(window_normed, up_weight, preferred_element_type=jnp.float32)]
    dot_general x3, matrix products: 22.5 us -> 25.4 us  [contract_last(): lax.dot_general(left, right, (((1,), (1,)), ((), ())), preferred_element_...]
  transfers between devices with their start and end apart: 3 -> 3, of which waited for: 3 -> 2; matrix products, arithmetic and copies ran while one was open for 15% -> 19% of each run, Pallas kernels for 0% -> 0%
where the time goes in v2:
time: 112 us
  matrix products  45.9 us (41%)
  blocking collectives  17.4 us (16%)
  waiting for transfers between devices  16.4 us (15%)
  between operations  14.2 us (13%)
  starting transfers between devices  9.98 us (9%)
  local copies, waits for them, and re-layouts  4.14 us (4%)
  other arithmetic  3.87 us (3%)
    dot_general x3, matrix products, contract_last(): lax.dot_general(left, right, (((1,), (1,)), ((), ())), preferred_element_...  25.4 us
    all_gather x1, blocking collectives, local(): lax.all_gather(jnp.concatenate([send_normed, send_masked], axis=0), 'seq'...  17.4 us
    dot_general x4, matrix products, contract_first(): lax.dot_general(left, right, (((0,), (0,)), ((), ())), preferred_element_...  13.7 us
    all_to_all x1, waiting for transfers between devices, local(): incoming = lax.all_to_all(outgoing, ('seq', 'fsdp'), 0, 0, tiled=True)  9.44 us
    all_to_all x1, waiting for transfers between devices, local(): columns = lax.all_to_all(columns, 'rep', 0, 0, tiled=True)  6.92 us
    all_to_all x1, starting transfers between devices, local(): incoming = lax.all_to_all(outgoing, ('seq', 'fsdp'), 0, 0, tiled=True)  6.29 us
    all_to_all x1, starting transfers between devices, local(): columns = lax.all_to_all(columns, 'rep', 0, 0, tiled=True)  3.65 us
    unnamed x12, local copies, waits for them, and re-layouts  2.56 us
  transfers between devices with their start and end apart: 3, of which 2 were waited for; matrix products, arithmetic and copies ran while one was open for 19% of the time, Pallas kernels for 0%

profile of v2, /device:TPU:0, one launch (start us, length us, event | category | flops | bytes accessed | tf_op | source)
XLA Modules:
  0.0 111.8 jit_solution(18228367559652819452)
XLA Ops:
  7.2 0.8 convert_bitcast_fusion
  8.1 0.3 reduce-window.9
  8.4 0.1 slice.28
  8.5 0.1 slice_reduce_fusion
  8.6 0.1 add_bitcast_fusion
  8.7 0.1 copy-done
  8.8 0.5 multiply_reduce_fusion.1
  9.3 2.0 %convolution_convert_fusion.1 = bf16[8,4096]{1,0:T(8,128)(2,1)S(1)} fusion(bf16[256,4096]{1,0:T(8,128)(2,1)} %param.8, s32[256]{0:T(256)S(1)} %add_bitcast_fusion, pred[256]{0:T(512)(128)(4,1)S(1)} %get-tuple-element.5), kind=kOutput, calls=%fused_computation.4 | convolution fusion | flops 16814080 | bytes 2163968 | tf_op jit(solution)/shard_map/dot_general | solution.py:46
  11.3 0.8 multiply_convert_fusion.3
  12.1 17.4 %all-gather = bf16[64,4096]{1,0:T(8,128)(2,1)S(1)} all-gather(bf16[16,4096]{1,0:T(8,128)(2,1)S(1)} %pad_maximum_fusion.1), channel_id=2, replica_groups=mesh['rep'=4,'seq'=4,'fsdp'=2] {'seq'}, dimensions={0}, use_global_device_ids=true | all-gather | bytes 655360 | tf_op jit(solution)/shard_map/all_gather | solution.py:48
  29.5 8.5 %fusion.10 = f32[32,1536]{1,0:T(8,128)S(1)} fusion(bf16[1536,4096]{1,0:T(8,128)(2,1)} %param.12, bf16[4,16,4096]{2,1,0:T(8,128)(2,1)S(1)} %bitcast.36), kind=kOutput, calls=%fused_computation.19 | convolution fusion | flops 402653184 | bytes 13041664 | tf_op jit(solution)/shard_map/dot_general | solution.py:27
  38.0 2.2 %fusion.6 = f32[32,1536]{1,0:T(8,128)S(1)} fusion(bf16[4096,1536]{1,0:T(8,128)(2,1)S(1)} %copy-done.2, bf16[4,16,4096]{2,1,0:T(8,128)(2,1)S(1)} %bitcast.37), kind=kOutput, calls=%fused_computation.15 | convolution fusion | flops 402653184 | bytes 13041664 | tf_op jit(solution)/shard_map/dot_general | solution.py:54
  40.2 2.4 %copy-done.3 = bf16[4096,1536]{1,0:T(8,128)(2,1)S(1)} copy-done((bf16[4096,1536]{1,0:T(8,128)(2,1)S(1)}, bf16[4096,1536]{1,0:T(8,128)(2,1)}, u32[]{:S(2)}) %copy-start.3) | copy-done | bytes 12582936
  42.6 2.2 %multiply_convert_fusion = (bf16[32,1536]{1,0:T(8,128)(2,1)S(1)}, bf16[32,1536]{1,0:T(8,128)(2,1)S(1)}, bf16[32,1536]{1,0:T(8,128)(2,1)S(1)}) fusion(f32[32,1536]{1,0:T(8,128)S(1)} %fusion.6, f32[32,1536]{1,0:T(8,128)S(1)} %fusion.10, bf16[4096,1536]{1,0:T(8,128)(2,1)S(1)} %copy-done.3, bf16[4,16,4096]{2,1,0:T(8,128)(2,1)S(1)} %bitcast.38), kind=kOutput, calls=%fused_computation.23 | convolution fusion | flops 403390464 | bytes 13533184 | tf_op jit(solution)/shard_map/dot_general | solution.py:55
  44.8 0.7 pad_maximum_fusion
  45.5 8.3 %fusion.31 = f32[32,4096]{1,0:T(8,128)S(1)} fusion(bf16[32,1536]{1,0:T(8,128)(2,1)S(1)} %get-tuple-element.9, bf16[4096,1536]{1,0:T(8,128)(2,1)} %param.10), kind=kOutput, calls=%fused_computation.53 | convolution fusion | flops 402653184 | bytes 13205504 | tf_op jit(solution)/shard_map/dot_general | solution.py:27
  53.8 8.6 %fusion.1 = bf16[4,8,4096]{2,1,0:T(8,128)(2,1)S(1)} fusion(f32[32,4096]{1,0:T(8,128)S(1)} %fusion.31, bf16[32,1536]{1,0:T(8,128)(2,1)S(1)} %get-tuple-element.10, bf16[4096,1536]{1,0:T(8,128)(2,1)} %param.11), kind=kOutput, calls=%fused_computation.3 | convolution fusion | flops 402915328 | bytes 13467648 | tf_op jit(solution)/shard_map/dot_general | solution.py:27
  62.4 0.8 broadcast_in_dim.7
  63.2 6.3 %all-to-all-start = ((bf16[8,8,4096]{2,1,0:T(8,128)(2,1)}), bf16[8,8,4096]{2,1,0:T(8,128)(2,1)S(1)}, u32[]{:S(2)}, u32[]{:S(2)}) async-start(bf16[8,8,4096]{2,1,0:T(8,128)(2,1)} %bitcast.6), calls=%async_computation | async-start | bytes 1048576 | tf_op jit(solution)/shard_map/all_to_all | solution.py:69
  69.6 0.2 concatenate.15
  69.8 0.1 copy.13
  69.8 0.2 concatenate.16
  70.0 0.1 copy.14
  70.1 0.8 maximum_bitcast_fusion
  71.0 9.4 %all-to-all-done = bf16[8,8,4096]{2,1,0:T(8,128)(2,1)S(1)} async-done(((bf16[8,8,4096]{2,1,0:T(8,128)(2,1)}), bf16[8,8,4096]{2,1,0:T(8,128)(2,1)S(1)}, u32[]{:S(2)}, u32[]{:S(2)}) %all-to-all-start) | async-done | bytes 524320 | tf_op jit(solution)/shard_map/all_to_all | solution.py:69
  80.4 3.7 %all-to-all-start.1 = ((bf16[4,64,1024]{2,1,0:T(8,128)(2,1)}), bf16[4,64,1024]{2,1,0:T(8,128)(2,1)S(1)}, u32[]{:S(2)}, u32[]{:S(2)}) async-start(bf16[4,64,1024]{2,1,0:T(8,128)(2,1)} %maximum_bitcast_fusion), calls=%async_computation.1 | async-start | bytes 1048576 | tf_op jit(solution)/shard_map/all_to_all | solution.py:79
  84.1 0.1 multiply_reduce_fusion
  84.3 1.5 %convolution_convert_fusion = bf16[128,4096]{1,0:T(8,128)(2,1)} fusion(f32[8,4096]{1,0:T(8,128)S(1)} %get-tuple-element.12, f32[8,4096]{1,0:T(8,128)S(1)} %convert_reduce_fusion, f32[8]{0:T(128)S(1)} %multiply_multiply_fusion, f32[4096]{0:T(1024)S(1)} %copy-done.4, f32[8]{0:T(128)S(1)} %fusion.23, pred[8,256]{1,0:T(8,128)(4,1)S(1)} %fusion.20, s32[]{:T(128)S(6)} %select_n.3), kind=kOutput, calls=%fused_computation | convolution fusion | flops 9109504 | bytes 1329156 | tf_op jit(solution)/shard_map/dot_general | solution.py:21
  85.8 6.9 %all-to-all-done.1 = bf16[4,64,1024]{2,1,0:T(8,128)(2,1)S(1)} async-done(((bf16[4,64,1024]{2,1,0:T(8,128)(2,1)}), bf16[4,64,1024]{2,1,0:T(8,128)(2,1)S(1)}, u32[]{:S(2)}, u32[]{:S(2)}) %all-to-all-start.1) | async-done | bytes 524320 | tf_op jit(solution)/shard_map/all_to_all | solution.py:79
  92.7 4.8 %convolution_bitcast_fusion = f32[1536,1024]{1,0:T(8,128)} fusion(bf16[4,96,1536]{2,1,0:T(8,128)(2,1)} %bitcast.40, bf16[4,64,1024]{2,1,0:T(8,128)(2,1)S(1)} %all-to-all-done.1), kind=kOutput, calls=%fused_computation.5 | convolution fusion | flops 402653184 | bytes 6946816 | tf_op jit(solution)/shard_map/dot_general | solution.py:21
  97.5 3.7 %convolution_bitcast_fusion.1 = f32[1024,1536]{1,0:T(8,128)} fusion(bf16[4,96,1536]{2,1,0:T(8,128)(2,1)S(1)} %bitcast.41, bf16[4,64,1024]{2,1,0:T(8,128)(2,1)S(1)} %all-to-all-done.1), kind=kOutput, calls=%fused_computation.6 | convolution fusion | flops 402653184 | bytes 6946816 | tf_op jit(solution)/shard_map/dot_general | solution.py:21
  101.2 3.7 %convolution_bitcast_fusion.2 = f32[1024,1536]{1,0:T(8,128)} fusion(bf16[4,96,1536]{2,1,0:T(8,128)(2,1)S(1)} %bitcast.42, bf16[4,64,1024]{2,1,0:T(8,128)(2,1)S(1)} %all-to-all-done.1), kind=kOutput, calls=%fused_computation.7 | convolution fusion | flops 402653184 | bytes 6946816 | tf_op jit(solution)/shard_map/dot_general | solution.py:21
  (20 shorter events, 0.3 us)
Async XLA Ops:
  7.2 1.6 %copy-start = (bf16[256,4096]{1,0:T(8,128)(2,1)S(1)}, bf16[256,4096]{1,0:T(8,128)(2,1)}, u32[]{:S(2)}) copy-start(bf16[256,4096]{1,0:T(8,128)(2,1)} %param.7) | copy-start | bytes 6291460
  7.2 85.5 %all-gather.4.cloned.1.call-start = ((), (), s32[]{:S(2)}) async-start(), calls=%async_computation.2 | async-start | bytes 1474560 | tf_op jit(solution)/shard_map/all_gather | solution.py:71
  29.5 8.5 %copy-start.2 = (bf16[4096,1536]{1,0:T(8,128)(2,1)S(1)}, bf16[4096,1536]{1,0:T(8,128)(2,1)}, u32[]{:S(2)}) copy-start(bf16[4096,1536]{1,0:T(8,128)(2,1)} %param.10) | copy-start | bytes 37748740
  38.0 4.6 %copy-start.3 = (bf16[4096,1536]{1,0:T(8,128)(2,1)S(1)}, bf16[4096,1536]{1,0:T(8,128)(2,1)}, u32[]{:S(2)}) copy-start(bf16[4096,1536]{1,0:T(8,128)(2,1)} %param.11) | copy-start | bytes 37748740
  62.4 21.7 %copy-start.4 = (f32[4096]{0:T(1024)S(1)}, f32[4096]{0:T(1024)}, u32[]{:S(2)}) copy-start(f32[4096]{0:T(1024)} %param.9) | copy-start | bytes 49156
  63.2 17.2 %all-to-all-start = ((bf16[8,8,4096]{2,1,0:T(8,128)(2,1)}), bf16[8,8,4096]{2,1,0:T(8,128)(2,1)S(1)}, u32[]{:S(2)}, u32[]{:S(2)}) async-start(bf16[8,8,4096]{2,1,0:T(8,128)(2,1)} %bitcast.6), calls=%async_computation | async-start | bytes 1048576 | tf_op jit(solution)/shard_map/all_to_all | solution.py:69
  80.4 12.3 %all-to-all-start.1 = ((bf16[4,64,1024]{2,1,0:T(8,128)(2,1)}), bf16[4,64,1024]{2,1,0:T(8,128)(2,1)S(1)}, u32[]{:S(2)}, u32[]{:S(2)}) async-start(bf16[4,64,1024]{2,1,0:T(8,128)(2,1)} %maximum_bitcast_fusion), calls=%async_computation.1 | async-start | bytes 1048576 | tf_op jit(solution)/shard_map/all_to_all | solution.py:79
  92.7 4.8 %copy-start.5 = (bf16[384,1536]{1,0:T(8,128)(2,1)S(1)}, bf16[384,1536]{1,0:T(8,128)(2,1)}, u32[]{:S(2)}) copy-start(bf16[384,1536]{1,0:T(8,128)(2,1)} %all-gather.4.cloned.1.call-done) | copy-start | bytes 3538948
  97.5 7.4 %copy-start.1 = (bf16[256,4096]{1,0:T(8,128)(2,1)S(1)}, bf16[256,4096]{1,0:T(8,128)(2,1)}, u32[]{:S(2)}) copy-start(bf16[256,4096]{1,0:T(8,128)(2,1)} %param.7) | copy-start | bytes 6291460
Sparse Core Ops, SparseCore 0:
  45.7 19.2 all-gather.3

commit v3 on v2

--- a/solution.py
+++ b/solution.py
@@ -29,6 +29,25 @@
     )
 
 
+def shifted(value, axes, sizes, steps):
+    total = 1
+    for size in sizes:
+        total *= size
+    pairs = []
+    for index in range(total):
+        coords, rest = [], index
+        for size in reversed(sizes):
+            coords.append(rest % size)
+            rest //= size
+        coords = coords[::-1]
+        target, scale = 0, 1
+        for axis in reversed(range(len(sizes))):
+            target += ((coords[axis] + steps[axis]) % sizes[axis]) * scale
+            scale *= sizes[axis]
+        pairs.append((index, target))
+    return lax.ppermute(value, axes, pairs)
+
+
 def local(tokens, cotangent, norm_gain, gate_weight, up_weight, down_weight, depths):
     parts = lax.axis_size("fsdp")
     place = lax.axis_index("fsdp")
@@ -45,11 +64,10 @@
     source = jnp.dot(picker, tokens, preferred_element_type=jnp.float32)
     send_masked = jnp.dot(picker, cotangent, preferred_element_type=jnp.float32).astype(jnp.bfloat16)
     send_normed = normalize(source, norm_gain).astype(jnp.bfloat16)
-    packed = lax.all_gather(
-        jnp.concatenate([send_normed, send_masked], axis=0), "seq", axis=0, tiled=False
-    )
-    window_normed = packed[:, :MAXACT].reshape(shards * MAXACT, features)
-    window_masked = packed[:, MAXACT:].reshape(shards * MAXACT, features)
+    packed = jnp.concatenate([send_normed, send_masked], axis=0)
+    blocks = [packed] + [shifted(packed, "seq", (shards,), (k,)) for k in range(1, shards)]
+    window_normed = jnp.concatenate([b[:MAXACT] for b in blocks], axis=0)
+    window_masked = jnp.concatenate([b[MAXACT:] for b in blocks], axis=0)
     window = window_normed.shape[0]
     gate = jnp.dot(window_normed, gate_weight, preferred_element_type=jnp.float32)
     up = jnp.dot(window_normed, up_weight, preferred_element_type=jnp.float32)
@@ -61,24 +79,32 @@
         jnp.bfloat16
     )
     up_rows = (hidden_grad * swished).astype(jnp.bfloat16)
-    partial_features = contract_last(gate_rows, gate_weight) + contract_last(up_rows, up_weight)
-    outgoing = jnp.broadcast_to(
-        partial_features.astype(jnp.bfloat16).reshape(shards, 1, MAXACT, features),
-        (shards, parts, MAXACT, features),
-    ).reshape(shards * parts, MAXACT, features)
-    incoming = lax.all_to_all(outgoing, ("seq", "fsdp"), 0, 0, tiled=True)
-    feature_grad = jnp.sum(incoming.astype(jnp.float32), axis=0)
-    factors = lax.all_gather(
-        jnp.concatenate([gate_rows, up_rows, hidden], axis=0), "rep", axis=0, tiled=False
-    )
-    every_gate = factors[:, :window].reshape(replicas * window, -1)
-    every_up = factors[:, window : 2 * window].reshape(replicas * window, -1)
-    every_hidden = factors[:, 2 * window :].reshape(replicas * window, -1)
+    factors = jnp.concatenate([gate_rows, up_rows, hidden], axis=0)
     columns = jnp.concatenate([window_normed, window_masked], axis=0)
-    columns = columns.reshape(2 * window, replicas, feature_share).transpose(1, 0, 2)
-    columns = lax.all_to_all(columns, "rep", 0, 0, tiled=True)
-    normed_cols = columns[:, :window].reshape(replicas * window, feature_share)
-    masked_cols = columns[:, window:].reshape(replicas * window, feature_share)
+    columns = columns.reshape(2 * window, replicas, feature_share)
+    replica = lax.axis_index("rep")
+    every_factors = [factors]
+    every_columns = [lax.dynamic_index_in_dim(columns, replica, 1, keepdims=False)]
+    for j in range(1, replicas):
+        every_factors.append(shifted(factors, "rep", (replicas,), (j,)))
+        outgoing = lax.dynamic_index_in_dim(columns, (replica + j) % replicas, 1, keepdims=False)
+        every_columns.append(shifted(outgoing, "rep", (replicas,), (j,)))
+    partial_features = (
+        contract_last(gate_rows, gate_weight) + contract_last(up_rows, up_weight)
+    ).astype(jnp.bfloat16)
+    feature_grad = partial_features[:MAXACT].astype(jnp.float32)
+    for k in range(shards):
+        piece = partial_features[k * MAXACT : (k + 1) * MAXACT]
+        for step in range(parts):
+            if k == 0 and step == 0:
+                continue
+            arrived = shifted(piece, ("seq", "fsdp"), (shards, parts), (-k, step))
+            feature_grad = feature_grad + arrived.astype(jnp.float32)
+    every_gate = jnp.concatenate([f[:window] for f in every_factors], axis=0)
+    every_up = jnp.concatenate([f[window : 2 * window] for f in every_factors], axis=0)
+    every_hidden = jnp.concatenate([f[2 * window :] for f in every_factors], axis=0)
+    normed_cols = jnp.concatenate([c[:window] for c in every_columns], axis=0)
+    masked_cols = jnp.concatenate([c[window:] for c in every_columns], axis=0)
     gate_grad = contract_first(normed_cols, every_gate)
     up_grad = contract_first(normed_cols, every_up)
     down_grad = contract_first(every_hidden, masked_cols)

time: 112 us -> 99.7 us (0.89); the launches traced: 112 us -> 98 us
  blocking collectives: 17.4 us -> 0 us
  starting transfers between devices: 9.98 us -> 24.2 us
  between operations: 14.2 us -> 0.89 us
  waiting for transfers between devices: 16.4 us -> 24 us
  local copies, waits for them, and re-layouts: 4.14 us -> 2.21 us
  other arithmetic: 3.87 us -> 2.32 us
  matrix products: 45.9 us -> 44.5 us
    ppermute x0 -> x16, starting transfers between devices: none -> 24.2 us  [shifted(): return lax.ppermute(value, axes, pairs)]
    ppermute x0 -> x16, waiting for transfers between devices: none -> 24 us  [shifted(): return lax.ppermute(value, axes, pairs)]
    all_gather x1 -> x0, blocking collectives: 17.4 us -> none  [local(): lax.all_gather(jnp.concatenate([send_normed, send_masked], axis=0), 'seq'...]
    all_to_all x2 -> x0, waiting for transfers between devices: 16.4 us -> none  [the longest x1 9.44 us: local(): incoming = lax.all_to_all(outgoing, ('seq', 'fsdp'), 0, 0, tiled=True)]
    all_to_all x2 -> x0, starting transfers between devices: 9.94 us -> none  [the longest x1 6.29 us: local(): incoming = lax.all_to_all(outgoing, ('seq', 'fsdp'), 0, 0, tiled=True)]
    dot_general x3, matrix products: 25.4 us -> 20.5 us  [contract_last(): lax.dot_general(left, right, (((1,), (1,)), ((), ())), preferred_element_...]
    dot_general x1, matrix products: 2.19 us -> 6.76 us  [local(): up = jnp.dot(window_normed, up_weight, preferred_element_type=jnp.float32)]
    unnamed x12 -> x17, local copies, waits for them, and re-layouts: 2.56 us -> 0.38 us
  transfers between devices with their start and end apart: 3 -> 16, of which waited for: 2 -> 7; matrix products, arithmetic and copies ran while one was open for 19% -> 4% of each run, Pallas kernels for 0% -> 0%
where the time goes in v3:
time: 99.7 us; the launch traced here: 98 us
  matrix products  44.5 us (45%)
  starting transfers between devices  24.2 us (24%)
  waiting for transfers between devices  24 us (24%)
  other arithmetic  2.32 us (2%)
  local copies, waits for them, and re-layouts  2.21 us (2%)
    ppermute x16, starting transfers between devices, shifted(): return lax.ppermute(value, axes, pairs)  24.2 us
    ppermute x16, waiting for transfers between devices, shifted(): return lax.ppermute(value, axes, pairs)  24 us
    dot_general x3, matrix products, contract_last(): lax.dot_general(left, right, (((1,), (1,)), ((), ())), preferred_element_...  20.5 us
    dot_general x4, matrix products, contract_first(): lax.dot_general(left, right, (((0,), (0,)), ((), ())), preferred_element_...  12.6 us
    dot_general x1, matrix products, local(): up = jnp.dot(window_normed, up_weight, preferred_element_type=jnp.float32)  6.76 us
    dot_general x1, matrix products, local(): jnp.dot(window_normed, gate_weight, preferred_element_type=jnp.float32)  2.16 us
  transfers between devices with their start and end apart: 16, of which 7 were waited for; matrix products, arithmetic and copies ran while one was open for 4% of the time, Pallas kernels for 0%

profile of v3, /device:TPU:0, one launch (start us, length us, event | category | flops | bytes accessed | tf_op | source)
XLA Modules:
  0.0 98.0 jit_solution(9670180126378245356)
XLA Ops:
  0.6 0.8 convert_bitcast_fusion
  2.8 2.0 %convolution_convert_fusion.1 = bf16[8,4096]{1,0:T(8,128)(2,1)S(1)} fusion(bf16[256,4096]{1,0:T(8,128)(2,1)} %param.8, s32[256]{0:T(256)S(1)} %add_bitcast_fusion, pred[256]{0:T(512)(128)(4,1)S(1)} %get-tuple-element.9), kind=kOutput, calls=%fused_computation.3 | convolution fusion | flops 16814080 | bytes 2163968 | tf_op jit(solution)/shard_map/dot_general | solution.py:65
  4.7 0.8 constant_dynamic-update-slice_fusion.7
  5.6 3.1 %collective-permute-start = (bf16[16,4096]{1,0:T(8,128)(2,1)S(1)}, bf16[16,4096]{1,0:T(8,128)(2,1)S(1)}, u32[]{:S(2)}, u32[]{:S(2)}) collective-permute-start(bf16[16,4096]{1,0:T(8,128)(2,1)S(1)} %pad_maximum_fusion.3), channel_id=1, source_target_pairs={{0,2},{2,4},{4,6},{6,0},{1,3},{3,5},{5,7},{7,1},{8,10},{10,12},{12... | collective-permute-start | bytes 393224 | tf_op jit(solution)/shard_map/ppermute | solution.py:48
  8.6 2.6 %collective-permute-start.1 = (bf16[16,4096]{1,0:T(8,128)(2,1)S(1)}, bf16[16,4096]{1,0:T(8,128)(2,1)S(1)}, u32[]{:S(2)}, u32[]{:S(2)}) collective-permute-start(bf16[16,4096]{1,0:T(8,128)(2,1)S(1)} %pad_maximum_fusion.3), channel_id=1, source_target_pairs={{0,4},{2,6},{4,0},{6,2},{1,5},{3,7},{5,1},{7,3},{8,12},{10,14},{12... | collective-permute-start | bytes 393224 | tf_op jit(solution)/shard_map/ppermute | solution.py:48
  11.2 1.3 %collective-permute-start.2 = (bf16[16,4096]{1,0:T(8,128)(2,1)S(1)}, bf16[16,4096]{1,0:T(8,128)(2,1)S(1)}, u32[]{:S(2)}, u32[]{:S(2)}) collective-permute-start(bf16[16,4096]{1,0:T(8,128)(2,1)S(1)} %pad_maximum_fusion.3), channel_id=1, source_target_pairs={{0,6},{2,0},{4,2},{6,4},{1,7},{3,1},{5,3},{7,5},{8,14},{10,8},{12,... | collective-permute-start | bytes 393224 | tf_op jit(solution)/shard_map/ppermute | solution.py:48
  12.6 2.5 %collective-permute-done = bf16[16,4096]{1,0:T(8,128)(2,1)S(1)} collective-permute-done((bf16[16,4096]{1,0:T(8,128)(2,1)S(1)}, bf16[16,4096]{1,0:T(8,128)(2,1)S(1)}, u32[]{:S(2)}, u32[]{:S(2)}) %collective-permute-start) | collective-permute-done | bytes 131104 | tf_op jit(solution)/shard_map/ppermute | solution.py:48
  15.1 4.8 %collective-permute-done.1 = bf16[16,4096]{1,0:T(8,128)(2,1)S(1)} collective-permute-done((bf16[16,4096]{1,0:T(8,128)(2,1)S(1)}, bf16[16,4096]{1,0:T(8,128)(2,1)S(1)}, u32[]{:S(2)}, u32[]{:S(2)}) %collective-permute-start.1) | collective-permute-done | bytes 131104 | tf_op jit(solution)/shard_map/ppermute | solution.py:48
  20.0 8.4 %fusion.25 = f32[32,1536]{1,0:T(8,128)S(1)} fusion(bf16[1536,4096]{1,0:T(8,128)(2,1)} %param.12, bf16[8,4096]{1,0:T(8,128)(2,1)S(1)} %get-tuple-element.39, bf16[8,4096]{1,0:T(8,128)(2,1)S(1)} %get-tuple-element.42, bf16[8,4096]{1,0:T(8,128)(2,1)S(1)} %get-tuple-element.45, bf16[8,4096]{1,0:T(8,128)(2,1)S(1)} %convolution_convert_fusion.1), kind=kOutput, calls=%fused_computation.29 | convolution fusion | flops 403701760 | bytes 13041664 | tf_op jit(solution)/shard_map/dot_general | solution.py:27
  28.4 2.2 %fusion.45 = f32[32,1536]{1,0:T(8,128)S(1)} fusion(bf16[4096,1536]{1,0:T(8,128)(2,1)S(1)} %copy-done.2, bf16[8,4096]{1,0:T(8,128)(2,1)S(1)} %get-tuple-element.38, bf16[8,4096]{1,0:T(8,128)(2,1)S(1)} %get-tuple-element.41, bf16[8,4096]{1,0:T(8,128)(2,1)S(1)} %get-tuple-element.44, bf16[8,4096]{1,0:T(8,128)(2,1)S(1)} %get-tuple-element.5), kind=kOutput, calls=%fused_computation.65 | convolution fusion | flops 403701760 | bytes 13041664 | tf_op jit(solution)/shard_map/dot_general | solution.py:72
  30.5 6.8 %multiply_convert_fusion = (bf16[32,1536]{1,0:T(8,128)(2,1)S(1)}, bf16[32,1536]{1,0:T(8,128)(2,1)S(1)}, bf16[32,1536]{1,0:T(8,128)(2,1)S(1)}) fusion(f32[32,1536]{1,0:T(8,128)S(1)} %fusion.45, f32[32,1536]{1,0:T(8,128)S(1)} %fusion.25, bf16[4096,1536]{1,0:T(8,128)(2,1)} %param.11, bf16[8,4096]{1,0:T(8,128)(2,1)S(1)} %get-tuple-element.38, ...), kind=kOutput, calls=%fused_computation.46 | convolution fusion | flops 404439040 | bytes 13533184 | tf_op jit(solution)/shard_map/dot_general | solution.py:73
  37.3 3.7 %fusion.67 = f32[32,4096]{1,0:T(8,128)S(1)} fusion(bf16[32,1536]{1,0:T(8,128)(2,1)S(1)} %get-tuple-element.16, bf16[4096,1536]{1,0:T(8,128)(2,1)S(1)} %copy-done.2), kind=kOutput, calls=%fused_computation.105 | convolution fusion | flops 402653184 | bytes 13205504 | tf_op jit(solution)/shard_map/dot_general | solution.py:27
  41.0 8.4 %fusion = bf16[32,4096]{1,0:T(8,128)(2,1)S(1)} fusion(f32[32,4096]{1,0:T(8,128)S(1)} %fusion.67, bf16[32,1536]{1,0:T(8,128)(2,1)S(1)} %get-tuple-element.17, bf16[4096,1536]{1,0:T(8,128)(2,1)} %param.11), kind=kOutput, calls=%fused_computation.2 | convolution fusion | flops 402915328 | bytes 13467648 | tf_op jit(solution)/shard_map/dot_general | solution.py:27
  49.4 4.4 %collective-permute-start.4 = (bf16[8,4096]{1,0:T(8,128)(2,1)S(1)}, bf16[8,4096]{1,0:T(8,128)(2,1)S(1)}, u32[]{:S(2)}, u32[]{:S(2)}) collective-permute-start(bf16[8,4096]{1,0:T(8,128)(2,1)S(1)} %get-tuple-element.30), channel_id=1, source_target_pairs={{0,6},{1,7},{2,0},{3,1},{4,2},{5,3},{6,4},{7,5},{8,14},{9,15},{10,... | collective-permute-start | bytes 196616 | tf_op jit(solution)/shard_map/ppermute | solution.py:48
  53.8 1.0 %collective-permute-start.5 = (bf16[8,4096]{1,0:T(8,128)(2,1)S(1)}, bf16[8,4096]{1,0:T(8,128)(2,1)S(1)}, u32[]{:S(2)}, u32[]{:S(2)}) collective-permute-start(bf16[8,4096]{1,0:T(8,128)(2,1)S(1)} %get-tuple-element.30), channel_id=1, source_target_pairs={{0,7},{1,6},{2,1},{3,0},{4,3},{5,2},{6,5},{7,4},{8,15},{9,14},{10,... | collective-permute-start | bytes 196616 | tf_op jit(solution)/shard_map/ppermute | solution.py:48
  55.2 2.5 %collective-permute-start.7 = (bf16[8,4096]{1,0:T(8,128)(2,1)S(1)}, bf16[8,4096]{1,0:T(8,128)(2,1)S(1)}, u32[]{:S(2)}, u32[]{:S(2)}) collective-permute-start(bf16[8,4096]{1,0:T(8,128)(2,1)S(1)} %get-tuple-element.29), channel_id=1, source_target_pairs={{0,5},{1,4},{2,7},{3,6},{4,1},{5,0},{6,3},{7,2},{8,13},{9,12},{10,... | collective-permute-start | bytes 196616 | tf_op jit(solution)/shard_map/ppermute | solution.py:48
  58.1 1.6 %collective-permute-start.3 = (bf16[8,4096]{1,0:T(8,128)(2,1)S(1)}, bf16[8,4096]{1,0:T(8,128)(2,1)S(1)}, u32[]{:S(2)}, u32[]{:S(2)}) collective-permute-start(bf16[8,4096]{1,0:T(8,128)(2,1)S(1)} %get-tuple-element.27), channel_id=1, source_target_pairs={{0,1},{1,0},{2,3},{3,2},{4,5},{5,4},{6,7},{7,6},{8,9},{9,8},{10,11... | collective-permute-start | bytes 196616 | tf_op jit(solution)/shard_map/ppermute | solution.py:48
  60.0 2.5 %collective-permute-done.3 = bf16[8,4096]{1,0:T(8,128)(2,1)S(1)} collective-permute-done((bf16[8,4096]{1,0:T(8,128)(2,1)S(1)}, bf16[8,4096]{1,0:T(8,128)(2,1)S(1)}, u32[]{:S(2)}, u32[]{:S(2)}) %collective-permute-start.3) | collective-permute-done | bytes 65568 | tf_op jit(solution)/shard_map/ppermute | solution.py:48
  62.6 1.9 %collective-permute-start.8 = (bf16[8,4096]{1,0:T(8,128)(2,1)S(1)}, bf16[8,4096]{1,0:T(8,128)(2,1)S(1)}, u32[]{:S(2)}, u32[]{:S(2)}) collective-permute-start(bf16[8,4096]{1,0:T(8,128)(2,1)S(1)} %get-tuple-element.28), channel_id=1, source_target_pairs={{0,2},{1,3},{2,4},{3,5},{4,6},{5,7},{6,0},{7,1},{8,10},{9,11},{10,... | collective-permute-start | bytes 196616 | tf_op jit(solution)/shard_map/ppermute | solution.py:48
  64.4 0.9 collective-permute-start.9
  65.4 0.8 constant_dynamic-slice_fusion.3
  66.4 1.6 %collective-permute-start.14 = (bf16[96,1536]{1,0:T(8,128)(2,1)S(1)}, bf16[96,1536]{1,0:T(8,128)(2,1)S(1)}, u32[]{:S(2)}, u32[]{:S(2)}) collective-permute-start(bf16[96,1536]{1,0:T(8,128)(2,1)S(1)} %pad_maximum_fusion), channel_id=1, source_target_pairs={{0,16},{8,24},{16,0},{24,8},{1,17},{9,25},{17,1},{25,9},{2,18},{10... | collective-permute-start | bytes 884744 | tf_op jit(solution)/shard_map/ppermute | solution.py:48
  68.0 1.4 %collective-permute-start.15 = (bf16[96,1536]{1,0:T(8,128)(2,1)S(1)}, bf16[96,1536]{1,0:T(8,128)(2,1)S(1)}, u32[]{:S(2)}, u32[]{:S(2)}) collective-permute-start(bf16[96,1536]{1,0:T(8,128)(2,1)S(1)} %pad_maximum_fusion), channel_id=1, source_target_pairs={{0,24},{8,0},{16,8},{24,16},{1,25},{9,1},{17,9},{25,17},{2,26},{10... | collective-permute-start | bytes 884744 | tf_op jit(solution)/shard_map/ppermute | solution.py:48
  69.4 2.0 %collective-permute-done.9 = bf16[8,4096]{1,0:T(8,128)(2,1)S(1)} collective-permute-done((bf16[8,4096]{1,0:T(8,128)(2,1)S(1)}, bf16[8,4096]{1,0:T(8,128)(2,1)S(1)}, u32[]{:S(2)}, u32[]{:S(2)}) %collective-permute-start.9) | collective-permute-done | bytes 65568 | tf_op jit(solution)/shard_map/ppermute | solution.py:48
  71.4 1.5 %collective-permute-start.11 = (bf16[64,1024]{1,0:T(8,128)(2,1)S(1)}, bf16[64,1024]{1,0:T(8,128)(2,1)S(1)}, u32[]{:S(2)}, u32[]{:S(2)}) collective-permute-start(bf16[64,1024]{1,0:T(8,128)(2,1)S(1)} %bitcast.27), channel_id=1, source_target_pairs={{0,16},{8,24},{16,0},{24,8},{1,17},{9,25},{17,1},{25,9},{2,18},{10... | collective-permute-start | bytes 393224 | tf_op jit(solution)/shard_map/ppermute | solution.py:48
  73.1 1.5 %convolution_convert_fusion = bf16[128,4096]{1,0:T(8,128)(2,1)} fusion(f32[8,4096]{1,0:T(8,128)S(1)} %get-tuple-element.47, f32[8,4096]{1,0:T(8,128)S(1)} %get-tuple-element.7, f32[8]{0:T(128)S(1)} %multiply_multiply_fusion, f32[8]{0:T(128)S(1)} %fusion.50, pred[8,256]{1,0:T(8,128)(4,1)S(1)} %fusion.47, s32[]{:T(128)S(6)} %select_n.31), kind=kOutput, calls=%fused_computation | convolution fusion | flops 9076736 | bytes 1312772 | tf_op jit(solution)/shard_map/dot_general | solution.py:21
  74.6 9.6 %collective-permute-done.10 = bf16[64,1024]{1,0:T(8,128)(2,1)S(1)} collective-permute-done((bf16[64,1024]{1,0:T(8,128)(2,1)S(1)}, bf16[64,1024]{1,0:T(8,128)(2,1)S(1)}, u32[]{:S(2)}, u32[]{:S(2)}) %collective-permute-start.10) | collective-permute-done | bytes 131104 | tf_op jit(solution)/shard_map/ppermute | solution.py:48
  84.2 1.2 %collective-permute-done.11 = bf16[64,1024]{1,0:T(8,128)(2,1)S(1)} collective-permute-done((bf16[64,1024]{1,0:T(8,128)(2,1)S(1)}, bf16[64,1024]{1,0:T(8,128)(2,1)S(1)}, u32[]{:S(2)}, u32[]{:S(2)}) %collective-permute-start.11) | collective-permute-done | bytes 131104 | tf_op jit(solution)/shard_map/ppermute | solution.py:48
  85.5 1.3 %collective-permute-done.12 = bf16[64,1024]{1,0:T(8,128)(2,1)S(1)} collective-permute-done((bf16[64,1024]{1,0:T(8,128)(2,1)S(1)}, bf16[64,1024]{1,0:T(8,128)(2,1)S(1)}, u32[]{:S(2)}, u32[]{:S(2)}) %collective-permute-start.12) | collective-permute-done | bytes 131104 | tf_op jit(solution)/shard_map/ppermute | solution.py:48
  86.9 3.7 %fusion.9 = f32[1024,1536]{1,0:T(8,128)} fusion(bf16[32,1536]{1,0:T(8,128)(2,1)S(1)} %get-tuple-element.25, bf16[32,1536]{1,0:T(8,128)(2,1)S(1)} %get-tuple-element.22, bf16[32,1536]{1,0:T(8,128)(2,1)S(1)} %get-tuple-element.19, bf16[32,1536]{1,0:T(8,128)(2,1)S(1)} %get-tuple-element.17, bf16[32,1024]{1,0:T(8,128)(2,1)S(1)} %get-tuple-element.36, ...), kind=kOutput, calls=%fused_computation.12 | convolution fusion | flops 405274624 | bytes 6946816 | tf_op jit(solution)/shard_map/dot_general | solution.py:21
  90.6 3.7 %fusion.1 = f32[1024,1536]{1,0:T(8,128)} fusion(bf16[32,1536]{1,0:T(8,128)(2,1)S(1)} %get-tuple-element.26, bf16[32,1536]{1,0:T(8,128)(2,1)S(1)} %get-tuple-element.23, bf16[32,1536]{1,0:T(8,128)(2,1)S(1)} %get-tuple-element.20, bf16[32,1536]{1,0:T(8,128)(2,1)S(1)} %get-tuple-element.16, bf16[32,1024]{1,0:T(8,128)(2,1)S(1)} %get-tuple-element.36, ...), kind=kOutput, calls=%fused_computation.4 | convolution fusion | flops 405274624 | bytes 6946816 | tf_op jit(solution)/shard_map/dot_general | solution.py:21
  94.3 3.7 %fusion.17 = f32[1536,1024]{1,0:T(8,128)} fusion(bf16[32,1536]{1,0:T(8,128)(2,1)S(1)} %get-tuple-element.24, bf16[32,1536]{1,0:T(8,128)(2,1)S(1)} %get-tuple-element.21, bf16[32,1536]{1,0:T(8,128)(2,1)S(1)} %get-tuple-element.18, bf16[32,1536]{1,0:T(8,128)(2,1)S(1)} %get-tuple-element.15, bf16[32,1024]{1,0:T(8,128)(2,1)S(1)} %get-tuple-element.35, ...), kind=kOutput, calls=%fused_computation.20 | convolution fusion | flops 405274624 | bytes 6946816 | tf_op jit(solution)/shard_map/dot_general | solution.py:21
  (53 shorter events, 3.0 us)
Async XLA Ops:
  0.6 1.6 %copy-start = (bf16[256,4096]{1,0:T(8,128)(2,1)S(1)}, bf16[256,4096]{1,0:T(8,128)(2,1)}, u32[]{:S(2)}) copy-start(bf16[256,4096]{1,0:T(8,128)(2,1)} %param.7) | copy-start | bytes 6291460
  5.6 9.5 %collective-permute-start = (bf16[16,4096]{1,0:T(8,128)(2,1)S(1)}, bf16[16,4096]{1,0:T(8,128)(2,1)S(1)}, u32[]{:S(2)}, u32[]{:S(2)}) collective-permute-start(bf16[16,4096]{1,0:T(8,128)(2,1)S(1)} %pad_maximum_fusion.3), channel_id=1, source_target_pairs={{0,2},{2,4},{4,6},{6,0},{1,3},{3,5},{5,7},{7,1},{8,10},{10,12},{12... | collective-permute-start | bytes 393224 | tf_op jit(solution)/shard_map/ppermute | solution.py:48
  8.6 11.2 %collective-permute-start.1 = (bf16[16,4096]{1,0:T(8,128)(2,1)S(1)}, bf16[16,4096]{1,0:T(8,128)(2,1)S(1)}, u32[]{:S(2)}, u32[]{:S(2)}) collective-permute-start(bf16[16,4096]{1,0:T(8,128)(2,1)S(1)} %pad_maximum_fusion.3), channel_id=1, source_target_pairs={{0,4},{2,6},{4,0},{6,2},{1,5},{3,7},{5,1},{7,3},{8,12},{10,14},{12... | collective-permute-start | bytes 393224 | tf_op jit(solution)/shard_map/ppermute | solution.py:48
  11.2 8.7 %collective-permute-start.2 = (bf16[16,4096]{1,0:T(8,128)(2,1)S(1)}, bf16[16,4096]{1,0:T(8,128)(2,1)S(1)}, u32[]{:S(2)}, u32[]{:S(2)}) collective-permute-start(bf16[16,4096]{1,0:T(8,128)(2,1)S(1)} %pad_maximum_fusion.3), channel_id=1, source_target_pairs={{0,6},{2,0},{4,2},{6,4},{1,7},{3,1},{5,3},{7,5},{8,14},{10,8},{12,... | collective-permute-start | bytes 393224 | tf_op jit(solution)/shard_map/ppermute | solution.py:48
  12.6 15.8 %copy-start.2 = (bf16[4096,1536]{1,0:T(8,128)(2,1)S(1)}, bf16[4096,1536]{1,0:T(8,128)(2,1)}, u32[]{:S(2)}) copy-start(bf16[4096,1536]{1,0:T(8,128)(2,1)} %param.10) | copy-start | bytes 37748740
  41.0 31.9 %copy-start.3 = (f32[4096]{0:T(1024)S(1)}, f32[4096]{0:T(1024)}, u32[]{:S(2)}) copy-start(f32[4096]{0:T(1024)} %param.9) | copy-start | bytes 49156
  49.4 15.0 %collective-permute-start.4 = (bf16[8,4096]{1,0:T(8,128)(2,1)S(1)}, bf16[8,4096]{1,0:T(8,128)(2,1)S(1)}, u32[]{:S(2)}, u32[]{:S(2)}) collective-permute-start(bf16[8,4096]{1,0:T(8,128)(2,1)S(1)} %get-tuple-element.30), channel_id=1, source_target_pairs={{0,6},{1,7},{2,0},{3,1},{4,2},{5,3},{6,4},{7,5},{8,14},{9,15},{10,... | collective-permute-start | bytes 196616 | tf_op jit(solution)/shard_map/ppermute | solution.py:48
  53.8 12.5 %collective-permute-start.5 = (bf16[8,4096]{1,0:T(8,128)(2,1)S(1)}, bf16[8,4096]{1,0:T(8,128)(2,1)S(1)}, u32[]{:S(2)}, u32[]{:S(2)}) collective-permute-start(bf16[8,4096]{1,0:T(8,128)(2,1)S(1)} %get-tuple-element.30), channel_id=1, source_target_pairs={{0,7},{1,6},{2,1},{3,0},{4,3},{5,2},{6,5},{7,4},{8,15},{9,14},{10,... | collective-permute-start | bytes 196616 | tf_op jit(solution)/shard_map/ppermute | solution.py:48
  54.8 11.6 %collective-permute-start.6 = (bf16[8,4096]{1,0:T(8,128)(2,1)S(1)}, bf16[8,4096]{1,0:T(8,128)(2,1)S(1)}, u32[]{:S(2)}, u32[]{:S(2)}) collective-permute-start(bf16[8,4096]{1,0:T(8,128)(2,1)S(1)} %get-tuple-element.29), channel_id=1, source_target_pairs={{0,4},{1,5},{2,6},{3,7},{4,0},{5,1},{6,2},{7,3},{8,12},{9,13},{10,... | collective-permute-start | bytes 196616 | tf_op jit(solution)/shard_map/ppermute | solution.py:48
  55.2 12.8 %collective-permute-start.7 = (bf16[8,4096]{1,0:T(8,128)(2,1)S(1)}, bf16[8,4096]{1,0:T(8,128)(2,1)S(1)}, u32[]{:S(2)}, u32[]{:S(2)}) collective-permute-start(bf16[8,4096]{1,0:T(8,128)(2,1)S(1)} %get-tuple-element.29), channel_id=1, source_target_pairs={{0,5},{1,4},{2,7},{3,6},{4,1},{5,0},{6,3},{7,2},{8,13},{9,12},{10,... | collective-permute-start | bytes 196616 | tf_op jit(solution)/shard_map/ppermute | solution.py:48
  58.1 4.4 %collective-permute-start.3 = (bf16[8,4096]{1,0:T(8,128)(2,1)S(1)}, bf16[8,4096]{1,0:T(8,128)(2,1)S(1)}, u32[]{:S(2)}, u32[]{:S(2)}) collective-permute-start(bf16[8,4096]{1,0:T(8,128)(2,1)S(1)} %get-tuple-element.27), channel_id=1, source_target_pairs={{0,1},{1,0},{2,3},{3,2},{4,5},{5,4},{6,7},{7,6},{8,9},{9,8},{10,11... | collective-permute-start | bytes 196616 | tf_op jit(solution)/shard_map/ppermute | solution.py:48
  62.6 6.8 %collective-permute-start.8 = (bf16[8,4096]{1,0:T(8,128)(2,1)S(1)}, bf16[8,4096]{1,0:T(8,128)(2,1)S(1)}, u32[]{:S(2)}, u32[]{:S(2)}) collective-permute-start(bf16[8,4096]{1,0:T(8,128)(2,1)S(1)} %get-tuple-element.28), channel_id=1, source_target_pairs={{0,2},{1,3},{2,4},{3,5},{4,6},{5,7},{6,0},{7,1},{8,10},{9,11},{10,... | collective-permute-start | bytes 196616 | tf_op jit(solution)/shard_map/ppermute | solution.py:48
  64.4 7.0 %collective-permute-start.9 = (bf16[8,4096]{1,0:T(8,128)(2,1)S(1)}, bf16[8,4096]{1,0:T(8,128)(2,1)S(1)}, u32[]{:S(2)}, u32[]{:S(2)}) collective-permute-start(bf16[8,4096]{1,0:T(8,128)(2,1)S(1)} %get-tuple-element.28), channel_id=1, source_target_pairs={{0,3},{1,2},{2,5},{3,4},{4,7},{5,6},{6,1},{7,0},{8,11},{9,10},{10,... | collective-permute-start | bytes 196616 | tf_op jit(solution)/shard_map/ppermute | solution.py:48
  66.3 20.4 %collective-permute-start.13 = (bf16[96,1536]{1,0:T(8,128)(2,1)S(1)}, bf16[96,1536]{1,0:T(8,128)(2,1)S(1)}, u32[]{:S(2)}, u32[]{:S(2)}) collective-permute-start(bf16[96,1536]{1,0:T(8,128)(2,1)S(1)} %pad_maximum_fusion), channel_id=1, source_target_pairs={{0,8},{8,16},{16,24},{24,0},{1,9},{9,17},{17,25},{25,1},{2,10},{10... | collective-permute-start | bytes 884744 | tf_op jit(solution)/shard_map/ppermute | solution.py:48
  66.4 20.4 %collective-permute-start.14 = (bf16[96,1536]{1,0:T(8,128)(2,1)S(1)}, bf16[96,1536]{1,0:T(8,128)(2,1)S(1)}, u32[]{:S(2)}, u32[]{:S(2)}) collective-permute-start(bf16[96,1536]{1,0:T(8,128)(2,1)S(1)} %pad_maximum_fusion), channel_id=1, source_target_pairs={{0,16},{8,24},{16,0},{24,8},{1,17},{9,25},{17,1},{25,9},{2,18},{10... | collective-permute-start | bytes 884744 | tf_op jit(solution)/shard_map/ppermute | solution.py:48
  68.0 18.8 %collective-permute-start.15 = (bf16[96,1536]{1,0:T(8,128)(2,1)S(1)}, bf16[96,1536]{1,0:T(8,128)(2,1)S(1)}, u32[]{:S(2)}, u32[]{:S(2)}) collective-permute-start(bf16[96,1536]{1,0:T(8,128)(2,1)S(1)} %pad_maximum_fusion), channel_id=1, source_target_pairs={{0,24},{8,0},{16,8},{24,16},{1,25},{9,1},{17,9},{25,17},{2,26},{10... | collective-permute-start | bytes 884744 | tf_op jit(solution)/shard_map/ppermute | solution.py:48
  69.4 14.8 %collective-permute-start.10 = (bf16[64,1024]{1,0:T(8,128)(2,1)S(1)}, bf16[64,1024]{1,0:T(8,128)(2,1)S(1)}, u32[]{:S(2)}, u32[]{:S(2)}) collective-permute-start(bf16[64,1024]{1,0:T(8,128)(2,1)S(1)} %bitcast.28), channel_id=1, source_target_pairs={{0,8},{8,16},{16,24},{24,0},{1,9},{9,17},{17,25},{25,1},{2,10},{10... | collective-permute-start | bytes 393224 | tf_op jit(solution)/shard_map/ppermute | solution.py:48
  71.4 14.1 %collective-permute-start.11 = (bf16[64,1024]{1,0:T(8,128)(2,1)S(1)}, bf16[64,1024]{1,0:T(8,128)(2,1)S(1)}, u32[]{:S(2)}, u32[]{:S(2)}) collective-permute-start(bf16[64,1024]{1,0:T(8,128)(2,1)S(1)} %bitcast.27), channel_id=1, source_target_pairs={{0,16},{8,24},{16,0},{24,8},{1,17},{9,25},{17,1},{25,9},{2,18},{10... | collective-permute-start | bytes 393224 | tf_op jit(solution)/shard_map/ppermute | solution.py:48
  84.2 2.5 %collective-permute-start.12 = (bf16[64,1024]{1,0:T(8,128)(2,1)S(1)}, bf16[64,1024]{1,0:T(8,128)(2,1)S(1)}, u32[]{:S(2)}, u32[]{:S(2)}) collective-permute-start(bf16[64,1024]{1,0:T(8,128)(2,1)S(1)} %bitcast.26), channel_id=1, source_target_pairs={{0,24},{8,0},{16,8},{24,16},{1,25},{9,1},{17,9},{25,17},{2,26},{10... | collective-permute-start | bytes 393224 | tf_op jit(solution)/shard_map/ppermute | solution.py:48
  86.9 11.2 %copy-start.1 = (bf16[256,4096]{1,0:T(8,128)(2,1)S(1)}, bf16[256,4096]{1,0:T(8,128)(2,1)}, u32[]{:S(2)}) copy-start(bf16[256,4096]{1,0:T(8,128)(2,1)} %param.7) | copy-start | bytes 6291460

commit v4 on v3

--- a/solution.py
+++ b/solution.py
@@ -48,6 +48,81 @@
     return lax.ppermute(value, axes, pairs)
 
 
+def swapped(value, axis, size, distance):
+    return lax.ppermute(value, axis, [(i, i ^ distance) for i in range(size)])
+
+
+def power_of_two(size):
+    return size & (size - 1) == 0
+
+
+def gather_blocks(value, axis, size):
+    if power_of_two(size):
+        blocks, distance = [value], 1
+        while distance < size:
+            arrived = swapped(jnp.stack(blocks), axis, size, distance)
+            blocks = blocks + [arrived[k] for k in range(distance)]
+            distance *= 2
+        return blocks, lambda k: ("xor", k)
+    blocks = [value] + [shifted(value, axis, (size,), (k,)) for k in range(1, size)]
+    return blocks, lambda k: ("shift", k)
+
+
+def scatter_sum(pieces, axis, size):
+    if power_of_two(size):
+        held = {k: piece.astype(jnp.float32) for k, piece in enumerate(pieces)}
+        distance = size // 2
+        while distance >= 1:
+            leaving = sorted(k for k in held if k & distance)
+            arrived = swapped(
+                jnp.stack([held[k] for k in leaving]).astype(jnp.bfloat16), axis, size, distance
+            )
+            for position, k in enumerate(leaving):
+                held[k ^ distance] = held[k ^ distance] + arrived[position].astype(jnp.float32)
+            held = {k: v for k, v in held.items() if not k & distance}
+            distance //= 2
+        return held[0]
+    total = pieces[0].astype(jnp.float32)
+    for k in range(1, size):
+        total = total + shifted(pieces[k], axis, (size,), (-k,)).astype(jnp.float32)
+    return total
+
+
+def all_sum(value, axis, size):
+    if power_of_two(size):
+        total, distance = value, 1
+        while distance < size:
+            total = total + swapped(total.astype(jnp.bfloat16), axis, size, distance).astype(jnp.float32)
+            distance *= 2
+        return total
+    total = value
+    for k in range(1, size):
+        total = total + shifted(value.astype(jnp.bfloat16), axis, (size,), (k,)).astype(jnp.float32)
+    return total
+
+
+def exchange_blocks(blocks, axis, size):
+    index = lax.axis_index(axis)
+    if power_of_two(size):
+        stacked = jnp.stack(blocks)
+        held = {(0, k): lax.dynamic_index_in_dim(stacked, index ^ k, 0, keepdims=False) for k in range(size)}
+        distance = 1
+        while distance < size:
+            leaving = sorted(key for key in held if key[1] & distance)
+            arrived = swapped(jnp.stack([held[key] for key in leaving]), axis, size, distance)
+            held = {key: v for key, v in held.items() if not key[1] & distance}
+            for position, (origin, target) in enumerate(leaving):
+                held[(origin ^ distance, target ^ distance)] = arrived[position]
+            distance *= 2
+        return [held[(k, 0)] for k in range(size)]
+    stacked = jnp.stack(blocks)
+    out = [lax.dynamic_index_in_dim(stacked, index, 0, keepdims=False)]
+    for k in range(1, size):
+        outgoing = lax.dynamic_index_in_dim(stacked, (index + k) % size, 0, keepdims=False)
+        out.append(shifted(outgoing, axis, (size,), (k,)))
+    return out
+
+
 def local(tokens, cotangent, norm_gain, gate_weight, up_weight, down_weight, depths):
     parts = lax.axis_size("fsdp")
     place = lax.axis_index("fsdp")
@@ -64,11 +139,15 @@
     source = jnp.dot(picker, tokens, preferred_element_type=jnp.float32)
     send_masked = jnp.dot(picker, cotangent, preferred_element_type=jnp.float32).astype(jnp.bfloat16)
     send_normed = normalize(source, norm_gain).astype(jnp.bfloat16)
-    packed = jnp.concatenate([send_normed, send_masked], axis=0)
-    blocks = [packed] + [shifted(packed, "seq", (shards,), (k,)) for k in range(1, shards)]
+    blocks, _ = gather_blocks(jnp.concatenate([send_normed, send_masked], axis=0), "seq", shards)
     window_normed = jnp.concatenate([b[:MAXACT] for b in blocks], axis=0)
     window_masked = jnp.concatenate([b[MAXACT:] for b in blocks], axis=0)
     window = window_normed.shape[0]
+    columns = jnp.concatenate([window_normed, window_masked], axis=0)
+    columns = columns.reshape(2 * window, replicas, feature_share)
+    every_columns = exchange_blocks(
+        [columns[:, b] for b in range(replicas)], "rep", replicas
+    )
     gate = jnp.dot(window_normed, gate_weight, preferred_element_type=jnp.float32)
     up = jnp.dot(window_normed, up_weight, preferred_element_type=jnp.float32)
     sigmoid_gate = jax.nn.sigmoid(gate)
@@ -79,27 +158,12 @@
         jnp.bfloat16
     )
     up_rows = (hidden_grad * swished).astype(jnp.bfloat16)
-    factors = jnp.concatenate([gate_rows, up_rows, hidden], axis=0)
-    columns = jnp.concatenate([window_normed, window_masked], axis=0)
-    columns = columns.reshape(2 * window, replicas, feature_share)
-    replica = lax.axis_index("rep")
-    every_factors = [factors]
-    every_columns = [lax.dynamic_index_in_dim(columns, replica, 1, keepdims=False)]
-    for j in range(1, replicas):
-        every_factors.append(shifted(factors, "rep", (replicas,), (j,)))
-        outgoing = lax.dynamic_index_in_dim(columns, (replica + j) % replicas, 1, keepdims=False)
-        every_columns.append(shifted(outgoing, "rep", (replicas,), (j,)))
-    partial_features = (
-        contract_last(gate_rows, gate_weight) + contract_last(up_rows, up_weight)
-    ).astype(jnp.bfloat16)
-    feature_grad = partial_features[:MAXACT].astype(jnp.float32)
-    for k in range(shards):
-        piece = partial_features[k * MAXACT : (k + 1) * MAXACT]
-        for step in range(parts):
-            if k == 0 and step == 0:
-                continue
-            arrived = shifted(piece, ("seq", "fsdp"), (shards, parts), (-k, step))
-            feature_grad = feature_grad + arrived.astype(jnp.float32)
+    every_factors, _ = gather_blocks(
+        jnp.concatenate([gate_rows, up_rows, hidden], axis=0), "rep", replicas
+    )
+    partial_features = contract_last(gate_rows, gate_weight) + contract_last(up_rows, up_weight)
+    pieces = [partial_features[k * MAXACT : (k + 1) * MAXACT] for k in range(shards)]
+    feature_grad = all_sum(scatter_sum(pieces, "seq", shards), "fsdp", parts)
     every_gate = jnp.concatenate([f[:window] for f in every_factors], axis=0)
     every_up = jnp.concatenate([f[window : 2 * window] for f in every_factors], axis=0)
     every_hidden = jnp.concatenate([f[2 * window :] for f in every_factors], axis=0)

time: 99.7 us -> 106 us (1.063)
  waiting for transfers between devices: 24 us -> 47.1 us
  starting transfers between devices: 24.2 us -> 9.75 us
  local copies, waits for them, and re-layouts: 2.21 us -> 0.53 us
    ppermute x16 -> x9, waiting for transfers between devices: 24 us -> 47.1 us  [swapped(): return lax.ppermute(value, axis, [(i, i ^ distance) for i in range(size)])]
    ppermute x16 -> x9, starting transfers between devices: 24.2 us -> 9.75 us  [swapped(): return lax.ppermute(value, axis, [(i, i ^ distance) for i in range(size)])]
  transfers between devices with their start and end apart: 16 -> 9, of which waited for: 7 -> 7; matrix products, arithmetic and copies ran while one was open for 4% -> 10% of each run, Pallas kernels for 0% -> 0%
where the time goes in v4:
time: 106 us; the launch traced here: 105 us
  waiting for transfers between devices  47.1 us (44%)
  matrix products  44.4 us (42%)
  starting transfers between devices  9.75 us (9%)
  other arithmetic  2.58 us (2%)
    ppermute x9, waiting for transfers between devices, swapped(): return lax.ppermute(value, axis, [(i, i ^ distance) for i in range(size)])  47.1 us
    dot_general x3, matrix products, contract_last(): lax.dot_general(left, right, (((1,), (1,)), ((), ())), preferred_element_...  20.4 us
    dot_general x4, matrix products, contract_first(): lax.dot_general(left, right, (((0,), (0,)), ((), ())), preferred_element_...  12.6 us
    ppermute x9, starting transfers between devices, swapped(): return lax.ppermute(value, axis, [(i, i ^ distance) for i in range(size)])  9.75 us
    dot_general x1, matrix products, local(): up = jnp.dot(window_normed, up_weight, preferred_element_type=jnp.float32)  6.76 us
    dot_general x1, matrix products, local(): jnp.dot(window_normed, gate_weight, preferred_element_type=jnp.float32)  2.16 us
  transfers between devices with their start and end apart: 9, of which 7 were waited for; matrix products, arithmetic and copies ran while one was open for 10% of the time, Pallas kernels for 0%

profile of v4, /device:TPU:0, one launch (start us, length us, event | category | flops | bytes accessed | tf_op | source)
XLA Modules:
  0.0 105.3 jit_solution(545049335227033643)
XLA Ops:
  0.6 0.8 convert_bitcast_fusion
  1.5 0.3 reduce-window.9
  1.8 0.1 slice.203
  1.9 0.1 slice_reduce_fusion
  2.0 0.1 add_bitcast_fusion
  2.1 2.0 %convolution_convert_fusion.1 = bf16[8,4096]{1,0:T(8,128)(2,1)S(1)} fusion(bf16[256,4096]{1,0:T(8,128)(2,1)} %param.8, s32[256]{0:T(256)S(1)} %add_bitcast_fusion, pred[256]{0:T(512)(128)(4,1)S(1)} %get-tuple-element.5), kind=kOutput, calls=%fused_computation.2 | convolution fusion | flops 16814080 | bytes 2163968 | tf_op jit(solution)/shard_map/dot_general | solution.py:140
  4.1 0.5 multiply_reduce_fusion.1
  4.6 0.8 multiply_convert_fusion.3
  5.4 3.1 %collective-permute-start = (bf16[1,16,4096]{2,1,0:T(8,128)(2,1)S(1)}, bf16[1,16,4096]{2,1,0:T(8,128)(2,1)S(1)}, u32[]{:S(2)}, u32[]{:S(2)}) collective-permute-start(bf16[1,16,4096]{2,1,0:T(8,128)(2,1)S(1)} %maximum_bitcast_fusion.1), channel_id=1, source_target_pairs={{0,2},{2,0},{4,6},{6,4},{1,3},{3,1},{5,7},{7,5},{8,10},{10,8},{12,... | collective-permute-start | bytes 393224 | tf_op jit(solution)/shard_map/ppermute | solution.py:52
  8.6 3.4 %collective-permute-done = bf16[1,16,4096]{2,1,0:T(8,128)(2,1)S(1)} collective-permute-done((bf16[1,16,4096]{2,1,0:T(8,128)(2,1)S(1)}, bf16[1,16,4096]{2,1,0:T(8,128)(2,1)S(1)}, u32[]{:S(2)}, u32[]{:S(2)}) %collective-permute-start) | collective-permute-done | bytes 131104 | tf_op jit(solution)/shard_map/ppermute | solution.py:52
  12.0 2.8 %collective-permute-start.1 = (bf16[2,16,4096]{2,1,0:T(8,128)(2,1)S(1)}, bf16[2,16,4096]{2,1,0:T(8,128)(2,1)S(1)}, u32[]{:S(2)}, u32[]{:S(2)}) collective-permute-start(bf16[2,16,4096]{2,1,0:T(8,128)(2,1)S(1)} %pad_maximum_fusion.2), channel_id=1, source_target_pairs={{0,4},{2,6},{4,0},{6,2},{1,5},{3,7},{5,1},{7,3},{8,12},{10,14},{12... | collective-permute-start | bytes 786440 | tf_op jit(solution)/shard_map/ppermute | solution.py:52
  14.9 11.2 %collective-permute-done.1 = bf16[2,16,4096]{2,1,0:T(8,128)(2,1)S(1)} collective-permute-done((bf16[2,16,4096]{2,1,0:T(8,128)(2,1)S(1)}, bf16[2,16,4096]{2,1,0:T(8,128)(2,1)S(1)}, u32[]{:S(2)}, u32[]{:S(2)}) %collective-permute-start.1) | collective-permute-done | bytes 262176 | tf_op jit(solution)/shard_map/ppermute | solution.py:52
  26.1 8.4 %fusion.24 = f32[32,1536]{1,0:T(8,128)S(1)} fusion(bf16[1536,4096]{1,0:T(8,128)(2,1)} %param.12, bf16[8,4096]{1,0:T(8,128)(2,1)S(1)} %get-tuple-element.35, bf16[8,4096]{1,0:T(8,128)(2,1)S(1)} %get-tuple-element.34, bf16[8,4096]{1,0:T(8,128)(2,1)S(1)} %get-tuple-element.44, bf16[8,4096]{1,0:T(8,128)(2,1)S(1)} %convolution_convert_fusion.1), kind=kOutput, calls=%fused_computation.31 | convolution fusion | flops 403701760 | bytes 13041664 | tf_op jit(solution)/shard_map/dot_general | solution.py:27
  34.5 2.2 %fusion.48 = f32[32,1536]{1,0:T(8,128)S(1)} fusion(bf16[4096,1536]{1,0:T(8,128)(2,1)S(1)} %copy-done.2, bf16[8,4096]{1,0:T(8,128)(2,1)S(1)} %get-tuple-element.37, bf16[8,4096]{1,0:T(8,128)(2,1)S(1)} %get-tuple-element.36, bf16[8,4096]{1,0:T(8,128)(2,1)S(1)} %get-tuple-element.45, bf16[8,4096]{1,0:T(8,128)(2,1)S(1)} %multiply_convert_fusion.3), kind=kOutput, calls=%fused_computation.96 | convolution fusion | flops 403701760 | bytes 13041664 | tf_op jit(solution)/shard_map/dot_general | solution.py:151
  36.7 6.8 %multiply_convert_fusion = (bf16[32,1536]{1,0:T(8,128)(2,1)S(1)}, bf16[32,1536]{1,0:T(8,128)(2,1)S(1)}, bf16[32,1536]{1,0:T(8,128)(2,1)S(1)}) fusion(f32[32,1536]{1,0:T(8,128)S(1)} %fusion.48, f32[32,1536]{1,0:T(8,128)S(1)} %fusion.24, bf16[4096,1536]{1,0:T(8,128)(2,1)} %param.11, bf16[8,4096]{1,0:T(8,128)(2,1)S(1)} %get-tuple-element.37, ...), kind=kOutput, calls=%fused_computation.50 | convolution fusion | flops 404439040 | bytes 13533184 | tf_op jit(solution)/shard_map/dot_general | solution.py:152
  43.5 3.7 %fusion.68 = f32[32,4096]{1,0:T(8,128)S(1)} fusion(bf16[32,1536]{1,0:T(8,128)(2,1)S(1)} %get-tuple-element.22, bf16[4096,1536]{1,0:T(8,128)(2,1)S(1)} %copy-done.2), kind=kOutput, calls=%fused_computation.137 | convolution fusion | flops 402653184 | bytes 13205504 | tf_op jit(solution)/shard_map/dot_general | solution.py:27
  47.2 0.1 collective-permute-start.7
  47.3 8.3 %fusion.67 = (bf16[32,4096]{1,0:T(8,128)(2,1)S(1)}, f32[32,4096]{1,0:T(8,128)S(1)}) fusion(f32[32,4096]{1,0:T(8,128)S(1)} %fusion.68, bf16[32,1536]{1,0:T(8,128)(2,1)S(1)} %get-tuple-element.23, bf16[4096,1536]{1,0:T(8,128)(2,1)} %param.11), kind=kOutput, calls=%fused_computation.136 | convolution fusion | flops 402915328 | bytes 13991936 | tf_op jit(solution)/shard_map/dot_general | solution.py:27
  56.0 9.3 %collective-permute-done.2 = bf16[2,8,4096]{2,1,0:T(8,128)(2,1)S(1)} collective-permute-done((bf16[2,8,4096]{2,1,0:T(8,128)(2,1)S(1)}, bf16[2,8,4096]{2,1,0:T(8,128)(2,1)S(1)}, u32[]{:S(2)}, u32[]{:S(2)}) %collective-permute-start.2) | collective-permute-done | bytes 131104 | tf_op jit(solution)/shard_map/ppermute | solution.py:52
  65.4 0.1 collective-permute-start.3
  65.6 4.1 %collective-permute-done.3 = bf16[1,8,4096]{2,1,0:T(8,128)(2,1)S(1)} collective-permute-done((bf16[1,8,4096]{2,1,0:T(8,128)(2,1)S(1)}, bf16[1,8,4096]{2,1,0:T(8,128)(2,1)S(1)}, u32[]{:S(2)}, u32[]{:S(2)}) %collective-permute-start.3) | collective-permute-done | bytes 65568 | tf_op jit(solution)/shard_map/ppermute | solution.py:52
  69.7 1.4 %collective-permute-start.4 = (bf16[8,4096]{1,0:T(8,128)(2,1)S(1)}, bf16[8,4096]{1,0:T(8,128)(2,1)S(1)}, u32[]{:S(2)}, u32[]{:S(2)}) collective-permute-start(bf16[8,4096]{1,0:T(8,128)(2,1)S(1)} %fusion.64), channel_id=1, source_target_pairs={{0,1},{1,0},{2,3},{3,2},{4,5},{5,4},{6,7},{7,6},{8,9},{9,8},{10,11... | collective-permute-start | bytes 196616 | tf_op jit(solution)/shard_map/ppermute | solution.py:52
  71.2 2.9 %collective-permute-done.4 = bf16[8,4096]{1,0:T(8,128)(2,1)S(1)} collective-permute-done((bf16[8,4096]{1,0:T(8,128)(2,1)S(1)}, bf16[8,4096]{1,0:T(8,128)(2,1)S(1)}, u32[]{:S(2)}, u32[]{:S(2)}) %collective-permute-start.4) | collective-permute-done | bytes 65568 | tf_op jit(solution)/shard_map/ppermute | solution.py:52
  74.1 0.2 multiply_reduce_fusion
  74.3 1.5 %convolution_convert_fusion = bf16[128,4096]{1,0:T(8,128)(2,1)} fusion(f32[8,4096]{1,0:T(8,128)S(1)} %get-tuple-element.48, bf16[8,4096]{1,0:T(8,128)(2,1)S(1)} %collective-permute-done.4, f32[8]{0:T(128)S(1)} %multiply_multiply_fusion, f32[4096]{0:T(1024)S(1)} %copy-done.3, f32[8]{0:T(128)S(1)} %fusion.53, pred[8,256]{1,0:T(8,128)(4,1)S(1)} %fusion.50, ...), kind=kOutput, calls=%fused_computation | convolution fusion | flops 9306112 | bytes 1525764 | tf_op jit(solution)/shard_map/dot_general | solution.py:21
  75.8 1.4 %collective-permute-start.6 = (bf16[2,64,1024]{2,1,0:T(8,128)(2,1)S(1)}, bf16[2,64,1024]{2,1,0:T(8,128)(2,1)S(1)}, u32[]{:S(2)}, u32[]{:S(2)}) collective-permute-start(bf16[2,64,1024]{2,1,0:T(8,128)(2,1)S(1)} %pad_maximum_fusion.5), channel_id=1, source_target_pairs={{0,16},{8,24},{16,0},{24,8},{1,17},{9,25},{17,1},{25,9},{2,18},{10... | collective-permute-start | bytes 786440 | tf_op jit(solution)/shard_map/ppermute | solution.py:52
  77.3 0.7 collective-permute-start.8
  78.0 7.0 %collective-permute-done.6 = bf16[2,64,1024]{2,1,0:T(8,128)(2,1)S(1)} collective-permute-done((bf16[2,64,1024]{2,1,0:T(8,128)(2,1)S(1)}, bf16[2,64,1024]{2,1,0:T(8,128)(2,1)S(1)}, u32[]{:S(2)}, u32[]{:S(2)}) %collective-permute-start.6) | collective-permute-done | bytes 262176 | tf_op jit(solution)/shard_map/ppermute | solution.py:52
  85.1 9.0 %collective-permute-done.8 = bf16[2,96,1536]{2,1,0:T(8,128)(2,1)S(1)} collective-permute-done((bf16[2,96,1536]{2,1,0:T(8,128)(2,1)S(1)}, bf16[2,96,1536]{2,1,0:T(8,128)(2,1)S(1)}, u32[]{:S(2)}, u32[]{:S(2)}) %collective-permute-start.8) | collective-permute-done | bytes 589856 | tf_op jit(solution)/shard_map/ppermute | solution.py:52
  94.2 3.7 %fusion.8 = f32[1024,1536]{1,0:T(8,128)} fusion(bf16[32,1536]{1,0:T(8,128)(2,1)S(1)} %get-tuple-element.8, bf16[32,1536]{1,0:T(8,128)(2,1)S(1)} %get-tuple-element.9, bf16[32,1536]{1,0:T(8,128)(2,1)S(1)} %get-tuple-element.25, bf16[32,1536]{1,0:T(8,128)(2,1)S(1)} %get-tuple-element.23, bf16[32,1024]{1,0:T(8,128)(2,1)S(1)} %get-tuple-element.31, ...), kind=kOutput, calls=%fused_computation.13 | convolution fusion | flops 405274624 | bytes 6946816 | tf_op jit(solution)/shard_map/dot_general | solution.py:21
  97.9 3.7 %fusion = f32[1024,1536]{1,0:T(8,128)} fusion(bf16[32,1536]{1,0:T(8,128)(2,1)S(1)} %get-tuple-element.10, bf16[32,1536]{1,0:T(8,128)(2,1)S(1)} %get-tuple-element.11, bf16[32,1536]{1,0:T(8,128)(2,1)S(1)} %get-tuple-element.26, bf16[32,1536]{1,0:T(8,128)(2,1)S(1)} %get-tuple-element.22, bf16[32,1024]{1,0:T(8,128)(2,1)S(1)} %get-tuple-element.31, ...), kind=kOutput, calls=%fused_computation.5 | convolution fusion | flops 405274624 | bytes 6946816 | tf_op jit(solution)/shard_map/dot_general | solution.py:21
  101.6 3.7 %fusion.16 = f32[1536,1024]{1,0:T(8,128)} fusion(bf16[32,1536]{1,0:T(8,128)(2,1)S(1)} %get-tuple-element.7, bf16[32,1536]{1,0:T(8,128)(2,1)S(1)} %get-tuple-element.6, bf16[32,1536]{1,0:T(8,128)(2,1)S(1)} %get-tuple-element.24, bf16[32,1536]{1,0:T(8,128)(2,1)S(1)} %get-tuple-element.21, bf16[32,1024]{1,0:T(8,128)(2,1)S(1)} %get-tuple-element.30, ...), kind=kOutput, calls=%fused_computation.21 | convolution fusion | flops 405274624 | bytes 6946816 | tf_op jit(solution)/shard_map/dot_general | solution.py:21
  (45 shorter events, 0.9 us)
Async XLA Ops:
  0.6 3.4 %copy-start = (bf16[256,4096]{1,0:T(8,128)(2,1)S(1)}, bf16[256,4096]{1,0:T(8,128)(2,1)}, u32[]{:S(2)}) copy-start(bf16[256,4096]{1,0:T(8,128)(2,1)} %param.7) | copy-start | bytes 6291460
  5.4 6.6 %collective-permute-start = (bf16[1,16,4096]{2,1,0:T(8,128)(2,1)S(1)}, bf16[1,16,4096]{2,1,0:T(8,128)(2,1)S(1)}, u32[]{:S(2)}, u32[]{:S(2)}) collective-permute-start(bf16[1,16,4096]{2,1,0:T(8,128)(2,1)S(1)} %maximum_bitcast_fusion.1), channel_id=1, source_target_pairs={{0,2},{2,0},{4,6},{6,4},{1,3},{3,1},{5,7},{7,5},{8,10},{10,8},{12,... | collective-permute-start | bytes 393224 | tf_op jit(solution)/shard_map/ppermute | solution.py:52
  8.5 26.0 %copy-start.2 = (bf16[4096,1536]{1,0:T(8,128)(2,1)S(1)}, bf16[4096,1536]{1,0:T(8,128)(2,1)}, u32[]{:S(2)}) copy-start(bf16[4096,1536]{1,0:T(8,128)(2,1)} %param.10) | copy-start | bytes 37748740
  12.0 14.1 %collective-permute-start.1 = (bf16[2,16,4096]{2,1,0:T(8,128)(2,1)S(1)}, bf16[2,16,4096]{2,1,0:T(8,128)(2,1)S(1)}, u32[]{:S(2)}, u32[]{:S(2)}) collective-permute-start(bf16[2,16,4096]{2,1,0:T(8,128)(2,1)S(1)} %pad_maximum_fusion.2), channel_id=1, source_target_pairs={{0,4},{2,6},{4,0},{6,2},{1,5},{3,7},{5,1},{7,3},{8,12},{10,14},{12... | collective-permute-start | bytes 786440 | tf_op jit(solution)/shard_map/ppermute | solution.py:52
  47.2 26.9 %copy-start.3 = (f32[4096]{0:T(1024)S(1)}, f32[4096]{0:T(1024)}, u32[]{:S(2)}) copy-start(f32[4096]{0:T(1024)} %param.9) | copy-start | bytes 49156
  47.2 30.0 %collective-permute-start.7 = (bf16[1,96,1536]{2,1,0:T(8,128)(2,1)S(1)}, bf16[1,96,1536]{2,1,0:T(8,128)(2,1)S(1)}, u32[]{:S(2)}, u32[]{:S(2)}) collective-permute-start(bf16[1,96,1536]{2,1,0:T(8,128)(2,1)S(1)} %maximum_bitcast_fusion), channel_id=1, source_target_pairs={{0,8},{8,0},{16,24},{24,16},{1,9},{9,1},{17,25},{25,17},{2,10},{10... | collective-permute-start | bytes 884744 | tf_op jit(solution)/shard_map/ppermute | solution.py:52
  55.7 9.7 %collective-permute-start.2 = (bf16[2,8,4096]{2,1,0:T(8,128)(2,1)S(1)}, bf16[2,8,4096]{2,1,0:T(8,128)(2,1)S(1)}, u32[]{:S(2)}, u32[]{:S(2)}) collective-permute-start(bf16[2,8,4096]{2,1,0:T(8,128)(2,1)S(1)} %pad_maximum_fusion.7), channel_id=1, source_target_pairs={{0,4},{2,6},{4,0},{6,2},{1,5},{3,7},{5,1},{7,3},{8,12},{10,14},{12... | collective-permute-start | bytes 393224 | tf_op jit(solution)/shard_map/ppermute | solution.py:52
  65.4 4.3 %collective-permute-start.3 = (bf16[1,8,4096]{2,1,0:T(8,128)(2,1)S(1)}, bf16[1,8,4096]{2,1,0:T(8,128)(2,1)S(1)}, u32[]{:S(2)}, u32[]{:S(2)}) collective-permute-start(bf16[1,8,4096]{2,1,0:T(8,128)(2,1)S(1)} %fusion.43), channel_id=1, source_target_pairs={{0,2},{2,0},{4,6},{6,4},{1,3},{3,1},{5,7},{7,5},{8,10},{10,8},{12,... | collective-permute-start | bytes 196616 | tf_op jit(solution)/shard_map/ppermute | solution.py:52
  65.5 10.2 %collective-permute-start.5 = (bf16[2,64,1024]{2,1,0:T(8,128)(2,1)S(1)}, bf16[2,64,1024]{2,1,0:T(8,128)(2,1)S(1)}, u32[]{:S(2)}, u32[]{:S(2)}) collective-permute-start(bf16[2,64,1024]{2,1,0:T(8,128)(2,1)S(1)} %pad_maximum_fusion.4), channel_id=1, source_target_pairs={{0,8},{8,0},{16,24},{24,16},{1,9},{9,1},{17,25},{25,17},{2,10},{10... | collective-permute-start | bytes 786440 | tf_op jit(solution)/shard_map/ppermute | solution.py:52
  69.7 4.3 %collective-permute-start.4 = (bf16[8,4096]{1,0:T(8,128)(2,1)S(1)}, bf16[8,4096]{1,0:T(8,128)(2,1)S(1)}, u32[]{:S(2)}, u32[]{:S(2)}) collective-permute-start(bf16[8,4096]{1,0:T(8,128)(2,1)S(1)} %fusion.64), channel_id=1, source_target_pairs={{0,1},{1,0},{2,3},{3,2},{4,5},{5,4},{6,7},{7,6},{8,9},{9,8},{10,11... | collective-permute-start | bytes 196616 | tf_op jit(solution)/shard_map/ppermute | solution.py:52
  75.8 9.3 %collective-permute-start.6 = (bf16[2,64,1024]{2,1,0:T(8,128)(2,1)S(1)}, bf16[2,64,1024]{2,1,0:T(8,128)(2,1)S(1)}, u32[]{:S(2)}, u32[]{:S(2)}) collective-permute-start(bf16[2,64,1024]{2,1,0:T(8,128)(2,1)S(1)} %pad_maximum_fusion.5), channel_id=1, source_target_pairs={{0,16},{8,24},{16,0},{24,8},{1,17},{9,25},{17,1},{25,9},{2,18},{10... | collective-permute-start | bytes 786440 | tf_op jit(solution)/shard_map/ppermute | solution.py:52
  77.3 16.8 %collective-permute-start.8 = (bf16[2,96,1536]{2,1,0:T(8,128)(2,1)S(1)}, bf16[2,96,1536]{2,1,0:T(8,128)(2,1)S(1)}, u32[]{:S(2)}, u32[]{:S(2)}) collective-permute-start(bf16[2,96,1536]{2,1,0:T(8,128)(2,1)S(1)} %pad_maximum_fusion), channel_id=1, source_target_pairs={{0,16},{8,24},{16,0},{24,8},{1,17},{9,25},{17,1},{25,9},{2,18},{10... | collective-permute-start | bytes 1769480 | tf_op jit(solution)/shard_map/ppermute | solution.py:52
  94.2 11.1 %copy-start.1 = (bf16[256,4096]{1,0:T(8,128)(2,1)S(1)}, bf16[256,4096]{1,0:T(8,128)(2,1)}, u32[]{:S(2)}) copy-start(bf16[256,4096]{1,0:T(8,128)(2,1)} %param.7) | copy-start | bytes 6291460

commit v5 on v4

--- a/solution.py
+++ b/solution.py
@@ -3,6 +3,7 @@
 import jax
 import jax.numpy as jnp
 from jax import lax
+from jax.experimental import pallas as pl
 from jax.sharding import PartitionSpec as P
 
 REC = 1
@@ -123,10 +124,75 @@
     return out
 
 
+def weight_pass_kernel(normed_ref, masked_ref, gate_w_ref, up_w_ref, down_w_ref,
+                       gate_rows_ref, up_rows_ref, hidden_ref, features_ref):
+    step = pl.program_id(0)
+    normed = normed_ref[...]
+    gate_w = gate_w_ref[...]
+    up_w = up_w_ref[...]
+    gate = jnp.dot(normed, gate_w, preferred_element_type=jnp.float32)
+    up = jnp.dot(normed, up_w, preferred_element_type=jnp.float32)
+    hidden_grad = contract_last(masked_ref[...], down_w_ref[...])
+    sigmoid_gate = 1.0 / (1.0 + jnp.exp(-gate))
+    swished = gate * sigmoid_gate
+    gate_rows = (hidden_grad * up * sigmoid_gate * (1.0 + gate * (1.0 - sigmoid_gate))).astype(
+        jnp.bfloat16
+    )
+    up_rows = (hidden_grad * swished).astype(jnp.bfloat16)
+    hidden_ref[...] = (swished * up).astype(jnp.bfloat16)
+    gate_rows_ref[...] = gate_rows
+    up_rows_ref[...] = up_rows
+    partial_features = contract_last(gate_rows, gate_w) + contract_last(up_rows, up_w)
+
+    @pl.when(step == 0)
+    def _():
+        features_ref[...] = partial_features
+
+    @pl.when(step > 0)
+    def _():
+        features_ref[...] += partial_features
+
+
+def weight_pass(window_normed, window_masked, gate_weight, up_weight, down_weight):
+    rows, features = window_normed.shape
+    units = gate_weight.shape[1]
+    chunk = 256 if units % 256 == 0 else units
+    factor_shape = jax.ShapeDtypeStruct((rows, units), jnp.bfloat16)
+    return pl.pallas_call(
+        weight_pass_kernel,
+        grid=(units // chunk,),
+        in_specs=[
+            pl.BlockSpec((rows, features), lambda j: (0, 0)),
+            pl.BlockSpec((rows, features), lambda j: (0, 0)),
+            pl.BlockSpec((features, chunk), lambda j: (0, j)),
+            pl.BlockSpec((features, chunk), lambda j: (0, j)),
+            pl.BlockSpec((chunk, features), lambda j: (j, 0)),
+        ],
+        out_specs=[
+            pl.BlockSpec((rows, chunk), lambda j: (0, j)),
+            pl.BlockSpec((rows, chunk), lambda j: (0, j)),
+            pl.BlockSpec((rows, chunk), lambda j: (0, j)),
+            pl.BlockSpec((rows, features), lambda j: (0, 0)),
+        ],
+        out_shape=[
+            factor_shape,
+            factor_shape,
+            factor_shape,
+            jax.ShapeDtypeStruct((rows, features), jnp.float32),
+        ],
+        cost_estimate=pl.CostEstimate(
+            flops=10 * rows * features * units,
+            transcendentals=rows * units,
+            bytes_accessed=6 * features * units + 4 * rows * features * 2,
+        ),
+    )(window_normed, window_masked, gate_weight, up_weight, down_weight)
+
+
 def local(tokens, cotangent, norm_gain, gate_weight, up_weight, down_weight, depths):
     parts = lax.axis_size("fsdp")
     place = lax.axis_index("fsdp")
     replicas = lax.axis_size("rep")
+    replica = lax.axis_index("rep")
     shards = lax.axis_size("seq")
     features = tokens.shape[1]
     feature_share = features // replicas
@@ -139,31 +205,30 @@
     source = jnp.dot(picker, tokens, preferred_element_type=jnp.float32)
     send_masked = jnp.dot(picker, cotangent, preferred_element_type=jnp.float32).astype(jnp.bfloat16)
     send_normed = normalize(source, norm_gain).astype(jnp.bfloat16)
-    blocks, _ = gather_blocks(jnp.concatenate([send_normed, send_masked], axis=0), "seq", shards)
+    packed = jnp.concatenate([send_normed, send_masked], axis=0)
+    blocks = [packed] + [shifted(packed, "seq", (shards,), (k,)) for k in range(1, shards)]
     window_normed = jnp.concatenate([b[:MAXACT] for b in blocks], axis=0)
     window_masked = jnp.concatenate([b[MAXACT:] for b in blocks], axis=0)
     window = window_normed.shape[0]
     columns = jnp.concatenate([window_normed, window_masked], axis=0)
     columns = columns.reshape(2 * window, replicas, feature_share)
-    every_columns = exchange_blocks(
-        [columns[:, b] for b in range(replicas)], "rep", replicas
-    )
-    gate = jnp.dot(window_normed, gate_weight, preferred_element_type=jnp.float32)
-    up = jnp.dot(window_normed, up_weight, preferred_element_type=jnp.float32)
-    sigmoid_gate = jax.nn.sigmoid(gate)
-    swished = gate * sigmoid_gate
-    hidden = (swished * up).astype(jnp.bfloat16)
-    hidden_grad = contract_last(window_masked, down_weight)
-    gate_rows = (hidden_grad * up * sigmoid_gate * (1.0 + gate * (1.0 - sigmoid_gate))).astype(
-        jnp.bfloat16
-    )
-    up_rows = (hidden_grad * swished).astype(jnp.bfloat16)
-    every_factors, _ = gather_blocks(
-        jnp.concatenate([gate_rows, up_rows, hidden], axis=0), "rep", replicas
-    )
-    partial_features = contract_last(gate_rows, gate_weight) + contract_last(up_rows, up_weight)
-    pieces = [partial_features[k * MAXACT : (k + 1) * MAXACT] for k in range(shards)]
-    feature_grad = all_sum(scatter_sum(pieces, "seq", shards), "fsdp", parts)
+    every_columns = [lax.dynamic_index_in_dim(columns, replica, 1, keepdims=False)]
+    for j in range(1, replicas):
+        outgoing = lax.dynamic_index_in_dim(columns, (replica + j) % replicas, 1, keepdims=False)
+        every_columns.append(shifted(outgoing, "rep", (replicas,), (j,)))
+    gate_rows, up_rows, hidden, partial_features = weight_pass(
+        window_normed, window_masked, gate_weight, up_weight, down_weight
+    )
+    factors = jnp.concatenate([gate_rows, up_rows, hidden], axis=0)
+    every_factors = [factors] + [shifted(factors, "rep", (replicas,), (j,)) for j in range(1, replicas)]
+    partial_features = partial_features.astype(jnp.bfloat16)
+    feature_grad = partial_features[:MAXACT].astype(jnp.float32)
+    for k in range(1, shards):
+        piece = partial_features[k * MAXACT : (k + 1) * MAXACT]
+        feature_grad = feature_grad + shifted(piece, "seq", (shards,), (-k,)).astype(jnp.float32)
+    seq_sum = feature_grad.astype(jnp.bfloat16)
+    for step in range(1, parts):
+        feature_grad = feature_grad + shifted(seq_sum, "fsdp", (parts,), (step,)).astype(jnp.float32)
     every_gate = jnp.concatenate([f[:window] for f in every_factors], axis=0)
     every_up = jnp.concatenate([f[window : 2 * window] for f in every_factors], axis=0)
     every_hidden = jnp.concatenate([f[2 * window :] for f in every_factors], axis=0)

time: 106 us -> 89.1 us (0.84)
  matrix products: 44.4 us -> 15.1 us
  Pallas kernels: 0 us -> 26.6 us
  waiting for transfers between devices: 47.1 us -> 21.2 us
  starting transfers between devices: 9.75 us -> 16 us
  local copies, waits for them, and re-layouts: 0.53 us -> 4.79 us
  other arithmetic: 2.58 us -> 4.2 us
    dot_general x5 -> x0, matrix products: 29.3 us -> none  [the longest x3 20.4 us: contract_last(): lax.dot_general(left, right, (((1,), (1,)), ((), ())), preferred_element_...]
    pallas_call x0 -> x1, Pallas kernels: none -> 26.6 us  [weight_pass(): pl.pallas_call(weight_pass_kernel, grid=(units // chunk,), in_specs=[pl.B...]
    ppermute x9 -> x13, waiting for transfers between devices: 47.1 us -> 21.2 us  [shifted(): return lax.ppermute(value, axes, pairs)]
    ppermute x9 -> x13, starting transfers between devices: 9.75 us -> 16 us  [shifted(): return lax.ppermute(value, axes, pairs)]
    unnamed x15 -> x23, local copies, waits for them, and re-layouts: 0.09 us -> 2.06 us
  transfers between devices with their start and end apart: 9 -> 13, of which waited for: 7 -> 8; matrix products, arithmetic and copies ran while one was open for 10% -> 5% of each run, Pallas kernels for 0% -> 0%
where the time goes in v5:
time: 89.1 us; the launch traced here: 88.7 us
  Pallas kernels  26.6 us (30%)
  waiting for transfers between devices  21.2 us (24%)
  starting transfers between devices  16 us (18%)
  matrix products  15.1 us (17%)
  local copies, waits for them, and re-layouts  4.79 us (5%)
  other arithmetic  4.2 us (5%)
    pallas_call x1, Pallas kernels, weight_pass(): pl.pallas_call(weight_pass_kernel, grid=(units // chunk,), in_specs=[pl.B...  26.6 us
    ppermute x13, waiting for transfers between devices, shifted(): return lax.ppermute(value, axes, pairs)  21.2 us
    ppermute x13, starting transfers between devices, shifted(): return lax.ppermute(value, axes, pairs)  16 us
    dot_general x4, matrix products, contract_first(): lax.dot_general(left, right, (((0,), (0,)), ((), ())), preferred_element_...  12.6 us
    unnamed x23, local copies, waits for them, and re-layouts  2.06 us
    dot_general x1, matrix products, local(): jnp.dot(picker, cotangent, preferred_element_type=jnp.float32)  1.97 us
  transfers between devices with their start and end apart: 13, of which 8 were waited for; matrix products, arithmetic and copies ran while one was open for 5% of the time, Pallas kernels for 0%

profile of v5, /device:TPU:0, one launch (start us, length us, event | category | flops | bytes accessed | tf_op | source)
XLA Modules:
  0.0 88.7 jit_solution(3412241831341809051)
XLA Ops:
  0.6 0.8 convert_bitcast_fusion
  2.1 2.0 %convolution_convert_fusion.1 = bf16[8,4096]{1,0:T(8,128)(2,1)S(1)} fusion(bf16[256,4096]{1,0:T(8,128)(2,1)} %param.8, s32[256]{0:T(256)S(1)} %add_bitcast_fusion, pred[256]{0:T(512)(128)(4,1)S(1)} %get-tuple-element.15), kind=kOutput, calls=%fused_computation.1 | convolution fusion | flops 16814080 | bytes 2163968 | tf_op jit(solution)/shard_map/dot_general | solution.py:206
  4.1 0.5 multiply_reduce_fusion.1
  4.6 0.8 constant_dynamic-update-slice_fusion.7
  5.4 5.1 %collective-permute-start.2 = (bf16[16,4096]{1,0:T(8,128)(2,1)S(1)}, bf16[16,4096]{1,0:T(8,128)(2,1)S(1)}, u32[]{:S(2)}, u32[]{:S(2)}) collective-permute-start(bf16[16,4096]{1,0:T(8,128)(2,1)S(1)} %pad_maximum_fusion.3), channel_id=1, source_target_pairs={{0,6},{2,0},{4,2},{6,4},{1,7},{3,1},{5,3},{7,5},{8,14},{10,8},{12,... | collective-permute-start | bytes 393224 | tf_op jit(solution)/shard_map/ppermute | solution.py:49
  10.5 1.0 %collective-permute-start = (bf16[16,4096]{1,0:T(8,128)(2,1)S(1)}, bf16[16,4096]{1,0:T(8,128)(2,1)S(1)}, u32[]{:S(2)}, u32[]{:S(2)}) collective-permute-start(bf16[16,4096]{1,0:T(8,128)(2,1)S(1)} %pad_maximum_fusion.3), channel_id=1, source_target_pairs={{0,2},{2,4},{4,6},{6,0},{1,3},{3,5},{5,7},{7,1},{8,10},{10,12},{12... | collective-permute-start | bytes 393224 | tf_op jit(solution)/shard_map/ppermute | solution.py:49
  11.5 8.4 %collective-permute-done = bf16[16,4096]{1,0:T(8,128)(2,1)S(1)} collective-permute-done((bf16[16,4096]{1,0:T(8,128)(2,1)S(1)}, bf16[16,4096]{1,0:T(8,128)(2,1)S(1)}, u32[]{:S(2)}, u32[]{:S(2)}) %collective-permute-start) | collective-permute-done | bytes 131104 | tf_op jit(solution)/shard_map/ppermute | solution.py:49
  19.9 1.8 %collective-permute-done.1 = bf16[16,4096]{1,0:T(8,128)(2,1)S(1)} collective-permute-done((bf16[16,4096]{1,0:T(8,128)(2,1)S(1)}, bf16[16,4096]{1,0:T(8,128)(2,1)S(1)}, u32[]{:S(2)}, u32[]{:S(2)}) %collective-permute-start.1) | collective-permute-done | bytes 131104 | tf_op jit(solution)/shard_map/ppermute | solution.py:49
  21.8 0.8 pad_maximum_fusion
  22.7 26.6 %shard_map.102 = (bf16[32,1536]{1,0:T(8,128)(2,1)}, bf16[32,1536]{1,0:T(8,128)(2,1)}, bf16[32,1536]{1,0:T(8,128)(2,1)}, f32[32,4096]{1,0:T(8,128)}) custom-call(bf16[32,4096]{1,0:T(8,128)(2,1)} %get-tuple-element.50.normed_ref, bf16[32,4096]{1,0:T(8,128)(2,1)} %get-tuple-element.51.masked_ref, bf16[4096,1536]{1,0:T(8,128)(2,1)} %gate_w_ref.1, ...), custom_call_target="tpu_custom_call" | custom-call | flops 2013265920 | bytes 38797312 | tf_op jit(solution)/shard_map/pallas_call | solution.py:161
  49.3 0.9 %constant_dynamic-update-slice_fusion.10 = bf16[96,1536]{1,0:T(8,128)(2,1)S(1)} fusion(bf16[32,1536]{1,0:T(8,128)(2,1)} %get-tuple-element.9), kind=kLoop, calls=%fused_computation.62 | loop fusion | bytes 196608
  50.2 0.9 %constant_dynamic-update-slice_fusion.9 = bf16[96,1536]{1,0:T(8,128)(2,1)S(1)} fusion(bf16[96,1536]{1,0:T(8,128)(2,1)S(1)} %constant_dynamic-update-slice_fusion.10, bf16[32,1536]{1,0:T(8,128)(2,1)} %get-tuple-element.10), kind=kLoop, calls=%fused_computation.61 | loop fusion | bytes 196608
  51.1 0.9 %constant_dynamic-update-slice_fusion.8 = bf16[96,1536]{1,0:T(8,128)(2,1)S(1)} fusion(bf16[96,1536]{1,0:T(8,128)(2,1)S(1)} %constant_dynamic-update-slice_fusion.9, bf16[32,1536]{1,0:T(8,128)(2,1)} %get-tuple-element.11), kind=kLoop, calls=%fused_computation.60 | loop fusion | bytes 196608 | tf_op jit(solution)/shard_map/concatenate | solution.py:222
  52.0 0.5 collective-permute-start.12
  52.5 1.1 %collective-permute-start.11 = (bf16[96,1536]{1,0:T(8,128)(2,1)S(1)}, bf16[96,1536]{1,0:T(8,128)(2,1)S(1)}, u32[]{:S(2)}, u32[]{:S(2)}) collective-permute-start(bf16[96,1536]{1,0:T(8,128)(2,1)S(1)} %constant_dynamic-update-slice_fusion.8), channel_id=1, source_target_pairs={{0,16},{8,24},{16,0},{24,8},{1,17},{9,25},{17,1},{25,9},{2,18},{10... | collective-permute-start | bytes 884744 | tf_op jit(solution)/shard_map/ppermute | solution.py:49
  54.0 1.1 %convert_element_type.37 = bf16[32,4096]{1,0:T(8,128)(2,1)S(1)} convert(f32[32,4096]{1,0:T(8,128)} %get-tuple-element.8) | non-fusion elementwise | flops 131072 | bytes 786432 | tf_op jit(solution)/shard_map/convert_element_type | solution.py:224
  55.1 1.7 %collective-permute-start.3 = (bf16[8,4096]{1,0:T(8,128)(2,1)S(1)}, bf16[8,4096]{1,0:T(8,128)(2,1)S(1)}, u32[]{:S(2)}, u32[]{:S(2)}) collective-permute-start(bf16[8,4096]{1,0:T(8,128)(2,1)S(1)} %get-tuple-element.30), channel_id=1, source_target_pairs={{0,6},{2,0},{4,2},{6,4},{1,7},{3,1},{5,3},{7,5},{8,14},{10,8},{12,... | collective-permute-start | bytes 196616 | tf_op jit(solution)/shard_map/ppermute | solution.py:49
  56.8 0.4 collective-permute-start.5
  57.2 2.7 %collective-permute-start.4 = (bf16[8,4096]{1,0:T(8,128)(2,1)S(1)}, bf16[8,4096]{1,0:T(8,128)(2,1)S(1)}, u32[]{:S(2)}, u32[]{:S(2)}) collective-permute-start(bf16[8,4096]{1,0:T(8,128)(2,1)S(1)} %get-tuple-element.32), channel_id=1, source_target_pairs={{0,4},{2,6},{4,0},{6,2},{1,5},{3,7},{5,1},{7,3},{8,12},{10,14},{12... | collective-permute-start | bytes 196616 | tf_op jit(solution)/shard_map/ppermute | solution.py:49
  60.2 0.8 constant_dynamic-slice_fusion.3
  61.2 2.4 %collective-permute-done.5 = bf16[8,4096]{1,0:T(8,128)(2,1)S(1)} collective-permute-done((bf16[8,4096]{1,0:T(8,128)(2,1)S(1)}, bf16[8,4096]{1,0:T(8,128)(2,1)S(1)}, u32[]{:S(2)}, u32[]{:S(2)}) %collective-permute-start.5) | collective-permute-done | bytes 65568 | tf_op jit(solution)/shard_map/ppermute | solution.py:49
  63.6 1.2 %collective-permute-done.4 = bf16[8,4096]{1,0:T(8,128)(2,1)S(1)} collective-permute-done((bf16[8,4096]{1,0:T(8,128)(2,1)S(1)}, bf16[8,4096]{1,0:T(8,128)(2,1)S(1)}, u32[]{:S(2)}, u32[]{:S(2)}) %collective-permute-start.4) | collective-permute-done | bytes 65568 | tf_op jit(solution)/shard_map/ppermute | solution.py:49
  64.9 0.7 collective-permute-start.8
  65.6 2.0 %collective-permute-done.9 = bf16[64,1024]{1,0:T(8,128)(2,1)S(1)} collective-permute-done((bf16[64,1024]{1,0:T(8,128)(2,1)S(1)}, bf16[64,1024]{1,0:T(8,128)(2,1)S(1)}, u32[]{:S(2)}, u32[]{:S(2)}) %collective-permute-start.9) | collective-permute-done | bytes 131104 | tf_op jit(solution)/shard_map/ppermute | solution.py:49
  67.6 1.3 %collective-permute-start.7 = (bf16[64,1024]{1,0:T(8,128)(2,1)S(1)}, bf16[64,1024]{1,0:T(8,128)(2,1)S(1)}, u32[]{:S(2)}, u32[]{:S(2)}) collective-permute-start(bf16[64,1024]{1,0:T(8,128)(2,1)S(1)} %bitcast.19), channel_id=1, source_target_pairs={{0,8},{8,16},{16,24},{24,0},{1,9},{9,17},{17,25},{25,1},{2,10},{10... | collective-permute-start | bytes 393224 | tf_op jit(solution)/shard_map/ppermute | solution.py:49
  68.9 2.7 %collective-permute-done.8 = bf16[64,1024]{1,0:T(8,128)(2,1)S(1)} collective-permute-done((bf16[64,1024]{1,0:T(8,128)(2,1)S(1)}, bf16[64,1024]{1,0:T(8,128)(2,1)S(1)}, u32[]{:S(2)}, u32[]{:S(2)}) %collective-permute-start.8) | collective-permute-done | bytes 131104 | tf_op jit(solution)/shard_map/ppermute | solution.py:49
  71.6 1.5 %collective-permute-start.6 = (bf16[8,4096]{1,0:T(8,128)(2,1)S(1)}, bf16[8,4096]{1,0:T(8,128)(2,1)S(1)}, u32[]{:S(2)}, u32[]{:S(2)}) collective-permute-start(bf16[8,4096]{1,0:T(8,128)(2,1)S(1)} %fusion.46), channel_id=1, source_target_pairs={{0,1},{1,0},{2,3},{3,2},{4,5},{5,4},{6,7},{7,6},{8,9},{9,8},{10,11... | collective-permute-start | bytes 196616 | tf_op jit(solution)/shard_map/ppermute | solution.py:49
  73.4 2.5 %collective-permute-done.6 = bf16[8,4096]{1,0:T(8,128)(2,1)S(1)} collective-permute-done((bf16[8,4096]{1,0:T(8,128)(2,1)S(1)}, bf16[8,4096]{1,0:T(8,128)(2,1)S(1)}, u32[]{:S(2)}, u32[]{:S(2)}) %collective-permute-start.6) | collective-permute-done | bytes 65568 | tf_op jit(solution)/shard_map/ppermute | solution.py:49
  76.0 1.5 %convolution_convert_fusion = bf16[128,4096]{1,0:T(8,128)(2,1)} fusion(f32[8,4096]{1,0:T(8,128)S(1)} %get-tuple-element.49, bf16[8,4096]{1,0:T(8,128)(2,1)S(1)} %collective-permute-done.6, f32[8]{0:T(128)S(1)} %multiply_multiply_fusion, f32[4096]{0:T(1024)S(1)} %copy-done.5, f32[8]{0:T(128)S(1)} %fusion.39, pred[8,256]{1,0:T(8,128)(4,1)S(1)} %fusion.36, ...), kind=kOutput, calls=%fused_computation | convolution fusion | flops 9404416 | bytes 1525764 | tf_op jit(solution)/shard_map/dot_general | solution.py:22
  77.6 3.7 %fusion.8 = f32[1024,1536]{1,0:T(8,128)} fusion(bf16[32,1536]{1,0:T(8,128)(2,1)S(1)} %get-tuple-element.28, bf16[32,1536]{1,0:T(8,128)(2,1)S(1)} %get-tuple-element.25, bf16[32,1536]{1,0:T(8,128)(2,1)S(1)} %get-tuple-element.22, bf16[32,1536]{1,0:T(8,128)(2,1)S(1)} %copy-done.4, bf16[32,1024]{1,0:T(8,128)(2,1)S(1)} %get-tuple-element.38, ...), kind=kOutput, calls=%fused_computation.10 | convolution fusion | flops 405274624 | bytes 6946816 | tf_op jit(solution)/shard_map/dot_general | solution.py:22
  81.3 3.7 %fusion = f32[1024,1536]{1,0:T(8,128)} fusion(bf16[32,1536]{1,0:T(8,128)(2,1)S(1)} %get-tuple-element.29, bf16[32,1536]{1,0:T(8,128)(2,1)S(1)} %get-tuple-element.26, bf16[32,1536]{1,0:T(8,128)(2,1)S(1)} %get-tuple-element.23, bf16[32,1536]{1,0:T(8,128)(2,1)S(1)} %copy-done.3, bf16[32,1024]{1,0:T(8,128)(2,1)S(1)} %get-tuple-element.38, ...), kind=kOutput, calls=%fused_computation.2 | convolution fusion | flops 405274624 | bytes 6946816 | tf_op jit(solution)/shard_map/dot_general | solution.py:22
  85.0 3.7 %fusion.16 = f32[1536,1024]{1,0:T(8,128)} fusion(bf16[32,1536]{1,0:T(8,128)(2,1)S(1)} %get-tuple-element.27, bf16[32,1536]{1,0:T(8,128)(2,1)S(1)} %get-tuple-element.24, bf16[32,1536]{1,0:T(8,128)(2,1)S(1)} %get-tuple-element.21, bf16[32,1536]{1,0:T(8,128)(2,1)S(1)} %copy-done.2, bf16[32,1024]{1,0:T(8,128)(2,1)S(1)} %get-tuple-element.37, ...), kind=kOutput, calls=%fused_computation.18 | convolution fusion | flops 405274624 | bytes 6946816 | tf_op jit(solution)/shard_map/dot_general | solution.py:22
  (52 shorter events, 2.2 us)
Async XLA Ops:
  0.6 3.4 %copy-start = (bf16[256,4096]{1,0:T(8,128)(2,1)S(1)}, bf16[256,4096]{1,0:T(8,128)(2,1)}, u32[]{:S(2)}) copy-start(bf16[256,4096]{1,0:T(8,128)(2,1)} %param.7) | copy-start | bytes 6291460
  5.4 16.3 %collective-permute-start.2 = (bf16[16,4096]{1,0:T(8,128)(2,1)S(1)}, bf16[16,4096]{1,0:T(8,128)(2,1)S(1)}, u32[]{:S(2)}, u32[]{:S(2)}) collective-permute-start(bf16[16,4096]{1,0:T(8,128)(2,1)S(1)} %pad_maximum_fusion.3), channel_id=1, source_target_pairs={{0,6},{2,0},{4,2},{6,4},{1,7},{3,1},{5,3},{7,5},{8,14},{10,8},{12,... | collective-permute-start | bytes 393224 | tf_op jit(solution)/shard_map/ppermute | solution.py:49
  10.5 11.2 %collective-permute-start.1 = (bf16[16,4096]{1,0:T(8,128)(2,1)S(1)}, bf16[16,4096]{1,0:T(8,128)(2,1)S(1)}, u32[]{:S(2)}, u32[]{:S(2)}) collective-permute-start(bf16[16,4096]{1,0:T(8,128)(2,1)S(1)} %pad_maximum_fusion.3), channel_id=1, source_target_pairs={{0,4},{2,6},{4,0},{6,2},{1,5},{3,7},{5,1},{7,3},{8,12},{10,14},{12... | collective-permute-start | bytes 393224 | tf_op jit(solution)/shard_map/ppermute | solution.py:49
  10.5 9.4 %collective-permute-start = (bf16[16,4096]{1,0:T(8,128)(2,1)S(1)}, bf16[16,4096]{1,0:T(8,128)(2,1)S(1)}, u32[]{:S(2)}, u32[]{:S(2)}) collective-permute-start(bf16[16,4096]{1,0:T(8,128)(2,1)S(1)} %pad_maximum_fusion.3), channel_id=1, source_target_pairs={{0,2},{2,4},{4,6},{6,0},{1,3},{3,5},{5,7},{7,1},{8,10},{10,12},{12... | collective-permute-start | bytes 393224 | tf_op jit(solution)/shard_map/ppermute | solution.py:49
  49.3 26.6 %copy-start.5 = (f32[4096]{0:T(1024)S(1)}, f32[4096]{0:T(1024)}, u32[]{:S(2)}) copy-start(f32[4096]{0:T(1024)} %param.9) | copy-start | bytes 49156
  49.3 28.3 %copy-start.4 = (bf16[32,1536]{1,0:T(8,128)(2,1)S(1)}, bf16[32,1536]{1,0:T(8,128)(2,1)}, u32[]{:S(2)}) copy-start(bf16[32,1536]{1,0:T(8,128)(2,1)} %get-tuple-element.10) | copy-start | bytes 294916
  52.0 25.4 %collective-permute-start.12 = (bf16[96,1536]{1,0:T(8,128)(2,1)S(1)}, bf16[96,1536]{1,0:T(8,128)(2,1)S(1)}, u32[]{:S(2)}, u32[]{:S(2)}) collective-permute-start(bf16[96,1536]{1,0:T(8,128)(2,1)S(1)} %constant_dynamic-update-slice_fusion.8), channel_id=1, source_target_pairs={{0,24},{8,0},{16,8},{24,16},{1,25},{9,1},{17,9},{25,17},{2,26},{10... | collective-permute-start | bytes 884744 | tf_op jit(solution)/shard_map/ppermute | solution.py:49
  52.5 25.0 %collective-permute-start.11 = (bf16[96,1536]{1,0:T(8,128)(2,1)S(1)}, bf16[96,1536]{1,0:T(8,128)(2,1)S(1)}, u32[]{:S(2)}, u32[]{:S(2)}) collective-permute-start(bf16[96,1536]{1,0:T(8,128)(2,1)S(1)} %constant_dynamic-update-slice_fusion.8), channel_id=1, source_target_pairs={{0,16},{8,24},{16,0},{24,8},{1,17},{9,25},{17,1},{25,9},{2,18},{10... | collective-permute-start | bytes 884744 | tf_op jit(solution)/shard_map/ppermute | solution.py:49
  55.1 6.1 %collective-permute-start.3 = (bf16[8,4096]{1,0:T(8,128)(2,1)S(1)}, bf16[8,4096]{1,0:T(8,128)(2,1)S(1)}, u32[]{:S(2)}, u32[]{:S(2)}) collective-permute-start(bf16[8,4096]{1,0:T(8,128)(2,1)S(1)} %get-tuple-element.30), channel_id=1, source_target_pairs={{0,6},{2,0},{4,2},{6,4},{1,7},{3,1},{5,3},{7,5},{8,14},{10,8},{12,... | collective-permute-start | bytes 196616 | tf_op jit(solution)/shard_map/ppermute | solution.py:49
  56.8 6.9 %collective-permute-start.5 = (bf16[8,4096]{1,0:T(8,128)(2,1)S(1)}, bf16[8,4096]{1,0:T(8,128)(2,1)S(1)}, u32[]{:S(2)}, u32[]{:S(2)}) collective-permute-start(bf16[8,4096]{1,0:T(8,128)(2,1)S(1)} %get-tuple-element.31), channel_id=1, source_target_pairs={{0,2},{2,4},{4,6},{6,0},{1,3},{3,5},{5,7},{7,1},{8,10},{10,12},{12... | collective-permute-start | bytes 196616 | tf_op jit(solution)/shard_map/ppermute | solution.py:49
  57.2 7.7 %collective-permute-start.4 = (bf16[8,4096]{1,0:T(8,128)(2,1)S(1)}, bf16[8,4096]{1,0:T(8,128)(2,1)S(1)}, u32[]{:S(2)}, u32[]{:S(2)}) collective-permute-start(bf16[8,4096]{1,0:T(8,128)(2,1)S(1)} %get-tuple-element.32), channel_id=1, source_target_pairs={{0,4},{2,6},{4,0},{6,2},{1,5},{3,7},{5,1},{7,3},{8,12},{10,14},{12... | collective-permute-start | bytes 196616 | tf_op jit(solution)/shard_map/ppermute | solution.py:49
  61.2 16.4 %collective-permute-start.10 = (bf16[96,1536]{1,0:T(8,128)(2,1)S(1)}, bf16[96,1536]{1,0:T(8,128)(2,1)S(1)}, u32[]{:S(2)}, u32[]{:S(2)}) collective-permute-start(bf16[96,1536]{1,0:T(8,128)(2,1)S(1)} %constant_dynamic-update-slice_fusion.8), channel_id=1, source_target_pairs={{0,8},{8,16},{16,24},{24,0},{1,9},{9,17},{17,25},{25,1},{2,10},{10... | collective-permute-start | bytes 884744 | tf_op jit(solution)/shard_map/ppermute | solution.py:49
  63.6 4.0 %collective-permute-start.9 = (bf16[64,1024]{1,0:T(8,128)(2,1)S(1)}, bf16[64,1024]{1,0:T(8,128)(2,1)S(1)}, u32[]{:S(2)}, u32[]{:S(2)}) collective-permute-start(bf16[64,1024]{1,0:T(8,128)(2,1)S(1)} %bitcast.21), channel_id=1, source_target_pairs={{0,24},{8,0},{16,8},{24,16},{1,25},{9,1},{17,9},{25,17},{2,26},{10... | collective-permute-start | bytes 393224 | tf_op jit(solution)/shard_map/ppermute | solution.py:49
  64.9 6.7 %collective-permute-start.8 = (bf16[64,1024]{1,0:T(8,128)(2,1)S(1)}, bf16[64,1024]{1,0:T(8,128)(2,1)S(1)}, u32[]{:S(2)}, u32[]{:S(2)}) collective-permute-start(bf16[64,1024]{1,0:T(8,128)(2,1)S(1)} %bitcast.20), channel_id=1, source_target_pairs={{0,16},{8,24},{16,0},{24,8},{1,17},{9,25},{17,1},{25,9},{2,18},{10... | collective-permute-start | bytes 393224 | tf_op jit(solution)/shard_map/ppermute | solution.py:49
  67.6 5.8 %collective-permute-start.7 = (bf16[64,1024]{1,0:T(8,128)(2,1)S(1)}, bf16[64,1024]{1,0:T(8,128)(2,1)S(1)}, u32[]{:S(2)}, u32[]{:S(2)}) collective-permute-start(bf16[64,1024]{1,0:T(8,128)(2,1)S(1)} %bitcast.19), channel_id=1, source_target_pairs={{0,8},{8,16},{16,24},{24,0},{1,9},{9,17},{17,25},{25,1},{2,10},{10... | collective-permute-start | bytes 393224 | tf_op jit(solution)/shard_map/ppermute | solution.py:49
  71.6 4.3 %collective-permute-start.6 = (bf16[8,4096]{1,0:T(8,128)(2,1)S(1)}, bf16[8,4096]{1,0:T(8,128)(2,1)S(1)}, u32[]{:S(2)}, u32[]{:S(2)}) collective-permute-start(bf16[8,4096]{1,0:T(8,128)(2,1)S(1)} %fusion.46), channel_id=1, source_target_pairs={{0,1},{1,0},{2,3},{3,2},{4,5},{5,4},{6,7},{7,6},{8,9},{9,8},{10,11... | collective-permute-start | bytes 196616 | tf_op jit(solution)/shard_map/ppermute | solution.py:49
  77.5 3.8 %copy-start.3 = (bf16[32,1536]{1,0:T(8,128)(2,1)S(1)}, bf16[32,1536]{1,0:T(8,128)(2,1)}, u32[]{:S(2)}) copy-start(bf16[32,1536]{1,0:T(8,128)(2,1)} %get-tuple-element.9) | copy-start | bytes 294916
  81.3 3.7 %copy-start.2 = (bf16[32,1536]{1,0:T(8,128)(2,1)S(1)}, bf16[32,1536]{1,0:T(8,128)(2,1)}, u32[]{:S(2)}) copy-start(bf16[32,1536]{1,0:T(8,128)(2,1)} %get-tuple-element.11) | copy-start | bytes 294916
  81.3 7.4 %copy-start.1 = (bf16[256,4096]{1,0:T(8,128)(2,1)S(1)}, bf16[256,4096]{1,0:T(8,128)(2,1)}, u32[]{:S(2)}) copy-start(bf16[256,4096]{1,0:T(8,128)(2,1)} %param.7) | copy-start | bytes 6291460

commit v6 on v5

--- a/solution.py
+++ b/solution.py
@@ -4,6 +4,7 @@
 import jax.numpy as jnp
 from jax import lax
 from jax.experimental import pallas as pl
+from jax.experimental.pallas import tpu as pltpu
 from jax.sharding import PartitionSpec as P
 
 REC = 1
@@ -156,7 +157,7 @@
 def weight_pass(window_normed, window_masked, gate_weight, up_weight, down_weight):
     rows, features = window_normed.shape
     units = gate_weight.shape[1]
-    chunk = 256 if units % 256 == 0 else units
+    chunk = next((size for size in (512, 256, 128) if units % size == 0), units)
     factor_shape = jax.ShapeDtypeStruct((rows, units), jnp.bfloat16)
     return pl.pallas_call(
         weight_pass_kernel,
@@ -180,6 +181,7 @@
             factor_shape,
             jax.ShapeDtypeStruct((rows, features), jnp.float32),
         ],
+        compiler_params=pltpu.CompilerParams(vmem_limit_bytes=56 * 1024 * 1024),
         cost_estimate=pl.CostEstimate(
             flops=10 * rows * features * units,
             transcendentals=rows * units,
@@ -226,9 +228,6 @@
     for k in range(1, shards):
         piece = partial_features[k * MAXACT : (k + 1) * MAXACT]
         feature_grad = feature_grad + shifted(piece, "seq", (shards,), (-k,)).astype(jnp.float32)
-    seq_sum = feature_grad.astype(jnp.bfloat16)
-    for step in range(1, parts):
-        feature_grad = feature_grad + shifted(seq_sum, "fsdp", (parts,), (step,)).astype(jnp.float32)
     every_gate = jnp.concatenate([f[:window] for f in every_factors], axis=0)
     every_up = jnp.concatenate([f[window : 2 * window] for f in every_factors], axis=0)
     every_hidden = jnp.concatenate([f[2 * window :] for f in every_factors], axis=0)
@@ -237,6 +236,12 @@
     gate_grad = contract_first(normed_cols, every_gate)
     up_grad = contract_first(normed_cols, every_up)
     down_grad = contract_first(every_hidden, masked_cols)
+    feature_grad, gate_grad, up_grad, down_grad = lax.optimization_barrier(
+        (feature_grad, gate_grad, up_grad, down_grad)
+    )
+    seq_sum = feature_grad.astype(jnp.bfloat16)
+    for step in range(1, parts):
+        feature_grad = feature_grad + shifted(seq_sum, "fsdp", (parts,), (step,)).astype(jnp.float32)
     _, pullback = jax.vjp(partial(normalize, norm_gain=norm_gain), source)
     slot_grad = pullback(feature_grad)[0].astype(jnp.bfloat16)
     own_columns = lax.dynamic_slice_in_dim(picker, place * own_rows, own_rows, 1)

time: 89.1 us -> 87.7 us (0.984)
  waiting for transfers between devices: 21.2 us -> 25.4 us
  Pallas kernels: 26.6 us -> 22.6 us
  starting transfers between devices: 16 us -> 14.4 us
    ppermute x13, waiting for transfers between devices: 21.2 us -> 25.4 us  [shifted(): return lax.ppermute(value, axes, pairs)]
    pallas_call x1, Pallas kernels: 26.6 us -> 22.6 us  [weight_pass(): pl.pallas_call(weight_pass_kernel, grid=(units // chunk,), in_specs=[pl.B...]
    ppermute x13, starting transfers between devices: 16 us -> 14.4 us  [shifted(): return lax.ppermute(value, axes, pairs)]
  transfers between devices with their start and end apart: 13 -> 13, of which waited for: 8 -> 9; matrix products, arithmetic and copies ran while one was open for 5% -> 3% of each run, Pallas kernels for 0% -> 0%
where the time goes in v6:
time: 87.7 us; the launch traced here: 87.4 us
  waiting for transfers between devices  25.4 us (29%)
  Pallas kernels  22.6 us (26%)
  matrix products  15.1 us (17%)
  starting transfers between devices  14.4 us (16%)
  local copies, waits for them, and re-layouts  4.79 us (5%)
  other arithmetic  4.19 us (5%)
    ppermute x13, waiting for transfers between devices, shifted(): return lax.ppermute(value, axes, pairs)  25.4 us
    pallas_call x1, Pallas kernels, weight_pass(): pl.pallas_call(weight_pass_kernel, grid=(units // chunk,), in_specs=[pl.B...  22.6 us
    ppermute x13, starting transfers between devices, shifted(): return lax.ppermute(value, axes, pairs)  14.4 us
    dot_general x4, matrix products, contract_first(): lax.dot_general(left, right, (((0,), (0,)), ((), ())), preferred_element_...  12.6 us
    unnamed x23, local copies, waits for them, and re-layouts  2.06 us
    dot_general x1, matrix products, local(): jnp.dot(picker, cotangent, preferred_element_type=jnp.float32)  1.97 us
  transfers between devices with their start and end apart: 13, of which 9 were waited for; matrix products, arithmetic and copies ran while one was open for 3% of the time, Pallas kernels for 0%

profile of v6, /device:TPU:0, one launch (start us, length us, event | category | flops | bytes accessed | tf_op | source)
XLA Modules:
  0.0 87.4 jit_solution(7289426916094556660)
XLA Ops:
  0.6 0.8 convert_bitcast_fusion
  2.1 2.0 %convolution_convert_fusion.1 = bf16[8,4096]{1,0:T(8,128)(2,1)S(1)} fusion(bf16[256,4096]{1,0:T(8,128)(2,1)} %param.8, s32[256]{0:T(256)S(1)} %add_bitcast_fusion, pred[256]{0:T(512)(128)(4,1)S(1)} %get-tuple-element.23), kind=kOutput, calls=%fused_computation.1 | convolution fusion | flops 16814080 | bytes 2163968 | tf_op jit(solution)/shard_map/dot_general | solution.py:208
  4.6 0.8 constant_dynamic-update-slice_fusion.7
  5.4 3.1 %collective-permute-start = (bf16[16,4096]{1,0:T(8,128)(2,1)S(1)}, bf16[16,4096]{1,0:T(8,128)(2,1)S(1)}, u32[]{:S(2)}, u32[]{:S(2)}) collective-permute-start(bf16[16,4096]{1,0:T(8,128)(2,1)S(1)} %pad_maximum_fusion.3), channel_id=1, source_target_pairs={{0,2},{2,4},{4,6},{6,0},{1,3},{3,5},{5,7},{7,1},{8,10},{10,12},{12... | collective-permute-start | bytes 393224 | tf_op jit(solution)/shard_map/ppermute | solution.py:50
  8.5 2.1 %collective-permute-start.2 = (bf16[16,4096]{1,0:T(8,128)(2,1)S(1)}, bf16[16,4096]{1,0:T(8,128)(2,1)S(1)}, u32[]{:S(2)}, u32[]{:S(2)}) collective-permute-start(bf16[16,4096]{1,0:T(8,128)(2,1)S(1)} %pad_maximum_fusion.3), channel_id=1, source_target_pairs={{0,6},{2,0},{4,2},{6,4},{1,7},{3,1},{5,3},{7,5},{8,14},{10,8},{12,... | collective-permute-start | bytes 393224 | tf_op jit(solution)/shard_map/ppermute | solution.py:50
  10.6 0.9 %collective-permute-start.1 = (bf16[16,4096]{1,0:T(8,128)(2,1)S(1)}, bf16[16,4096]{1,0:T(8,128)(2,1)S(1)}, u32[]{:S(2)}, u32[]{:S(2)}) collective-permute-start(bf16[16,4096]{1,0:T(8,128)(2,1)S(1)} %pad_maximum_fusion.3), channel_id=1, source_target_pairs={{0,4},{2,6},{4,0},{6,2},{1,5},{3,7},{5,1},{7,3},{8,12},{10,14},{12... | collective-permute-start | bytes 393224 | tf_op jit(solution)/shard_map/ppermute | solution.py:50
  11.5 3.3 %collective-permute-done = bf16[16,4096]{1,0:T(8,128)(2,1)S(1)} collective-permute-done((bf16[16,4096]{1,0:T(8,128)(2,1)S(1)}, bf16[16,4096]{1,0:T(8,128)(2,1)S(1)}, u32[]{:S(2)}, u32[]{:S(2)}) %collective-permute-start) | collective-permute-done | bytes 131104 | tf_op jit(solution)/shard_map/ppermute | solution.py:50
  14.9 7.6 %collective-permute-done.1 = bf16[16,4096]{1,0:T(8,128)(2,1)S(1)} collective-permute-done((bf16[16,4096]{1,0:T(8,128)(2,1)S(1)}, bf16[16,4096]{1,0:T(8,128)(2,1)S(1)}, u32[]{:S(2)}, u32[]{:S(2)}) %collective-permute-start.1) | collective-permute-done | bytes 131104 | tf_op jit(solution)/shard_map/ppermute | solution.py:50
  22.6 0.8 pad_maximum_fusion
  23.4 22.6 %shard_map.102 = (bf16[32,1536]{1,0:T(8,128)(2,1)}, bf16[32,1536]{1,0:T(8,128)(2,1)}, bf16[32,1536]{1,0:T(8,128)(2,1)}, f32[32,4096]{1,0:T(8,128)}) custom-call(bf16[32,4096]{1,0:T(8,128)(2,1)} %get-tuple-element.58.normed_ref, bf16[32,4096]{1,0:T(8,128)(2,1)} %get-tuple-element.59.masked_ref, bf16[4096,1536]{1,0:T(8,128)(2,1)} %gate_w_ref.1, ...), custom_call_target="tpu_custom_call" | custom-call | flops 2013265920 | bytes 38797312 | tf_op jit(solution)/shard_map/pallas_call | solution.py:162
  46.0 0.9 %constant_dynamic-update-slice_fusion.10 = bf16[96,1536]{1,0:T(8,128)(2,1)S(1)} fusion(bf16[32,1536]{1,0:T(8,128)(2,1)} %get-tuple-element.13), kind=kLoop, calls=%fused_computation.62 | loop fusion | bytes 196608
  47.0 0.9 %constant_dynamic-update-slice_fusion.9 = bf16[96,1536]{1,0:T(8,128)(2,1)S(1)} fusion(bf16[96,1536]{1,0:T(8,128)(2,1)S(1)} %constant_dynamic-update-slice_fusion.10, bf16[32,1536]{1,0:T(8,128)(2,1)} %get-tuple-element.14), kind=kLoop, calls=%fused_computation.61 | loop fusion | bytes 196608
  47.9 0.9 %constant_dynamic-update-slice_fusion.8 = bf16[96,1536]{1,0:T(8,128)(2,1)S(1)} fusion(bf16[96,1536]{1,0:T(8,128)(2,1)S(1)} %constant_dynamic-update-slice_fusion.9, bf16[32,1536]{1,0:T(8,128)(2,1)} %get-tuple-element.15), kind=kLoop, calls=%fused_computation.60 | loop fusion | bytes 196608 | tf_op jit(solution)/shard_map/concatenate | solution.py:224
  48.8 1.1 %collective-permute-start.11 = (bf16[96,1536]{1,0:T(8,128)(2,1)S(1)}, bf16[96,1536]{1,0:T(8,128)(2,1)S(1)}, u32[]{:S(2)}, u32[]{:S(2)}) collective-permute-start(bf16[96,1536]{1,0:T(8,128)(2,1)S(1)} %constant_dynamic-update-slice_fusion.8), channel_id=1, source_target_pairs={{0,24},{8,0},{16,8},{24,16},{1,25},{9,1},{17,9},{25,17},{2,26},{10... | collective-permute-start | bytes 884744 | tf_op jit(solution)/shard_map/ppermute | solution.py:50
  49.9 0.5 collective-permute-start.10
  50.8 1.1 %convert_element_type.37 = bf16[32,4096]{1,0:T(8,128)(2,1)S(1)} convert(f32[32,4096]{1,0:T(8,128)} %get-tuple-element.12) | non-fusion elementwise | flops 131072 | bytes 786432 | tf_op jit(solution)/shard_map/convert_element_type | solution.py:226
  51.9 1.6 %collective-permute-start.3 = (bf16[8,4096]{1,0:T(8,128)(2,1)S(1)}, bf16[8,4096]{1,0:T(8,128)(2,1)S(1)}, u32[]{:S(2)}, u32[]{:S(2)}) collective-permute-start(bf16[8,4096]{1,0:T(8,128)(2,1)S(1)} %get-tuple-element.38), channel_id=1, source_target_pairs={{0,6},{2,0},{4,2},{6,4},{1,7},{3,1},{5,3},{7,5},{8,14},{10,8},{12,... | collective-permute-start | bytes 196616 | tf_op jit(solution)/shard_map/ppermute | solution.py:50
  54.5 0.8 constant_dynamic-slice_fusion.3
  55.5 0.8 collective-permute-done.3
  56.2 3.8 %collective-permute-done.5 = bf16[8,4096]{1,0:T(8,128)(2,1)S(1)} collective-permute-done((bf16[8,4096]{1,0:T(8,128)(2,1)S(1)}, bf16[8,4096]{1,0:T(8,128)(2,1)S(1)}, u32[]{:S(2)}, u32[]{:S(2)}) %collective-permute-start.5) | collective-permute-done | bytes 65568 | tf_op jit(solution)/shard_map/ppermute | solution.py:50
  60.0 1.3 %collective-permute-done.4 = bf16[8,4096]{1,0:T(8,128)(2,1)S(1)} collective-permute-done((bf16[8,4096]{1,0:T(8,128)(2,1)S(1)}, bf16[8,4096]{1,0:T(8,128)(2,1)S(1)}, u32[]{:S(2)}, u32[]{:S(2)}) %collective-permute-start.4) | collective-permute-done | bytes 65568 | tf_op jit(solution)/shard_map/ppermute | solution.py:50
  61.3 0.8 collective-permute-start.7
  62.1 1.8 %collective-permute-done.8 = bf16[64,1024]{1,0:T(8,128)(2,1)S(1)} collective-permute-done((bf16[64,1024]{1,0:T(8,128)(2,1)S(1)}, bf16[64,1024]{1,0:T(8,128)(2,1)S(1)}, u32[]{:S(2)}, u32[]{:S(2)}) %collective-permute-start.8) | collective-permute-done | bytes 131104 | tf_op jit(solution)/shard_map/ppermute | solution.py:50
  63.9 2.1 %collective-permute-start.6 = (bf16[64,1024]{1,0:T(8,128)(2,1)S(1)}, bf16[64,1024]{1,0:T(8,128)(2,1)S(1)}, u32[]{:S(2)}, u32[]{:S(2)}) collective-permute-start(bf16[64,1024]{1,0:T(8,128)(2,1)S(1)} %bitcast.19), channel_id=1, source_target_pairs={{0,8},{8,16},{16,24},{24,0},{1,9},{9,17},{17,25},{25,1},{2,10},{10... | collective-permute-start | bytes 393224 | tf_op jit(solution)/shard_map/ppermute | solution.py:50
  66.0 3.0 %collective-permute-done.7 = bf16[64,1024]{1,0:T(8,128)(2,1)S(1)} collective-permute-done((bf16[64,1024]{1,0:T(8,128)(2,1)S(1)}, bf16[64,1024]{1,0:T(8,128)(2,1)S(1)}, u32[]{:S(2)}, u32[]{:S(2)}) %collective-permute-start.7) | collective-permute-done | bytes 131104 | tf_op jit(solution)/shard_map/ppermute | solution.py:50
  69.0 1.1 %collective-permute-done.6 = bf16[64,1024]{1,0:T(8,128)(2,1)S(1)} collective-permute-done((bf16[64,1024]{1,0:T(8,128)(2,1)S(1)}, bf16[64,1024]{1,0:T(8,128)(2,1)S(1)}, u32[]{:S(2)}, u32[]{:S(2)}) %collective-permute-start.6) | collective-permute-done | bytes 131104 | tf_op jit(solution)/shard_map/ppermute | solution.py:50
  70.3 3.7 %fusion.8 = f32[1024,1536]{1,0:T(8,128)} fusion(bf16[32,1536]{1,0:T(8,128)(2,1)S(1)} %get-tuple-element.36, bf16[32,1536]{1,0:T(8,128)(2,1)S(1)} %get-tuple-element.33, bf16[32,1536]{1,0:T(8,128)(2,1)S(1)} %get-tuple-element.30, bf16[32,1536]{1,0:T(8,128)(2,1)S(1)} %copy-done.4, bf16[32,1024]{1,0:T(8,128)(2,1)S(1)} %get-tuple-element.46, ...), kind=kOutput, calls=%fused_computation.10 | convolution fusion | flops 405274624 | bytes 6946816 | tf_op jit(solution)/shard_map/dot_general | solution.py:23
  74.0 3.7 %fusion = f32[1024,1536]{1,0:T(8,128)} fusion(bf16[32,1536]{1,0:T(8,128)(2,1)S(1)} %get-tuple-element.37, bf16[32,1536]{1,0:T(8,128)(2,1)S(1)} %get-tuple-element.34, bf16[32,1536]{1,0:T(8,128)(2,1)S(1)} %get-tuple-element.31, bf16[32,1536]{1,0:T(8,128)(2,1)S(1)} %copy-done.3, bf16[32,1024]{1,0:T(8,128)(2,1)S(1)} %get-tuple-element.46, ...), kind=kOutput, calls=%fused_computation.2 | convolution fusion | flops 405274624 | bytes 6946816 | tf_op jit(solution)/shard_map/dot_general | solution.py:23
  77.7 3.7 %fusion.16 = f32[1536,1024]{1,0:T(8,128)} fusion(bf16[32,1536]{1,0:T(8,128)(2,1)S(1)} %get-tuple-element.35, bf16[32,1536]{1,0:T(8,128)(2,1)S(1)} %get-tuple-element.32, bf16[32,1536]{1,0:T(8,128)(2,1)S(1)} %get-tuple-element.29, bf16[32,1536]{1,0:T(8,128)(2,1)S(1)} %copy-done.2, bf16[32,1024]{1,0:T(8,128)(2,1)S(1)} %get-tuple-element.45, ...), kind=kOutput, calls=%fused_computation.18 | convolution fusion | flops 405274624 | bytes 6946816 | tf_op jit(solution)/shard_map/dot_general | solution.py:23
  81.4 1.6 %collective-permute-start.12 = (bf16[8,4096]{1,0:T(8,128)(2,1)S(1)}, bf16[8,4096]{1,0:T(8,128)(2,1)S(1)}, u32[]{:S(2)}, u32[]{:S(2)}) collective-permute-start(bf16[8,4096]{1,0:T(8,128)(2,1)S(1)} %convert_element_type.42), channel_id=1, source_target_pairs={{0,1},{1,0},{2,3},{3,2},{4,5},{5,4},{6,7},{7,6},{8,9},{9,8},{10,11... | collective-permute-start | bytes 196616 | tf_op jit(solution)/shard_map/ppermute | solution.py:50
  83.0 2.8 %collective-permute-done.12 = bf16[8,4096]{1,0:T(8,128)(2,1)S(1)} collective-permute-done((bf16[8,4096]{1,0:T(8,128)(2,1)S(1)}, bf16[8,4096]{1,0:T(8,128)(2,1)S(1)}, u32[]{:S(2)}, u32[]{:S(2)}) %collective-permute-start.12) | collective-permute-done | bytes 65568 | tf_op jit(solution)/shard_map/ppermute | solution.py:50
  85.9 1.5 %convolution_convert_fusion = bf16[128,4096]{1,0:T(8,128)(2,1)} fusion(f32[8,4096]{1,0:T(8,128)S(1)} %get-tuple-element.57, f32[8,4096]{1,0:T(8,128)S(1)} %convert_add_fusion, bf16[8,4096]{1,0:T(8,128)(2,1)S(1)} %collective-permute-done.12, f32[8]{0:T(128)S(1)} %multiply_multiply_fusion, f32[4096]{0:T(1024)S(1)} %copy-done.5, f32[8]{0:T(128)S(1)} %fusion.39, ...), kind=kOutput, calls=%fused_computation | convolution fusion | flops 9175040 | bytes 1394692 | tf_op jit(solution)/shard_map/dot_general | solution.py:23
  (53 shorter events, 3.0 us)
Async XLA Ops:
  0.6 3.4 %copy-start = (bf16[256,4096]{1,0:T(8,128)(2,1)S(1)}, bf16[256,4096]{1,0:T(8,128)(2,1)}, u32[]{:S(2)}) copy-start(bf16[256,4096]{1,0:T(8,128)(2,1)} %param.7) | copy-start | bytes 6291460
  5.4 9.4 %collective-permute-start = (bf16[16,4096]{1,0:T(8,128)(2,1)S(1)}, bf16[16,4096]{1,0:T(8,128)(2,1)S(1)}, u32[]{:S(2)}, u32[]{:S(2)}) collective-permute-start(bf16[16,4096]{1,0:T(8,128)(2,1)S(1)} %pad_maximum_fusion.3), channel_id=1, source_target_pairs={{0,2},{2,4},{4,6},{6,0},{1,3},{3,5},{5,7},{7,1},{8,10},{10,12},{12... | collective-permute-start | bytes 393224 | tf_op jit(solution)/shard_map/ppermute | solution.py:50
  8.5 14.0 %collective-permute-start.2 = (bf16[16,4096]{1,0:T(8,128)(2,1)S(1)}, bf16[16,4096]{1,0:T(8,128)(2,1)S(1)}, u32[]{:S(2)}, u32[]{:S(2)}) collective-permute-start(bf16[16,4096]{1,0:T(8,128)(2,1)S(1)} %pad_maximum_fusion.3), channel_id=1, source_target_pairs={{0,6},{2,0},{4,2},{6,4},{1,7},{3,1},{5,3},{7,5},{8,14},{10,8},{12,... | collective-permute-start | bytes 393224 | tf_op jit(solution)/shard_map/ppermute | solution.py:50
  10.6 11.9 %collective-permute-start.1 = (bf16[16,4096]{1,0:T(8,128)(2,1)S(1)}, bf16[16,4096]{1,0:T(8,128)(2,1)S(1)}, u32[]{:S(2)}, u32[]{:S(2)}) collective-permute-start(bf16[16,4096]{1,0:T(8,128)(2,1)S(1)} %pad_maximum_fusion.3), channel_id=1, source_target_pairs={{0,4},{2,6},{4,0},{6,2},{1,5},{3,7},{5,1},{7,3},{8,12},{10,14},{12... | collective-permute-start | bytes 393224 | tf_op jit(solution)/shard_map/ppermute | solution.py:50
  46.0 24.2 %copy-start.4 = (bf16[32,1536]{1,0:T(8,128)(2,1)S(1)}, bf16[32,1536]{1,0:T(8,128)(2,1)}, u32[]{:S(2)}) copy-start(bf16[32,1536]{1,0:T(8,128)(2,1)} %get-tuple-element.14) | copy-start | bytes 294916
  48.8 21.4 %collective-permute-start.11 = (bf16[96,1536]{1,0:T(8,128)(2,1)S(1)}, bf16[96,1536]{1,0:T(8,128)(2,1)S(1)}, u32[]{:S(2)}, u32[]{:S(2)}) collective-permute-start(bf16[96,1536]{1,0:T(8,128)(2,1)S(1)} %constant_dynamic-update-slice_fusion.8), channel_id=1, source_target_pairs={{0,24},{8,0},{16,8},{24,16},{1,25},{9,1},{17,9},{25,17},{2,26},{10... | collective-permute-start | bytes 884744 | tf_op jit(solution)/shard_map/ppermute | solution.py:50
  49.9 20.3 %collective-permute-start.10 = (bf16[96,1536]{1,0:T(8,128)(2,1)S(1)}, bf16[96,1536]{1,0:T(8,128)(2,1)S(1)}, u32[]{:S(2)}, u32[]{:S(2)}) collective-permute-start(bf16[96,1536]{1,0:T(8,128)(2,1)S(1)} %constant_dynamic-update-slice_fusion.8), channel_id=1, source_target_pairs={{0,16},{8,24},{16,0},{24,8},{1,17},{9,25},{17,1},{25,9},{2,18},{10... | collective-permute-start | bytes 884744 | tf_op jit(solution)/shard_map/ppermute | solution.py:50
  51.9 4.3 %collective-permute-start.3 = (bf16[8,4096]{1,0:T(8,128)(2,1)S(1)}, bf16[8,4096]{1,0:T(8,128)(2,1)S(1)}, u32[]{:S(2)}, u32[]{:S(2)}) collective-permute-start(bf16[8,4096]{1,0:T(8,128)(2,1)S(1)} %get-tuple-element.38), channel_id=1, source_target_pairs={{0,6},{2,0},{4,2},{6,4},{1,7},{3,1},{5,3},{7,5},{8,14},{10,8},{12,... | collective-permute-start | bytes 196616 | tf_op jit(solution)/shard_map/ppermute | solution.py:50
  53.5 6.5 %collective-permute-start.5 = (bf16[8,4096]{1,0:T(8,128)(2,1)S(1)}, bf16[8,4096]{1,0:T(8,128)(2,1)S(1)}, u32[]{:S(2)}, u32[]{:S(2)}) collective-permute-start(bf16[8,4096]{1,0:T(8,128)(2,1)S(1)} %get-tuple-element.39), channel_id=1, source_target_pairs={{0,2},{2,4},{4,6},{6,0},{1,3},{3,5},{5,7},{7,1},{8,10},{10,12},{12... | collective-permute-start | bytes 196616 | tf_op jit(solution)/shard_map/ppermute | solution.py:50
  54.0 7.3 %collective-permute-start.4 = (bf16[8,4096]{1,0:T(8,128)(2,1)S(1)}, bf16[8,4096]{1,0:T(8,128)(2,1)S(1)}, u32[]{:S(2)}, u32[]{:S(2)}) collective-permute-start(bf16[8,4096]{1,0:T(8,128)(2,1)S(1)} %get-tuple-element.40), channel_id=1, source_target_pairs={{0,4},{2,6},{4,0},{6,2},{1,5},{3,7},{5,1},{7,3},{8,12},{10,14},{12... | collective-permute-start | bytes 196616 | tf_op jit(solution)/shard_map/ppermute | solution.py:50
  56.2 14.0 %collective-permute-start.9 = (bf16[96,1536]{1,0:T(8,128)(2,1)S(1)}, bf16[96,1536]{1,0:T(8,128)(2,1)S(1)}, u32[]{:S(2)}, u32[]{:S(2)}) collective-permute-start(bf16[96,1536]{1,0:T(8,128)(2,1)S(1)} %constant_dynamic-update-slice_fusion.8), channel_id=1, source_target_pairs={{0,8},{8,16},{16,24},{24,0},{1,9},{9,17},{17,25},{25,1},{2,10},{10... | collective-permute-start | bytes 884744 | tf_op jit(solution)/shard_map/ppermute | solution.py:50
  60.0 4.0 %collective-permute-start.8 = (bf16[64,1024]{1,0:T(8,128)(2,1)S(1)}, bf16[64,1024]{1,0:T(8,128)(2,1)S(1)}, u32[]{:S(2)}, u32[]{:S(2)}) collective-permute-start(bf16[64,1024]{1,0:T(8,128)(2,1)S(1)} %bitcast.21), channel_id=1, source_target_pairs={{0,24},{8,0},{16,8},{24,16},{1,25},{9,1},{17,9},{25,17},{2,26},{10... | collective-permute-start | bytes 393224 | tf_op jit(solution)/shard_map/ppermute | solution.py:50
  61.3 7.7 %collective-permute-start.7 = (bf16[64,1024]{1,0:T(8,128)(2,1)S(1)}, bf16[64,1024]{1,0:T(8,128)(2,1)S(1)}, u32[]{:S(2)}, u32[]{:S(2)}) collective-permute-start(bf16[64,1024]{1,0:T(8,128)(2,1)S(1)} %bitcast.20), channel_id=1, source_target_pairs={{0,16},{8,24},{16,0},{24,8},{1,17},{9,25},{17,1},{25,9},{2,18},{10... | collective-permute-start | bytes 393224 | tf_op jit(solution)/shard_map/ppermute | solution.py:50
  63.9 10.0 %copy-start.3 = (bf16[32,1536]{1,0:T(8,128)(2,1)S(1)}, bf16[32,1536]{1,0:T(8,128)(2,1)}, u32[]{:S(2)}) copy-start(bf16[32,1536]{1,0:T(8,128)(2,1)} %get-tuple-element.13) | copy-start | bytes 294916
  63.9 6.2 %collective-permute-start.6 = (bf16[64,1024]{1,0:T(8,128)(2,1)S(1)}, bf16[64,1024]{1,0:T(8,128)(2,1)S(1)}, u32[]{:S(2)}, u32[]{:S(2)}) collective-permute-start(bf16[64,1024]{1,0:T(8,128)(2,1)S(1)} %bitcast.19), channel_id=1, source_target_pairs={{0,8},{8,16},{16,24},{24,0},{1,9},{9,17},{17,25},{25,1},{2,10},{10... | collective-permute-start | bytes 393224 | tf_op jit(solution)/shard_map/ppermute | solution.py:50
  74.0 3.7 %copy-start.2 = (bf16[32,1536]{1,0:T(8,128)(2,1)S(1)}, bf16[32,1536]{1,0:T(8,128)(2,1)}, u32[]{:S(2)}) copy-start(bf16[32,1536]{1,0:T(8,128)(2,1)} %get-tuple-element.15) | copy-start | bytes 294916
  77.7 8.1 %copy-start.5 = (f32[4096]{0:T(1024)S(1)}, f32[4096]{0:T(1024)}, u32[]{:S(2)}) copy-start(f32[4096]{0:T(1024)} %param.9) | copy-start | bytes 49156
  77.7 9.7 %copy-start.1 = (bf16[256,4096]{1,0:T(8,128)(2,1)S(1)}, bf16[256,4096]{1,0:T(8,128)(2,1)}, u32[]{:S(2)}) copy-start(bf16[256,4096]{1,0:T(8,128)(2,1)} %param.7) | copy-start | bytes 6291460
  81.4 4.3 %collective-permute-start.12 = (bf16[8,4096]{1,0:T(8,128)(2,1)S(1)}, bf16[8,4096]{1,0:T(8,128)(2,1)S(1)}, u32[]{:S(2)}, u32[]{:S(2)}) collective-permute-start(bf16[8,4096]{1,0:T(8,128)(2,1)S(1)} %convert_element_type.42), channel_id=1, source_target_pairs={{0,1},{1,0},{2,3},{3,2},{4,5},{5,4},{6,7},{7,6},{8,9},{9,8},{10,11... | collective-permute-start | bytes 196616 | tf_op jit(solution)/shard_map/ppermute | solution.py:50

commit v7 on v6

--- a/solution.py
+++ b/solution.py
@@ -212,27 +212,38 @@
     window_normed = jnp.concatenate([b[:MAXACT] for b in blocks], axis=0)
     window_masked = jnp.concatenate([b[MAXACT:] for b in blocks], axis=0)
     window = window_normed.shape[0]
-    columns = jnp.concatenate([window_normed, window_masked], axis=0)
-    columns = columns.reshape(2 * window, replicas, feature_share)
-    every_columns = [lax.dynamic_index_in_dim(columns, replica, 1, keepdims=False)]
-    for j in range(1, replicas):
-        outgoing = lax.dynamic_index_in_dim(columns, (replica + j) % replicas, 1, keepdims=False)
-        every_columns.append(shifted(outgoing, "rep", (replicas,), (j,)))
     gate_rows, up_rows, hidden, partial_features = weight_pass(
         window_normed, window_masked, gate_weight, up_weight, down_weight
     )
-    factors = jnp.concatenate([gate_rows, up_rows, hidden], axis=0)
-    every_factors = [factors] + [shifted(factors, "rep", (replicas,), (j,)) for j in range(1, replicas)]
+    units = gate_rows.shape[1]
+    factors = jnp.concatenate([gate_rows, up_rows, hidden], axis=1)
+
+    def message(target):
+        start = target * feature_share
+        return jnp.concatenate(
+            [
+                factors,
+                lax.dynamic_slice_in_dim(window_normed, start, feature_share, 1),
+                lax.dynamic_slice_in_dim(window_masked, start, feature_share, 1),
+            ],
+            axis=1,
+        )
+
+    every_message = [message(replica)] + [
+        shifted(message((replica + j) % replicas), "rep", (replicas,), (j,))
+        for j in range(1, replicas)
+    ]
     partial_features = partial_features.astype(jnp.bfloat16)
     feature_grad = partial_features[:MAXACT].astype(jnp.float32)
     for k in range(1, shards):
         piece = partial_features[k * MAXACT : (k + 1) * MAXACT]
         feature_grad = feature_grad + shifted(piece, "seq", (shards,), (-k,)).astype(jnp.float32)
-    every_gate = jnp.concatenate([f[:window] for f in every_factors], axis=0)
-    every_up = jnp.concatenate([f[window : 2 * window] for f in every_factors], axis=0)
-    every_hidden = jnp.concatenate([f[2 * window :] for f in every_factors], axis=0)
-    normed_cols = jnp.concatenate([c[:window] for c in every_columns], axis=0)
-    masked_cols = jnp.concatenate([c[window:] for c in every_columns], axis=0)
+    received = jnp.concatenate(every_message, axis=0)
+    every_gate = received[:, :units]
+    every_up = received[:, units : 2 * units]
+    every_hidden = received[:, 2 * units : 3 * units]
+    normed_cols = received[:, 3 * units : 3 * units + feature_share]
+    masked_cols = received[:, 3 * units + feature_share :]
     gate_grad = contract_first(normed_cols, every_gate)
     up_grad = contract_first(normed_cols, every_up)
     down_grad = contract_first(every_hidden, masked_cols)

time: 87.7 us -> 93.9 us (1.071)
  waiting for transfers between devices: 25.4 us -> 32.4 us
  local copies, waits for them, and re-layouts: 4.79 us -> 3.28 us
    ppermute x13 -> x10, waiting for transfers between devices: 25.4 us -> 32.4 us  [shifted(): return lax.ppermute(value, axes, pairs)]
    unnamed x23 -> x20, local copies, waits for them, and re-layouts: 2.06 us -> 3.01 us
    ppermute x13 -> x10, starting transfers between devices: 14.4 us -> 15.1 us  [shifted(): return lax.ppermute(value, axes, pairs)]
  transfers between devices with their start and end apart: 13 -> 10, of which waited for: 9 -> 7; matrix products, arithmetic and copies ran while one was open for 3% -> 0% of each run, Pallas kernels for 0% -> 0%
where the time goes in v7:
time: 93.9 us; the launch traced here: 93.5 us
  waiting for transfers between devices  32.4 us (35%)
  Pallas kernels  22.6 us (24%)
  matrix products  15.1 us (16%)
  starting transfers between devices  15.1 us (16%)
  other arithmetic  4.19 us (4%)
  local copies, waits for them, and re-layouts  3.28 us (3%)
    ppermute x10, waiting for transfers between devices, shifted(): return lax.ppermute(value, axes, pairs)  32.4 us
    pallas_call x1, Pallas kernels, weight_pass(): pl.pallas_call(weight_pass_kernel, grid=(units // chunk,), in_specs=[pl.B...  22.6 us
    ppermute x10, starting transfers between devices, shifted(): return lax.ppermute(value, axes, pairs)  15.1 us
    dot_general x4, matrix products, contract_first(): lax.dot_general(left, right, (((0,), (0,)), ((), ())), preferred_element_...  12.6 us
    unnamed x20, local copies, waits for them, and re-layouts  3.01 us
    dot_general x1, matrix products, local(): jnp.dot(picker, cotangent, preferred_element_type=jnp.float32)  1.97 us
  transfers between devices with their start and end apart: 10, of which 7 were waited for; matrix products, arithmetic and copies ran while one was open for 0% of the time, Pallas kernels for 0%

profile of v7, /device:TPU:0, one launch (start us, length us, event | category | flops | bytes accessed | tf_op | source)
XLA Modules:
  0.0 93.5 jit_solution(2093720029552951049)
XLA Ops:
  0.6 0.8 convert_bitcast_fusion
  1.5 0.3 reduce-window.9
  1.9 0.1 slice_reduce_fusion
  2.1 0.2 copy-done
  2.2 0.5 multiply_reduce_fusion.1
  2.7 2.0 %convolution_convert_fusion.1 = bf16[8,4096]{1,0:T(8,128)(2,1)S(1)} fusion(bf16[256,4096]{1,0:T(8,128)(2,1)} %param.8, s32[256]{0:T(256)S(1)} %add_bitcast_fusion, pred[256]{0:T(512)(128)(4,1)S(1)} %get-tuple-element.21), kind=kOutput, calls=%fused_computation.1 | convolution fusion | flops 16814080 | bytes 2163968 | tf_op jit(solution)/shard_map/dot_general | solution.py:208
  4.7 0.8 multiply_convert_fusion
  5.6 5.1 %collective-permute-start.2 = (bf16[16,4096]{1,0:T(8,128)(2,1)S(1)}, bf16[16,4096]{1,0:T(8,128)(2,1)S(1)}, u32[]{:S(2)}, u32[]{:S(2)}) collective-permute-start(bf16[16,4096]{1,0:T(8,128)(2,1)S(1)} %pad_maximum_fusion.17), channel_id=1, source_target_pairs={{0,6},{2,0},{4,2},{6,4},{1,7},{3,1},{5,3},{7,5},{8,14},{10,8},{12,... | collective-permute-start | bytes 393224 | tf_op jit(solution)/shard_map/ppermute | solution.py:50
  10.7 1.0 %collective-permute-start = (bf16[16,4096]{1,0:T(8,128)(2,1)S(1)}, bf16[16,4096]{1,0:T(8,128)(2,1)S(1)}, u32[]{:S(2)}, u32[]{:S(2)}) collective-permute-start(bf16[16,4096]{1,0:T(8,128)(2,1)S(1)} %pad_maximum_fusion.17), channel_id=1, source_target_pairs={{0,2},{2,4},{4,6},{6,0},{1,3},{3,5},{5,7},{7,1},{8,10},{10,12},{12... | collective-permute-start | bytes 393224 | tf_op jit(solution)/shard_map/ppermute | solution.py:50
  11.7 2.9 %collective-permute-done.2 = bf16[16,4096]{1,0:T(8,128)(2,1)S(1)} collective-permute-done((bf16[16,4096]{1,0:T(8,128)(2,1)S(1)}, bf16[16,4096]{1,0:T(8,128)(2,1)S(1)}, u32[]{:S(2)}, u32[]{:S(2)}) %collective-permute-start.2) | collective-permute-done | bytes 131104 | tf_op jit(solution)/shard_map/ppermute | solution.py:50
  14.6 7.3 %collective-permute-done.1 = bf16[16,4096]{1,0:T(8,128)(2,1)S(1)} collective-permute-done((bf16[16,4096]{1,0:T(8,128)(2,1)S(1)}, bf16[16,4096]{1,0:T(8,128)(2,1)S(1)}, u32[]{:S(2)}, u32[]{:S(2)}) %collective-permute-start.1) | collective-permute-done | bytes 131104 | tf_op jit(solution)/shard_map/ppermute | solution.py:50
  21.9 0.8 pad_maximum_fusion.15
  22.7 22.6 %shard_map.102 = (bf16[32,1536]{1,0:T(8,128)(2,1)}, bf16[32,1536]{1,0:T(8,128)(2,1)}, bf16[32,1536]{1,0:T(8,128)(2,1)}, f32[32,4096]{1,0:T(8,128)}) custom-call(bf16[32,4096]{1,0:T(8,128)(2,1)} %get-tuple-element.37.normed_ref, bf16[32,4096]{1,0:T(8,128)(2,1)} %get-tuple-element.38.masked_ref, bf16[4096,1536]{1,0:T(8,128)(2,1)} %gate_w_ref.1, ...), custom_call_target="tpu_custom_call" | custom-call | flops 2013265920 | bytes 38797312 | tf_op jit(solution)/shard_map/pallas_call | solution.py:162
  45.4 0.9 constant_dynamic-update-slice_fusion.11
  46.3 0.9 constant_dynamic-update-slice_fusion.10
  47.2 0.9 constant_dynamic-update-slice_fusion.9
  48.2 1.1 %convert_element_type.37 = bf16[32,4096]{1,0:T(8,128)(2,1)S(1)} convert(f32[32,4096]{1,0:T(8,128)} %get-tuple-element.12) | non-fusion elementwise | flops 131072 | bytes 786432 | tf_op jit(solution)/shard_map/convert_element_type | solution.py:236
  49.3 0.7 collective-permute-start.5
  50.0 2.0 %collective-permute-start.4 = (bf16[8,4096]{1,0:T(8,128)(2,1)S(1)}, bf16[8,4096]{1,0:T(8,128)(2,1)S(1)}, u32[]{:S(2)}, u32[]{:S(2)}) collective-permute-start(bf16[8,4096]{1,0:T(8,128)(2,1)S(1)} %get-tuple-element.28), channel_id=1, source_target_pairs={{0,4},{2,6},{4,0},{6,2},{1,5},{3,7},{5,1},{7,3},{8,12},{10,14},{12... | collective-permute-start | bytes 196616 | tf_op jit(solution)/shard_map/ppermute | solution.py:50
  52.0 2.8 %collective-permute-start.3 = (bf16[8,4096]{1,0:T(8,128)(2,1)S(1)}, bf16[8,4096]{1,0:T(8,128)(2,1)S(1)}, u32[]{:S(2)}, u32[]{:S(2)}) collective-permute-start(bf16[8,4096]{1,0:T(8,128)(2,1)S(1)} %get-tuple-element.26), channel_id=1, source_target_pairs={{0,6},{2,0},{4,2},{6,4},{1,7},{3,1},{5,3},{7,5},{8,14},{10,8},{12,... | collective-permute-start | bytes 196616 | tf_op jit(solution)/shard_map/ppermute | solution.py:50
  55.1 1.6 %collective-permute-start.7 = (bf16[32,6656]{1,0:T(8,128)(2,1)S(1)}, bf16[32,6656]{1,0:T(8,128)(2,1)S(1)}, u32[]{:S(2)}, u32[]{:S(2)}) collective-permute-start(bf16[32,6656]{1,0:T(8,128)(2,1)S(1)} %get-tuple-element.24), channel_id=1, source_target_pairs={{0,16},{8,24},{16,0},{24,8},{1,17},{9,25},{17,1},{25,9},{2,18},{10... | collective-permute-start | bytes 1277960 | tf_op jit(solution)/shard_map/ppermute | solution.py:50
  56.6 0.2 collective-permute-start.6
  56.8 1.1 %collective-permute-done.4 = bf16[8,4096]{1,0:T(8,128)(2,1)S(1)} collective-permute-done((bf16[8,4096]{1,0:T(8,128)(2,1)S(1)}, bf16[8,4096]{1,0:T(8,128)(2,1)S(1)}, u32[]{:S(2)}, u32[]{:S(2)}) %collective-permute-start.4) | collective-permute-done | bytes 65568 | tf_op jit(solution)/shard_map/ppermute | solution.py:50
  57.9 6.2 %collective-permute-done.8 = bf16[32,6656]{1,0:T(8,128)(2,1)S(1)} collective-permute-done((bf16[32,6656]{1,0:T(8,128)(2,1)S(1)}, bf16[32,6656]{1,0:T(8,128)(2,1)S(1)}, u32[]{:S(2)}, u32[]{:S(2)}) %collective-permute-start.8) | collective-permute-done | bytes 426016 | tf_op jit(solution)/shard_map/ppermute | solution.py:50
  64.2 12.1 %collective-permute-done.7 = bf16[32,6656]{1,0:T(8,128)(2,1)S(1)} collective-permute-done((bf16[32,6656]{1,0:T(8,128)(2,1)S(1)}, bf16[32,6656]{1,0:T(8,128)(2,1)S(1)}, u32[]{:S(2)}, u32[]{:S(2)}) %collective-permute-start.7) | collective-permute-done | bytes 426016 | tf_op jit(solution)/shard_map/ppermute | solution.py:50
  76.4 3.7 %fusion.16 = f32[1024,1536]{1,0:T(8,128)} fusion(bf16[32,6656]{1,0:T(8,128)(2,1)S(1)} %collective-permute-done.8, bf16[32,6656]{1,0:T(8,128)(2,1)S(1)} %collective-permute-done.7, bf16[32,6656]{1,0:T(8,128)(2,1)S(1)} %collective-permute-done.6, bf16[32,6656]{1,0:T(8,128)(2,1)S(1)} %get-tuple-element.22), kind=kOutput, calls=%fused_computation.18 | convolution fusion | flops 405274624 | bytes 7995392 | tf_op jit(solution)/shard_map/dot_general | solution.py:23
  80.1 3.7 %fusion.8 = f32[1024,1536]{1,0:T(8,128)} fusion(bf16[32,6656]{1,0:T(8,128)(2,1)S(1)} %collective-permute-done.8, bf16[32,6656]{1,0:T(8,128)(2,1)S(1)} %collective-permute-done.7, bf16[32,6656]{1,0:T(8,128)(2,1)S(1)} %collective-permute-done.6, bf16[32,6656]{1,0:T(8,128)(2,1)S(1)} %get-tuple-element.22), kind=kOutput, calls=%fused_computation.10 | convolution fusion | flops 405274624 | bytes 7995392 | tf_op jit(solution)/shard_map/dot_general | solution.py:23
  83.8 3.7 %fusion = f32[1536,1024]{1,0:T(8,128)} fusion(bf16[32,6656]{1,0:T(8,128)(2,1)S(1)} %collective-permute-done.8, bf16[32,6656]{1,0:T(8,128)(2,1)S(1)} %collective-permute-done.7, bf16[32,6656]{1,0:T(8,128)(2,1)S(1)} %collective-permute-done.6, bf16[32,6656]{1,0:T(8,128)(2,1)S(1)} %get-tuple-element.22), kind=kOutput, calls=%fused_computation.2 | convolution fusion | flops 405274624 | bytes 7995392 | tf_op jit(solution)/shard_map/dot_general | solution.py:23
  87.5 1.6 %collective-permute-start.9 = (bf16[8,4096]{1,0:T(8,128)(2,1)S(1)}, bf16[8,4096]{1,0:T(8,128)(2,1)S(1)}, u32[]{:S(2)}, u32[]{:S(2)}) collective-permute-start(bf16[8,4096]{1,0:T(8,128)(2,1)S(1)} %convert_element_type.42), channel_id=1, source_target_pairs={{0,1},{1,0},{2,3},{3,2},{4,5},{5,4},{6,7},{7,6},{8,9},{9,8},{10,11... | collective-permute-start | bytes 196616 | tf_op jit(solution)/shard_map/ppermute | solution.py:50
  89.1 2.8 %collective-permute-done.9 = bf16[8,4096]{1,0:T(8,128)(2,1)S(1)} collective-permute-done((bf16[8,4096]{1,0:T(8,128)(2,1)S(1)}, bf16[8,4096]{1,0:T(8,128)(2,1)S(1)}, u32[]{:S(2)}, u32[]{:S(2)}) %collective-permute-start.9) | collective-permute-done | bytes 65568 | tf_op jit(solution)/shard_map/ppermute | solution.py:50
  91.9 0.1 multiply_reduce_fusion
  92.0 1.5 %convolution_convert_fusion = bf16[128,4096]{1,0:T(8,128)(2,1)} fusion(f32[8,4096]{1,0:T(8,128)S(1)} %get-tuple-element.36, f32[8,4096]{1,0:T(8,128)S(1)} %convert_add_fusion, bf16[8,4096]{1,0:T(8,128)(2,1)S(1)} %collective-permute-done.9, f32[8]{0:T(128)S(1)} %multiply_multiply_fusion, f32[4096]{0:T(1024)S(1)} %copy-done.4, f32[8]{0:T(128)S(1)} %fusion.35, ...), kind=kOutput, calls=%fused_computation | convolution fusion | flops 9175040 | bytes 1394692 | tf_op jit(solution)/shard_map/dot_general | solution.py:23
  (36 shorter events, 0.6 us)
Async XLA Ops:
  0.6 1.6 %copy-start = (bf16[256,4096]{1,0:T(8,128)(2,1)S(1)}, bf16[256,4096]{1,0:T(8,128)(2,1)}, u32[]{:S(2)}) copy-start(bf16[256,4096]{1,0:T(8,128)(2,1)} %param.7) | copy-start | bytes 6291460
  5.6 9.0 %collective-permute-start.2 = (bf16[16,4096]{1,0:T(8,128)(2,1)S(1)}, bf16[16,4096]{1,0:T(8,128)(2,1)S(1)}, u32[]{:S(2)}, u32[]{:S(2)}) collective-permute-start(bf16[16,4096]{1,0:T(8,128)(2,1)S(1)} %pad_maximum_fusion.17), channel_id=1, source_target_pairs={{0,6},{2,0},{4,2},{6,4},{1,7},{3,1},{5,3},{7,5},{8,14},{10,8},{12,... | collective-permute-start | bytes 393224 | tf_op jit(solution)/shard_map/ppermute | solution.py:50
  10.7 11.2 %collective-permute-start.1 = (bf16[16,4096]{1,0:T(8,128)(2,1)S(1)}, bf16[16,4096]{1,0:T(8,128)(2,1)S(1)}, u32[]{:S(2)}, u32[]{:S(2)}) collective-permute-start(bf16[16,4096]{1,0:T(8,128)(2,1)S(1)} %pad_maximum_fusion.17), channel_id=1, source_target_pairs={{0,4},{2,6},{4,0},{6,2},{1,5},{3,7},{5,1},{7,3},{8,12},{10,14},{12... | collective-permute-start | bytes 393224 | tf_op jit(solution)/shard_map/ppermute | solution.py:50
  10.7 11.2 %collective-permute-start = (bf16[16,4096]{1,0:T(8,128)(2,1)S(1)}, bf16[16,4096]{1,0:T(8,128)(2,1)S(1)}, u32[]{:S(2)}, u32[]{:S(2)}) collective-permute-start(bf16[16,4096]{1,0:T(8,128)(2,1)S(1)} %pad_maximum_fusion.17), channel_id=1, source_target_pairs={{0,2},{2,4},{4,6},{6,0},{1,3},{3,5},{5,7},{7,1},{8,10},{10,12},{12... | collective-permute-start | bytes 393224 | tf_op jit(solution)/shard_map/ppermute | solution.py:50
  22.7 32.1 %copy-start.2 = (bf16[32,4096]{1,0:T(8,128)(2,1)S(1)}, bf16[32,4096]{1,0:T(8,128)(2,1)}, u32[]{:S(2)}) copy-start(bf16[32,4096]{1,0:T(8,128)(2,1)} %get-tuple-element.37.normed_ref) | copy-start | bytes 786436
  22.7 32.2 %copy-start.3 = (bf16[32,4096]{1,0:T(8,128)(2,1)S(1)}, bf16[32,4096]{1,0:T(8,128)(2,1)}, u32[]{:S(2)}) copy-start(bf16[32,4096]{1,0:T(8,128)(2,1)} %get-tuple-element.38.masked_ref) | copy-start | bytes 786436
  49.3 7.4 %collective-permute-start.5 = (bf16[8,4096]{1,0:T(8,128)(2,1)S(1)}, bf16[8,4096]{1,0:T(8,128)(2,1)S(1)}, u32[]{:S(2)}, u32[]{:S(2)}) collective-permute-start(bf16[8,4096]{1,0:T(8,128)(2,1)S(1)} %get-tuple-element.27), channel_id=1, source_target_pairs={{0,2},{2,4},{4,6},{6,0},{1,3},{3,5},{5,7},{7,1},{8,10},{10,12},{12... | collective-permute-start | bytes 196616 | tf_op jit(solution)/shard_map/ppermute | solution.py:50
  50.0 7.9 %collective-permute-start.4 = (bf16[8,4096]{1,0:T(8,128)(2,1)S(1)}, bf16[8,4096]{1,0:T(8,128)(2,1)S(1)}, u32[]{:S(2)}, u32[]{:S(2)}) collective-permute-start(bf16[8,4096]{1,0:T(8,128)(2,1)S(1)} %get-tuple-element.28), channel_id=1, source_target_pairs={{0,4},{2,6},{4,0},{6,2},{1,5},{3,7},{5,1},{7,3},{8,12},{10,14},{12... | collective-permute-start | bytes 196616 | tf_op jit(solution)/shard_map/ppermute | solution.py:50
  52.0 5.9 %collective-permute-start.3 = (bf16[8,4096]{1,0:T(8,128)(2,1)S(1)}, bf16[8,4096]{1,0:T(8,128)(2,1)S(1)}, u32[]{:S(2)}, u32[]{:S(2)}) collective-permute-start(bf16[8,4096]{1,0:T(8,128)(2,1)S(1)} %get-tuple-element.26), channel_id=1, source_target_pairs={{0,6},{2,0},{4,2},{6,4},{1,7},{3,1},{5,3},{7,5},{8,14},{10,8},{12,... | collective-permute-start | bytes 196616 | tf_op jit(solution)/shard_map/ppermute | solution.py:50
  55.0 9.2 %collective-permute-start.8 = (bf16[32,6656]{1,0:T(8,128)(2,1)S(1)}, bf16[32,6656]{1,0:T(8,128)(2,1)S(1)}, u32[]{:S(2)}, u32[]{:S(2)}) collective-permute-start(bf16[32,6656]{1,0:T(8,128)(2,1)S(1)} %get-tuple-element.23), channel_id=1, source_target_pairs={{0,24},{8,0},{16,8},{24,16},{1,25},{9,1},{17,9},{25,17},{2,26},{10... | collective-permute-start | bytes 1277960 | tf_op jit(solution)/shard_map/ppermute | solution.py:50
  55.1 21.3 %collective-permute-start.7 = (bf16[32,6656]{1,0:T(8,128)(2,1)S(1)}, bf16[32,6656]{1,0:T(8,128)(2,1)S(1)}, u32[]{:S(2)}, u32[]{:S(2)}) collective-permute-start(bf16[32,6656]{1,0:T(8,128)(2,1)S(1)} %get-tuple-element.24), channel_id=1, source_target_pairs={{0,16},{8,24},{16,0},{24,8},{1,17},{9,25},{17,1},{25,9},{2,18},{10... | collective-permute-start | bytes 1277960 | tf_op jit(solution)/shard_map/ppermute | solution.py:50
  56.6 19.7 %collective-permute-start.6 = (bf16[32,6656]{1,0:T(8,128)(2,1)S(1)}, bf16[32,6656]{1,0:T(8,128)(2,1)S(1)}, u32[]{:S(2)}, u32[]{:S(2)}) collective-permute-start(bf16[32,6656]{1,0:T(8,128)(2,1)S(1)} %get-tuple-element.25), channel_id=1, source_target_pairs={{0,8},{8,16},{16,24},{24,0},{1,9},{9,17},{17,25},{25,1},{2,10},{10... | collective-permute-start | bytes 1277960 | tf_op jit(solution)/shard_map/ppermute | solution.py:50
  80.1 13.4 %copy-start.1 = (bf16[256,4096]{1,0:T(8,128)(2,1)S(1)}, bf16[256,4096]{1,0:T(8,128)(2,1)}, u32[]{:S(2)}) copy-start(bf16[256,4096]{1,0:T(8,128)(2,1)} %param.7) | copy-start | bytes 6291460
  83.8 8.1 %copy-start.4 = (f32[4096]{0:T(1024)S(1)}, f32[4096]{0:T(1024)}, u32[]{:S(2)}) copy-start(f32[4096]{0:T(1024)} %param.9) | copy-start | bytes 49156
  87.5 4.3 %collective-permute-start.9 = (bf16[8,4096]{1,0:T(8,128)(2,1)S(1)}, bf16[8,4096]{1,0:T(8,128)(2,1)S(1)}, u32[]{:S(2)}, u32[]{:S(2)}) collective-permute-start(bf16[8,4096]{1,0:T(8,128)(2,1)S(1)} %convert_element_type.42), channel_id=1, source_target_pairs={{0,1},{1,0},{2,3},{3,2},{4,5},{5,4},{6,7},{7,6},{8,9},{9,8},{10,11... | collective-permute-start | bytes 196616 | tf_op jit(solution)/shard_map/ppermute | solution.py:50

commit v8 on v6

--- a/solution.py
+++ b/solution.py
@@ -123,6 +123,34 @@
         outgoing = lax.dynamic_index_in_dim(stacked, (index + k) % size, 0, keepdims=False)
         out.append(shifted(outgoing, axis, (size,), (k,)))
     return out
+
+
+def rep_exchange(factors, column_blocks, axis, size):
+    index = lax.axis_index(axis)
+    stacked = jnp.stack(column_blocks)
+    if power_of_two(size):
+        gathered = {0: factors}
+        held = {(0, k): lax.dynamic_index_in_dim(stacked, index ^ k, 0, keepdims=False) for k in range(size)}
+        distance = size // 2
+        while distance >= 1:
+            origins = sorted(gathered)
+            arrived = swapped(jnp.stack([gathered[o] for o in origins]), axis, size, distance)
+            for position, origin in enumerate(origins):
+                gathered[origin ^ distance] = arrived[position]
+            leaving = sorted(key for key in held if key[1] & distance)
+            arrived = swapped(jnp.stack([held[key] for key in leaving]), axis, size, distance)
+            held = {key: v for key, v in held.items() if not key[1] & distance}
+            for position, (origin, target) in enumerate(leaving):
+                held[(origin ^ distance, target ^ distance)] = arrived[position]
+            distance //= 2
+        return [gathered[o] for o in range(size)], [held[(o, 0)] for o in range(size)]
+    every_factors = [factors]
+    every_columns = [lax.dynamic_index_in_dim(stacked, index, 0, keepdims=False)]
+    for k in range(1, size):
+        every_factors.append(shifted(factors, axis, (size,), (k,)))
+        outgoing = lax.dynamic_index_in_dim(stacked, (index + k) % size, 0, keepdims=False)
+        every_columns.append(shifted(outgoing, axis, (size,), (k,)))
+    return every_factors, every_columns
 
 
 def weight_pass_kernel(normed_ref, masked_ref, gate_w_ref, up_w_ref, down_w_ref,
@@ -212,17 +240,17 @@
     window_normed = jnp.concatenate([b[:MAXACT] for b in blocks], axis=0)
     window_masked = jnp.concatenate([b[MAXACT:] for b in blocks], axis=0)
     window = window_normed.shape[0]
+    gate_rows, up_rows, hidden, partial_features = weight_pass(
+        window_normed, window_masked, gate_weight, up_weight, down_weight
+    )
     columns = jnp.concatenate([window_normed, window_masked], axis=0)
     columns = columns.reshape(2 * window, replicas, feature_share)
-    every_columns = [lax.dynamic_index_in_dim(columns, replica, 1, keepdims=False)]
-    for j in range(1, replicas):
-        outgoing = lax.dynamic_index_in_dim(columns, (replica + j) % replicas, 1, keepdims=False)
-        every_columns.append(shifted(outgoing, "rep", (replicas,), (j,)))
-    gate_rows, up_rows, hidden, partial_features = weight_pass(
-        window_normed, window_masked, gate_weight, up_weight, down_weight
-    )
-    factors = jnp.concatenate([gate_rows, up_rows, hidden], axis=0)
-    every_factors = [factors] + [shifted(factors, "rep", (replicas,), (j,)) for j in range(1, replicas)]
+    every_factors, every_columns = rep_exchange(
+        jnp.concatenate([gate_rows, up_rows, hidden], axis=0),
+        [columns[:, b] for b in range(replicas)],
+        "rep",
+        replicas,
+    )
     partial_features = partial_features.astype(jnp.bfloat16)
     feature_grad = partial_features[:MAXACT].astype(jnp.float32)
     for k in range(1, shards):

time: 87.7 us -> 84.9 us (0.968)
  local copies, waits for them, and re-layouts: 4.79 us -> 1.75 us
  starting transfers between devices: 14.4 us -> 12.8 us
  other arithmetic: 4.19 us -> 5.38 us
    ppermute x0 -> x4, waiting for transfers between devices: none -> 9.53 us  [swapped(): return lax.ppermute(value, axis, [(i, i ^ distance) for i in range(size)])]
    ppermute x13 -> x7, waiting for transfers between devices: 25.4 us -> 16.3 us  [shifted(): return lax.ppermute(value, axes, pairs)]
    ppermute x13 -> x7, starting transfers between devices: 14.4 us -> 9.98 us  [shifted(): return lax.ppermute(value, axes, pairs)]
    ppermute x0 -> x4, starting transfers between devices: none -> 2.78 us  [swapped(): return lax.ppermute(value, axis, [(i, i ^ distance) for i in range(size)])]
    unnamed x23 -> x18, local copies, waits for them, and re-layouts: 2.06 us -> 0.09 us
    another operation x3 -> x8, other arithmetic: 1.18 us -> 2.37 us
    concatenate x1 -> x0, local copies, waits for them, and re-layouts: 0.9 us -> none  [local(): factors = jnp.concatenate([gate_rows, up_rows, hidden], axis=0)]
  transfers between devices with their start and end apart: 13 -> 11, of which waited for: 9 -> 8; matrix products, arithmetic and copies ran while one was open for 3% -> 3% of each run, Pallas kernels for 0% -> 0%
where the time goes in v8:
time: 84.9 us; the launch traced here: 84.3 us
  waiting for transfers between devices  25.9 us (31%)
  Pallas kernels  22.6 us (27%)
  matrix products  15.1 us (18%)
  starting transfers between devices  12.8 us (15%)
  other arithmetic  5.38 us (6%)
  local copies, waits for them, and re-layouts  1.75 us (2%)
  between operations  0.88 us (1%)
    pallas_call x1, Pallas kernels, weight_pass(): pl.pallas_call(weight_pass_kernel, grid=(units // chunk,), in_specs=[pl.B...  22.6 us
    ppermute x7, waiting for transfers between devices, shifted(): return lax.ppermute(value, axes, pairs)  16.3 us
    dot_general x4, matrix products, contract_first(): lax.dot_general(left, right, (((0,), (0,)), ((), ())), preferred_element_...  12.6 us
    ppermute x7, starting transfers between devices, shifted(): return lax.ppermute(value, axes, pairs)  9.98 us
    ppermute x4, waiting for transfers between devices, swapped(): return lax.ppermute(value, axis, [(i, i ^ distance) for i in range(size)])  9.53 us
    ppermute x4, starting transfers between devices, swapped(): return lax.ppermute(value, axis, [(i, i ^ distance) for i in range(size)])  2.78 us
    dot_general x1, matrix products, local(): jnp.dot(picker, cotangent, preferred_element_type=jnp.float32)  1.97 us
  transfers between devices with their start and end apart: 11, of which 8 were waited for; matrix products, arithmetic and copies ran while one was open for 3% of the time, Pallas kernels for 0%

profile of v8, /device:TPU:0, one launch (start us, length us, event | category | flops | bytes accessed | tf_op | source)
XLA Modules:
  0.0 84.3 jit_solution(12092276681375838108)
XLA Ops:
  0.6 0.8 convert_bitcast_fusion
  1.5 0.3 reduce-window.9
  2.1 2.0 %convolution_convert_fusion.1 = bf16[8,4096]{1,0:T(8,128)(2,1)S(1)} fusion(bf16[256,4096]{1,0:T(8,128)(2,1)} %param.8, s32[256]{0:T(256)S(1)} %add_bitcast_fusion, pred[256]{0:T(512)(128)(4,1)S(1)} %get-tuple-element.23), kind=kOutput, calls=%fused_computation.1 | convolution fusion | flops 16814080 | bytes 2163968 | tf_op jit(solution)/shard_map/dot_general | solution.py:236
  4.1 0.5 multiply_reduce_fusion.1
  4.6 0.8 constant_dynamic-update-slice_fusion.7
  5.4 3.1 %collective-permute-start = (bf16[16,4096]{1,0:T(8,128)(2,1)S(1)}, bf16[16,4096]{1,0:T(8,128)(2,1)S(1)}, u32[]{:S(2)}, u32[]{:S(2)}) collective-permute-start(bf16[16,4096]{1,0:T(8,128)(2,1)S(1)} %pad_maximum_fusion.7), channel_id=1, source_target_pairs={{0,2},{2,4},{4,6},{6,0},{1,3},{3,5},{5,7},{7,1},{8,10},{10,12},{12... | collective-permute-start | bytes 393224 | tf_op jit(solution)/shard_map/ppermute | solution.py:50
  8.5 2.1 %collective-permute-start.2 = (bf16[16,4096]{1,0:T(8,128)(2,1)S(1)}, bf16[16,4096]{1,0:T(8,128)(2,1)S(1)}, u32[]{:S(2)}, u32[]{:S(2)}) collective-permute-start(bf16[16,4096]{1,0:T(8,128)(2,1)S(1)} %pad_maximum_fusion.7), channel_id=1, source_target_pairs={{0,6},{2,0},{4,2},{6,4},{1,7},{3,1},{5,3},{7,5},{8,14},{10,8},{12,... | collective-permute-start | bytes 393224 | tf_op jit(solution)/shard_map/ppermute | solution.py:50
  10.6 0.9 %collective-permute-start.1 = (bf16[16,4096]{1,0:T(8,128)(2,1)S(1)}, bf16[16,4096]{1,0:T(8,128)(2,1)S(1)}, u32[]{:S(2)}, u32[]{:S(2)}) collective-permute-start(bf16[16,4096]{1,0:T(8,128)(2,1)S(1)} %pad_maximum_fusion.7), channel_id=1, source_target_pairs={{0,4},{2,6},{4,0},{6,2},{1,5},{3,7},{5,1},{7,3},{8,12},{10,14},{12... | collective-permute-start | bytes 393224 | tf_op jit(solution)/shard_map/ppermute | solution.py:50
  11.5 3.3 %collective-permute-done = bf16[16,4096]{1,0:T(8,128)(2,1)S(1)} collective-permute-done((bf16[16,4096]{1,0:T(8,128)(2,1)S(1)}, bf16[16,4096]{1,0:T(8,128)(2,1)S(1)}, u32[]{:S(2)}, u32[]{:S(2)}) %collective-permute-start) | collective-permute-done | bytes 131104 | tf_op jit(solution)/shard_map/ppermute | solution.py:50
  14.9 7.6 %collective-permute-done.1 = bf16[16,4096]{1,0:T(8,128)(2,1)S(1)} collective-permute-done((bf16[16,4096]{1,0:T(8,128)(2,1)S(1)}, bf16[16,4096]{1,0:T(8,128)(2,1)S(1)}, u32[]{:S(2)}, u32[]{:S(2)}) %collective-permute-start.1) | collective-permute-done | bytes 131104 | tf_op jit(solution)/shard_map/ppermute | solution.py:50
  22.6 0.4 reshape.75
  22.9 0.8 pad_maximum_fusion.2
  23.8 22.6 %shard_map.102 = (bf16[32,1536]{1,0:T(8,128)(2,1)}, bf16[32,1536]{1,0:T(8,128)(2,1)}, bf16[32,1536]{1,0:T(8,128)(2,1)}, f32[32,4096]{1,0:T(8,128)}) custom-call(bf16[32,4096]{1,0:T(8,128)(2,1)} %get-tuple-element.62.normed_ref, bf16[32,4096]{1,0:T(8,128)(2,1)} %get-tuple-element.63.masked_ref, bf16[4096,1536]{1,0:T(8,128)(2,1)} %gate_w_ref.1, ...), custom_call_target="tpu_custom_call" | custom-call | flops 2013265920 | bytes 38797312 | tf_op jit(solution)/shard_map/pallas_call | solution.py:190
  46.4 1.1 %convert_element_type.37 = bf16[32,4096]{1,0:T(8,128)(2,1)S(1)} convert(f32[32,4096]{1,0:T(8,128)} %get-tuple-element.12) | non-fusion elementwise | flops 131072 | bytes 786432 | tf_op jit(solution)/shard_map/convert_element_type | solution.py:254
  47.5 1.7 %collective-permute-start.3 = (bf16[8,4096]{1,0:T(8,128)(2,1)S(1)}, bf16[8,4096]{1,0:T(8,128)(2,1)S(1)}, u32[]{:S(2)}, u32[]{:S(2)}) collective-permute-start(bf16[8,4096]{1,0:T(8,128)(2,1)S(1)} %get-tuple-element.48), channel_id=1, source_target_pairs={{0,6},{2,0},{4,2},{6,4},{1,7},{3,1},{5,3},{7,5},{8,14},{10,8},{12,... | collective-permute-start | bytes 196616 | tf_op jit(solution)/shard_map/ppermute | solution.py:50
  49.2 0.4 collective-permute-start.5
  49.8 1.0 %maximum_bitcast_fusion = bf16[1,96,1536]{2,1,0:T(8,128)(2,1)S(1)} fusion(bf16[32,1536]{1,0:T(8,128)(2,1)} %get-tuple-element.15, bf16[32,1536]{1,0:T(8,128)(2,1)} %get-tuple-element.14, bf16[32,1536]{1,0:T(8,128)(2,1)} %get-tuple-element.13), kind=kLoop, calls=%fused_computation.28 | loop fusion | flops 884736 | bytes 589824 | tf_op jit(solution)/shard_map/stack | solution.py:137
  50.8 1.6 %collective-permute-start.8 = (bf16[1,96,1536]{2,1,0:T(8,128)(2,1)S(1)}, bf16[1,96,1536]{2,1,0:T(8,128)(2,1)S(1)}, u32[]{:S(2)}, u32[]{:S(2)}) collective-permute-start(bf16[1,96,1536]{2,1,0:T(8,128)(2,1)S(1)} %maximum_bitcast_fusion), channel_id=1, source_target_pairs={{0,16},{8,24},{16,0},{24,8},{1,17},{9,25},{17,1},{25,9},{2,18},{10... | collective-permute-start | bytes 884744 | tf_op jit(solution)/shard_map/ppermute | solution.py:54
  52.4 0.8 fusion.46
  53.5 0.6 collective-permute-start.6
  54.1 1.1 %collective-permute-done.5 = bf16[8,4096]{1,0:T(8,128)(2,1)S(1)} collective-permute-done((bf16[8,4096]{1,0:T(8,128)(2,1)S(1)}, bf16[8,4096]{1,0:T(8,128)(2,1)S(1)}, u32[]{:S(2)}, u32[]{:S(2)}) %collective-permute-start.5) | collective-permute-done | bytes 65568 | tf_op jit(solution)/shard_map/ppermute | solution.py:50
  55.2 1.5 %collective-permute-done.4 = bf16[8,4096]{1,0:T(8,128)(2,1)S(1)} collective-permute-done((bf16[8,4096]{1,0:T(8,128)(2,1)S(1)}, bf16[8,4096]{1,0:T(8,128)(2,1)S(1)}, u32[]{:S(2)}, u32[]{:S(2)}) %collective-permute-start.4) | collective-permute-done | bytes 65568 | tf_op jit(solution)/shard_map/ppermute | solution.py:50
  56.8 7.9 %collective-permute-done.6 = bf16[2,64,1024]{2,1,0:T(8,128)(2,1)S(1)} collective-permute-done((bf16[2,64,1024]{2,1,0:T(8,128)(2,1)S(1)}, bf16[2,64,1024]{2,1,0:T(8,128)(2,1)S(1)}, u32[]{:S(2)}, u32[]{:S(2)}) %collective-permute-start.6) | collective-permute-done | bytes 262176 | tf_op jit(solution)/shard_map/ppermute | solution.py:54
  64.9 0.6 collective-permute-start.9
  65.5 0.8 collective-permute-done.7
  66.3 0.8 collective-permute-done.9
  67.2 3.7 %fusion.8 = f32[1024,1536]{1,0:T(8,128)} fusion(bf16[32,1536]{1,0:T(8,128)(2,1)S(1)} %get-tuple-element.26, bf16[32,1536]{1,0:T(8,128)(2,1)S(1)} %get-tuple-element.40, bf16[32,1536]{1,0:T(8,128)(2,1)S(1)} %get-tuple-element.27, bf16[32,1536]{1,0:T(8,128)(2,1)S(1)} %copy-done.4, bf16[32,1024]{1,0:T(8,128)(2,1)S(1)} %get-tuple-element.44, ...), kind=kOutput, calls=%fused_computation.12 | convolution fusion | flops 405274624 | bytes 6946816 | tf_op jit(solution)/shard_map/dot_general | solution.py:23
  70.9 3.7 %fusion = f32[1024,1536]{1,0:T(8,128)} fusion(bf16[32,1536]{1,0:T(8,128)(2,1)S(1)} %get-tuple-element.28, bf16[32,1536]{1,0:T(8,128)(2,1)S(1)} %get-tuple-element.41, bf16[32,1536]{1,0:T(8,128)(2,1)S(1)} %get-tuple-element.29, bf16[32,1536]{1,0:T(8,128)(2,1)S(1)} %copy-done.3, bf16[32,1024]{1,0:T(8,128)(2,1)S(1)} %get-tuple-element.44, ...), kind=kOutput, calls=%fused_computation.4 | convolution fusion | flops 405274624 | bytes 6946816 | tf_op jit(solution)/shard_map/dot_general | solution.py:23
  74.6 3.7 %fusion.16 = f32[1536,1024]{1,0:T(8,128)} fusion(bf16[32,1536]{1,0:T(8,128)(2,1)S(1)} %get-tuple-element.25, bf16[32,1536]{1,0:T(8,128)(2,1)S(1)} %get-tuple-element.39, bf16[32,1536]{1,0:T(8,128)(2,1)S(1)} %get-tuple-element.24, bf16[32,1536]{1,0:T(8,128)(2,1)S(1)} %copy-done.2, bf16[32,1024]{1,0:T(8,128)(2,1)S(1)} %get-tuple-element.43, ...), kind=kOutput, calls=%fused_computation.20 | convolution fusion | flops 405274624 | bytes 6946816 | tf_op jit(solution)/shard_map/dot_general | solution.py:23
  78.3 1.6 %collective-permute-start.10 = (bf16[8,4096]{1,0:T(8,128)(2,1)S(1)}, bf16[8,4096]{1,0:T(8,128)(2,1)S(1)}, u32[]{:S(2)}, u32[]{:S(2)}) collective-permute-start(bf16[8,4096]{1,0:T(8,128)(2,1)S(1)} %convert_element_type.42), channel_id=1, source_target_pairs={{0,1},{1,0},{2,3},{3,2},{4,5},{5,4},{6,7},{7,6},{8,9},{9,8},{10,11... | collective-permute-start | bytes 196616 | tf_op jit(solution)/shard_map/ppermute | solution.py:50
  79.9 2.8 %collective-permute-done.10 = bf16[8,4096]{1,0:T(8,128)(2,1)S(1)} collective-permute-done((bf16[8,4096]{1,0:T(8,128)(2,1)S(1)}, bf16[8,4096]{1,0:T(8,128)(2,1)S(1)}, u32[]{:S(2)}, u32[]{:S(2)}) %collective-permute-start.10) | collective-permute-done | bytes 65568 | tf_op jit(solution)/shard_map/ppermute | solution.py:50
  82.9 1.5 %convolution_convert_fusion = bf16[128,4096]{1,0:T(8,128)(2,1)} fusion(f32[8,4096]{1,0:T(8,128)S(1)} %get-tuple-element.61, f32[8,4096]{1,0:T(8,128)S(1)} %convert_add_fusion, bf16[8,4096]{1,0:T(8,128)(2,1)S(1)} %collective-permute-done.10, f32[8]{0:T(128)S(1)} %multiply_multiply_fusion, f32[4096]{0:T(1024)S(1)} %copy-done.5, f32[8]{0:T(128)S(1)} %fusion.39, ...), kind=kOutput, calls=%fused_computation | convolution fusion | flops 9175040 | bytes 1394692 | tf_op jit(solution)/shard_map/dot_general | solution.py:23
  (49 shorter events, 1.5 us)
Async XLA Ops:
  0.6 3.4 %copy-start = (bf16[256,4096]{1,0:T(8,128)(2,1)S(1)}, bf16[256,4096]{1,0:T(8,128)(2,1)}, u32[]{:S(2)}) copy-start(bf16[256,4096]{1,0:T(8,128)(2,1)} %param.7) | copy-start | bytes 6291460
  5.4 9.4 %collective-permute-start = (bf16[16,4096]{1,0:T(8,128)(2,1)S(1)}, bf16[16,4096]{1,0:T(8,128)(2,1)S(1)}, u32[]{:S(2)}, u32[]{:S(2)}) collective-permute-start(bf16[16,4096]{1,0:T(8,128)(2,1)S(1)} %pad_maximum_fusion.7), channel_id=1, source_target_pairs={{0,2},{2,4},{4,6},{6,0},{1,3},{3,5},{5,7},{7,1},{8,10},{10,12},{12... | collective-permute-start | bytes 393224 | tf_op jit(solution)/shard_map/ppermute | solution.py:50
  8.5 14.0 %collective-permute-start.2 = (bf16[16,4096]{1,0:T(8,128)(2,1)S(1)}, bf16[16,4096]{1,0:T(8,128)(2,1)S(1)}, u32[]{:S(2)}, u32[]{:S(2)}) collective-permute-start(bf16[16,4096]{1,0:T(8,128)(2,1)S(1)} %pad_maximum_fusion.7), channel_id=1, source_target_pairs={{0,6},{2,0},{4,2},{6,4},{1,7},{3,1},{5,3},{7,5},{8,14},{10,8},{12,... | collective-permute-start | bytes 393224 | tf_op jit(solution)/shard_map/ppermute | solution.py:50
  10.6 11.9 %collective-permute-start.1 = (bf16[16,4096]{1,0:T(8,128)(2,1)S(1)}, bf16[16,4096]{1,0:T(8,128)(2,1)S(1)}, u32[]{:S(2)}, u32[]{:S(2)}) collective-permute-start(bf16[16,4096]{1,0:T(8,128)(2,1)S(1)} %pad_maximum_fusion.7), channel_id=1, source_target_pairs={{0,4},{2,6},{4,0},{6,2},{1,5},{3,7},{5,1},{7,3},{8,12},{10,14},{12... | collective-permute-start | bytes 393224 | tf_op jit(solution)/shard_map/ppermute | solution.py:50
  47.5 19.7 %copy-start.4 = (bf16[32,1536]{1,0:T(8,128)(2,1)S(1)}, bf16[32,1536]{1,0:T(8,128)(2,1)}, u32[]{:S(2)}) copy-start(bf16[32,1536]{1,0:T(8,128)(2,1)} %get-tuple-element.14) | copy-start | bytes 294916
  47.5 6.6 %collective-permute-start.3 = (bf16[8,4096]{1,0:T(8,128)(2,1)S(1)}, bf16[8,4096]{1,0:T(8,128)(2,1)S(1)}, u32[]{:S(2)}, u32[]{:S(2)}) collective-permute-start(bf16[8,4096]{1,0:T(8,128)(2,1)S(1)} %get-tuple-element.48), channel_id=1, source_target_pairs={{0,6},{2,0},{4,2},{6,4},{1,7},{3,1},{5,3},{7,5},{8,14},{10,8},{12,... | collective-permute-start | bytes 196616 | tf_op jit(solution)/shard_map/ppermute | solution.py:50
  49.2 6.1 %collective-permute-start.5 = (bf16[8,4096]{1,0:T(8,128)(2,1)S(1)}, bf16[8,4096]{1,0:T(8,128)(2,1)S(1)}, u32[]{:S(2)}, u32[]{:S(2)}) collective-permute-start(bf16[8,4096]{1,0:T(8,128)(2,1)S(1)} %get-tuple-element.49), channel_id=1, source_target_pairs={{0,2},{2,4},{4,6},{6,0},{1,3},{3,5},{5,7},{7,1},{8,10},{10,12},{12... | collective-permute-start | bytes 196616 | tf_op jit(solution)/shard_map/ppermute | solution.py:50
  49.6 7.2 %collective-permute-start.4 = (bf16[8,4096]{1,0:T(8,128)(2,1)S(1)}, bf16[8,4096]{1,0:T(8,128)(2,1)S(1)}, u32[]{:S(2)}, u32[]{:S(2)}) collective-permute-start(bf16[8,4096]{1,0:T(8,128)(2,1)S(1)} %get-tuple-element.50), channel_id=1, source_target_pairs={{0,4},{2,6},{4,0},{6,2},{1,5},{3,7},{5,1},{7,3},{8,12},{10,14},{12... | collective-permute-start | bytes 196616 | tf_op jit(solution)/shard_map/ppermute | solution.py:50
  50.8 14.0 %collective-permute-start.8 = (bf16[1,96,1536]{2,1,0:T(8,128)(2,1)S(1)}, bf16[1,96,1536]{2,1,0:T(8,128)(2,1)S(1)}, u32[]{:S(2)}, u32[]{:S(2)}) collective-permute-start(bf16[1,96,1536]{2,1,0:T(8,128)(2,1)S(1)} %maximum_bitcast_fusion), channel_id=1, source_target_pairs={{0,16},{8,24},{16,0},{24,8},{1,17},{9,25},{17,1},{25,9},{2,18},{10... | collective-permute-start | bytes 884744 | tf_op jit(solution)/shard_map/ppermute | solution.py:54
  53.5 11.1 %collective-permute-start.6 = (bf16[2,64,1024]{2,1,0:T(8,128)(2,1)S(1)}, bf16[2,64,1024]{2,1,0:T(8,128)(2,1)S(1)}, u32[]{:S(2)}, u32[]{:S(2)}) collective-permute-start(bf16[2,64,1024]{2,1,0:T(8,128)(2,1)S(1)} %pad_maximum_fusion.4), channel_id=1, source_target_pairs={{0,16},{8,24},{16,0},{24,8},{1,17},{9,25},{17,1},{25,9},{2,18},{10... | collective-permute-start | bytes 786440 | tf_op jit(solution)/shard_map/ppermute | solution.py:54
  64.7 1.6 %collective-permute-start.7 = (bf16[2,64,1024]{2,1,0:T(8,128)(2,1)S(1)}, bf16[2,64,1024]{2,1,0:T(8,128)(2,1)S(1)}, u32[]{:S(2)}, u32[]{:S(2)}) collective-permute-start(bf16[2,64,1024]{2,1,0:T(8,128)(2,1)S(1)} %pad_maximum_fusion.5), channel_id=1, source_target_pairs={{0,8},{8,0},{16,24},{24,16},{1,9},{9,1},{17,25},{25,17},{2,10},{10... | collective-permute-start | bytes 786440 | tf_op jit(solution)/shard_map/ppermute | solution.py:54
  64.9 6.0 %copy-start.3 = (bf16[32,1536]{1,0:T(8,128)(2,1)S(1)}, bf16[32,1536]{1,0:T(8,128)(2,1)}, u32[]{:S(2)}) copy-start(bf16[32,1536]{1,0:T(8,128)(2,1)} %get-tuple-element.13) | copy-start | bytes 294916
  64.9 2.3 %collective-permute-start.9 = (bf16[2,96,1536]{2,1,0:T(8,128)(2,1)S(1)}, bf16[2,96,1536]{2,1,0:T(8,128)(2,1)S(1)}, u32[]{:S(2)}, u32[]{:S(2)}) collective-permute-start(bf16[2,96,1536]{2,1,0:T(8,128)(2,1)S(1)} %pad_maximum_fusion), channel_id=1, source_target_pairs={{0,8},{8,0},{16,24},{24,16},{1,9},{9,1},{17,25},{25,17},{2,10},{10... | collective-permute-start | bytes 1769480 | tf_op jit(solution)/shard_map/ppermute | solution.py:54
  70.9 3.7 %copy-start.2 = (bf16[32,1536]{1,0:T(8,128)(2,1)S(1)}, bf16[32,1536]{1,0:T(8,128)(2,1)}, u32[]{:S(2)}) copy-start(bf16[32,1536]{1,0:T(8,128)(2,1)} %get-tuple-element.15) | copy-start | bytes 294916
  74.6 8.1 %copy-start.5 = (f32[4096]{0:T(1024)S(1)}, f32[4096]{0:T(1024)}, u32[]{:S(2)}) copy-start(f32[4096]{0:T(1024)} %param.9) | copy-start | bytes 49156
  74.6 9.7 %copy-start.1 = (bf16[256,4096]{1,0:T(8,128)(2,1)S(1)}, bf16[256,4096]{1,0:T(8,128)(2,1)}, u32[]{:S(2)}) copy-start(bf16[256,4096]{1,0:T(8,128)(2,1)} %param.7) | copy-start | bytes 6291460
  78.3 4.4 %collective-permute-start.10 = (bf16[8,4096]{1,0:T(8,128)(2,1)S(1)}, bf16[8,4096]{1,0:T(8,128)(2,1)S(1)}, u32[]{:S(2)}, u32[]{:S(2)}) collective-permute-start(bf16[8,4096]{1,0:T(8,128)(2,1)S(1)} %convert_element_type.42), channel_id=1, source_target_pairs={{0,1},{1,0},{2,3},{3,2},{4,5},{5,4},{6,7},{7,6},{8,9},{9,8},{10,11... | collective-permute-start | bytes 196616 | tf_op jit(solution)/shard_map/ppermute | solution.py:50

commit v9 on v8

--- a/solution.py
+++ b/solution.py
@@ -216,6 +216,48 @@
             bytes_accessed=6 * features * units + 4 * rows * features * 2,
         ),
     )(window_normed, window_masked, gate_weight, up_weight, down_weight)
+
+
+def grads_kernel(normed_t_ref, gate_ref, up_ref, hidden_t_ref, masked_ref,
+                 gate_grad_ref, up_grad_ref, down_grad_ref):
+    normed_t = normed_t_ref[...]
+    gate_grad_ref[...] = jnp.dot(normed_t, gate_ref[...], preferred_element_type=jnp.float32)
+    up_grad_ref[...] = jnp.dot(normed_t, up_ref[...], preferred_element_type=jnp.float32)
+    down_grad_ref[...] = jnp.dot(hidden_t_ref[...], masked_ref[...], preferred_element_type=jnp.float32)
+
+
+def weight_grads(normed_cols, every_gate, every_up, every_hidden, masked_cols):
+    rows, share = normed_cols.shape
+    units = every_gate.shape[1]
+    steps = 4 if share % 32 == 0 and units % 32 == 0 else 1
+    share_block, unit_block = share // steps, units // steps
+    return pl.pallas_call(
+        grads_kernel,
+        grid=(steps,),
+        in_specs=[
+            pl.BlockSpec((share_block, rows), lambda i: (i, 0)),
+            pl.BlockSpec((rows, units), lambda i: (0, 0)),
+            pl.BlockSpec((rows, units), lambda i: (0, 0)),
+            pl.BlockSpec((unit_block, rows), lambda i: (i, 0)),
+            pl.BlockSpec((rows, share), lambda i: (0, 0)),
+        ],
+        out_specs=[
+            pl.BlockSpec((share_block, units), lambda i: (i, 0)),
+            pl.BlockSpec((share_block, units), lambda i: (i, 0)),
+            pl.BlockSpec((unit_block, share), lambda i: (i, 0)),
+        ],
+        out_shape=[
+            jax.ShapeDtypeStruct((share, units), jnp.float32),
+            jax.ShapeDtypeStruct((share, units), jnp.float32),
+            jax.ShapeDtypeStruct((units, share), jnp.float32),
+        ],
+        compiler_params=pltpu.CompilerParams(vmem_limit_bytes=48 * 1024 * 1024),
+        cost_estimate=pl.CostEstimate(
+            flops=6 * rows * share * units,
+            transcendentals=0,
+            bytes_accessed=12 * share * units + 2 * rows * (2 * share + 3 * units),
+        ),
+    )(normed_cols.T, every_gate, every_up, every_hidden.T, masked_cols)
 
 
 def local(tokens, cotangent, norm_gain, gate_weight, up_weight, down_weight, depths):
@@ -261,9 +303,9 @@
     every_hidden = jnp.concatenate([f[2 * window :] for f in every_factors], axis=0)
     normed_cols = jnp.concatenate([c[:window] for c in every_columns], axis=0)
     masked_cols = jnp.concatenate([c[window:] for c in every_columns], axis=0)
-    gate_grad = contract_first(normed_cols, every_gate)
-    up_grad = contract_first(normed_cols, every_up)
-    down_grad = contract_first(every_hidden, masked_cols)
+    gate_grad, up_grad, down_grad = weight_grads(
+        normed_cols, every_gate, every_up, every_hidden, masked_cols
+    )
     feature_grad, gate_grad, up_grad, down_grad = lax.optimization_barrier(
         (feature_grad, gate_grad, up_grad, down_grad)
     )

time: 84.9 us -> 98.7 us (1.16)
  local copies, waits for them, and re-layouts: 1.75 us -> 15.4 us
  matrix products: 15.1 us -> 3.24 us
  Pallas kernels: 22.6 us -> 29.7 us
  other arithmetic: 5.38 us -> 11.6 us
  waiting for transfers between devices: 25.9 us -> 20.8 us
  starting transfers between devices: 12.8 us -> 16.3 us
    dot_general x4 -> x1, matrix products: 12.6 us -> 2.37 us  [contract_first(): lax.dot_general(left, right, (((0,), (0,)), ((), ())), preferred_element_...]
    unnamed x18 -> x44, local copies, waits for them, and re-layouts: 0.09 us -> 7.21 us
    pallas_call x0 -> x1, Pallas kernels: none -> 7.06 us  [weight_grads(): pl.pallas_call(grads_kernel, grid=(steps,), in_specs=[pl.BlockSpec((share...]
    ppermute x7, waiting for transfers between devices: 16.3 us -> 10 us  [shifted(): return lax.ppermute(value, axes, pairs)]
    ppermute x7, starting transfers between devices: 9.98 us -> 14.2 us  [shifted(): return lax.ppermute(value, axes, pairs)]
    concatenate x0 -> x3, other arithmetic: none -> 3.16 us  [the longest x1 1.63 us: local(): every_gate = jnp.concatenate([f[:window] for f in every_factors], axis=0)]
    slice x2, local copies, waits for them, and re-layouts: 0.06 us -> 2.11 us  [local(): f[2 * window:]]
    dot_general x1, matrix products: 1.97 us -> 0.38 us  [local(): jnp.dot(picker, cotangent, preferred_element_type=jnp.float32)]
  transfers between devices with their start and end apart: 11 -> 11, of which waited for: 8 -> 6; matrix products, arithmetic and copies ran while one was open for 3% -> 8% of each run, Pallas kernels for 0% -> 0%
where the time goes in v9:
time: 98.7 us; the launch traced here: 98.2 us
  Pallas kernels  29.7 us (30%)
  waiting for transfers between devices  20.8 us (21%)
  starting transfers between devices  16.3 us (17%)
  local copies, waits for them, and re-layouts  15.4 us (16%)
  other arithmetic  11.6 us (12%)
  matrix products  3.24 us (3%)
  between operations  1.03 us (1%)
    pallas_call x1, Pallas kernels, weight_pass(): pl.pallas_call(weight_pass_kernel, grid=(units // chunk,), in_specs=[pl.B...  22.6 us
    ppermute x7, starting transfers between devices, shifted(): return lax.ppermute(value, axes, pairs)  14.2 us
    ppermute x4, waiting for transfers between devices, swapped(): return lax.ppermute(value, axis, [(i, i ^ distance) for i in range(size)])  10.8 us
    ppermute x7, waiting for transfers between devices, shifted(): return lax.ppermute(value, axes, pairs)  10 us
    unnamed x44, local copies, waits for them, and re-layouts  7.21 us
    pallas_call x1, Pallas kernels, weight_grads(): pl.pallas_call(grads_kernel, grid=(steps,), in_specs=[pl.BlockSpec((share...  7.06 us
    dot_general x1, matrix products, contract_first(): lax.dot_general(left, right, (((0,), (0,)), ((), ())), preferred_element_...  2.37 us
    ppermute x4, starting transfers between devices, swapped(): return lax.ppermute(value, axis, [(i, i ^ distance) for i in range(size)])  2.16 us
  transfers between devices with their start and end apart: 11, of which 6 were waited for; matrix products, arithmetic and copies ran while one was open for 8% of the time, Pallas kernels for 0%

profile of v9, /device:TPU:0, one launch (start us, length us, event | category | flops | bytes accessed | tf_op | source)
XLA Modules:
  0.0 98.2 jit_solution(12484784092939386004)
XLA Ops:
  0.6 0.8 convert_bitcast_fusion
  2.8 0.8 copy-done.3
  4.1 3.1 %collective-permute-start = (bf16[16,4096]{1,0:T(8,128)(2,1)S(1)}, bf16[16,4096]{1,0:T(8,128)(2,1)S(1)}, u32[]{:S(2)}, u32[]{:S(2)}) collective-permute-start(bf16[16,4096]{1,0:T(8,128)(2,1)S(1)} %pad_maximum_fusion.9), channel_id=1, source_target_pairs={{0,2},{2,4},{4,6},{6,0},{1,3},{3,5},{5,7},{7,1},{8,10},{10,12},{12... | collective-permute-start | bytes 393224 | tf_op jit(solution)/shard_map/ppermute | solution.py:50
  7.2 2.6 %collective-permute-start.1 = (bf16[16,4096]{1,0:T(8,128)(2,1)S(1)}, bf16[16,4096]{1,0:T(8,128)(2,1)S(1)}, u32[]{:S(2)}, u32[]{:S(2)}) collective-permute-start(bf16[16,4096]{1,0:T(8,128)(2,1)S(1)} %pad_maximum_fusion.9), channel_id=1, source_target_pairs={{0,4},{2,6},{4,0},{6,2},{1,5},{3,7},{5,1},{7,3},{8,12},{10,14},{12... | collective-permute-start | bytes 393224 | tf_op jit(solution)/shard_map/ppermute | solution.py:50
  9.8 1.3 %collective-permute-start.2 = (bf16[16,4096]{1,0:T(8,128)(2,1)S(1)}, bf16[16,4096]{1,0:T(8,128)(2,1)S(1)}, u32[]{:S(2)}, u32[]{:S(2)}) collective-permute-start(bf16[16,4096]{1,0:T(8,128)(2,1)S(1)} %pad_maximum_fusion.9), channel_id=1, source_target_pairs={{0,6},{2,0},{4,2},{6,4},{1,7},{3,1},{5,3},{7,5},{8,14},{10,8},{12,... | collective-permute-start | bytes 393224 | tf_op jit(solution)/shard_map/ppermute | solution.py:50
  11.1 2.5 %collective-permute-done = bf16[16,4096]{1,0:T(8,128)(2,1)S(1)} collective-permute-done((bf16[16,4096]{1,0:T(8,128)(2,1)S(1)}, bf16[16,4096]{1,0:T(8,128)(2,1)S(1)}, u32[]{:S(2)}, u32[]{:S(2)}) %collective-permute-start) | collective-permute-done | bytes 131104 | tf_op jit(solution)/shard_map/ppermute | solution.py:50
  13.6 4.8 %collective-permute-done.1 = bf16[16,4096]{1,0:T(8,128)(2,1)S(1)} collective-permute-done((bf16[16,4096]{1,0:T(8,128)(2,1)S(1)}, bf16[16,4096]{1,0:T(8,128)(2,1)S(1)}, u32[]{:S(2)}, u32[]{:S(2)}) %collective-permute-start.1) | collective-permute-done | bytes 131104 | tf_op jit(solution)/shard_map/ppermute | solution.py:50
  18.5 0.8 pad_maximum_fusion.4
  19.3 22.6 %shard_map.102 = (bf16[32,1536]{1,0:T(8,128)(2,1)}, bf16[32,1536]{1,0:T(8,128)(2,1)}, bf16[32,1536]{1,0:T(8,128)(2,1)}, f32[32,4096]{1,0:T(8,128)}) custom-call(bf16[32,4096]{1,0:T(8,128)(2,1)} %get-tuple-element.68.normed_ref, bf16[32,4096]{1,0:T(8,128)(2,1)} %get-tuple-element.69.masked_ref, bf16[4096,1536]{1,0:T(8,128)(2,1)} %gate_w_ref.1, ...), custom_call_target="tpu_custom_call" | custom-call | flops 2013265920 | bytes 38797312 | tf_op jit(solution)/shard_map/pallas_call | solution.py:190
  42.0 1.1 %convert_element_type.37 = bf16[32,4096]{1,0:T(8,128)(2,1)S(1)} convert(f32[32,4096]{1,0:T(8,128)} %get-tuple-element.15) | non-fusion elementwise | flops 131072 | bytes 786432 | tf_op jit(solution)/shard_map/convert_element_type | solution.py:296
  43.7 3.3 %collective-permute-start.5 = (bf16[8,4096]{1,0:T(8,128)(2,1)}, bf16[8,4096]{1,0:T(8,128)(2,1)}, u32[]{:S(2)}, u32[]{:S(2)}) collective-permute-start(bf16[8,4096]{1,0:T(8,128)(2,1)} %get-tuple-element.55), channel_id=1, source_target_pairs={{0,2},{2,4},{4,6},{6,0},{1,3},{3,5},{5,7},{7,1},{8,10},{10,12},{12... | collective-permute-start | bytes 196616 | tf_op jit(solution)/shard_map/ppermute | solution.py:50
  47.0 1.7 %collective-permute-start.4 = (bf16[8,4096]{1,0:T(8,128)(2,1)}, bf16[8,4096]{1,0:T(8,128)(2,1)}, u32[]{:S(2)}, u32[]{:S(2)}) collective-permute-start(bf16[8,4096]{1,0:T(8,128)(2,1)} %get-tuple-element.56), channel_id=1, source_target_pairs={{0,4},{2,6},{4,0},{6,2},{1,5},{3,7},{5,1},{7,3},{8,12},{10,14},{12... | collective-permute-start | bytes 196616 | tf_op jit(solution)/shard_map/ppermute | solution.py:50
  50.9 1.6 %collective-permute-start.6 = (bf16[2,64,1024]{2,1,0:T(8,128)(2,1)S(1)}, bf16[2,64,1024]{2,1,0:T(8,128)(2,1)S(1)}, u32[]{:S(2)}, u32[]{:S(2)}) collective-permute-start(bf16[2,64,1024]{2,1,0:T(8,128)(2,1)S(1)} %pad_maximum_fusion.6), channel_id=1, source_target_pairs={{0,16},{8,24},{16,0},{24,8},{1,17},{9,25},{17,1},{25,9},{2,18},{10... | collective-permute-start | bytes 786440 | tf_op jit(solution)/shard_map/ppermute | solution.py:54
  54.8 1.6 %convert_add_fusion = f32[8,4096]{1,0:T(8,128)} fusion(bf16[8,4096]{1,0:T(8,128)(2,1)} %collective-permute-done.5, bf16[8,4096]{1,0:T(8,128)(2,1)} %collective-permute-done.4, bf16[8,4096]{1,0:T(8,128)(2,1)} %collective-permute-done.3, bf16[32,4096]{1,0:T(8,128)(2,1)S(1)} %convert_element_type.37), kind=kLoop, calls=%fused_computation.26 | loop fusion | flops 229376 | bytes 393216 | tf_op jit(solution)/shard_map/add | solution.py:300
  56.4 3.8 %collective-permute-done.6 = bf16[2,64,1024]{2,1,0:T(8,128)(2,1)S(1)} collective-permute-done((bf16[2,64,1024]{2,1,0:T(8,128)(2,1)S(1)}, bf16[2,64,1024]{2,1,0:T(8,128)(2,1)S(1)}, u32[]{:S(2)}, u32[]{:S(2)}) %collective-permute-start.6) | collective-permute-done | bytes 262176 | tf_op jit(solution)/shard_map/ppermute | solution.py:54
  60.9 6.1 %collective-permute-done.8 = bf16[1,96,1536]{1,2,0:T(8,128)(2,1)S(1)} collective-permute-done((bf16[1,96,1536]{1,2,0:T(8,128)(2,1)S(1)}, bf16[1,96,1536]{1,2,0:T(8,128)(2,1)S(1)}, u32[]{:S(2)}, u32[]{:S(2)}) %collective-permute-start.8) | collective-permute-done | bytes 294944 | tf_op jit(solution)/shard_map/ppermute | solution.py:54
  67.2 1.1 %copy.40 = bf16[2,96,1536]{2,1,0:T(8,128)(2,1)} copy(bf16[2,96,1536]{1,2,0:T(8,128)(2,1)S(1)} %pad_maximum_fusion) | data formatting | bytes 1179648 | tf_op jit(solution)/shard_map/stack | solution.py:137
  68.6 1.0 slice_bitcast_fusion.5
  69.8 0.8 collective-permute-done.9
  70.7 1.8 %fusion.12 = (bf16[1,32,1536]{2,1,0:T(8,128)(2,1)S(1)}, bf16[1,32,1536]{2,1,0:T(8,128)(2,1)}, bf16[1,32,1536]{2,1,0:T(8,128)(2,1)}, bf16[1,32,1536]{2,1,0:T(8,12...) fusion(bf16[2,96,1536]{2,1,0:T(8,128)(2,1)} %collective-permute-done.9), kind=kLoop, calls=%fused_computation.63 | loop fusion | bytes 1179648 | tf_op jit(solution)/shard_map/slice | solution.py:303
  72.5 0.9 copy.58
  73.4 0.9 copy.57
  74.3 1.6 %pad_maximum_fusion.2 = bf16[128,1536]{0,1:T(8,128)(2,1)S(1)} fusion(bf16[32,1536]{0,1:T(8,128)(2,1)} %bitcast.49, bf16[32,1536]{0,1:T(8,128)(2,1)S(1)} %get-tuple-element.47, bf16[32,1536]{0,1:T(8,128)(2,1)} %bitcast.52, bf16[32,1536]{0,1:T(8,128)(2,1)S(1)} %copy.43), kind=kLoop, calls=%fused_computation.8 | loop fusion | flops 1572864 | bytes 786432 | tf_op jit(solution)/shard_map/concatenate | solution.py:301
  76.2 1.1 %copy.60 = bf16[1,32,1536]{1,2,0:T(8,128)(2,1)S(1)} copy(bf16[1,32,1536]{2,1,0:T(8,128)(2,1)} %get-tuple-element.31) | data formatting | bytes 196608
  77.3 1.8 %copy.59 = bf16[1,32,1536]{1,2,0:T(8,128)(2,1)} copy(bf16[1,32,1536]{2,1,0:T(8,128)(2,1)} %get-tuple-element.32) | data formatting | bytes 196608
  79.1 1.5 %pad_maximum_fusion.3 = bf16[128,1536]{0,1:T(8,128)(2,1)S(1)} fusion(bf16[32,1536]{0,1:T(8,128)(2,1)S(1)} %bitcast.50, bf16[32,1536]{0,1:T(8,128)(2,1)S(1)} %get-tuple-element.46, bf16[32,1536]{0,1:T(8,128)(2,1)} %bitcast.53, bf16[32,1536]{0,1:T(8,128)(2,1)S(1)} %copy.38), kind=kLoop, calls=%fused_computation.9 | loop fusion | flops 1572864 | bytes 786432 | tf_op jit(solution)/shard_map/concatenate | solution.py:302
  80.8 1.1 %copy.62 = bf16[1,32,1536]{1,2,0:T(8,128)(2,1)S(1)} copy(bf16[1,32,1536]{2,1,0:T(8,128)(2,1)} %get-tuple-element.35) | data formatting | bytes 196608
  82.7 7.1 %shard_map.103 = (f32[1024,1536]{1,0:T(8,128)}, f32[1024,1536]{1,0:T(8,128)}, f32[1536,1024]{1,0:T(8,128)}) custom-call(bf16[1024,128]{1,0:T(8,128)(2,1)S(1)} %copy.50.normed_t_ref, bf16[128,1536]{1,0:T(8,128)(2,1)S(1)} %copy.51.gate_ref, bf16[128,1536]{1,0:T(8,128)(2,1)S(1)} %copy.52.up_ref, bf16[1536,128]{1,0:T(8,128)(2,1)S(1)} %maximum_bitcast_fusion.1.hidden_t_ref, ...), custom_call_target="tpu_custom_call" | custom-call | flops 1207959552 | bytes 20578304 | tf_op jit(solution)/shard_map/pallas_call | solution.py:234
  89.8 1.6 %collective-permute-start.10 = (bf16[8,4096]{1,0:T(8,128)(2,1)S(1)}, bf16[8,4096]{1,0:T(8,128)(2,1)S(1)}, u32[]{:S(2)}, u32[]{:S(2)}) collective-permute-start(bf16[8,4096]{1,0:T(8,128)(2,1)S(1)} %convert_element_type.42), channel_id=1, source_target_pairs={{0,1},{1,0},{2,3},{3,2},{4,5},{5,4},{6,7},{7,6},{8,9},{9,8},{10,11... | collective-permute-start | bytes 196616 | tf_op jit(solution)/shard_map/ppermute | solution.py:50
  91.4 2.8 %collective-permute-done.10 = bf16[8,4096]{1,0:T(8,128)(2,1)S(1)} collective-permute-done((bf16[8,4096]{1,0:T(8,128)(2,1)S(1)}, bf16[8,4096]{1,0:T(8,128)(2,1)S(1)}, u32[]{:S(2)}, u32[]{:S(2)}) %collective-permute-start.10) | collective-permute-done | bytes 65568 | tf_op jit(solution)/shard_map/ppermute | solution.py:50
  94.1 1.1 %multiply_reduce_fusion = f32[8]{0:T(128)S(1)} fusion(f32[8,4096]{1,0:T(8,128)S(1)} %get-tuple-element.67, f32[8,4096]{1,0:T(8,128)} %convert_add_fusion, bf16[8,4096]{1,0:T(8,128)(2,1)S(1)} %collective-permute-done.10, f32[4096]{0:T(1024)S(1)} %copy-done.6), kind=kLoop, calls=%fused_computation.24 | loop fusion | flops 163832 | bytes 344096 | tf_op jit(solution)/shard_map/transpose(jvp())/reduce_sum | solution.py:19
  95.8 2.4 %convolution_convert_fusion = bf16[128,4096]{1,0:T(8,128)(2,1)} fusion(f32[8,4096]{1,0:T(8,128)S(1)} %get-tuple-element.67, f32[8,4096]{1,0:T(8,128)} %convert_add_fusion, bf16[8,4096]{1,0:T(8,128)(2,1)S(1)} %collective-permute-done.10, f32[8]{0:T(128)S(1)} %multiply_multiply_fusion, f32[4096]{0:T(1024)S(1)} %copy-done.6, f32[8]{0:T(128)} %copy-done.14, ...), kind=kOutput, calls=%fused_computation | convolution fusion | flops 9175040 | bytes 1394212 | tf_op jit(solution)/shard_map/dot_general | solution.py:23
  (85 shorter events, 10.1 us)
Async XLA Ops:
  0.6 1.6 %copy-start = (bf16[256,4096]{1,0:T(8,128)(2,1)S(1)}, bf16[256,4096]{1,0:T(8,128)(2,1)}, u32[]{:S(2)}) copy-start(bf16[256,4096]{1,0:T(8,128)(2,1)} %param.7) | copy-start | bytes 6291460
  1.5 2.5 %copy-start.12 = (pred[256]{0:T(512)(128)(4,1)}, pred[256]{0:T(512)(128)(4,1)S(1)}, u32[]{:S(2)}) copy-start(pred[256]{0:T(512)(128)(4,1)S(1)} %get-tuple-element.29) | copy-start | bytes 772
  1.9 1.7 %copy-start.3 = (bf16[256,4096]{1,0:T(8,128)(2,1)S(1)}, bf16[256,4096]{1,0:T(8,128)(2,1)}, u32[]{:S(2)}) copy-start(bf16[256,4096]{1,0:T(8,128)(2,1)} %param.8) | copy-start | bytes 6291460
  2.1 1.9 %copy-start.10 = (s32[256]{0:T(256)}, s32[256]{0:T(256)S(1)}, u32[]{:S(2)}) copy-start(s32[256]{0:T(256)S(1)} %add_bitcast_fusion) | copy-start | bytes 3076
  2.2 1.7 %copy-start.6 = (f32[4096]{0:T(1024)S(1)}, f32[4096]{0:T(1024)}, u32[]{:S(2)}) copy-start(f32[4096]{0:T(1024)} %param.9) | copy-start | bytes 49156
  2.7 15.8 %copy-start.15 = (f32[8]{0:T(128)}, f32[8]{0:T(128)S(1)}, u32[]{:S(2)}) copy-start(f32[8]{0:T(128)S(1)} %get-tuple-element.66) | copy-start | bytes 100
  3.6 3.6 %copy-start.14 = (f32[8]{0:T(128)}, f32[8]{0:T(128)S(1)}, u32[]{:S(2)}) copy-start(f32[8]{0:T(128)S(1)} %fusion.8) | copy-start | bytes 100
  4.1 9.5 %collective-permute-start = (bf16[16,4096]{1,0:T(8,128)(2,1)S(1)}, bf16[16,4096]{1,0:T(8,128)(2,1)S(1)}, u32[]{:S(2)}, u32[]{:S(2)}) collective-permute-start(bf16[16,4096]{1,0:T(8,128)(2,1)S(1)} %pad_maximum_fusion.9), channel_id=1, source_target_pairs={{0,2},{2,4},{4,6},{6,0},{1,3},{3,5},{5,7},{7,1},{8,10},{10,12},{12... | collective-permute-start | bytes 393224 | tf_op jit(solution)/shard_map/ppermute | solution.py:50
  7.2 11.2 %collective-permute-start.1 = (bf16[16,4096]{1,0:T(8,128)(2,1)S(1)}, bf16[16,4096]{1,0:T(8,128)(2,1)S(1)}, u32[]{:S(2)}, u32[]{:S(2)}) collective-permute-start(bf16[16,4096]{1,0:T(8,128)(2,1)S(1)} %pad_maximum_fusion.9), channel_id=1, source_target_pairs={{0,4},{2,6},{4,0},{6,2},{1,5},{3,7},{5,1},{7,3},{8,12},{10,14},{12... | collective-permute-start | bytes 393224 | tf_op jit(solution)/shard_map/ppermute | solution.py:50
  9.8 8.6 %collective-permute-start.2 = (bf16[16,4096]{1,0:T(8,128)(2,1)S(1)}, bf16[16,4096]{1,0:T(8,128)(2,1)S(1)}, u32[]{:S(2)}, u32[]{:S(2)}) collective-permute-start(bf16[16,4096]{1,0:T(8,128)(2,1)S(1)} %pad_maximum_fusion.9), channel_id=1, source_target_pairs={{0,6},{2,0},{4,2},{6,4},{1,7},{3,1},{5,3},{7,5},{8,14},{10,8},{12,... | collective-permute-start | bytes 393224 | tf_op jit(solution)/shard_map/ppermute | solution.py:50
  43.7 11.0 %collective-permute-start.5 = (bf16[8,4096]{1,0:T(8,128)(2,1)}, bf16[8,4096]{1,0:T(8,128)(2,1)}, u32[]{:S(2)}, u32[]{:S(2)}) collective-permute-start(bf16[8,4096]{1,0:T(8,128)(2,1)} %get-tuple-element.55), channel_id=1, source_target_pairs={{0,2},{2,4},{4,6},{6,0},{1,3},{3,5},{5,7},{7,1},{8,10},{10,12},{12... | collective-permute-start | bytes 196616 | tf_op jit(solution)/shard_map/ppermute | solution.py:50
  47.0 7.8 %collective-permute-start.4 = (bf16[8,4096]{1,0:T(8,128)(2,1)}, bf16[8,4096]{1,0:T(8,128)(2,1)}, u32[]{:S(2)}, u32[]{:S(2)}) collective-permute-start(bf16[8,4096]{1,0:T(8,128)(2,1)} %get-tuple-element.56), channel_id=1, source_target_pairs={{0,4},{2,6},{4,0},{6,2},{1,5},{3,7},{5,1},{7,3},{8,12},{10,14},{12... | collective-permute-start | bytes 196616 | tf_op jit(solution)/shard_map/ppermute | solution.py:50
  48.6 6.1 %collective-permute-start.3 = (bf16[8,4096]{1,0:T(8,128)(2,1)}, bf16[8,4096]{1,0:T(8,128)(2,1)}, u32[]{:S(2)}, u32[]{:S(2)}) collective-permute-start(bf16[8,4096]{1,0:T(8,128)(2,1)} %get-tuple-element.54), channel_id=1, source_target_pairs={{0,6},{2,0},{4,2},{6,4},{1,7},{3,1},{5,3},{7,5},{8,14},{10,8},{12,... | collective-permute-start | bytes 196616 | tf_op jit(solution)/shard_map/ppermute | solution.py:50
  50.5 2.0 %copy-start.9 = (bf16[32,1536]{1,0:T(8,128)(2,1)S(1)}, bf16[32,1536]{1,0:T(8,128)(2,1)}, u32[]{:S(2)}) copy-start(bf16[32,1536]{1,0:T(8,128)(2,1)} %get-tuple-element.18) | copy-start | bytes 294916
  50.5 2.2 %copy-start.8 = (bf16[32,1536]{1,0:T(8,128)(2,1)S(1)}, bf16[32,1536]{1,0:T(8,128)(2,1)}, u32[]{:S(2)}) copy-start(bf16[32,1536]{1,0:T(8,128)(2,1)} %get-tuple-element.17) | copy-start | bytes 294916
  50.6 2.3 %copy-start.7 = (bf16[32,1536]{1,0:T(8,128)(2,1)S(1)}, bf16[32,1536]{1,0:T(8,128)(2,1)}, u32[]{:S(2)}) copy-start(bf16[32,1536]{1,0:T(8,128)(2,1)} %get-tuple-element.16) | copy-start | bytes 294916
  50.9 9.3 %collective-permute-start.6 = (bf16[2,64,1024]{2,1,0:T(8,128)(2,1)S(1)}, bf16[2,64,1024]{2,1,0:T(8,128)(2,1)S(1)}, u32[]{:S(2)}, u32[]{:S(2)}) collective-permute-start(bf16[2,64,1024]{2,1,0:T(8,128)(2,1)S(1)} %pad_maximum_fusion.6), channel_id=1, source_target_pairs={{0,16},{8,24},{16,0},{24,8},{1,17},{9,25},{17,1},{25,9},{2,18},{10... | collective-permute-start | bytes 786440 | tf_op jit(solution)/shard_map/ppermute | solution.py:54
  53.5 13.5 %collective-permute-start.8 = (bf16[1,96,1536]{1,2,0:T(8,128)(2,1)S(1)}, bf16[1,96,1536]{1,2,0:T(8,128)(2,1)S(1)}, u32[]{:S(2)}, u32[]{:S(2)}) collective-permute-start(bf16[1,96,1536]{1,2,0:T(8,128)(2,1)S(1)} %maximum_bitcast_fusion), channel_id=1, source_target_pairs={{0,16},{8,24},{16,0},{24,8},{1,17},{9,25},{17,1},{25,9},{2,18},{10... | collective-permute-start | bytes 884744 | tf_op jit(solution)/shard_map/ppermute | solution.py:54
  60.9 7.7 %collective-permute-start.7 = (bf16[2,64,1024]{2,1,0:T(8,128)(2,1)}, bf16[2,64,1024]{2,1,0:T(8,128)(2,1)}, u32[]{:S(2)}, u32[]{:S(2)}) collective-permute-start(bf16[2,64,1024]{2,1,0:T(8,128)(2,1)} %pad_maximum_fusion.7), channel_id=1, source_target_pairs={{0,8},{8,0},{16,24},{24,16},{1,9},{9,1},{17,25},{25,17},{2,10},{10... | collective-permute-start | bytes 786440 | tf_op jit(solution)/shard_map/ppermute | solution.py:54
  67.2 2.4 %copy-start.5 = (bf16[32,1024]{1,0:T(8,128)(2,1)S(1)}, bf16[32,1024]{1,0:T(8,128)(2,1)}, u32[]{:S(2)}) copy-start(bf16[32,1024]{1,0:T(8,128)(2,1)} %get-tuple-element.37) | copy-start | bytes 196612
  68.3 1.5 %copy-start.4 = (bf16[32,1024]{1,0:T(8,128)(2,1)S(1)}, bf16[32,1024]{1,0:T(8,128)(2,1)}, u32[]{:S(2)}) copy-start(bf16[32,1024]{1,0:T(8,128)(2,1)} %get-tuple-element.36) | copy-start | bytes 196612
  68.3 2.3 %collective-permute-start.9 = (bf16[2,96,1536]{2,1,0:T(8,128)(2,1)}, bf16[2,96,1536]{2,1,0:T(8,128)(2,1)}, u32[]{:S(2)}, u32[]{:S(2)}) collective-permute-start(bf16[2,96,1536]{2,1,0:T(8,128)(2,1)} %copy.40), channel_id=1, source_target_pairs={{0,8},{8,0},{16,24},{24,16},{1,9},{9,1},{17,25},{25,17},{2,10},{10... | collective-permute-start | bytes 1769480 | tf_op jit(solution)/shard_map/ppermute | solution.py:54
  82.7 7.1 %copy-start.2 = (f32[8,4096]{1,0:T(8,128)S(1)}, f32[8,4096]{1,0:T(8,128)}, u32[]{:S(2)}) copy-start(f32[8,4096]{1,0:T(8,128)} %convert_add_fusion) | copy-start | bytes 393220
  82.7 8.7 %copy-start.11 = (s32[256]{0:T(256)S(1)}, s32[256]{0:T(256)}, u32[]{:S(2)}) copy-start(s32[256]{0:T(256)} %copy-done.10) | copy-start | bytes 3076
  82.7 8.7 %copy-start.13 = (pred[256]{0:T(512)(128)(4,1)S(1)}, pred[256]{0:T(512)(128)(4,1)}, u32[]{:S(2)}) copy-start(pred[256]{0:T(512)(128)(4,1)} %copy-done.12) | copy-start | bytes 772
  82.7 15.5 %copy-start.1 = (bf16[256,4096]{1,0:T(8,128)(2,1)S(1)}, bf16[256,4096]{1,0:T(8,128)(2,1)}, u32[]{:S(2)}) copy-start(bf16[256,4096]{1,0:T(8,128)(2,1)} %param.7) | copy-start | bytes 6291460
  89.8 4.3 %collective-permute-start.10 = (bf16[8,4096]{1,0:T(8,128)(2,1)S(1)}, bf16[8,4096]{1,0:T(8,128)(2,1)S(1)}, u32[]{:S(2)}, u32[]{:S(2)}) collective-permute-start(bf16[8,4096]{1,0:T(8,128)(2,1)S(1)} %convert_element_type.42), channel_id=1, source_target_pairs={{0,1},{1,0},{2,3},{3,2},{4,5},{5,4},{6,7},{7,6},{8,9},{9,8},{10,11... | collective-permute-start | bytes 196616 | tf_op jit(solution)/shard_map/ppermute | solution.py:50

commit v10 on v9

--- a/solution.py
+++ b/solution.py
@@ -218,27 +218,27 @@
     )(window_normed, window_masked, gate_weight, up_weight, down_weight)
 
 
-def grads_kernel(normed_t_ref, gate_ref, up_ref, hidden_t_ref, masked_ref,
+def grads_kernel(normed_ref, gate_ref, up_ref, hidden_ref, masked_ref,
                  gate_grad_ref, up_grad_ref, down_grad_ref):
-    normed_t = normed_t_ref[...]
-    gate_grad_ref[...] = jnp.dot(normed_t, gate_ref[...], preferred_element_type=jnp.float32)
-    up_grad_ref[...] = jnp.dot(normed_t, up_ref[...], preferred_element_type=jnp.float32)
-    down_grad_ref[...] = jnp.dot(hidden_t_ref[...], masked_ref[...], preferred_element_type=jnp.float32)
+    normed = normed_ref[...]
+    gate_grad_ref[...] = contract_first(normed, gate_ref[...])
+    up_grad_ref[...] = contract_first(normed, up_ref[...])
+    down_grad_ref[...] = contract_first(hidden_ref[...], masked_ref[...])
 
 
 def weight_grads(normed_cols, every_gate, every_up, every_hidden, masked_cols):
     rows, share = normed_cols.shape
     units = every_gate.shape[1]
-    steps = 4 if share % 32 == 0 and units % 32 == 0 else 1
+    steps = 4 if share % 512 == 0 and units % 512 == 0 else 1
     share_block, unit_block = share // steps, units // steps
     return pl.pallas_call(
         grads_kernel,
         grid=(steps,),
         in_specs=[
-            pl.BlockSpec((share_block, rows), lambda i: (i, 0)),
+            pl.BlockSpec((rows, share_block), lambda i: (0, i)),
             pl.BlockSpec((rows, units), lambda i: (0, 0)),
             pl.BlockSpec((rows, units), lambda i: (0, 0)),
-            pl.BlockSpec((unit_block, rows), lambda i: (i, 0)),
+            pl.BlockSpec((rows, unit_block), lambda i: (0, i)),
             pl.BlockSpec((rows, share), lambda i: (0, 0)),
         ],
         out_specs=[
@@ -257,7 +257,7 @@
             transcendentals=0,
             bytes_accessed=12 * share * units + 2 * rows * (2 * share + 3 * units),
         ),
-    )(normed_cols.T, every_gate, every_up, every_hidden.T, masked_cols)
+    )(normed_cols, every_gate, every_up, every_hidden, masked_cols)
 
 
 def local(tokens, cotangent, norm_gain, gate_weight, up_weight, down_weight, depths):

time: 98.7 us -> 80 us (0.81)
  local copies, waits for them, and re-layouts: 15.4 us -> 2.73 us
  other arithmetic: 11.6 us -> 3.79 us
  waiting for transfers between devices: 20.8 us -> 23.5 us
    unnamed x44 -> x20, local copies, waits for them, and re-layouts: 7.21 us -> 1.06 us
    ppermute x4, waiting for transfers between devices: 10.8 us -> 12.8 us  [swapped(): return lax.ppermute(value, axis, [(i, i ^ distance) for i in range(size)])]
    slice x2, local copies, waits for them, and re-layouts: 2.11 us -> 0.06 us  [local(): f[2 * window:]]
    concatenate x1, other arithmetic: 1.63 us -> 0.03 us  [local(): every_gate = jnp.concatenate([f[:window] for f in every_factors], axis=0)]
    slice x3, local copies, waits for them, and re-layouts: 1.61 us -> 0.04 us  [local(): masked_cols = jnp.concatenate([c[window:] for c in every_columns], axis=0)]
    add x1, other arithmetic: 1.59 us -> 0.03 us  [local(): feature_grad + shifted(piece, 'seq', (shards,), (-k,)).astype(jnp.float32)]
    concatenate x1, other arithmetic: 1.51 us -> 0.03 us  [local(): jnp.concatenate([f[window:2 * window] for f in every_factors], axis=0)]
    another operation x2 -> x1, local copies, waits for them, and re-layouts: 1.2 us -> 0.12 us  [the longest x1 1.09 us: rep_exchange(): jnp.stack([gathered[o] for o in origins])]
  transfers between devices with their start and end apart: 11 -> 11, of which waited for: 6 -> 7; matrix products, arithmetic and copies ran while one was open for 8% -> 2% of each run, Pallas kernels for 0% -> 0%
where the time goes in v10:
time: 80 us; the launch traced here: 79.8 us
  Pallas kernels  29.8 us (37%)
  waiting for transfers between devices  23.5 us (29%)
  starting transfers between devices  16.7 us (21%)
  other arithmetic  3.79 us (5%)
  local copies, waits for them, and re-layouts  2.73 us (3%)
  matrix products  2.34 us (3%)
  between operations  0.95 us (1%)
    pallas_call x1, Pallas kernels, weight_pass(): pl.pallas_call(weight_pass_kernel, grid=(units // chunk,), in_specs=[pl.B...  22.6 us
    ppermute x7, starting transfers between devices, shifted(): return lax.ppermute(value, axes, pairs)  14.3 us
    ppermute x4, waiting for transfers between devices, swapped(): return lax.ppermute(value, axis, [(i, i ^ distance) for i in range(size)])  12.8 us
    ppermute x7, waiting for transfers between devices, shifted(): return lax.ppermute(value, axes, pairs)  10.7 us
    pallas_call x1, Pallas kernels, weight_grads(): pl.pallas_call(grads_kernel, grid=(steps,), in_specs=[pl.BlockSpec((rows,...  7.15 us
    ppermute x4, starting transfers between devices, swapped(): return lax.ppermute(value, axis, [(i, i ^ distance) for i in range(size)])  2.34 us
  transfers between devices with their start and end apart: 11, of which 7 were waited for; matrix products, arithmetic and copies ran while one was open for 2% of the time, Pallas kernels for 0%

profile of v10, /device:TPU:0, one launch (start us, length us, event | category | flops | bytes accessed | tf_op | source)
XLA Modules:
  0.0 79.8 jit_solution(7641815156970804532)
XLA Ops:
  0.6 0.8 %convert_bitcast_fusion = (s32[2,128]{1,0:T(2,128)S(1)}, pred[256]{0:T(512)(128)(4,1)S(1)}) fusion(s32[256]{0:T(256)} %param.13), kind=kLoop, calls=%fused_computation.61 | loop fusion | flops 512 | bytes 2304 | tf_op jit(solution)/shard_map/convert
  1.5 0.3 reduce-window.9
  1.9 0.1 slice_reduce_fusion
  2.1 0.2 copy-done
  2.2 0.5 multiply_reduce_fusion.1
  2.8 0.8 %copy-done.2 = bf16[256,4096]{1,0:T(8,128)(2,1)S(1)} copy-done((bf16[256,4096]{1,0:T(8,128)(2,1)S(1)}, bf16[256,4096]{1,0:T(8,128)(2,1)}, u32[]{:S(2)}) %copy-start.2) | copy-done | bytes 2097176
  3.6 0.4 convolution_convert_fusion.1
  4.0 0.1 constant_dynamic-update-slice_fusion.7
  4.1 3.1 %collective-permute-start = (bf16[16,4096]{1,0:T(8,128)(2,1)S(1)}, bf16[16,4096]{1,0:T(8,128)(2,1)S(1)}, u32[]{:S(2)}, u32[]{:S(2)}) collective-permute-start(bf16[16,4096]{1,0:T(8,128)(2,1)S(1)} %pad_maximum_fusion.11), channel_id=1, source_target_pairs={{0,2},{2,4},{4,6},{6,0},{1,3},{3,5},{5,7},{7,1},{8,10},{10,12},{12... | collective-permute-start | bytes 393224 | tf_op jit(solution)/shard_map/ppermute | solution.py:50
  7.2 2.6 %collective-permute-start.1 = (bf16[16,4096]{1,0:T(8,128)(2,1)S(1)}, bf16[16,4096]{1,0:T(8,128)(2,1)S(1)}, u32[]{:S(2)}, u32[]{:S(2)}) collective-permute-start(bf16[16,4096]{1,0:T(8,128)(2,1)S(1)} %pad_maximum_fusion.11), channel_id=1, source_target_pairs={{0,4},{2,6},{4,0},{6,2},{1,5},{3,7},{5,1},{7,3},{8,12},{10,14},{12... | collective-permute-start | bytes 393224 | tf_op jit(solution)/shard_map/ppermute | solution.py:50
  9.7 1.3 %collective-permute-start.2 = (bf16[16,4096]{1,0:T(8,128)(2,1)S(1)}, bf16[16,4096]{1,0:T(8,128)(2,1)S(1)}, u32[]{:S(2)}, u32[]{:S(2)}) collective-permute-start(bf16[16,4096]{1,0:T(8,128)(2,1)S(1)} %pad_maximum_fusion.11), channel_id=1, source_target_pairs={{0,6},{2,0},{4,2},{6,4},{1,7},{3,1},{5,3},{7,5},{8,14},{10,8},{12,... | collective-permute-start | bytes 393224 | tf_op jit(solution)/shard_map/ppermute | solution.py:50
  11.1 2.5 %collective-permute-done = bf16[16,4096]{1,0:T(8,128)(2,1)S(1)} collective-permute-done((bf16[16,4096]{1,0:T(8,128)(2,1)S(1)}, bf16[16,4096]{1,0:T(8,128)(2,1)S(1)}, u32[]{:S(2)}, u32[]{:S(2)}) %collective-permute-start) | collective-permute-done | bytes 131104 | tf_op jit(solution)/shard_map/ppermute | solution.py:50
  13.6 4.8 %collective-permute-done.1 = bf16[16,4096]{1,0:T(8,128)(2,1)S(1)} collective-permute-done((bf16[16,4096]{1,0:T(8,128)(2,1)S(1)}, bf16[16,4096]{1,0:T(8,128)(2,1)S(1)}, u32[]{:S(2)}, u32[]{:S(2)}) %collective-permute-start.1) | collective-permute-done | bytes 131104 | tf_op jit(solution)/shard_map/ppermute | solution.py:50
  18.5 0.8 %pad_maximum_fusion.5 = (bf16[32,4096]{1,0:T(8,128)(2,1)}, bf16[32,4096]{1,0:T(8,128)(2,1)}) fusion(bf16[8,4096]{1,0:T(8,128)(2,1)S(1)} %get-tuple-element.59, bf16[8,4096]{1,0:T(8,128)(2,1)S(1)} %get-tuple-element.62, bf16[8,4096]{1,0:T(8,128)(2,1)S(1)} %get-tuple-element.65, bf16[8,4096]{1,0:T(8,128)(2,1)S(1)} %get-tuple-element.27, ...), kind=kLoop, calls=%fused_computation.8 | loop fusion | flops 2097152 | bytes 1048576 | tf_op jit(solution)/shard_map/concatenate | solution.py:282
  19.3 22.6 %shard_map.102 = (bf16[32,1536]{1,0:T(8,128)(2,1)}, bf16[32,1536]{1,0:T(8,128)(2,1)}, bf16[32,1536]{1,0:T(8,128)(2,1)}, f32[32,4096]{1,0:T(8,128)}) custom-call(bf16[32,4096]{1,0:T(8,128)(2,1)} %get-tuple-element.68.normed_ref, bf16[32,4096]{1,0:T(8,128)(2,1)} %get-tuple-element.69.masked_ref, bf16[4096,1536]{1,0:T(8,128)(2,1)} %gate_w_ref.1, ...), custom_call_target="tpu_custom_call" | custom-call | flops 2013265920 | bytes 38797312 | tf_op jit(solution)/shard_map/pallas_call | solution.py:190
  42.0 1.1 %convert_element_type.37 = bf16[32,4096]{1,0:T(8,128)(2,1)S(1)} convert(f32[32,4096]{1,0:T(8,128)} %get-tuple-element.15) | non-fusion elementwise | flops 131072 | bytes 786432 | tf_op jit(solution)/shard_map/convert_element_type | solution.py:296
  43.1 3.3 %collective-permute-start.5 = (bf16[8,4096]{1,0:T(8,128)(2,1)S(1)}, bf16[8,4096]{1,0:T(8,128)(2,1)S(1)}, u32[]{:S(2)}, u32[]{:S(2)}) collective-permute-start(bf16[8,4096]{1,0:T(8,128)(2,1)S(1)} %get-tuple-element.55), channel_id=1, source_target_pairs={{0,2},{2,4},{4,6},{6,0},{1,3},{3,5},{5,7},{7,1},{8,10},{10,12},{12... | collective-permute-start | bytes 196616 | tf_op jit(solution)/shard_map/ppermute | solution.py:50
  46.4 1.7 %collective-permute-start.4 = (bf16[8,4096]{1,0:T(8,128)(2,1)S(1)}, bf16[8,4096]{1,0:T(8,128)(2,1)S(1)}, u32[]{:S(2)}, u32[]{:S(2)}) collective-permute-start(bf16[8,4096]{1,0:T(8,128)(2,1)S(1)} %get-tuple-element.56), channel_id=1, source_target_pairs={{0,4},{2,6},{4,0},{6,2},{1,5},{3,7},{5,1},{7,3},{8,12},{10,14},{12... | collective-permute-start | bytes 196616 | tf_op jit(solution)/shard_map/ppermute | solution.py:50
  48.0 0.8 collective-permute-start.3
  48.8 0.4 reshape.75
  49.2 0.8 fusion.12
  50.3 1.6 %collective-permute-start.6 = (bf16[2,64,1024]{2,1,0:T(8,128)(2,1)S(1)}, bf16[2,64,1024]{2,1,0:T(8,128)(2,1)S(1)}, u32[]{:S(2)}, u32[]{:S(2)}) collective-permute-start(bf16[2,64,1024]{2,1,0:T(8,128)(2,1)S(1)} %pad_maximum_fusion.7), channel_id=1, source_target_pairs={{0,16},{8,24},{16,0},{24,8},{1,17},{9,25},{17,1},{25,9},{2,18},{10... | collective-permute-start | bytes 786440 | tf_op jit(solution)/shard_map/ppermute | solution.py:54
  51.9 0.6 collective-permute-start.8
  52.6 0.6 collective-permute-done.3
  53.2 6.4 %collective-permute-done.6 = bf16[2,64,1024]{2,1,0:T(8,128)(2,1)S(1)} collective-permute-done((bf16[2,64,1024]{2,1,0:T(8,128)(2,1)S(1)}, bf16[2,64,1024]{2,1,0:T(8,128)(2,1)S(1)}, u32[]{:S(2)}, u32[]{:S(2)}) %collective-permute-start.6) | collective-permute-done | bytes 262176 | tf_op jit(solution)/shard_map/ppermute | solution.py:54
  59.8 4.6 %collective-permute-done.8 = bf16[1,96,1536]{2,1,0:T(8,128)(2,1)S(1)} collective-permute-done((bf16[1,96,1536]{2,1,0:T(8,128)(2,1)S(1)}, bf16[1,96,1536]{2,1,0:T(8,128)(2,1)S(1)}, u32[]{:S(2)}, u32[]{:S(2)}) %collective-permute-start.8) | collective-permute-done | bytes 294944 | tf_op jit(solution)/shard_map/ppermute | solution.py:54
  64.6 1.9 %collective-permute-done.9 = bf16[2,96,1536]{2,1,0:T(8,128)(2,1)S(1)} collective-permute-done((bf16[2,96,1536]{2,1,0:T(8,128)(2,1)S(1)}, bf16[2,96,1536]{2,1,0:T(8,128)(2,1)S(1)}, u32[]{:S(2)}, u32[]{:S(2)}) %collective-permute-start.9) | collective-permute-done | bytes 589856 | tf_op jit(solution)/shard_map/ppermute | solution.py:54
  66.7 7.1 %shard_map.103 = (f32[1024,1536]{1,0:T(8,128)}, f32[1024,1536]{1,0:T(8,128)}, f32[1536,1024]{1,0:T(8,128)}) custom-call(bf16[128,1024]{1,0:T(8,128)(2,1)S(1)} %pad_maximum_fusion.9.normed_ref, bf16[128,1536]{1,0:T(8,128)(2,1)S(1)} %pad_maximum_fusion.2.gate_ref, bf16[128,1536]{1,0:T(8,128)(2,1)S(1)} %pad_maximum_fusion.3.up_ref, ...), custom_call_target="tpu_custom_call" | custom-call | flops 1207959552 | bytes 20578304 | tf_op jit(solution)/shard_map/pallas_call | solution.py:234
  73.8 1.6 %collective-permute-start.10 = (bf16[8,4096]{1,0:T(8,128)(2,1)S(1)}, bf16[8,4096]{1,0:T(8,128)(2,1)S(1)}, u32[]{:S(2)}, u32[]{:S(2)}) collective-permute-start(bf16[8,4096]{1,0:T(8,128)(2,1)S(1)} %convert_element_type.42), channel_id=1, source_target_pairs={{0,1},{1,0},{2,3},{3,2},{4,5},{5,4},{6,7},{7,6},{8,9},{9,8},{10,11... | collective-permute-start | bytes 196616 | tf_op jit(solution)/shard_map/ppermute | solution.py:50
  75.4 2.8 %collective-permute-done.10 = bf16[8,4096]{1,0:T(8,128)(2,1)S(1)} collective-permute-done((bf16[8,4096]{1,0:T(8,128)(2,1)S(1)}, bf16[8,4096]{1,0:T(8,128)(2,1)S(1)}, u32[]{:S(2)}, u32[]{:S(2)}) %collective-permute-start.10) | collective-permute-done | bytes 65568 | tf_op jit(solution)/shard_map/ppermute | solution.py:50
  78.2 0.1 multiply_reduce_fusion
  78.3 1.5 %convolution_convert_fusion = bf16[128,4096]{1,0:T(8,128)(2,1)} fusion(f32[8,4096]{1,0:T(8,128)S(1)} %get-tuple-element.67, f32[8,4096]{1,0:T(8,128)S(1)} %convert_add_fusion, bf16[8,4096]{1,0:T(8,128)(2,1)S(1)} %collective-permute-done.10, f32[8]{0:T(128)S(1)} %multiply_multiply_fusion, f32[4096]{0:T(1024)S(1)} %copy-done.6, f32[8]{0:T(128)S(1)} %fusion.8, ...), kind=kOutput, calls=%fused_computation | convolution fusion | flops 9175040 | bytes 1394692 | tf_op jit(solution)/shard_map/dot_general | solution.py:23
  (54 shorter events, 1.2 us)
Async XLA Ops:
  0.6 1.6 %copy-start = (bf16[256,4096]{1,0:T(8,128)(2,1)S(1)}, bf16[256,4096]{1,0:T(8,128)(2,1)}, u32[]{:S(2)}) copy-start(bf16[256,4096]{1,0:T(8,128)(2,1)} %param.7) | copy-start | bytes 6291460
  1.9 1.7 %copy-start.2 = (bf16[256,4096]{1,0:T(8,128)(2,1)S(1)}, bf16[256,4096]{1,0:T(8,128)(2,1)}, u32[]{:S(2)}) copy-start(bf16[256,4096]{1,0:T(8,128)(2,1)} %param.8) | copy-start | bytes 6291460
  2.2 1.7 %copy-start.6 = (f32[4096]{0:T(1024)S(1)}, f32[4096]{0:T(1024)}, u32[]{:S(2)}) copy-start(f32[4096]{0:T(1024)} %param.9) | copy-start | bytes 49156
  4.1 9.5 %collective-permute-start = (bf16[16,4096]{1,0:T(8,128)(2,1)S(1)}, bf16[16,4096]{1,0:T(8,128)(2,1)S(1)}, u32[]{:S(2)}, u32[]{:S(2)}) collective-permute-start(bf16[16,4096]{1,0:T(8,128)(2,1)S(1)} %pad_maximum_fusion.11), channel_id=1, source_target_pairs={{0,2},{2,4},{4,6},{6,0},{1,3},{3,5},{5,7},{7,1},{8,10},{10,12},{12... | collective-permute-start | bytes 393224 | tf_op jit(solution)/shard_map/ppermute | solution.py:50
  7.2 11.2 %collective-permute-start.1 = (bf16[16,4096]{1,0:T(8,128)(2,1)S(1)}, bf16[16,4096]{1,0:T(8,128)(2,1)S(1)}, u32[]{:S(2)}, u32[]{:S(2)}) collective-permute-start(bf16[16,4096]{1,0:T(8,128)(2,1)S(1)} %pad_maximum_fusion.11), channel_id=1, source_target_pairs={{0,4},{2,6},{4,0},{6,2},{1,5},{3,7},{5,1},{7,3},{8,12},{10,14},{12... | collective-permute-start | bytes 393224 | tf_op jit(solution)/shard_map/ppermute | solution.py:50
  9.7 8.7 %collective-permute-start.2 = (bf16[16,4096]{1,0:T(8,128)(2,1)S(1)}, bf16[16,4096]{1,0:T(8,128)(2,1)S(1)}, u32[]{:S(2)}, u32[]{:S(2)}) collective-permute-start(bf16[16,4096]{1,0:T(8,128)(2,1)S(1)} %pad_maximum_fusion.11), channel_id=1, source_target_pairs={{0,6},{2,0},{4,2},{6,4},{1,7},{3,1},{5,3},{7,5},{8,14},{10,8},{12,... | collective-permute-start | bytes 393224 | tf_op jit(solution)/shard_map/ppermute | solution.py:50
  43.1 9.5 %collective-permute-start.5 = (bf16[8,4096]{1,0:T(8,128)(2,1)S(1)}, bf16[8,4096]{1,0:T(8,128)(2,1)S(1)}, u32[]{:S(2)}, u32[]{:S(2)}) collective-permute-start(bf16[8,4096]{1,0:T(8,128)(2,1)S(1)} %get-tuple-element.55), channel_id=1, source_target_pairs={{0,2},{2,4},{4,6},{6,0},{1,3},{3,5},{5,7},{7,1},{8,10},{10,12},{12... | collective-permute-start | bytes 196616 | tf_op jit(solution)/shard_map/ppermute | solution.py:50
  46.4 6.2 %collective-permute-start.4 = (bf16[8,4096]{1,0:T(8,128)(2,1)S(1)}, bf16[8,4096]{1,0:T(8,128)(2,1)S(1)}, u32[]{:S(2)}, u32[]{:S(2)}) collective-permute-start(bf16[8,4096]{1,0:T(8,128)(2,1)S(1)} %get-tuple-element.56), channel_id=1, source_target_pairs={{0,4},{2,6},{4,0},{6,2},{1,5},{3,7},{5,1},{7,3},{8,12},{10,14},{12... | collective-permute-start | bytes 196616 | tf_op jit(solution)/shard_map/ppermute | solution.py:50
  48.0 5.2 %collective-permute-start.3 = (bf16[8,4096]{1,0:T(8,128)(2,1)S(1)}, bf16[8,4096]{1,0:T(8,128)(2,1)S(1)}, u32[]{:S(2)}, u32[]{:S(2)}) collective-permute-start(bf16[8,4096]{1,0:T(8,128)(2,1)S(1)} %get-tuple-element.54), channel_id=1, source_target_pairs={{0,6},{2,0},{4,2},{6,4},{1,7},{3,1},{5,3},{7,5},{8,14},{10,8},{12,... | collective-permute-start | bytes 196616 | tf_op jit(solution)/shard_map/ppermute | solution.py:50
  49.9 2.0 %copy-start.3 = (bf16[32,1536]{1,0:T(8,128)(2,1)S(1)}, bf16[32,1536]{1,0:T(8,128)(2,1)}, u32[]{:S(2)}) copy-start(bf16[32,1536]{1,0:T(8,128)(2,1)} %get-tuple-element.18) | copy-start | bytes 294916
  49.9 2.0 %copy-start.4 = (bf16[32,1536]{1,0:T(8,128)(2,1)S(1)}, bf16[32,1536]{1,0:T(8,128)(2,1)}, u32[]{:S(2)}) copy-start(bf16[32,1536]{1,0:T(8,128)(2,1)} %get-tuple-element.17) | copy-start | bytes 294916
  50.0 1.9 %copy-start.5 = (bf16[32,1536]{1,0:T(8,128)(2,1)S(1)}, bf16[32,1536]{1,0:T(8,128)(2,1)}, u32[]{:S(2)}) copy-start(bf16[32,1536]{1,0:T(8,128)(2,1)} %get-tuple-element.16) | copy-start | bytes 294916
  50.3 9.3 %collective-permute-start.6 = (bf16[2,64,1024]{2,1,0:T(8,128)(2,1)S(1)}, bf16[2,64,1024]{2,1,0:T(8,128)(2,1)S(1)}, u32[]{:S(2)}, u32[]{:S(2)}) collective-permute-start(bf16[2,64,1024]{2,1,0:T(8,128)(2,1)S(1)} %pad_maximum_fusion.7), channel_id=1, source_target_pairs={{0,16},{8,24},{16,0},{24,8},{1,17},{9,25},{17,1},{25,9},{2,18},{10... | collective-permute-start | bytes 786440 | tf_op jit(solution)/shard_map/ppermute | solution.py:54
  51.9 12.4 %collective-permute-start.8 = (bf16[1,96,1536]{2,1,0:T(8,128)(2,1)S(1)}, bf16[1,96,1536]{2,1,0:T(8,128)(2,1)S(1)}, u32[]{:S(2)}, u32[]{:S(2)}) collective-permute-start(bf16[1,96,1536]{2,1,0:T(8,128)(2,1)S(1)} %maximum_bitcast_fusion), channel_id=1, source_target_pairs={{0,16},{8,24},{16,0},{24,8},{1,17},{9,25},{17,1},{25,9},{2,18},{10... | collective-permute-start | bytes 884744 | tf_op jit(solution)/shard_map/ppermute | solution.py:54
  59.7 4.9 %collective-permute-start.7 = (bf16[2,64,1024]{2,1,0:T(8,128)(2,1)S(1)}, bf16[2,64,1024]{2,1,0:T(8,128)(2,1)S(1)}, u32[]{:S(2)}, u32[]{:S(2)}) collective-permute-start(bf16[2,64,1024]{2,1,0:T(8,128)(2,1)S(1)} %pad_maximum_fusion.8), channel_id=1, source_target_pairs={{0,8},{8,0},{16,24},{24,16},{1,9},{9,1},{17,25},{25,17},{2,10},{10... | collective-permute-start | bytes 786440 | tf_op jit(solution)/shard_map/ppermute | solution.py:54
  64.4 2.1 %collective-permute-start.9 = (bf16[2,96,1536]{2,1,0:T(8,128)(2,1)S(1)}, bf16[2,96,1536]{2,1,0:T(8,128)(2,1)S(1)}, u32[]{:S(2)}, u32[]{:S(2)}) collective-permute-start(bf16[2,96,1536]{2,1,0:T(8,128)(2,1)S(1)} %pad_maximum_fusion), channel_id=1, source_target_pairs={{0,8},{8,0},{16,24},{24,16},{1,9},{9,1},{17,25},{25,17},{2,10},{10... | collective-permute-start | bytes 1769480 | tf_op jit(solution)/shard_map/ppermute | solution.py:54
  66.7 13.1 %copy-start.1 = (bf16[256,4096]{1,0:T(8,128)(2,1)S(1)}, bf16[256,4096]{1,0:T(8,128)(2,1)}, u32[]{:S(2)}) copy-start(bf16[256,4096]{1,0:T(8,128)(2,1)} %param.7) | copy-start | bytes 6291460
  73.8 4.3 %collective-permute-start.10 = (bf16[8,4096]{1,0:T(8,128)(2,1)S(1)}, bf16[8,4096]{1,0:T(8,128)(2,1)S(1)}, u32[]{:S(2)}, u32[]{:S(2)}) collective-permute-start(bf16[8,4096]{1,0:T(8,128)(2,1)S(1)} %convert_element_type.42), channel_id=1, source_target_pairs={{0,1},{1,0},{2,3},{3,2},{4,5},{5,4},{6,7},{7,6},{8,9},{9,8},{10,11... | collective-permute-start | bytes 196616 | tf_op jit(solution)/shard_map/ppermute | solution.py:50

commit v11 on v10

--- a/solution.py
+++ b/solution.py
@@ -306,9 +306,6 @@
     gate_grad, up_grad, down_grad = weight_grads(
         normed_cols, every_gate, every_up, every_hidden, masked_cols
     )
-    feature_grad, gate_grad, up_grad, down_grad = lax.optimization_barrier(
-        (feature_grad, gate_grad, up_grad, down_grad)
-    )
     seq_sum = feature_grad.astype(jnp.bfloat16)
     for step in range(1, parts):
         feature_grad = feature_grad + shifted(seq_sum, "fsdp", (parts,), (step,)).astype(jnp.float32)

time: 80 us -> 73.3 us (0.916)
  waiting for transfers between devices: 23.5 us -> 16.1 us
  other arithmetic: 3.79 us -> 4.79 us
    ppermute x4, waiting for transfers between devices: 12.8 us -> 1.59 us  [swapped(): return lax.ppermute(value, axis, [(i, i ^ distance) for i in range(size)])]
    ppermute x7, waiting for transfers between devices: 10.7 us -> 14.5 us  [shifted(): return lax.ppermute(value, axes, pairs)]
    another operation x2, other arithmetic: 0.08 us -> 1.06 us  [rep_exchange(): jnp.stack([gathered[o] for o in origins])]
  transfers between devices with their start and end apart: 11 -> 11, of which waited for: 7 -> 6; matrix products, arithmetic and copies ran while one was open for 2% -> 7% of each run, Pallas kernels for 0% -> 31%
where the time goes in v11:
time: 73.3 us; the launch traced here: 73.1 us
  Pallas kernels  29.8 us (41%)
  starting transfers between devices  16.4 us (22%)
  waiting for transfers between devices  16.1 us (22%)
  other arithmetic  4.79 us (7%)
  local copies, waits for them, and re-layouts  2.73 us (4%)
  matrix products  2.34 us (3%)
  between operations  0.95 us (1%)
    pallas_call x1, Pallas kernels, weight_pass(): pl.pallas_call(weight_pass_kernel, grid=(units // chunk,), in_specs=[pl.B...  22.6 us
    ppermute x7, waiting for transfers between devices, shifted(): return lax.ppermute(value, axes, pairs)  14.5 us
    ppermute x7, starting transfers between devices, shifted(): return lax.ppermute(value, axes, pairs)  13.6 us
    pallas_call x1, Pallas kernels, weight_grads(): pl.pallas_call(grads_kernel, grid=(steps,), in_specs=[pl.BlockSpec((rows,...  7.15 us
    ppermute x4, starting transfers between devices, swapped(): return lax.ppermute(value, axis, [(i, i ^ distance) for i in range(size)])  2.78 us
    ppermute x4, waiting for transfers between devices, swapped(): return lax.ppermute(value, axis, [(i, i ^ distance) for i in range(size)])  1.59 us
  transfers between devices with their start and end apart: 11, of which 6 were waited for; matrix products, arithmetic and copies ran while one was open for 7% of the time, Pallas kernels for 31%

profile of v11, /device:TPU:0, one launch (start us, length us, event | category | flops | bytes accessed | tf_op | source)
XLA Modules:
  0.0 73.1 jit_solution(13919355010519581688)
XLA Ops:
  0.6 0.8 %convert_bitcast_fusion = (s32[2,128]{1,0:T(2,128)S(1)}, pred[256]{0:T(512)(128)(4,1)S(1)}) fusion(s32[256]{0:T(256)} %param.13), kind=kLoop, calls=%fused_computation.61 | loop fusion | flops 512 | bytes 2304 | tf_op jit(solution)/shard_map/convert
  1.5 0.3 reduce-window.9
  1.9 0.1 slice_reduce_fusion
  2.1 0.2 copy-done
  2.2 0.5 multiply_reduce_fusion.1
  2.8 0.8 %copy-done.2 = bf16[256,4096]{1,0:T(8,128)(2,1)S(1)} copy-done((bf16[256,4096]{1,0:T(8,128)(2,1)S(1)}, bf16[256,4096]{1,0:T(8,128)(2,1)}, u32[]{:S(2)}) %copy-start.2) | copy-done | bytes 2097176
  3.6 0.4 convolution_convert_fusion.1
  4.1 3.1 %collective-permute-start = (bf16[16,4096]{1,0:T(8,128)(2,1)S(1)}, bf16[16,4096]{1,0:T(8,128)(2,1)S(1)}, u32[]{:S(2)}, u32[]{:S(2)}) collective-permute-start(bf16[16,4096]{1,0:T(8,128)(2,1)S(1)} %pad_maximum_fusion.11), channel_id=1, source_target_pairs={{0,2},{2,4},{4,6},{6,0},{1,3},{3,5},{5,7},{7,1},{8,10},{10,12},{12... | collective-permute-start | bytes 393224 | tf_op jit(solution)/shard_map/ppermute | solution.py:50
  7.2 2.6 %collective-permute-start.1 = (bf16[16,4096]{1,0:T(8,128)(2,1)S(1)}, bf16[16,4096]{1,0:T(8,128)(2,1)S(1)}, u32[]{:S(2)}, u32[]{:S(2)}) collective-permute-start(bf16[16,4096]{1,0:T(8,128)(2,1)S(1)} %pad_maximum_fusion.11), channel_id=1, source_target_pairs={{0,4},{2,6},{4,0},{6,2},{1,5},{3,7},{5,1},{7,3},{8,12},{10,14},{12... | collective-permute-start | bytes 393224 | tf_op jit(solution)/shard_map/ppermute | solution.py:50
  9.7 1.3 %collective-permute-start.2 = (bf16[16,4096]{1,0:T(8,128)(2,1)S(1)}, bf16[16,4096]{1,0:T(8,128)(2,1)S(1)}, u32[]{:S(2)}, u32[]{:S(2)}) collective-permute-start(bf16[16,4096]{1,0:T(8,128)(2,1)S(1)} %pad_maximum_fusion.11), channel_id=1, source_target_pairs={{0,6},{2,0},{4,2},{6,4},{1,7},{3,1},{5,3},{7,5},{8,14},{10,8},{12,... | collective-permute-start | bytes 393224 | tf_op jit(solution)/shard_map/ppermute | solution.py:50
  11.1 2.5 %collective-permute-done = bf16[16,4096]{1,0:T(8,128)(2,1)S(1)} collective-permute-done((bf16[16,4096]{1,0:T(8,128)(2,1)S(1)}, bf16[16,4096]{1,0:T(8,128)(2,1)S(1)}, u32[]{:S(2)}, u32[]{:S(2)}) %collective-permute-start) | collective-permute-done | bytes 131104 | tf_op jit(solution)/shard_map/ppermute | solution.py:50
  13.6 4.8 %collective-permute-done.1 = bf16[16,4096]{1,0:T(8,128)(2,1)S(1)} collective-permute-done((bf16[16,4096]{1,0:T(8,128)(2,1)S(1)}, bf16[16,4096]{1,0:T(8,128)(2,1)S(1)}, u32[]{:S(2)}, u32[]{:S(2)}) %collective-permute-start.1) | collective-permute-done | bytes 131104 | tf_op jit(solution)/shard_map/ppermute | solution.py:50
  18.5 0.4 reshape.75
  18.9 0.8 %fusion.13 = (bf16[64,1,1024]{2,1,0:T(2,128)(2,1)S(1)}, bf16[64,1,1024]{2,1,0:T(2,128)(2,1)S(1)}, bf16[64,1,1024]{2,1,0:T(2,128)(2,1)S(1)}, bf16[64,1,1024]{2,1,0:T(2,128)(2,1)S(1)}) fusion(bf16[64,4,1024]{2,1,0:T(4,128)(2,1)S(1)} %reshape.75), kind=kLoop, calls=%fused_computation.70 | loop fusion | bytes 1048576 | tf_op jit(solution)/shard_map/slice | solution.py:292
  20.0 1.6 %collective-permute-start.7 = (bf16[2,64,1024]{2,1,0:T(8,128)(2,1)S(1)}, bf16[2,64,1024]{2,1,0:T(8,128)(2,1)S(1)}, u32[]{:S(2)}, u32[]{:S(2)}) collective-permute-start(bf16[2,64,1024]{2,1,0:T(8,128)(2,1)S(1)} %pad_maximum_fusion.7), channel_id=1, source_target_pairs={{0,16},{8,24},{16,0},{24,8},{1,17},{9,25},{17,1},{25,9},{2,18},{10... | collective-permute-start | bytes 786440 | tf_op jit(solution)/shard_map/ppermute | solution.py:54
  21.6 0.8 %pad_maximum_fusion.5 = (bf16[32,4096]{1,0:T(8,128)(2,1)}, bf16[32,4096]{1,0:T(8,128)(2,1)}) fusion(bf16[8,4096]{1,0:T(8,128)(2,1)S(1)} %get-tuple-element.51, bf16[8,4096]{1,0:T(8,128)(2,1)S(1)} %get-tuple-element.54, bf16[8,4096]{1,0:T(8,128)(2,1)S(1)} %get-tuple-element.57, bf16[8,4096]{1,0:T(8,128)(2,1)S(1)} %get-tuple-element.19, ...), kind=kLoop, calls=%fused_computation.8 | loop fusion | flops 2097152 | bytes 1048576 | tf_op jit(solution)/shard_map/concatenate | solution.py:282
  22.4 22.6 %shard_map.102 = (bf16[32,1536]{1,0:T(8,128)(2,1)}, bf16[32,1536]{1,0:T(8,128)(2,1)}, bf16[32,1536]{1,0:T(8,128)(2,1)}, f32[32,4096]{1,0:T(8,128)}) custom-call(bf16[32,4096]{1,0:T(8,128)(2,1)} %get-tuple-element.60.normed_ref, bf16[32,4096]{1,0:T(8,128)(2,1)} %get-tuple-element.61.masked_ref, bf16[4096,1536]{1,0:T(8,128)(2,1)} %gate_w_ref.1, ...), custom_call_target="tpu_custom_call" | custom-call | flops 2013265920 | bytes 38797312 | tf_op jit(solution)/shard_map/pallas_call | solution.py:190
  45.0 1.1 %convert_element_type.37 = bf16[32,4096]{1,0:T(8,128)(2,1)S(1)} convert(f32[32,4096]{1,0:T(8,128)} %get-tuple-element.11) | non-fusion elementwise | flops 131072 | bytes 786432 | tf_op jit(solution)/shard_map/convert_element_type | solution.py:296
  46.1 4.4 %collective-permute-start.3 = (bf16[8,4096]{1,0:T(8,128)(2,1)S(1)}, bf16[8,4096]{1,0:T(8,128)(2,1)S(1)}, u32[]{:S(2)}, u32[]{:S(2)}) collective-permute-start(bf16[8,4096]{1,0:T(8,128)(2,1)S(1)} %get-tuple-element.46), channel_id=1, source_target_pairs={{0,6},{2,0},{4,2},{6,4},{1,7},{3,1},{5,3},{7,5},{8,14},{10,8},{12,... | collective-permute-start | bytes 196616 | tf_op jit(solution)/shard_map/ppermute | solution.py:50
  50.5 0.4 collective-permute-start.4
  50.9 0.3 collective-permute-start.5
  51.2 1.0 %maximum_bitcast_fusion = bf16[1,96,1536]{2,1,0:T(8,128)(2,1)S(1)} fusion(bf16[32,1536]{1,0:T(8,128)(2,1)} %get-tuple-element.14, bf16[32,1536]{1,0:T(8,128)(2,1)} %get-tuple-element.13, bf16[32,1536]{1,0:T(8,128)(2,1)} %get-tuple-element.12), kind=kLoop, calls=%fused_computation.7 | loop fusion | flops 884736 | bytes 589824 | tf_op jit(solution)/shard_map/stack | solution.py:137
  52.2 0.6 collective-permute-start.9
  52.7 4.5 %collective-permute-done.4 = bf16[8,4096]{1,0:T(8,128)(2,1)S(1)} collective-permute-done((bf16[8,4096]{1,0:T(8,128)(2,1)S(1)}, bf16[8,4096]{1,0:T(8,128)(2,1)S(1)}, u32[]{:S(2)}, u32[]{:S(2)}) %collective-permute-start.4) | collective-permute-done | bytes 65568 | tf_op jit(solution)/shard_map/ppermute | solution.py:50
  57.2 1.6 %collective-permute-start.6 = (bf16[8,4096]{1,0:T(8,128)(2,1)S(1)}, bf16[8,4096]{1,0:T(8,128)(2,1)S(1)}, u32[]{:S(2)}, u32[]{:S(2)}) collective-permute-start(bf16[8,4096]{1,0:T(8,128)(2,1)S(1)} %fusion.12), channel_id=1, source_target_pairs={{0,1},{1,0},{2,3},{3,2},{4,5},{5,4},{6,7},{7,6},{8,9},{9,8},{10,11... | collective-permute-start | bytes 196616 | tf_op jit(solution)/shard_map/ppermute | solution.py:50
  58.8 2.8 %collective-permute-done.6 = bf16[8,4096]{1,0:T(8,128)(2,1)S(1)} collective-permute-done((bf16[8,4096]{1,0:T(8,128)(2,1)S(1)}, bf16[8,4096]{1,0:T(8,128)(2,1)S(1)}, u32[]{:S(2)}, u32[]{:S(2)}) %collective-permute-start.6) | collective-permute-done | bytes 65568 | tf_op jit(solution)/shard_map/ppermute | solution.py:50
  61.6 0.2 multiply_reduce_fusion
  61.8 1.5 %convolution_convert_fusion = bf16[128,4096]{1,0:T(8,128)(2,1)} fusion(f32[8,4096]{1,0:T(8,128)S(1)} %get-tuple-element.59, bf16[8,4096]{1,0:T(8,128)(2,1)S(1)} %collective-permute-done.6, f32[8]{0:T(128)S(1)} %multiply_multiply_fusion, f32[4096]{0:T(1024)S(1)} %copy-done.6, f32[8]{0:T(128)S(1)} %fusion.8, pred[8,256]{1,0:T(8,128)(4,1)S(1)} %fusion.5, ...), kind=kOutput, calls=%fused_computation | convolution fusion | flops 9404416 | bytes 1525764 | tf_op jit(solution)/shard_map/dot_general | solution.py:23
  63.5 0.6 collective-permute-start.10
  64.1 0.8 %collective-permute-done.8 = bf16[2,64,1024]{2,1,0:T(8,128)(2,1)S(1)} collective-permute-done((bf16[2,64,1024]{2,1,0:T(8,128)(2,1)S(1)}, bf16[2,64,1024]{2,1,0:T(8,128)(2,1)S(1)}, u32[]{:S(2)}, u32[]{:S(2)}) %collective-permute-start.8) | collective-permute-done | bytes 262176 | tf_op jit(solution)/shard_map/ppermute | solution.py:54
  65.0 0.8 %collective-permute-done.10 = bf16[2,96,1536]{2,1,0:T(8,128)(2,1)S(1)} collective-permute-done((bf16[2,96,1536]{2,1,0:T(8,128)(2,1)S(1)}, bf16[2,96,1536]{2,1,0:T(8,128)(2,1)S(1)}, u32[]{:S(2)}, u32[]{:S(2)}) %collective-permute-start.10) | collective-permute-done | bytes 589856 | tf_op jit(solution)/shard_map/ppermute | solution.py:54
  65.9 7.1 %shard_map.103 = (f32[1024,1536]{1,0:T(8,128)}, f32[1024,1536]{1,0:T(8,128)}, f32[1536,1024]{1,0:T(8,128)}) custom-call(bf16[128,1024]{1,0:T(8,128)(2,1)S(1)} %pad_maximum_fusion.9.normed_ref, bf16[128,1536]{1,0:T(8,128)(2,1)S(1)} %pad_maximum_fusion.2.gate_ref, bf16[128,1536]{1,0:T(8,128)(2,1)S(1)} %pad_maximum_fusion.3.up_ref, ...), custom_call_target="tpu_custom_call" | custom-call | flops 1207959552 | bytes 20578304 | tf_op jit(solution)/shard_map/pallas_call | solution.py:234
  (53 shorter events, 1.2 us)
Async XLA Ops:
  0.6 1.6 %copy-start = (bf16[256,4096]{1,0:T(8,128)(2,1)S(1)}, bf16[256,4096]{1,0:T(8,128)(2,1)}, u32[]{:S(2)}) copy-start(bf16[256,4096]{1,0:T(8,128)(2,1)} %param.7) | copy-start | bytes 6291460
  1.9 1.7 %copy-start.2 = (bf16[256,4096]{1,0:T(8,128)(2,1)S(1)}, bf16[256,4096]{1,0:T(8,128)(2,1)}, u32[]{:S(2)}) copy-start(bf16[256,4096]{1,0:T(8,128)(2,1)} %param.8) | copy-start | bytes 6291460
  2.2 1.7 %copy-start.6 = (f32[4096]{0:T(1024)S(1)}, f32[4096]{0:T(1024)}, u32[]{:S(2)}) copy-start(f32[4096]{0:T(1024)} %param.9) | copy-start | bytes 49156
  4.1 9.5 %collective-permute-start = (bf16[16,4096]{1,0:T(8,128)(2,1)S(1)}, bf16[16,4096]{1,0:T(8,128)(2,1)S(1)}, u32[]{:S(2)}, u32[]{:S(2)}) collective-permute-start(bf16[16,4096]{1,0:T(8,128)(2,1)S(1)} %pad_maximum_fusion.11), channel_id=1, source_target_pairs={{0,2},{2,4},{4,6},{6,0},{1,3},{3,5},{5,7},{7,1},{8,10},{10,12},{12... | collective-permute-start | bytes 393224 | tf_op jit(solution)/shard_map/ppermute | solution.py:50
  7.2 11.2 %collective-permute-start.1 = (bf16[16,4096]{1,0:T(8,128)(2,1)S(1)}, bf16[16,4096]{1,0:T(8,128)(2,1)S(1)}, u32[]{:S(2)}, u32[]{:S(2)}) collective-permute-start(bf16[16,4096]{1,0:T(8,128)(2,1)S(1)} %pad_maximum_fusion.11), channel_id=1, source_target_pairs={{0,4},{2,6},{4,0},{6,2},{1,5},{3,7},{5,1},{7,3},{8,12},{10,14},{12... | collective-permute-start | bytes 393224 | tf_op jit(solution)/shard_map/ppermute | solution.py:50
  9.7 8.7 %collective-permute-start.2 = (bf16[16,4096]{1,0:T(8,128)(2,1)S(1)}, bf16[16,4096]{1,0:T(8,128)(2,1)S(1)}, u32[]{:S(2)}, u32[]{:S(2)}) collective-permute-start(bf16[16,4096]{1,0:T(8,128)(2,1)S(1)} %pad_maximum_fusion.11), channel_id=1, source_target_pairs={{0,6},{2,0},{4,2},{6,4},{1,7},{3,1},{5,3},{7,5},{8,14},{10,8},{12,... | collective-permute-start | bytes 393224 | tf_op jit(solution)/shard_map/ppermute | solution.py:50
  20.0 43.2 %collective-permute-start.7 = (bf16[2,64,1024]{2,1,0:T(8,128)(2,1)S(1)}, bf16[2,64,1024]{2,1,0:T(8,128)(2,1)S(1)}, u32[]{:S(2)}, u32[]{:S(2)}) collective-permute-start(bf16[2,64,1024]{2,1,0:T(8,128)(2,1)S(1)} %pad_maximum_fusion.7), channel_id=1, source_target_pairs={{0,16},{8,24},{16,0},{24,8},{1,17},{9,25},{17,1},{25,9},{2,18},{10... | collective-permute-start | bytes 786440 | tf_op jit(solution)/shard_map/ppermute | solution.py:54
  46.1 6.6 %collective-permute-start.3 = (bf16[8,4096]{1,0:T(8,128)(2,1)S(1)}, bf16[8,4096]{1,0:T(8,128)(2,1)S(1)}, u32[]{:S(2)}, u32[]{:S(2)}) collective-permute-start(bf16[8,4096]{1,0:T(8,128)(2,1)S(1)} %get-tuple-element.46), channel_id=1, source_target_pairs={{0,6},{2,0},{4,2},{6,4},{1,7},{3,1},{5,3},{7,5},{8,14},{10,8},{12,... | collective-permute-start | bytes 196616 | tf_op jit(solution)/shard_map/ppermute | solution.py:50
  50.5 6.7 %collective-permute-start.4 = (bf16[8,4096]{1,0:T(8,128)(2,1)S(1)}, bf16[8,4096]{1,0:T(8,128)(2,1)S(1)}, u32[]{:S(2)}, u32[]{:S(2)}) collective-permute-start(bf16[8,4096]{1,0:T(8,128)(2,1)S(1)} %get-tuple-element.48), channel_id=1, source_target_pairs={{0,4},{2,6},{4,0},{6,2},{1,5},{3,7},{5,1},{7,3},{8,12},{10,14},{12... | collective-permute-start | bytes 196616 | tf_op jit(solution)/shard_map/ppermute | solution.py:50
  50.9 6.3 %collective-permute-start.5 = (bf16[8,4096]{1,0:T(8,128)(2,1)S(1)}, bf16[8,4096]{1,0:T(8,128)(2,1)S(1)}, u32[]{:S(2)}, u32[]{:S(2)}) collective-permute-start(bf16[8,4096]{1,0:T(8,128)(2,1)S(1)} %get-tuple-element.47), channel_id=1, source_target_pairs={{0,2},{2,4},{4,6},{6,0},{1,3},{3,5},{5,7},{7,1},{8,10},{10,12},{12... | collective-permute-start | bytes 196616 | tf_op jit(solution)/shard_map/ppermute | solution.py:50
  52.2 11.2 %collective-permute-start.9 = (bf16[1,96,1536]{2,1,0:T(8,128)(2,1)S(1)}, bf16[1,96,1536]{2,1,0:T(8,128)(2,1)S(1)}, u32[]{:S(2)}, u32[]{:S(2)}) collective-permute-start(bf16[1,96,1536]{2,1,0:T(8,128)(2,1)S(1)} %maximum_bitcast_fusion), channel_id=1, source_target_pairs={{0,16},{8,24},{16,0},{24,8},{1,17},{9,25},{17,1},{25,9},{2,18},{10... | collective-permute-start | bytes 884744 | tf_op jit(solution)/shard_map/ppermute | solution.py:54
  57.2 4.3 %collective-permute-start.6 = (bf16[8,4096]{1,0:T(8,128)(2,1)S(1)}, bf16[8,4096]{1,0:T(8,128)(2,1)S(1)}, u32[]{:S(2)}, u32[]{:S(2)}) collective-permute-start(bf16[8,4096]{1,0:T(8,128)(2,1)S(1)} %fusion.12), channel_id=1, source_target_pairs={{0,1},{1,0},{2,3},{3,2},{4,5},{5,4},{6,7},{7,6},{8,9},{9,8},{10,11... | collective-permute-start | bytes 196616 | tf_op jit(solution)/shard_map/ppermute | solution.py:50
  63.3 1.6 %collective-permute-start.8 = (bf16[2,64,1024]{2,1,0:T(8,128)(2,1)S(1)}, bf16[2,64,1024]{2,1,0:T(8,128)(2,1)S(1)}, u32[]{:S(2)}, u32[]{:S(2)}) collective-permute-start(bf16[2,64,1024]{2,1,0:T(8,128)(2,1)S(1)} %pad_maximum_fusion.8), channel_id=1, source_target_pairs={{0,8},{8,0},{16,24},{24,16},{1,9},{9,1},{17,25},{25,17},{2,10},{10... | collective-permute-start | bytes 786440 | tf_op jit(solution)/shard_map/ppermute | solution.py:54
  63.4 2.4 %copy-start.5 = (bf16[32,1536]{1,0:T(8,128)(2,1)S(1)}, bf16[32,1536]{1,0:T(8,128)(2,1)}, u32[]{:S(2)}) copy-start(bf16[32,1536]{1,0:T(8,128)(2,1)} %get-tuple-element.14) | copy-start | bytes 294916
  63.5 2.4 %copy-start.4 = (bf16[32,1536]{1,0:T(8,128)(2,1)S(1)}, bf16[32,1536]{1,0:T(8,128)(2,1)}, u32[]{:S(2)}) copy-start(bf16[32,1536]{1,0:T(8,128)(2,1)} %get-tuple-element.13) | copy-start | bytes 294916
  63.5 2.3 %collective-permute-start.10 = (bf16[2,96,1536]{2,1,0:T(8,128)(2,1)S(1)}, bf16[2,96,1536]{2,1,0:T(8,128)(2,1)S(1)}, u32[]{:S(2)}, u32[]{:S(2)}) collective-permute-start(bf16[2,96,1536]{2,1,0:T(8,128)(2,1)S(1)} %pad_maximum_fusion), channel_id=1, source_target_pairs={{0,8},{8,0},{16,24},{24,16},{1,9},{9,1},{17,25},{25,17},{2,10},{10... | collective-permute-start | bytes 1769480 | tf_op jit(solution)/shard_map/ppermute | solution.py:54
  64.0 1.8 %copy-start.3 = (bf16[32,1536]{1,0:T(8,128)(2,1)S(1)}, bf16[32,1536]{1,0:T(8,128)(2,1)}, u32[]{:S(2)}) copy-start(bf16[32,1536]{1,0:T(8,128)(2,1)} %get-tuple-element.12) | copy-start | bytes 294916
  65.9 7.2 %copy-start.1 = (bf16[256,4096]{1,0:T(8,128)(2,1)S(1)}, bf16[256,4096]{1,0:T(8,128)(2,1)}, u32[]{:S(2)}) copy-start(bf16[256,4096]{1,0:T(8,128)(2,1)} %param.7) | copy-start | bytes 6291460

commit v12 on v11

--- a/solution.py
+++ b/solution.py
@@ -127,29 +127,36 @@
 
 def rep_exchange(factors, column_blocks, axis, size):
     index = lax.axis_index(axis)
-    stacked = jnp.stack(column_blocks)
+    stacked = jnp.stack(column_blocks) if column_blocks is not None else None
     if power_of_two(size):
         gathered = {0: factors}
-        held = {(0, k): lax.dynamic_index_in_dim(stacked, index ^ k, 0, keepdims=False) for k in range(size)}
+        held = {}
+        if stacked is not None:
+            held = {(0, k): lax.dynamic_index_in_dim(stacked, index ^ k, 0, keepdims=False) for k in range(size)}
         distance = size // 2
         while distance >= 1:
             origins = sorted(gathered)
             arrived = swapped(jnp.stack([gathered[o] for o in origins]), axis, size, distance)
             for position, origin in enumerate(origins):
                 gathered[origin ^ distance] = arrived[position]
-            leaving = sorted(key for key in held if key[1] & distance)
-            arrived = swapped(jnp.stack([held[key] for key in leaving]), axis, size, distance)
-            held = {key: v for key, v in held.items() if not key[1] & distance}
-            for position, (origin, target) in enumerate(leaving):
-                held[(origin ^ distance, target ^ distance)] = arrived[position]
+            if held:
+                leaving = sorted(key for key in held if key[1] & distance)
+                arrived = swapped(jnp.stack([held[key] for key in leaving]), axis, size, distance)
+                held = {key: v for key, v in held.items() if not key[1] & distance}
+                for position, (origin, target) in enumerate(leaving):
+                    held[(origin ^ distance, target ^ distance)] = arrived[position]
             distance //= 2
-        return [gathered[o] for o in range(size)], [held[(o, 0)] for o in range(size)]
+        every_columns = [held[(o, 0)] for o in range(size)] if held else None
+        return [gathered[o] for o in range(size)], every_columns
     every_factors = [factors]
-    every_columns = [lax.dynamic_index_in_dim(stacked, index, 0, keepdims=False)]
+    every_columns = None
+    if stacked is not None:
+        every_columns = [lax.dynamic_index_in_dim(stacked, index, 0, keepdims=False)]
     for k in range(1, size):
         every_factors.append(shifted(factors, axis, (size,), (k,)))
-        outgoing = lax.dynamic_index_in_dim(stacked, (index + k) % size, 0, keepdims=False)
-        every_columns.append(shifted(outgoing, axis, (size,), (k,)))
+        if stacked is not None:
+            outgoing = lax.dynamic_index_in_dim(stacked, (index + k) % size, 0, keepdims=False)
+            every_columns.append(shifted(outgoing, axis, (size,), (k,)))
     return every_factors, every_columns
 
 
@@ -182,20 +189,19 @@
         features_ref[...] += partial_features
 
 
-def weight_pass(window_normed, window_masked, gate_weight, up_weight, down_weight):
+def weight_pass(window_normed, window_masked, gate_weight, up_weight, down_weight, first, count, chunk):
     rows, features = window_normed.shape
-    units = gate_weight.shape[1]
-    chunk = next((size for size in (512, 256, 128) if units % size == 0), units)
+    units = count * chunk
     factor_shape = jax.ShapeDtypeStruct((rows, units), jnp.bfloat16)
     return pl.pallas_call(
         weight_pass_kernel,
-        grid=(units // chunk,),
+        grid=(count,),
         in_specs=[
             pl.BlockSpec((rows, features), lambda j: (0, 0)),
             pl.BlockSpec((rows, features), lambda j: (0, 0)),
-            pl.BlockSpec((features, chunk), lambda j: (0, j)),
-            pl.BlockSpec((features, chunk), lambda j: (0, j)),
-            pl.BlockSpec((chunk, features), lambda j: (j, 0)),
+            pl.BlockSpec((features, chunk), lambda j: (0, j + first)),
+            pl.BlockSpec((features, chunk), lambda j: (0, j + first)),
+            pl.BlockSpec((chunk, features), lambda j: (j + first, 0)),
         ],
         out_specs=[
             pl.BlockSpec((rows, chunk), lambda j: (0, j)),
@@ -282,22 +288,37 @@
     window_normed = jnp.concatenate([b[:MAXACT] for b in blocks], axis=0)
     window_masked = jnp.concatenate([b[MAXACT:] for b in blocks], axis=0)
     window = window_normed.shape[0]
-    gate_rows, up_rows, hidden, partial_features = weight_pass(
-        window_normed, window_masked, gate_weight, up_weight, down_weight
-    )
+    units = gate_weight.shape[1]
+    chunk = next((size for size in (512, 256, 128) if units % size == 0), units)
+    chunks = units // chunk
+    leading = chunks * 2 // 3
+    calls = [(0, leading), (leading, chunks - leading)] if leading else [(0, chunks)]
     columns = jnp.concatenate([window_normed, window_masked], axis=0)
     columns = columns.reshape(2 * window, replicas, feature_share)
-    every_factors, every_columns = rep_exchange(
-        jnp.concatenate([gate_rows, up_rows, hidden], axis=0),
-        [columns[:, b] for b in range(replicas)],
-        "rep",
-        replicas,
-    )
+    column_blocks = [columns[:, b] for b in range(replicas)]
+    factor_parts, feature_parts, every_columns = [], [], None
+    for first, count in calls:
+        gate_rows, up_rows, hidden, features_part = weight_pass(
+            window_normed, window_masked, gate_weight, up_weight, down_weight, first, count, chunk
+        )
+        feature_parts.append(features_part)
+        every_part, columns_now = rep_exchange(
+            jnp.concatenate([gate_rows, up_rows, hidden], axis=0),
+            column_blocks if every_columns is None else None,
+            "rep",
+            replicas,
+        )
+        every_columns = columns_now if every_columns is None else every_columns
+        factor_parts.append(every_part)
+    partial_features = sum(feature_parts[1:], feature_parts[0])
     partial_features = partial_features.astype(jnp.bfloat16)
     feature_grad = partial_features[:MAXACT].astype(jnp.float32)
     for k in range(1, shards):
         piece = partial_features[k * MAXACT : (k + 1) * MAXACT]
         feature_grad = feature_grad + shifted(piece, "seq", (shards,), (-k,)).astype(jnp.float32)
+    every_factors = [
+        jnp.concatenate([part[o] for part in factor_parts], axis=1) for o in range(replicas)
+    ]
     every_gate = jnp.concatenate([f[:window] for f in every_factors], axis=0)
     every_up = jnp.concatenate([f[window : 2 * window] for f in every_factors], axis=0)
     every_hidden = jnp.concatenate([f[2 * window :] for f in every_factors], axis=0)

time: 73.3 us -> 78.6 us (1.072)
  Pallas kernels: 29.8 us -> 35.3 us
  other arithmetic: 4.79 us -> 2.84 us
  matrix products: 2.34 us -> 3.95 us
  local copies, waits for them, and re-layouts: 2.73 us -> 1.81 us
    pallas_call x1 -> x2, Pallas kernels: 22.6 us -> 28.2 us  [weight_pass(): pl.pallas_call(weight_pass_kernel, grid=(count,), in_specs=[pl.BlockSpec(...]
    dot_general x1, matrix products: 0.38 us -> 1.98 us  [local(): jnp.dot(picker, cotangent, preferred_element_type=jnp.float32)]
    ppermute x4 -> x6, starting transfers between devices: 2.78 us -> 4.39 us  [swapped(): return lax.ppermute(value, axis, [(i, i ^ distance) for i in range(size)])]
    ppermute x7, starting transfers between devices: 13.6 us -> 12.4 us  [shifted(): return lax.ppermute(value, axes, pairs)]
    convert_element_type x1, other arithmetic: 1.07 us -> 0.06 us  [local(): partial_features = partial_features.astype(jnp.bfloat16)]
    another operation x2, other arithmetic: 1.06 us -> 0.06 us  [rep_exchange(): jnp.stack([gathered[o] for o in origins])]
    unnamed x20 -> x32, local copies, waits for them, and re-layouts: 1.06 us -> 0.13 us
    ppermute x4 -> x6, waiting for transfers between devices: 1.59 us -> 1.41 us  [swapped(): return lax.ppermute(value, axis, [(i, i ^ distance) for i in range(size)])]
  transfers between devices with their start and end apart: 11 -> 13, of which waited for: 6 -> 7; matrix products, arithmetic and copies ran while one was open for 7% -> 3% of each run, Pallas kernels for 31% -> 0%
where the time goes in v12:
time: 78.6 us; the launch traced here: 78.4 us
  Pallas kernels  35.3 us (45%)
  starting transfers between devices  16.8 us (21%)
  waiting for transfers between devices  16.6 us (21%)
  matrix products  3.95 us (5%)
  other arithmetic  2.84 us (4%)
  local copies, waits for them, and re-layouts  1.81 us (2%)
  between operations  1.1 us (1%)
    pallas_call x2, Pallas kernels, weight_pass(): pl.pallas_call(weight_pass_kernel, grid=(count,), in_specs=[pl.BlockSpec(...  28.2 us
    ppermute x7, waiting for transfers between devices, shifted(): return lax.ppermute(value, axes, pairs)  15.2 us
    ppermute x7, starting transfers between devices, shifted(): return lax.ppermute(value, axes, pairs)  12.4 us
    pallas_call x1, Pallas kernels, weight_grads(): pl.pallas_call(grads_kernel, grid=(steps,), in_specs=[pl.BlockSpec((rows,...  7.15 us
    ppermute x6, starting transfers between devices, swapped(): return lax.ppermute(value, axis, [(i, i ^ distance) for i in range(size)])  4.39 us
    dot_general x1, matrix products, local(): jnp.dot(picker, cotangent, preferred_element_type=jnp.float32)  1.98 us
  transfers between devices with their start and end apart: 13, of which 7 were waited for; matrix products, arithmetic and copies ran while one was open for 3% of the time, Pallas kernels for 0%

profile of v12, /device:TPU:0, one launch (start us, length us, event | category | flops | bytes accessed | tf_op | source)
XLA Modules:
  0.0 78.4 jit_solution(4271412692301901178)
XLA Ops:
  0.6 0.8 %convert_bitcast_fusion = (s32[2,128]{1,0:T(2,128)S(1)}, pred[256]{0:T(512)(128)(4,1)S(1)}) fusion(s32[256]{0:T(256)} %param.13), kind=kLoop, calls=%fused_computation.106 | loop fusion | flops 512 | bytes 2304 | tf_op jit(solution)/shard_map/convert
  1.5 0.3 reduce-window.9
  1.9 0.1 slice_reduce_fusion
  2.1 2.0 %convolution_convert_fusion.1 = bf16[8,4096]{1,0:T(8,128)(2,1)S(1)} fusion(bf16[256,4096]{1,0:T(8,128)(2,1)} %param.8, s32[256]{0:T(256)S(1)} %add_bitcast_fusion, pred[256]{0:T(512)(128)(4,1)S(1)} %get-tuple-element.29), kind=kOutput, calls=%fused_computation.1 | convolution fusion | flops 16814080 | bytes 2163968 | tf_op jit(solution)/shard_map/dot_general | solution.py:284
  4.1 0.5 multiply_reduce_fusion.1
  4.7 5.1 %collective-permute-start.2 = (bf16[16,4096]{1,0:T(8,128)(2,1)S(1)}, bf16[16,4096]{1,0:T(8,128)(2,1)S(1)}, u32[]{:S(2)}, u32[]{:S(2)}) collective-permute-start(bf16[16,4096]{1,0:T(8,128)(2,1)S(1)} %pad_maximum_fusion.12), channel_id=1, source_target_pairs={{0,6},{2,0},{4,2},{6,4},{1,7},{3,1},{5,3},{7,5},{8,14},{10,8},{12,... | collective-permute-start | bytes 393224 | tf_op jit(solution)/shard_map/ppermute | solution.py:50
  9.8 1.0 %collective-permute-start = (bf16[16,4096]{1,0:T(8,128)(2,1)S(1)}, bf16[16,4096]{1,0:T(8,128)(2,1)S(1)}, u32[]{:S(2)}, u32[]{:S(2)}) collective-permute-start(bf16[16,4096]{1,0:T(8,128)(2,1)S(1)} %pad_maximum_fusion.12), channel_id=1, source_target_pairs={{0,2},{2,4},{4,6},{6,0},{1,3},{3,5},{5,7},{7,1},{8,10},{10,12},{12... | collective-permute-start | bytes 393224 | tf_op jit(solution)/shard_map/ppermute | solution.py:50
  10.8 8.4 %collective-permute-done = bf16[16,4096]{1,0:T(8,128)(2,1)S(1)} collective-permute-done((bf16[16,4096]{1,0:T(8,128)(2,1)S(1)}, bf16[16,4096]{1,0:T(8,128)(2,1)S(1)}, u32[]{:S(2)}, u32[]{:S(2)}) %collective-permute-start) | collective-permute-done | bytes 131104 | tf_op jit(solution)/shard_map/ppermute | solution.py:50
  19.2 1.8 %collective-permute-done.1 = bf16[16,4096]{1,0:T(8,128)(2,1)S(1)} collective-permute-done((bf16[16,4096]{1,0:T(8,128)(2,1)S(1)}, bf16[16,4096]{1,0:T(8,128)(2,1)S(1)}, u32[]{:S(2)}, u32[]{:S(2)}) %collective-permute-start.1) | collective-permute-done | bytes 131104 | tf_op jit(solution)/shard_map/ppermute | solution.py:50
  21.1 0.8 %pad_maximum_fusion.5 = (bf16[32,4096]{1,0:T(8,128)(2,1)}, bf16[32,4096]{1,0:T(8,128)(2,1)}) fusion(bf16[8,4096]{1,0:T(8,128)(2,1)S(1)} %get-tuple-element.62, bf16[8,4096]{1,0:T(8,128)(2,1)S(1)} %get-tuple-element.65, bf16[8,4096]{1,0:T(8,128)(2,1)S(1)} %get-tuple-element.68, bf16[8,4096]{1,0:T(8,128)(2,1)S(1)} %get-tuple-element.27, ...), kind=kLoop, calls=%fused_computation.43 | loop fusion | flops 2097152 | bytes 1048576 | tf_op jit(solution)/shard_map/concatenate | solution.py:288
  22.0 10.9 %shard_map.103 = (bf16[32,512]{1,0:T(8,128)(2,1)}, bf16[32,512]{1,0:T(8,128)(2,1)}, bf16[32,512]{1,0:T(8,128)(2,1)}, f32[32,4096]{1,0:T(8,128)}) custom-call(bf16[32,4096]{1,0:T(8,128)(2,1)} %get-tuple-element.71.normed_ref, bf16[32,4096]{1,0:T(8,128)(2,1)} %get-tuple-element.72.masked_ref, bf16[4096,1536]{1,0:T(8,128)(2,1)} %gate_w_ref.3, ...), custom_call_target="tpu_custom_call" | custom-call | flops 671088640 | bytes 13631488 | tf_op jit(solution)/shard_map/pallas_call | solution.py:196
  32.8 17.3 %shard_map.102 = (bf16[32,1024]{1,0:T(8,128)(2,1)}, bf16[32,1024]{1,0:T(8,128)(2,1)}, bf16[32,1024]{1,0:T(8,128)(2,1)}, f32[32,4096]{1,0:T(8,128)}) custom-call(bf16[32,4096]{1,0:T(8,128)(2,1)} %get-tuple-element.71.normed_ref, bf16[32,4096]{1,0:T(8,128)(2,1)} %get-tuple-element.72.masked_ref, bf16[4096,1536]{1,0:T(8,128)(2,1)} %gate_w_ref.3, ...), custom_call_target="tpu_custom_call" | custom-call | flops 1342177280 | bytes 26214400 | tf_op jit(solution)/shard_map/pallas_call | solution.py:196
  50.1 0.4 reshape.66
  50.5 0.8 fusion.35
  51.3 0.1 copy_bitcast_fusion.2
  51.4 0.1 copy_bitcast_fusion
  51.7 1.6 %collective-permute-start.7 = (bf16[2,64,1024]{2,1,0:T(8,128)(2,1)S(1)}, bf16[2,64,1024]{2,1,0:T(8,128)(2,1)S(1)}, u32[]{:S(2)}, u32[]{:S(2)}) collective-permute-start(bf16[2,64,1024]{2,1,0:T(8,128)(2,1)S(1)} %pad_maximum_fusion.7), channel_id=1, source_target_pairs={{0,16},{8,24},{16,0},{24,8},{1,17},{9,25},{17,1},{25,9},{2,18},{10... | collective-permute-start | bytes 786440 | tf_op jit(solution)/shard_map/ppermute | solution.py:54
  53.3 0.6 collective-permute-start.11
  54.0 1.7 %collective-permute-start.3 = (bf16[8,4096]{1,0:T(8,128)(2,1)S(1)}, bf16[8,4096]{1,0:T(8,128)(2,1)S(1)}, u32[]{:S(2)}, u32[]{:S(2)}) collective-permute-start(bf16[8,4096]{1,0:T(8,128)(2,1)S(1)} %get-tuple-element.55), channel_id=1, source_target_pairs={{0,6},{2,0},{4,2},{6,4},{1,7},{3,1},{5,3},{7,5},{8,14},{10,8},{12,... | collective-permute-start | bytes 196616 | tf_op jit(solution)/shard_map/ppermute | solution.py:50
  55.7 0.4 collective-permute-start.5
  56.1 2.7 %collective-permute-start.4 = (bf16[8,4096]{1,0:T(8,128)(2,1)S(1)}, bf16[8,4096]{1,0:T(8,128)(2,1)S(1)}, u32[]{:S(2)}, u32[]{:S(2)}) collective-permute-start(bf16[8,4096]{1,0:T(8,128)(2,1)S(1)} %get-tuple-element.57), channel_id=1, source_target_pairs={{0,4},{2,6},{4,0},{6,2},{1,5},{3,7},{5,1},{7,3},{8,12},{10,14},{12... | collective-permute-start | bytes 196616 | tf_op jit(solution)/shard_map/ppermute | solution.py:50
  58.8 0.6 collective-permute-done.3
  59.4 1.5 %collective-permute-start.9 = (bf16[1,96,1024]{2,1,0:T(8,128)(2,1)S(1)}, bf16[1,96,1024]{2,1,0:T(8,128)(2,1)S(1)}, u32[]{:S(2)}, u32[]{:S(2)}) collective-permute-start(bf16[1,96,1024]{2,1,0:T(8,128)(2,1)S(1)} %bitcast.42), channel_id=1, source_target_pairs={{0,16},{8,24},{16,0},{24,8},{1,17},{9,25},{17,1},{25,9},{2,18},{10... | collective-permute-start | bytes 589832 | tf_op jit(solution)/shard_map/ppermute | solution.py:54
  61.0 0.9 %collective-permute-done.5 = bf16[8,4096]{1,0:T(8,128)(2,1)S(1)} collective-permute-done((bf16[8,4096]{1,0:T(8,128)(2,1)S(1)}, bf16[8,4096]{1,0:T(8,128)(2,1)S(1)}, u32[]{:S(2)}, u32[]{:S(2)}) %collective-permute-start.5) | collective-permute-done | bytes 65568 | tf_op jit(solution)/shard_map/ppermute | solution.py:50
  61.8 0.9 %collective-permute-done.4 = bf16[8,4096]{1,0:T(8,128)(2,1)S(1)} collective-permute-done((bf16[8,4096]{1,0:T(8,128)(2,1)S(1)}, bf16[8,4096]{1,0:T(8,128)(2,1)S(1)}, u32[]{:S(2)}, u32[]{:S(2)}) %collective-permute-start.4) | collective-permute-done | bytes 65568 | tf_op jit(solution)/shard_map/ppermute | solution.py:50
  62.8 1.6 %collective-permute-start.6 = (bf16[8,4096]{1,0:T(8,128)(2,1)S(1)}, bf16[8,4096]{1,0:T(8,128)(2,1)S(1)}, u32[]{:S(2)}, u32[]{:S(2)}) collective-permute-start(bf16[8,4096]{1,0:T(8,128)(2,1)S(1)} %fusion.34), channel_id=1, source_target_pairs={{0,1},{1,0},{2,3},{3,2},{4,5},{5,4},{6,7},{7,6},{8,9},{9,8},{10,11... | collective-permute-start | bytes 196616 | tf_op jit(solution)/shard_map/ppermute | solution.py:50
  64.5 2.7 %collective-permute-done.6 = bf16[8,4096]{1,0:T(8,128)(2,1)S(1)} collective-permute-done((bf16[8,4096]{1,0:T(8,128)(2,1)S(1)}, bf16[8,4096]{1,0:T(8,128)(2,1)S(1)}, u32[]{:S(2)}, u32[]{:S(2)}) %collective-permute-start.6) | collective-permute-done | bytes 65568 | tf_op jit(solution)/shard_map/ppermute | solution.py:50
  67.1 0.2 multiply_reduce_fusion
  67.3 1.5 %convolution_convert_fusion = bf16[128,4096]{1,0:T(8,128)(2,1)} fusion(f32[8,4096]{1,0:T(8,128)S(1)} %get-tuple-element.70, bf16[8,4096]{1,0:T(8,128)(2,1)S(1)} %collective-permute-done.6, f32[8]{0:T(128)S(1)} %multiply_multiply_fusion, f32[4096]{0:T(1024)S(1)} %copy-done.4, f32[8]{0:T(128)S(1)} %fusion.30, pred[8,256]{1,0:T(8,128)(4,1)S(1)} %fusion.27, ...), kind=kOutput, calls=%fused_computation | convolution fusion | flops 9404416 | bytes 1525764 | tf_op jit(solution)/shard_map/dot_general | solution.py:23
  69.0 0.6 collective-permute-start.8
  69.6 1.4 %collective-permute-done.8 = bf16[2,64,1024]{2,1,0:T(8,128)(2,1)S(1)} collective-permute-done((bf16[2,64,1024]{2,1,0:T(8,128)(2,1)S(1)}, bf16[2,64,1024]{2,1,0:T(8,128)(2,1)S(1)}, u32[]{:S(2)}, u32[]{:S(2)}) %collective-permute-start.8) | collective-permute-done | bytes 262176 | tf_op jit(solution)/shard_map/ppermute | solution.py:54
  71.3 7.1 %shard_map.104 = (f32[1024,1536]{1,0:T(8,128)}, f32[1024,1536]{1,0:T(8,128)}, f32[1536,1024]{1,0:T(8,128)}) custom-call(bf16[128,1024]{1,0:T(8,128)(2,1)S(1)} %pad_maximum_fusion.9.normed_ref, bf16[128,1536]{1,0:T(8,128)(2,1)S(1)} %pad_maximum_fusion.3.gate_ref, bf16[128,1536]{1,0:T(8,128)(2,1)S(1)} %pad_maximum_fusion.4.up_ref, ...), custom_call_target="tpu_custom_call" | custom-call | flops 1207959552 | bytes 20578304 | tf_op jit(solution)/shard_map/pallas_call | solution.py:240
  (76 shorter events, 1.3 us)
Async XLA Ops:
  0.6 3.5 %copy-start = (bf16[256,4096]{1,0:T(8,128)(2,1)S(1)}, bf16[256,4096]{1,0:T(8,128)(2,1)}, u32[]{:S(2)}) copy-start(bf16[256,4096]{1,0:T(8,128)(2,1)} %param.7) | copy-start | bytes 6291460
  2.1 2.5 %copy-start.4 = (f32[4096]{0:T(1024)S(1)}, f32[4096]{0:T(1024)}, u32[]{:S(2)}) copy-start(f32[4096]{0:T(1024)} %param.9) | copy-start | bytes 49156
  4.7 16.3 %collective-permute-start.2 = (bf16[16,4096]{1,0:T(8,128)(2,1)S(1)}, bf16[16,4096]{1,0:T(8,128)(2,1)S(1)}, u32[]{:S(2)}, u32[]{:S(2)}) collective-permute-start(bf16[16,4096]{1,0:T(8,128)(2,1)S(1)} %pad_maximum_fusion.12), channel_id=1, source_target_pairs={{0,6},{2,0},{4,2},{6,4},{1,7},{3,1},{5,3},{7,5},{8,14},{10,8},{12,... | collective-permute-start | bytes 393224 | tf_op jit(solution)/shard_map/ppermute | solution.py:50
  9.8 11.2 %collective-permute-start.1 = (bf16[16,4096]{1,0:T(8,128)(2,1)S(1)}, bf16[16,4096]{1,0:T(8,128)(2,1)S(1)}, u32[]{:S(2)}, u32[]{:S(2)}) collective-permute-start(bf16[16,4096]{1,0:T(8,128)(2,1)S(1)} %pad_maximum_fusion.12), channel_id=1, source_target_pairs={{0,4},{2,6},{4,0},{6,2},{1,5},{3,7},{5,1},{7,3},{8,12},{10,14},{12... | collective-permute-start | bytes 393224 | tf_op jit(solution)/shard_map/ppermute | solution.py:50
  9.8 9.4 %collective-permute-start = (bf16[16,4096]{1,0:T(8,128)(2,1)S(1)}, bf16[16,4096]{1,0:T(8,128)(2,1)S(1)}, u32[]{:S(2)}, u32[]{:S(2)}) collective-permute-start(bf16[16,4096]{1,0:T(8,128)(2,1)S(1)} %pad_maximum_fusion.12), channel_id=1, source_target_pairs={{0,2},{2,4},{4,6},{6,0},{1,3},{3,5},{5,7},{7,1},{8,10},{10,12},{12... | collective-permute-start | bytes 393224 | tf_op jit(solution)/shard_map/ppermute | solution.py:50
  51.3 2.0 %copy-start.10 = (bf16[32,512]{1,0:T(8,128)(2,1)S(1)}, bf16[32,512]{1,0:T(8,128)(2,1)}, u32[]{:S(2)}) copy-start(bf16[32,512]{1,0:T(8,128)(2,1)} %get-tuple-element.20) | copy-start | bytes 98308
  51.3 2.0 %copy-start.9 = (bf16[32,512]{1,0:T(8,128)(2,1)S(1)}, bf16[32,512]{1,0:T(8,128)(2,1)}, u32[]{:S(2)}) copy-start(bf16[32,512]{1,0:T(8,128)(2,1)} %get-tuple-element.21) | copy-start | bytes 98308
  51.3 2.0 %copy-start.8 = (bf16[32,512]{1,0:T(8,128)(2,1)S(1)}, bf16[32,512]{1,0:T(8,128)(2,1)}, u32[]{:S(2)}) copy-start(bf16[32,512]{1,0:T(8,128)(2,1)} %get-tuple-element.22) | copy-start | bytes 98308
  51.3 2.6 %copy-start.7 = (bf16[32,1024]{1,0:T(8,128)(2,1)S(1)}, bf16[32,1024]{1,0:T(8,128)(2,1)}, u32[]{:S(2)}) copy-start(bf16[32,1024]{1,0:T(8,128)(2,1)} %get-tuple-element.17) | copy-start | bytes 196612
  51.3 2.6 %copy-start.2 = (f32[32,4096]{1,0:T(8,128)S(1)}, f32[32,4096]{1,0:T(8,128)}, u32[]{:S(2)}) copy-start(f32[32,4096]{1,0:T(8,128)} %get-tuple-element.16) | copy-start | bytes 1572868
  51.3 2.6 %copy-start.3 = (f32[32,4096]{1,0:T(8,128)S(1)}, f32[32,4096]{1,0:T(8,128)}, u32[]{:S(2)}) copy-start(f32[32,4096]{1,0:T(8,128)} %get-tuple-element.15) | copy-start | bytes 1572868
  51.5 7.2 %copy-start.6 = (bf16[32,1024]{1,0:T(8,128)(2,1)S(1)}, bf16[32,1024]{1,0:T(8,128)(2,1)}, u32[]{:S(2)}) copy-start(bf16[32,1024]{1,0:T(8,128)(2,1)} %get-tuple-element.18) | copy-start | bytes 196612
  51.5 7.2 %copy-start.5 = (bf16[32,1024]{1,0:T(8,128)(2,1)S(1)}, bf16[32,1024]{1,0:T(8,128)(2,1)}, u32[]{:S(2)}) copy-start(bf16[32,1024]{1,0:T(8,128)(2,1)} %get-tuple-element.19) | copy-start | bytes 196612
  51.7 17.2 %collective-permute-start.7 = (bf16[2,64,1024]{2,1,0:T(8,128)(2,1)S(1)}, bf16[2,64,1024]{2,1,0:T(8,128)(2,1)S(1)}, u32[]{:S(2)}, u32[]{:S(2)}) collective-permute-start(bf16[2,64,1024]{2,1,0:T(8,128)(2,1)S(1)} %pad_maximum_fusion.7), channel_id=1, source_target_pairs={{0,16},{8,24},{16,0},{24,8},{1,17},{9,25},{17,1},{25,9},{2,18},{10... | collective-permute-start | bytes 786440 | tf_op jit(solution)/shard_map/ppermute | solution.py:54
  53.3 11.0 %collective-permute-start.11 = (bf16[1,96,512]{2,1,0:T(8,128)(2,1)S(1)}, bf16[1,96,512]{2,1,0:T(8,128)(2,1)S(1)}, u32[]{:S(2)}, u32[]{:S(2)}) collective-permute-start(bf16[1,96,512]{2,1,0:T(8,128)(2,1)S(1)} %bitcast.46), channel_id=1, source_target_pairs={{0,16},{8,24},{16,0},{24,8},{1,17},{9,25},{17,1},{25,9},{2,18},{10... | collective-permute-start | bytes 294920 | tf_op jit(solution)/shard_map/ppermute | solution.py:54
  54.0 5.4 %collective-permute-start.3 = (bf16[8,4096]{1,0:T(8,128)(2,1)S(1)}, bf16[8,4096]{1,0:T(8,128)(2,1)S(1)}, u32[]{:S(2)}, u32[]{:S(2)}) collective-permute-start(bf16[8,4096]{1,0:T(8,128)(2,1)S(1)} %get-tuple-element.55), channel_id=1, source_target_pairs={{0,6},{2,0},{4,2},{6,4},{1,7},{3,1},{5,3},{7,5},{8,14},{10,8},{12,... | collective-permute-start | bytes 196616 | tf_op jit(solution)/shard_map/ppermute | solution.py:50
  55.7 6.2 %collective-permute-start.5 = (bf16[8,4096]{1,0:T(8,128)(2,1)S(1)}, bf16[8,4096]{1,0:T(8,128)(2,1)S(1)}, u32[]{:S(2)}, u32[]{:S(2)}) collective-permute-start(bf16[8,4096]{1,0:T(8,128)(2,1)S(1)} %get-tuple-element.56), channel_id=1, source_target_pairs={{0,2},{2,4},{4,6},{6,0},{1,3},{3,5},{5,7},{7,1},{8,10},{10,12},{12... | collective-permute-start | bytes 196616 | tf_op jit(solution)/shard_map/ppermute | solution.py:50
  56.1 6.7 %collective-permute-start.4 = (bf16[8,4096]{1,0:T(8,128)(2,1)S(1)}, bf16[8,4096]{1,0:T(8,128)(2,1)S(1)}, u32[]{:S(2)}, u32[]{:S(2)}) collective-permute-start(bf16[8,4096]{1,0:T(8,128)(2,1)S(1)} %get-tuple-element.57), channel_id=1, source_target_pairs={{0,4},{2,6},{4,0},{6,2},{1,5},{3,7},{5,1},{7,3},{8,12},{10,14},{12... | collective-permute-start | bytes 196616 | tf_op jit(solution)/shard_map/ppermute | solution.py:50
  59.4 9.3 %collective-permute-start.9 = (bf16[1,96,1024]{2,1,0:T(8,128)(2,1)S(1)}, bf16[1,96,1024]{2,1,0:T(8,128)(2,1)S(1)}, u32[]{:S(2)}, u32[]{:S(2)}) collective-permute-start(bf16[1,96,1024]{2,1,0:T(8,128)(2,1)S(1)} %bitcast.42), channel_id=1, source_target_pairs={{0,16},{8,24},{16,0},{24,8},{1,17},{9,25},{17,1},{25,9},{2,18},{10... | collective-permute-start | bytes 589832 | tf_op jit(solution)/shard_map/ppermute | solution.py:54
  62.8 4.3 %collective-permute-start.6 = (bf16[8,4096]{1,0:T(8,128)(2,1)S(1)}, bf16[8,4096]{1,0:T(8,128)(2,1)S(1)}, u32[]{:S(2)}, u32[]{:S(2)}) collective-permute-start(bf16[8,4096]{1,0:T(8,128)(2,1)S(1)} %fusion.34), channel_id=1, source_target_pairs={{0,1},{1,0},{2,3},{3,2},{4,5},{5,4},{6,7},{7,6},{8,9},{9,8},{10,11... | collective-permute-start | bytes 196616 | tf_op jit(solution)/shard_map/ppermute | solution.py:50
  64.4 5.2 %collective-permute-start.12 = (bf16[2,96,512]{2,1,0:T(8,128)(2,1)S(1)}, bf16[2,96,512]{2,1,0:T(8,128)(2,1)S(1)}, u32[]{:S(2)}, u32[]{:S(2)}) collective-permute-start(bf16[2,96,512]{2,1,0:T(8,128)(2,1)S(1)} %pad_maximum_fusion.11), channel_id=1, source_target_pairs={{0,8},{8,0},{16,24},{24,16},{1,9},{9,1},{17,25},{25,17},{2,10},{10... | collective-permute-start | bytes 589832 | tf_op jit(solution)/shard_map/ppermute | solution.py:54
  68.8 2.2 %collective-permute-start.10 = (bf16[2,96,1024]{2,1,0:T(8,128)(2,1)S(1)}, bf16[2,96,1024]{2,1,0:T(8,128)(2,1)S(1)}, u32[]{:S(2)}, u32[]{:S(2)}) collective-permute-start(bf16[2,96,1024]{2,1,0:T(8,128)(2,1)S(1)} %pad_maximum_fusion.2), channel_id=1, source_target_pairs={{0,8},{8,0},{16,24},{24,16},{1,9},{9,1},{17,25},{25,17},{2,10},{10... | collective-permute-start | bytes 1179656 | tf_op jit(solution)/shard_map/ppermute | solution.py:54
  69.0 2.0 %collective-permute-start.8 = (bf16[2,64,1024]{2,1,0:T(8,128)(2,1)S(1)}, bf16[2,64,1024]{2,1,0:T(8,128)(2,1)S(1)}, u32[]{:S(2)}, u32[]{:S(2)}) collective-permute-start(bf16[2,64,1024]{2,1,0:T(8,128)(2,1)S(1)} %pad_maximum_fusion.8), channel_id=1, source_target_pairs={{0,8},{8,0},{16,24},{24,16},{1,9},{9,1},{17,25},{25,17},{2,10},{10... | collective-permute-start | bytes 786440 | tf_op jit(solution)/shard_map/ppermute | solution.py:54
  71.2 7.2 %copy-start.1 = (bf16[256,4096]{1,0:T(8,128)(2,1)S(1)}, bf16[256,4096]{1,0:T(8,128)(2,1)}, u32[]{:S(2)}) copy-start(bf16[256,4096]{1,0:T(8,128)(2,1)} %param.7) | copy-start | bytes 6291460

commit v13 on v11

--- a/solution.py
+++ b/solution.py
@@ -277,10 +277,19 @@
     source = jnp.dot(picker, tokens, preferred_element_type=jnp.float32)
     send_masked = jnp.dot(picker, cotangent, preferred_element_type=jnp.float32).astype(jnp.bfloat16)
     send_normed = normalize(source, norm_gain).astype(jnp.bfloat16)
-    packed = jnp.concatenate([send_normed, send_masked], axis=0)
-    blocks = [packed] + [shifted(packed, "seq", (shards,), (k,)) for k in range(1, shards)]
-    window_normed = jnp.concatenate([b[:MAXACT] for b in blocks], axis=0)
-    window_masked = jnp.concatenate([b[MAXACT:] for b in blocks], axis=0)
+    if parts % 2 == 0:
+        carries_normed = place % 2 == 0
+        mine = jnp.where(carries_normed, send_normed, send_masked)
+        blocks = [mine] + [shifted(mine, "seq", (shards,), (k,)) for k in range(1, shards)]
+        gathered = jnp.concatenate(blocks, axis=0)
+        swapped_half = lax.ppermute(gathered, "fsdp", [(i, i ^ 1) for i in range(parts)])
+        window_normed = jnp.where(carries_normed, gathered, swapped_half)
+        window_masked = jnp.where(carries_normed, swapped_half, gathered)
+    else:
+        packed = jnp.concatenate([send_normed, send_masked], axis=0)
+        blocks = [packed] + [shifted(packed, "seq", (shards,), (k,)) for k in range(1, shards)]
+        window_normed = jnp.concatenate([b[:MAXACT] for b in blocks], axis=0)
+        window_masked = jnp.concatenate([b[MAXACT:] for b in blocks], axis=0)
     window = window_normed.shape[0]
     gate_rows, up_rows, hidden, partial_features = weight_pass(
         window_normed, window_masked, gate_weight, up_weight, down_weight

time: 73.3 us -> 74.5 us (1.016)
  waiting for transfers between devices: 16.1 us -> 18.2 us
  other arithmetic: 4.79 us -> 4 us
    ppermute x0 -> x1, waiting for transfers between devices: none -> 6.25 us  [local(): lax.ppermute(gathered, 'fsdp', [(i, i ^ 1) for i in range(parts)])]
    ppermute x7, waiting for transfers between devices: 14.5 us -> 10.3 us  [shifted(): return lax.ppermute(value, axes, pairs)]
    ppermute x0 -> x1, starting transfers between devices: none -> 1.6 us  [local(): lax.ppermute(gathered, 'fsdp', [(i, i ^ 1) for i in range(parts)])]
    ppermute x7, starting transfers between devices: 13.6 us -> 12.4 us  [shifted(): return lax.ppermute(value, axes, pairs)]
    concatenate x3 -> x2, other arithmetic: 0.86 us -> 0.05 us  [the longest x1 0.04 us: local(): columns = jnp.concatenate([window_normed, window_masked], axis=0)]
  transfers between devices with their start and end apart: 11 -> 12, of which waited for: 6 -> 9; matrix products, arithmetic and copies ran while one was open for 7% -> 5% of each run, Pallas kernels for 31% -> 30%
where the time goes in v13:
time: 74.5 us; the launch traced here: 74.3 us
  Pallas kernels  29.8 us (40%)
  waiting for transfers between devices  18.2 us (24%)
  starting transfers between devices  16.4 us (22%)
  other arithmetic  4 us (5%)
  local copies, waits for them, and re-layouts  2.66 us (4%)
  matrix products  2.35 us (3%)
  between operations  0.95 us (1%)
    pallas_call x1, Pallas kernels, weight_pass(): pl.pallas_call(weight_pass_kernel, grid=(units // chunk,), in_specs=[pl.B...  22.6 us
    ppermute x7, starting transfers between devices, shifted(): return lax.ppermute(value, axes, pairs)  12.4 us
    ppermute x7, waiting for transfers between devices, shifted(): return lax.ppermute(value, axes, pairs)  10.3 us
    pallas_call x1, Pallas kernels, weight_grads(): pl.pallas_call(grads_kernel, grid=(steps,), in_specs=[pl.BlockSpec((rows,...  7.15 us
    ppermute x1, waiting for transfers between devices, local(): lax.ppermute(gathered, 'fsdp', [(i, i ^ 1) for i in range(parts)])  6.25 us
    ppermute x4, starting transfers between devices, swapped(): return lax.ppermute(value, axis, [(i, i ^ distance) for i in range(size)])  2.34 us
    ppermute x1, starting transfers between devices, local(): lax.ppermute(gathered, 'fsdp', [(i, i ^ 1) for i in range(parts)])  1.6 us
    ppermute x4, waiting for transfers between devices, swapped(): return lax.ppermute(value, axis, [(i, i ^ distance) for i in range(size)])  1.59 us
  transfers between devices with their start and end apart: 12, of which 9 were waited for; matrix products, arithmetic and copies ran while one was open for 5% of the time, Pallas kernels for 30%

profile of v13, /device:TPU:0, one launch (start us, length us, event | category | flops | bytes accessed | tf_op | source)
XLA Modules:
  0.0 74.3 jit_solution(17137925106565745538)
XLA Ops:
  0.7 0.8 %convert_bitcast_fusion = (s32[2,128]{1,0:T(2,128)S(1)}, pred[256]{0:T(512)(128)(4,1)S(1)}) fusion(s32[256]{0:T(256)} %param.13), kind=kLoop, calls=%fused_computation.55 | loop fusion | flops 512 | bytes 2304 | tf_op jit(solution)/shard_map/convert
  1.5 0.3 reduce-window.9
  2.2 0.5 multiply_reduce_fusion.1
  2.8 0.8 %copy-done.4 = bf16[256,4096]{1,0:T(8,128)(2,1)S(1)} copy-done((bf16[256,4096]{1,0:T(8,128)(2,1)S(1)}, bf16[256,4096]{1,0:T(8,128)(2,1)}, u32[]{:S(2)}) %copy-start.4) | copy-done | bytes 2097176
  3.6 0.4 fusion
  4.0 3.0 %collective-permute-start = (bf16[8,4096]{1,0:T(8,128)(2,1)S(1)}, bf16[8,4096]{1,0:T(8,128)(2,1)S(1)}, u32[]{:S(2)}, u32[]{:S(2)}) collective-permute-start(bf16[8,4096]{1,0:T(8,128)(2,1)S(1)} %fusion), channel_id=1, source_target_pairs={{0,2},{2,4},{4,6},{6,0},{1,3},{3,5},{5,7},{7,1},{8,10},{10,12},{12... | collective-permute-start | bytes 196616 | tf_op jit(solution)/shard_map/ppermute | solution.py:50
  7.0 2.6 %collective-permute-start.1 = (bf16[8,4096]{1,0:T(8,128)(2,1)S(1)}, bf16[8,4096]{1,0:T(8,128)(2,1)S(1)}, u32[]{:S(2)}, u32[]{:S(2)}) collective-permute-start(bf16[8,4096]{1,0:T(8,128)(2,1)S(1)} %fusion), channel_id=1, source_target_pairs={{0,4},{2,6},{4,0},{6,2},{1,5},{3,7},{5,1},{7,3},{8,12},{10,14},{12... | collective-permute-start | bytes 196616 | tf_op jit(solution)/shard_map/ppermute | solution.py:50
  9.6 1.3 %collective-permute-start.2 = (bf16[8,4096]{1,0:T(8,128)(2,1)S(1)}, bf16[8,4096]{1,0:T(8,128)(2,1)S(1)}, u32[]{:S(2)}, u32[]{:S(2)}) collective-permute-start(bf16[8,4096]{1,0:T(8,128)(2,1)S(1)} %fusion), channel_id=1, source_target_pairs={{0,6},{2,0},{4,2},{6,4},{1,7},{3,1},{5,3},{7,5},{8,14},{10,8},{12,... | collective-permute-start | bytes 196616 | tf_op jit(solution)/shard_map/ppermute | solution.py:50
  10.9 0.6 collective-permute-done
  11.6 2.5 %collective-permute-done.1 = bf16[8,4096]{1,0:T(8,128)(2,1)S(1)} collective-permute-done((bf16[8,4096]{1,0:T(8,128)(2,1)S(1)}, bf16[8,4096]{1,0:T(8,128)(2,1)S(1)}, u32[]{:S(2)}, u32[]{:S(2)}) %collective-permute-start.1) | collective-permute-done | bytes 65568 | tf_op jit(solution)/shard_map/ppermute | solution.py:50
  14.1 0.2 collective-permute-done.2
  14.3 1.6 %collective-permute-start.3 = (bf16[32,4096]{1,0:T(8,128)(2,1)S(1)}, bf16[32,4096]{1,0:T(8,128)(2,1)S(1)}, u32[]{:S(2)}, u32[]{:S(2)}) collective-permute-start(bf16[32,4096]{1,0:T(8,128)(2,1)S(1)} %pad_maximum_fusion.6), channel_id=1, source_target_pairs={{0,1},{1,0},{2,3},{3,2},{4,5},{5,4},{6,7},{7,6},{8,9},{9,8},{10,11... | collective-permute-start | bytes 786440 | tf_op jit(solution)/shard_map/ppermute | solution.py:285
  15.9 6.2 %collective-permute-done.3 = bf16[32,4096]{1,0:T(8,128)(2,1)S(1)} collective-permute-done((bf16[32,4096]{1,0:T(8,128)(2,1)S(1)}, bf16[32,4096]{1,0:T(8,128)(2,1)S(1)}, u32[]{:S(2)}, u32[]{:S(2)}) %collective-permute-start.3) | collective-permute-done | bytes 262176 | tf_op jit(solution)/shard_map/ppermute | solution.py:285
  22.4 0.4 reshape.75
  22.7 0.8 %fusion.14 = (bf16[64,1,1024]{2,1,0:T(2,128)(2,1)S(1)}, bf16[64,1,1024]{2,1,0:T(2,128)(2,1)S(1)}, bf16[64,1,1024]{2,1,0:T(2,128)(2,1)S(1)}, bf16[64,1,1024]{2,1,0:T(2,128)(2,1)S(1)}) fusion(bf16[64,4,1024]{2,1,0:T(4,128)(2,1)S(1)} %reshape.75), kind=kLoop, calls=%fused_computation.64 | loop fusion | bytes 1048576 | tf_op jit(solution)/shard_map/slice | solution.py:301
  23.9 0.9 %collective-permute-start.8 = (bf16[2,64,1024]{2,1,0:T(8,128)(2,1)S(1)}, bf16[2,64,1024]{2,1,0:T(8,128)(2,1)S(1)}, u32[]{:S(2)}, u32[]{:S(2)}) collective-permute-start(bf16[2,64,1024]{2,1,0:T(8,128)(2,1)S(1)} %pad_maximum_fusion.7), channel_id=1, source_target_pairs={{0,16},{8,24},{16,0},{24,8},{1,17},{9,25},{17,1},{25,9},{2,18},{10... | collective-permute-start | bytes 786440 | tf_op jit(solution)/shard_map/ppermute | solution.py:54
  24.7 22.6 %shard_map.102 = (bf16[32,1536]{1,0:T(8,128)(2,1)}, bf16[32,1536]{1,0:T(8,128)(2,1)}, bf16[32,1536]{1,0:T(8,128)(2,1)}, f32[32,4096]{1,0:T(8,128)}) custom-call(bf16[32,4096]{1,0:T(8,128)(2,1)} %copy-done.3, bf16[32,4096]{1,0:T(8,128)(2,1)} %copy-done.2, bf16[4096,1536]{1,0:T(8,128)(2,1)} %gate_w_ref.1, bf16[4096,1536]{1,0:T(8,128)(2,1)} %up_w_ref.1, ...), custom_call_target="tpu_custom_call" | custom-call | flops 2013265920 | bytes 38797312 | tf_op jit(solution)/shard_map/pallas_call | solution.py:190
  47.4 1.1 %convert_element_type.37 = bf16[32,4096]{1,0:T(8,128)(2,1)S(1)} convert(f32[32,4096]{1,0:T(8,128)} %get-tuple-element.11) | non-fusion elementwise | flops 131072 | bytes 786432 | tf_op jit(solution)/shard_map/convert_element_type | solution.py:305
  48.5 2.5 %collective-permute-start.4 = (bf16[8,4096]{1,0:T(8,128)(2,1)S(1)}, bf16[8,4096]{1,0:T(8,128)(2,1)S(1)}, u32[]{:S(2)}, u32[]{:S(2)}) collective-permute-start(bf16[8,4096]{1,0:T(8,128)(2,1)S(1)} %get-tuple-element.46), channel_id=1, source_target_pairs={{0,6},{2,0},{4,2},{6,4},{1,7},{3,1},{5,3},{7,5},{8,14},{10,8},{12,... | collective-permute-start | bytes 196616 | tf_op jit(solution)/shard_map/ppermute | solution.py:50
  50.9 1.5 %collective-permute-start.5 = (bf16[8,4096]{1,0:T(8,128)(2,1)S(1)}, bf16[8,4096]{1,0:T(8,128)(2,1)S(1)}, u32[]{:S(2)}, u32[]{:S(2)}) collective-permute-start(bf16[8,4096]{1,0:T(8,128)(2,1)S(1)} %get-tuple-element.48), channel_id=1, source_target_pairs={{0,4},{2,6},{4,0},{6,2},{1,5},{3,7},{5,1},{7,3},{8,12},{10,14},{12... | collective-permute-start | bytes 196616 | tf_op jit(solution)/shard_map/ppermute | solution.py:50
  52.4 1.0 %maximum_bitcast_fusion = bf16[1,96,1536]{2,1,0:T(8,128)(2,1)S(1)} fusion(bf16[32,1536]{1,0:T(8,128)(2,1)} %get-tuple-element.14, bf16[32,1536]{1,0:T(8,128)(2,1)} %get-tuple-element.13, bf16[32,1536]{1,0:T(8,128)(2,1)} %get-tuple-element.12), kind=kLoop, calls=%fused_computation.9 | loop fusion | flops 884736 | bytes 589824 | tf_op jit(solution)/shard_map/stack | solution.py:137
  53.4 0.8 %collective-permute-start.10 = (bf16[1,96,1536]{2,1,0:T(8,128)(2,1)S(1)}, bf16[1,96,1536]{2,1,0:T(8,128)(2,1)S(1)}, u32[]{:S(2)}, u32[]{:S(2)}) collective-permute-start(bf16[1,96,1536]{2,1,0:T(8,128)(2,1)S(1)} %maximum_bitcast_fusion), channel_id=1, source_target_pairs={{0,16},{8,24},{16,0},{24,8},{1,17},{9,25},{17,1},{25,9},{2,18},{10... | collective-permute-start | bytes 884744 | tf_op jit(solution)/shard_map/ppermute | solution.py:54
  54.2 2.6 %collective-permute-done.5 = bf16[8,4096]{1,0:T(8,128)(2,1)S(1)} collective-permute-done((bf16[8,4096]{1,0:T(8,128)(2,1)S(1)}, bf16[8,4096]{1,0:T(8,128)(2,1)S(1)}, u32[]{:S(2)}, u32[]{:S(2)}) %collective-permute-start.5) | collective-permute-done | bytes 65568 | tf_op jit(solution)/shard_map/ppermute | solution.py:50
  56.8 1.6 %collective-permute-done.6 = bf16[8,4096]{1,0:T(8,128)(2,1)S(1)} collective-permute-done((bf16[8,4096]{1,0:T(8,128)(2,1)S(1)}, bf16[8,4096]{1,0:T(8,128)(2,1)S(1)}, u32[]{:S(2)}, u32[]{:S(2)}) %collective-permute-start.6) | collective-permute-done | bytes 65568 | tf_op jit(solution)/shard_map/ppermute | solution.py:50
  58.5 1.6 %collective-permute-start.7 = (bf16[8,4096]{1,0:T(8,128)(2,1)S(1)}, bf16[8,4096]{1,0:T(8,128)(2,1)S(1)}, u32[]{:S(2)}, u32[]{:S(2)}) collective-permute-start(bf16[8,4096]{1,0:T(8,128)(2,1)S(1)} %fusion.13), channel_id=1, source_target_pairs={{0,1},{1,0},{2,3},{3,2},{4,5},{5,4},{6,7},{7,6},{8,9},{9,8},{10,11... | collective-permute-start | bytes 196616 | tf_op jit(solution)/shard_map/ppermute | solution.py:50
  60.1 2.8 %collective-permute-done.7 = bf16[8,4096]{1,0:T(8,128)(2,1)S(1)} collective-permute-done((bf16[8,4096]{1,0:T(8,128)(2,1)S(1)}, bf16[8,4096]{1,0:T(8,128)(2,1)S(1)}, u32[]{:S(2)}, u32[]{:S(2)}) %collective-permute-start.7) | collective-permute-done | bytes 65568 | tf_op jit(solution)/shard_map/ppermute | solution.py:50
  62.8 0.2 multiply_reduce_fusion
  63.0 1.5 %convolution_convert_fusion = bf16[128,4096]{1,0:T(8,128)(2,1)} fusion(f32[8,4096]{1,0:T(8,128)S(1)} %get-tuple-element.50, bf16[8,4096]{1,0:T(8,128)(2,1)S(1)} %collective-permute-done.7, f32[8]{0:T(128)S(1)} %multiply_multiply_fusion, f32[4096]{0:T(1024)S(1)} %copy-done.8, f32[8]{0:T(128)S(1)} %fusion.9, pred[8,256]{1,0:T(8,128)(4,1)S(1)} %fusion.6, ...), kind=kOutput, calls=%fused_computation | convolution fusion | flops 9404416 | bytes 1525764 | tf_op jit(solution)/shard_map/dot_general | solution.py:23
  64.7 0.6 collective-permute-start.11
  65.3 0.8 %collective-permute-done.9 = bf16[2,64,1024]{2,1,0:T(8,128)(2,1)S(1)} collective-permute-done((bf16[2,64,1024]{2,1,0:T(8,128)(2,1)S(1)}, bf16[2,64,1024]{2,1,0:T(8,128)(2,1)S(1)}, u32[]{:S(2)}, u32[]{:S(2)}) %collective-permute-start.9) | collective-permute-done | bytes 262176 | tf_op jit(solution)/shard_map/ppermute | solution.py:54
  66.2 0.8 %collective-permute-done.11 = bf16[2,96,1536]{2,1,0:T(8,128)(2,1)S(1)} collective-permute-done((bf16[2,96,1536]{2,1,0:T(8,128)(2,1)S(1)}, bf16[2,96,1536]{2,1,0:T(8,128)(2,1)S(1)}, u32[]{:S(2)}, u32[]{:S(2)}) %collective-permute-start.11) | collective-permute-done | bytes 589856 | tf_op jit(solution)/shard_map/ppermute | solution.py:54
  67.1 7.2 %shard_map.103 = (f32[1024,1536]{1,0:T(8,128)}, f32[1024,1536]{1,0:T(8,128)}, f32[1536,1024]{1,0:T(8,128)}) custom-call(bf16[128,1024]{1,0:T(8,128)(2,1)S(1)} %pad_maximum_fusion.9.normed_ref, bf16[128,1536]{1,0:T(8,128)(2,1)S(1)} %get-tuple-element.51.gate_ref, bf16[128,1536]{1,0:T(8,128)(2,1)S(1)} %get-tuple-element.52.up_ref, ...), custom_call_target="tpu_custom_call" | custom-call | flops 1207959552 | bytes 20578304 | tf_op jit(solution)/shard_map/pallas_call | solution.py:234
  (51 shorter events, 1.4 us)
Async XLA Ops:
  0.6 1.6 %copy-start = (bf16[256,4096]{1,0:T(8,128)(2,1)S(1)}, bf16[256,4096]{1,0:T(8,128)(2,1)}, u32[]{:S(2)}) copy-start(bf16[256,4096]{1,0:T(8,128)(2,1)} %param.7) | copy-start | bytes 6291460
  0.6 2.1 %copy-start.8 = (f32[4096]{0:T(1024)S(1)}, f32[4096]{0:T(1024)}, u32[]{:S(2)}) copy-start(f32[4096]{0:T(1024)} %param.9) | copy-start | bytes 49156
  1.9 1.7 %copy-start.4 = (bf16[256,4096]{1,0:T(8,128)(2,1)S(1)}, bf16[256,4096]{1,0:T(8,128)(2,1)}, u32[]{:S(2)}) copy-start(bf16[256,4096]{1,0:T(8,128)(2,1)} %param.8) | copy-start | bytes 6291460
  4.0 7.6 %collective-permute-start = (bf16[8,4096]{1,0:T(8,128)(2,1)S(1)}, bf16[8,4096]{1,0:T(8,128)(2,1)S(1)}, u32[]{:S(2)}, u32[]{:S(2)}) collective-permute-start(bf16[8,4096]{1,0:T(8,128)(2,1)S(1)} %fusion), channel_id=1, source_target_pairs={{0,2},{2,4},{4,6},{6,0},{1,3},{3,5},{5,7},{7,1},{8,10},{10,12},{12... | collective-permute-start | bytes 196616 | tf_op jit(solution)/shard_map/ppermute | solution.py:50
  7.0 7.1 %collective-permute-start.1 = (bf16[8,4096]{1,0:T(8,128)(2,1)S(1)}, bf16[8,4096]{1,0:T(8,128)(2,1)S(1)}, u32[]{:S(2)}, u32[]{:S(2)}) collective-permute-start(bf16[8,4096]{1,0:T(8,128)(2,1)S(1)} %fusion), channel_id=1, source_target_pairs={{0,4},{2,6},{4,0},{6,2},{1,5},{3,7},{5,1},{7,3},{8,12},{10,14},{12... | collective-permute-start | bytes 196616 | tf_op jit(solution)/shard_map/ppermute | solution.py:50
  9.6 4.7 %collective-permute-start.2 = (bf16[8,4096]{1,0:T(8,128)(2,1)S(1)}, bf16[8,4096]{1,0:T(8,128)(2,1)S(1)}, u32[]{:S(2)}, u32[]{:S(2)}) collective-permute-start(bf16[8,4096]{1,0:T(8,128)(2,1)S(1)} %fusion), channel_id=1, source_target_pairs={{0,6},{2,0},{4,2},{6,4},{1,7},{3,1},{5,3},{7,5},{8,14},{10,8},{12,... | collective-permute-start | bytes 196616 | tf_op jit(solution)/shard_map/ppermute | solution.py:50
  14.3 7.9 %collective-permute-start.3 = (bf16[32,4096]{1,0:T(8,128)(2,1)S(1)}, bf16[32,4096]{1,0:T(8,128)(2,1)S(1)}, u32[]{:S(2)}, u32[]{:S(2)}) collective-permute-start(bf16[32,4096]{1,0:T(8,128)(2,1)S(1)} %pad_maximum_fusion.6), channel_id=1, source_target_pairs={{0,1},{1,0},{2,3},{3,2},{4,5},{5,4},{6,7},{7,6},{8,9},{9,8},{10,11... | collective-permute-start | bytes 786440 | tf_op jit(solution)/shard_map/ppermute | solution.py:285
  22.3 1.2 %copy-start.2 = (bf16[32,4096]{1,0:T(8,128)(2,1)}, bf16[32,4096]{1,0:T(8,128)(2,1)S(1)}, u32[]{:S(2)}) copy-start(bf16[32,4096]{1,0:T(8,128)(2,1)S(1)} %get-tuple-element.35.masked_ref) | copy-start | bytes 786436
  22.3 1.2 %copy-start.3 = (bf16[32,4096]{1,0:T(8,128)(2,1)}, bf16[32,4096]{1,0:T(8,128)(2,1)S(1)}, u32[]{:S(2)}) copy-start(bf16[32,4096]{1,0:T(8,128)(2,1)S(1)} %get-tuple-element.36.normed_ref) | copy-start | bytes 786436
  23.9 40.6 %collective-permute-start.8 = (bf16[2,64,1024]{2,1,0:T(8,128)(2,1)S(1)}, bf16[2,64,1024]{2,1,0:T(8,128)(2,1)S(1)}, u32[]{:S(2)}, u32[]{:S(2)}) collective-permute-start(bf16[2,64,1024]{2,1,0:T(8,128)(2,1)S(1)} %pad_maximum_fusion.7), channel_id=1, source_target_pairs={{0,16},{8,24},{16,0},{24,8},{1,17},{9,25},{17,1},{25,9},{2,18},{10... | collective-permute-start | bytes 786440 | tf_op jit(solution)/shard_map/ppermute | solution.py:54
  48.5 5.8 %collective-permute-start.4 = (bf16[8,4096]{1,0:T(8,128)(2,1)S(1)}, bf16[8,4096]{1,0:T(8,128)(2,1)S(1)}, u32[]{:S(2)}, u32[]{:S(2)}) collective-permute-start(bf16[8,4096]{1,0:T(8,128)(2,1)S(1)} %get-tuple-element.46), channel_id=1, source_target_pairs={{0,6},{2,0},{4,2},{6,4},{1,7},{3,1},{5,3},{7,5},{8,14},{10,8},{12,... | collective-permute-start | bytes 196616 | tf_op jit(solution)/shard_map/ppermute | solution.py:50
  50.9 5.9 %collective-permute-start.5 = (bf16[8,4096]{1,0:T(8,128)(2,1)S(1)}, bf16[8,4096]{1,0:T(8,128)(2,1)S(1)}, u32[]{:S(2)}, u32[]{:S(2)}) collective-permute-start(bf16[8,4096]{1,0:T(8,128)(2,1)S(1)} %get-tuple-element.48), channel_id=1, source_target_pairs={{0,4},{2,6},{4,0},{6,2},{1,5},{3,7},{5,1},{7,3},{8,12},{10,14},{12... | collective-permute-start | bytes 196616 | tf_op jit(solution)/shard_map/ppermute | solution.py:50
  52.4 6.1 %collective-permute-start.6 = (bf16[8,4096]{1,0:T(8,128)(2,1)S(1)}, bf16[8,4096]{1,0:T(8,128)(2,1)S(1)}, u32[]{:S(2)}, u32[]{:S(2)}) collective-permute-start(bf16[8,4096]{1,0:T(8,128)(2,1)S(1)} %get-tuple-element.47), channel_id=1, source_target_pairs={{0,2},{2,4},{4,6},{6,0},{1,3},{3,5},{5,7},{7,1},{8,10},{10,12},{12... | collective-permute-start | bytes 196616 | tf_op jit(solution)/shard_map/ppermute | solution.py:50
  53.4 11.2 %collective-permute-start.10 = (bf16[1,96,1536]{2,1,0:T(8,128)(2,1)S(1)}, bf16[1,96,1536]{2,1,0:T(8,128)(2,1)S(1)}, u32[]{:S(2)}, u32[]{:S(2)}) collective-permute-start(bf16[1,96,1536]{2,1,0:T(8,128)(2,1)S(1)} %maximum_bitcast_fusion), channel_id=1, source_target_pairs={{0,16},{8,24},{16,0},{24,8},{1,17},{9,25},{17,1},{25,9},{2,18},{10... | collective-permute-start | bytes 884744 | tf_op jit(solution)/shard_map/ppermute | solution.py:54
  58.5 4.3 %collective-permute-start.7 = (bf16[8,4096]{1,0:T(8,128)(2,1)S(1)}, bf16[8,4096]{1,0:T(8,128)(2,1)S(1)}, u32[]{:S(2)}, u32[]{:S(2)}) collective-permute-start(bf16[8,4096]{1,0:T(8,128)(2,1)S(1)} %fusion.13), channel_id=1, source_target_pairs={{0,1},{1,0},{2,3},{3,2},{4,5},{5,4},{6,7},{7,6},{8,9},{9,8},{10,11... | collective-permute-start | bytes 196616 | tf_op jit(solution)/shard_map/ppermute | solution.py:50
  64.5 1.6 %collective-permute-start.9 = (bf16[2,64,1024]{2,1,0:T(8,128)(2,1)S(1)}, bf16[2,64,1024]{2,1,0:T(8,128)(2,1)S(1)}, u32[]{:S(2)}, u32[]{:S(2)}) collective-permute-start(bf16[2,64,1024]{2,1,0:T(8,128)(2,1)S(1)} %pad_maximum_fusion.8), channel_id=1, source_target_pairs={{0,8},{8,0},{16,24},{24,16},{1,9},{9,1},{17,25},{25,17},{2,10},{10... | collective-permute-start | bytes 786440 | tf_op jit(solution)/shard_map/ppermute | solution.py:54
  64.6 2.4 %copy-start.7 = (bf16[32,1536]{1,0:T(8,128)(2,1)S(1)}, bf16[32,1536]{1,0:T(8,128)(2,1)}, u32[]{:S(2)}) copy-start(bf16[32,1536]{1,0:T(8,128)(2,1)} %get-tuple-element.14) | copy-start | bytes 294916
  64.7 2.4 %copy-start.5 = (bf16[32,1536]{1,0:T(8,128)(2,1)S(1)}, bf16[32,1536]{1,0:T(8,128)(2,1)}, u32[]{:S(2)}) copy-start(bf16[32,1536]{1,0:T(8,128)(2,1)} %get-tuple-element.12) | copy-start | bytes 294916
  64.7 2.4 %copy-start.6 = (bf16[32,1536]{1,0:T(8,128)(2,1)S(1)}, bf16[32,1536]{1,0:T(8,128)(2,1)}, u32[]{:S(2)}) copy-start(bf16[32,1536]{1,0:T(8,128)(2,1)} %get-tuple-element.13) | copy-start | bytes 294916
  64.7 2.2 %collective-permute-start.11 = (bf16[2,96,1536]{2,1,0:T(8,128)(2,1)S(1)}, bf16[2,96,1536]{2,1,0:T(8,128)(2,1)S(1)}, u32[]{:S(2)}, u32[]{:S(2)}) collective-permute-start(bf16[2,96,1536]{2,1,0:T(8,128)(2,1)S(1)} %pad_maximum_fusion), channel_id=1, source_target_pairs={{0,8},{8,0},{16,24},{24,16},{1,9},{9,1},{17,25},{25,17},{2,10},{10... | collective-permute-start | bytes 1769480 | tf_op jit(solution)/shard_map/ppermute | solution.py:54
  67.1 7.2 %copy-start.1 = (bf16[256,4096]{1,0:T(8,128)(2,1)S(1)}, bf16[256,4096]{1,0:T(8,128)(2,1)}, u32[]{:S(2)}) copy-start(bf16[256,4096]{1,0:T(8,128)(2,1)} %param.7) | copy-start | bytes 6291460

commit v14 on v11

--- a/solution.py
+++ b/solution.py
@@ -125,7 +125,7 @@
     return out
 
 
-def rep_exchange(factors, column_blocks, axis, size):
+def rep_exchange(factors, column_blocks, axis, size, tied):
     index = lax.axis_index(axis)
     stacked = jnp.stack(column_blocks)
     if power_of_two(size):
@@ -142,15 +142,17 @@
             held = {key: v for key, v in held.items() if not key[1] & distance}
             for position, (origin, target) in enumerate(leaving):
                 held[(origin ^ distance, target ^ distance)] = arrived[position]
+            if distance == size // 2:
+                gathered, held, tied = lax.optimization_barrier((gathered, held, tied))
             distance //= 2
-        return [gathered[o] for o in range(size)], [held[(o, 0)] for o in range(size)]
+        return [gathered[o] for o in range(size)], [held[(o, 0)] for o in range(size)], tied
     every_factors = [factors]
     every_columns = [lax.dynamic_index_in_dim(stacked, index, 0, keepdims=False)]
     for k in range(1, size):
         every_factors.append(shifted(factors, axis, (size,), (k,)))
         outgoing = lax.dynamic_index_in_dim(stacked, (index + k) % size, 0, keepdims=False)
         every_columns.append(shifted(outgoing, axis, (size,), (k,)))
-    return every_factors, every_columns
+    return every_factors, every_columns, tied
 
 
 def weight_pass_kernel(normed_ref, masked_ref, gate_w_ref, up_w_ref, down_w_ref,
@@ -287,11 +289,12 @@
     )
     columns = jnp.concatenate([window_normed, window_masked], axis=0)
     columns = columns.reshape(2 * window, replicas, feature_share)
-    every_factors, every_columns = rep_exchange(
+    every_factors, every_columns, partial_features = rep_exchange(
         jnp.concatenate([gate_rows, up_rows, hidden], axis=0),
         [columns[:, b] for b in range(replicas)],
         "rep",
         replicas,
+        partial_features,
     )
     partial_features = partial_features.astype(jnp.bfloat16)
     feature_grad = partial_features[:MAXACT].astype(jnp.float32)

time: 73.3 us -> 81.8 us (1.12)
  waiting for transfers between devices: 16.1 us -> 24.6 us
  local copies, waits for them, and re-layouts: 2.73 us -> 5.52 us
  other arithmetic: 4.79 us -> 2.74 us
    ppermute x4, waiting for transfers between devices: 1.59 us -> 8.01 us  [swapped(): return lax.ppermute(value, axis, [(i, i ^ distance) for i in range(size)])]
    ppermute x7, waiting for transfers between devices: 14.5 us -> 16.6 us  [shifted(): return lax.ppermute(value, axes, pairs)]
    unnamed x20 -> x18, local copies, waits for them, and re-layouts: 1.06 us -> 2.91 us
    convert_element_type x1, other arithmetic: 1.07 us -> 0.03 us  [local(): partial_features = partial_features.astype(jnp.bfloat16)]
    another operation x2 -> x1, other arithmetic: 1.06 us -> 0.06 us  [rep_exchange(): jnp.stack([gathered[o] for o in origins])]
    concatenate x0 -> x1, local copies, waits for them, and re-layouts: none -> 0.9 us  [local(): jnp.concatenate([gate_rows, up_rows, hidden], axis=0)]
  transfers between devices with their start and end apart: 11 -> 11, of which waited for: 6 -> 6; matrix products, arithmetic and copies ran while one was open for 7% -> 7% of each run, Pallas kernels for 31% -> 28%
where the time goes in v14:
time: 81.8 us; the launch traced here: 81.6 us
  Pallas kernels  29.8 us (36%)
  waiting for transfers between devices  24.6 us (30%)
  starting transfers between devices  15.7 us (19%)
  local copies, waits for them, and re-layouts  5.52 us (7%)
  other arithmetic  2.74 us (3%)
  matrix products  2.34 us (3%)
  between operations  0.95 us (1%)
    pallas_call x1, Pallas kernels, weight_pass(): pl.pallas_call(weight_pass_kernel, grid=(units // chunk,), in_specs=[pl.B...  22.6 us
    ppermute x7, waiting for transfers between devices, shifted(): return lax.ppermute(value, axes, pairs)  16.6 us
    ppermute x7, starting transfers between devices, shifted(): return lax.ppermute(value, axes, pairs)  13.4 us
    ppermute x4, waiting for transfers between devices, swapped(): return lax.ppermute(value, axis, [(i, i ^ distance) for i in range(size)])  8.01 us
    pallas_call x1, Pallas kernels, weight_grads(): pl.pallas_call(grads_kernel, grid=(steps,), in_specs=[pl.BlockSpec((rows,...  7.15 us
    unnamed x18, local copies, waits for them, and re-layouts  2.91 us
    ppermute x4, starting transfers between devices, swapped(): return lax.ppermute(value, axis, [(i, i ^ distance) for i in range(size)])  2.23 us
  transfers between devices with their start and end apart: 11, of which 6 were waited for; matrix products, arithmetic and copies ran while one was open for 7% of the time, Pallas kernels for 28%

profile of v14, /device:TPU:0, one launch (start us, length us, event | category | flops | bytes accessed | tf_op | source)
XLA Modules:
  0.0 81.6 jit_solution(8007600624045837730)
XLA Ops:
  0.6 0.8 %convert_bitcast_fusion = (s32[2,128]{1,0:T(2,128)S(1)}, pred[256]{0:T(512)(128)(4,1)S(1)}) fusion(s32[256]{0:T(256)} %param.13), kind=kLoop, calls=%fused_computation.59 | loop fusion | flops 512 | bytes 2304 | tf_op jit(solution)/shard_map/convert
  1.5 0.3 reduce-window.9
  1.9 0.1 slice_reduce_fusion
  2.1 0.2 copy-done
  2.2 0.5 multiply_reduce_fusion.1
  2.8 0.8 %copy-done.2 = bf16[256,4096]{1,0:T(8,128)(2,1)S(1)} copy-done((bf16[256,4096]{1,0:T(8,128)(2,1)S(1)}, bf16[256,4096]{1,0:T(8,128)(2,1)}, u32[]{:S(2)}) %copy-start.2) | copy-done | bytes 2097176
  3.6 0.4 convolution_convert_fusion.1
  4.0 0.1 constant_dynamic-update-slice_fusion.10
  4.1 3.1 %collective-permute-start = (bf16[16,4096]{1,0:T(8,128)(2,1)S(1)}, bf16[16,4096]{1,0:T(8,128)(2,1)S(1)}, u32[]{:S(2)}, u32[]{:S(2)}) collective-permute-start(bf16[16,4096]{1,0:T(8,128)(2,1)S(1)} %pad_maximum_fusion.11), channel_id=1, source_target_pairs={{0,2},{2,4},{4,6},{6,0},{1,3},{3,5},{5,7},{7,1},{8,10},{10,12},{12... | collective-permute-start | bytes 393224 | tf_op jit(solution)/shard_map/ppermute | solution.py:50
  7.2 2.6 %collective-permute-start.1 = (bf16[16,4096]{1,0:T(8,128)(2,1)S(1)}, bf16[16,4096]{1,0:T(8,128)(2,1)S(1)}, u32[]{:S(2)}, u32[]{:S(2)}) collective-permute-start(bf16[16,4096]{1,0:T(8,128)(2,1)S(1)} %pad_maximum_fusion.11), channel_id=1, source_target_pairs={{0,4},{2,6},{4,0},{6,2},{1,5},{3,7},{5,1},{7,3},{8,12},{10,14},{12... | collective-permute-start | bytes 393224 | tf_op jit(solution)/shard_map/ppermute | solution.py:50
  9.7 1.3 %collective-permute-start.2 = (bf16[16,4096]{1,0:T(8,128)(2,1)S(1)}, bf16[16,4096]{1,0:T(8,128)(2,1)S(1)}, u32[]{:S(2)}, u32[]{:S(2)}) collective-permute-start(bf16[16,4096]{1,0:T(8,128)(2,1)S(1)} %pad_maximum_fusion.11), channel_id=1, source_target_pairs={{0,6},{2,0},{4,2},{6,4},{1,7},{3,1},{5,3},{7,5},{8,14},{10,8},{12,... | collective-permute-start | bytes 393224 | tf_op jit(solution)/shard_map/ppermute | solution.py:50
  11.1 2.5 %collective-permute-done = bf16[16,4096]{1,0:T(8,128)(2,1)S(1)} collective-permute-done((bf16[16,4096]{1,0:T(8,128)(2,1)S(1)}, bf16[16,4096]{1,0:T(8,128)(2,1)S(1)}, u32[]{:S(2)}, u32[]{:S(2)}) %collective-permute-start) | collective-permute-done | bytes 131104 | tf_op jit(solution)/shard_map/ppermute | solution.py:50
  13.6 4.8 %collective-permute-done.1 = bf16[16,4096]{1,0:T(8,128)(2,1)S(1)} collective-permute-done((bf16[16,4096]{1,0:T(8,128)(2,1)S(1)}, bf16[16,4096]{1,0:T(8,128)(2,1)S(1)}, u32[]{:S(2)}, u32[]{:S(2)}) %collective-permute-start.1) | collective-permute-done | bytes 131104 | tf_op jit(solution)/shard_map/ppermute | solution.py:50
  18.5 0.4 reshape.68
  18.9 0.8 fusion.13
  20.0 1.6 %collective-permute-start.4 = (bf16[2,64,1024]{2,1,0:T(8,128)(2,1)S(1)}, bf16[2,64,1024]{2,1,0:T(8,128)(2,1)S(1)}, u32[]{:S(2)}, u32[]{:S(2)}) collective-permute-start(bf16[2,64,1024]{2,1,0:T(8,128)(2,1)S(1)} %pad_maximum_fusion.7), channel_id=1, source_target_pairs={{0,16},{8,24},{16,0},{24,8},{1,17},{9,25},{17,1},{25,9},{2,18},{10... | collective-permute-start | bytes 786440 | tf_op jit(solution)/shard_map/ppermute | solution.py:54
  21.6 0.8 %pad_maximum_fusion.5 = (bf16[32,4096]{1,0:T(8,128)(2,1)}, bf16[32,4096]{1,0:T(8,128)(2,1)}) fusion(bf16[8,4096]{1,0:T(8,128)(2,1)S(1)} %get-tuple-element.71, bf16[8,4096]{1,0:T(8,128)(2,1)S(1)} %get-tuple-element.74, bf16[8,4096]{1,0:T(8,128)(2,1)S(1)} %get-tuple-element.77, bf16[8,4096]{1,0:T(8,128)(2,1)S(1)} %get-tuple-element.33, ...), kind=kLoop, calls=%fused_computation.7 | loop fusion | flops 2097152 | bytes 1048576 | tf_op jit(solution)/shard_map/concatenate | solution.py:284
  22.4 22.6 %shard_map.102 = (bf16[32,1536]{1,0:T(8,128)(2,1)}, bf16[32,1536]{1,0:T(8,128)(2,1)}, bf16[32,1536]{1,0:T(8,128)(2,1)}, f32[32,4096]{1,0:T(8,128)}) custom-call(bf16[32,4096]{1,0:T(8,128)(2,1)} %get-tuple-element.80.normed_ref, bf16[32,4096]{1,0:T(8,128)(2,1)} %get-tuple-element.81.masked_ref, bf16[4096,1536]{1,0:T(8,128)(2,1)} %gate_w_ref.1, ...), custom_call_target="tpu_custom_call" | custom-call | flops 2013265920 | bytes 38797312 | tf_op jit(solution)/shard_map/pallas_call | solution.py:192
  45.0 1.0 %constant_dynamic-update-slice_fusion.2 = bf16[96,1536]{1,0:T(8,128)(2,1)S(1)} fusion(bf16[32,1536]{1,0:T(8,128)(2,1)} %get-tuple-element.18), kind=kLoop, calls=%fused_computation.44 | loop fusion | bytes 196608
  46.0 0.9 %constant_dynamic-update-slice_fusion.1 = bf16[96,1536]{1,0:T(8,128)(2,1)S(1)} fusion(bf16[96,1536]{1,0:T(8,128)(2,1)S(1)} %constant_dynamic-update-slice_fusion.2, bf16[32,1536]{1,0:T(8,128)(2,1)} %get-tuple-element.19), kind=kLoop, calls=%fused_computation.43 | loop fusion | bytes 196608
  46.9 0.9 %constant_dynamic-update-slice_fusion = bf16[96,1536]{1,0:T(8,128)(2,1)S(1)} fusion(bf16[96,1536]{1,0:T(8,128)(2,1)S(1)} %constant_dynamic-update-slice_fusion.1, bf16[32,1536]{1,0:T(8,128)(2,1)} %get-tuple-element.20), kind=kLoop, calls=%fused_computation.42 | loop fusion | bytes 196608 | tf_op jit(solution)/shard_map/concatenate | solution.py:293
  47.8 0.5 collective-permute-start.3
  48.4 8.0 %collective-permute-done.3 = bf16[1,96,1536]{2,1,0:T(8,128)(2,1)S(1)} collective-permute-done((bf16[1,96,1536]{2,1,0:T(8,128)(2,1)S(1)}, bf16[1,96,1536]{2,1,0:T(8,128)(2,1)S(1)}, u32[]{:S(2)}, u32[]{:S(2)}) %collective-permute-start.3) | collective-permute-done | bytes 294944 | tf_op jit(solution)/shard_map/ppermute | solution.py:54
  56.6 3.4 %collective-permute-start.5 = (bf16[8,4096]{1,0:T(8,128)(2,1)S(1)}, bf16[8,4096]{1,0:T(8,128)(2,1)S(1)}, u32[]{:S(2)}, u32[]{:S(2)}) collective-permute-start(bf16[8,4096]{1,0:T(8,128)(2,1)S(1)} %get-tuple-element.60), channel_id=1, source_target_pairs={{0,6},{2,0},{4,2},{6,4},{1,7},{3,1},{5,3},{7,5},{8,14},{10,8},{12,... | collective-permute-start | bytes 196616 | tf_op jit(solution)/shard_map/ppermute | solution.py:50
  60.0 1.4 %collective-permute-start.6 = (bf16[8,4096]{1,0:T(8,128)(2,1)S(1)}, bf16[8,4096]{1,0:T(8,128)(2,1)S(1)}, u32[]{:S(2)}, u32[]{:S(2)}) collective-permute-start(bf16[8,4096]{1,0:T(8,128)(2,1)S(1)} %get-tuple-element.62), channel_id=1, source_target_pairs={{0,4},{2,6},{4,0},{6,2},{1,5},{3,7},{5,1},{7,3},{8,12},{10,14},{12... | collective-permute-start | bytes 196616 | tf_op jit(solution)/shard_map/ppermute | solution.py:50
  61.5 1.2 %collective-permute-done.5 = bf16[8,4096]{1,0:T(8,128)(2,1)S(1)} collective-permute-done((bf16[8,4096]{1,0:T(8,128)(2,1)S(1)}, bf16[8,4096]{1,0:T(8,128)(2,1)S(1)}, u32[]{:S(2)}, u32[]{:S(2)}) %collective-permute-start.5) | collective-permute-done | bytes 65568 | tf_op jit(solution)/shard_map/ppermute | solution.py:50
  62.7 5.4 %collective-permute-done.6 = bf16[8,4096]{1,0:T(8,128)(2,1)S(1)} collective-permute-done((bf16[8,4096]{1,0:T(8,128)(2,1)S(1)}, bf16[8,4096]{1,0:T(8,128)(2,1)S(1)}, u32[]{:S(2)}, u32[]{:S(2)}) %collective-permute-start.6) | collective-permute-done | bytes 65568 | tf_op jit(solution)/shard_map/ppermute | solution.py:50
  68.2 1.6 %collective-permute-start.8 = (bf16[8,4096]{1,0:T(8,128)(2,1)S(1)}, bf16[8,4096]{1,0:T(8,128)(2,1)S(1)}, u32[]{:S(2)}, u32[]{:S(2)}) collective-permute-start(bf16[8,4096]{1,0:T(8,128)(2,1)S(1)} %fusion.12), channel_id=1, source_target_pairs={{0,1},{1,0},{2,3},{3,2},{4,5},{5,4},{6,7},{7,6},{8,9},{9,8},{10,11... | collective-permute-start | bytes 196616 | tf_op jit(solution)/shard_map/ppermute | solution.py:50
  69.8 2.7 %collective-permute-done.8 = bf16[8,4096]{1,0:T(8,128)(2,1)S(1)} collective-permute-done((bf16[8,4096]{1,0:T(8,128)(2,1)S(1)}, bf16[8,4096]{1,0:T(8,128)(2,1)S(1)}, u32[]{:S(2)}, u32[]{:S(2)}) %collective-permute-start.8) | collective-permute-done | bytes 65568 | tf_op jit(solution)/shard_map/ppermute | solution.py:50
  72.5 0.2 multiply_reduce_fusion
  72.7 1.5 %convolution_convert_fusion = bf16[128,4096]{1,0:T(8,128)(2,1)} fusion(f32[8,4096]{1,0:T(8,128)S(1)} %get-tuple-element.79, bf16[8,4096]{1,0:T(8,128)(2,1)S(1)} %collective-permute-done.8, f32[8]{0:T(128)S(1)} %multiply_multiply_fusion, f32[4096]{0:T(1024)S(1)} %copy-done.4, f32[8]{0:T(128)S(1)} %fusion.8, pred[8,256]{1,0:T(8,128)(4,1)S(1)} %fusion.5, ...), kind=kOutput, calls=%fused_computation | convolution fusion | flops 9404416 | bytes 1525764 | tf_op jit(solution)/shard_map/dot_general | solution.py:23
  74.4 7.2 %shard_map.103 = (f32[1024,1536]{1,0:T(8,128)}, f32[1024,1536]{1,0:T(8,128)}, f32[1536,1024]{1,0:T(8,128)}) custom-call(bf16[128,1024]{1,0:T(8,128)(2,1)S(1)} %pad_maximum_fusion.9.normed_ref, bf16[128,1536]{1,0:T(8,128)(2,1)S(1)} %pad_maximum_fusion.2.gate_ref, bf16[128,1536]{1,0:T(8,128)(2,1)S(1)} %pad_maximum_fusion.3.up_ref, ...), custom_call_target="tpu_custom_call" | custom-call | flops 1207959552 | bytes 20578304 | tf_op jit(solution)/shard_map/pallas_call | solution.py:236
  (52 shorter events, 1.2 us)
Async XLA Ops:
  0.6 1.6 %copy-start = (bf16[256,4096]{1,0:T(8,128)(2,1)S(1)}, bf16[256,4096]{1,0:T(8,128)(2,1)}, u32[]{:S(2)}) copy-start(bf16[256,4096]{1,0:T(8,128)(2,1)} %param.7) | copy-start | bytes 6291460
  1.9 1.7 %copy-start.2 = (bf16[256,4096]{1,0:T(8,128)(2,1)S(1)}, bf16[256,4096]{1,0:T(8,128)(2,1)}, u32[]{:S(2)}) copy-start(bf16[256,4096]{1,0:T(8,128)(2,1)} %param.8) | copy-start | bytes 6291460
  2.2 1.7 %copy-start.4 = (f32[4096]{0:T(1024)S(1)}, f32[4096]{0:T(1024)}, u32[]{:S(2)}) copy-start(f32[4096]{0:T(1024)} %param.9) | copy-start | bytes 49156
  4.1 9.5 %collective-permute-start = (bf16[16,4096]{1,0:T(8,128)(2,1)S(1)}, bf16[16,4096]{1,0:T(8,128)(2,1)S(1)}, u32[]{:S(2)}, u32[]{:S(2)}) collective-permute-start(bf16[16,4096]{1,0:T(8,128)(2,1)S(1)} %pad_maximum_fusion.11), channel_id=1, source_target_pairs={{0,2},{2,4},{4,6},{6,0},{1,3},{3,5},{5,7},{7,1},{8,10},{10,12},{12... | collective-permute-start | bytes 393224 | tf_op jit(solution)/shard_map/ppermute | solution.py:50
  7.2 11.2 %collective-permute-start.1 = (bf16[16,4096]{1,0:T(8,128)(2,1)S(1)}, bf16[16,4096]{1,0:T(8,128)(2,1)S(1)}, u32[]{:S(2)}, u32[]{:S(2)}) collective-permute-start(bf16[16,4096]{1,0:T(8,128)(2,1)S(1)} %pad_maximum_fusion.11), channel_id=1, source_target_pairs={{0,4},{2,6},{4,0},{6,2},{1,5},{3,7},{5,1},{7,3},{8,12},{10,14},{12... | collective-permute-start | bytes 393224 | tf_op jit(solution)/shard_map/ppermute | solution.py:50
  9.7 8.7 %collective-permute-start.2 = (bf16[16,4096]{1,0:T(8,128)(2,1)S(1)}, bf16[16,4096]{1,0:T(8,128)(2,1)S(1)}, u32[]{:S(2)}, u32[]{:S(2)}) collective-permute-start(bf16[16,4096]{1,0:T(8,128)(2,1)S(1)} %pad_maximum_fusion.11), channel_id=1, source_target_pairs={{0,6},{2,0},{4,2},{6,4},{1,7},{3,1},{5,3},{7,5},{8,14},{10,8},{12,... | collective-permute-start | bytes 393224 | tf_op jit(solution)/shard_map/ppermute | solution.py:50
  20.0 28.3 %collective-permute-start.4 = (bf16[2,64,1024]{2,1,0:T(8,128)(2,1)S(1)}, bf16[2,64,1024]{2,1,0:T(8,128)(2,1)S(1)}, u32[]{:S(2)}, u32[]{:S(2)}) collective-permute-start(bf16[2,64,1024]{2,1,0:T(8,128)(2,1)S(1)} %pad_maximum_fusion.7), channel_id=1, source_target_pairs={{0,16},{8,24},{16,0},{24,8},{1,17},{9,25},{17,1},{25,9},{2,18},{10... | collective-permute-start | bytes 786440 | tf_op jit(solution)/shard_map/ppermute | solution.py:54
  45.0 11.5 %copy-start.3 = (f32[32,4096]{1,0:T(8,128)S(1)}, f32[32,4096]{1,0:T(8,128)}, u32[]{:S(2)}) copy-start(f32[32,4096]{1,0:T(8,128)} %get-tuple-element.22) | copy-start | bytes 1572868
  47.8 8.6 %collective-permute-start.3 = (bf16[1,96,1536]{2,1,0:T(8,128)(2,1)S(1)}, bf16[1,96,1536]{2,1,0:T(8,128)(2,1)S(1)}, u32[]{:S(2)}, u32[]{:S(2)}) collective-permute-start(bf16[1,96,1536]{2,1,0:T(8,128)(2,1)S(1)} %bitcast.48), channel_id=1, source_target_pairs={{0,16},{8,24},{16,0},{24,8},{1,17},{9,25},{17,1},{25,9},{2,18},{10... | collective-permute-start | bytes 884744 | tf_op jit(solution)/shard_map/ppermute | solution.py:54
  56.4 17.8 %collective-permute-start.9 = (bf16[2,64,1024]{2,1,0:T(8,128)(2,1)S(1)}, bf16[2,64,1024]{2,1,0:T(8,128)(2,1)S(1)}, u32[]{:S(2)}, u32[]{:S(2)}) collective-permute-start(bf16[2,64,1024]{2,1,0:T(8,128)(2,1)S(1)} %pad_maximum_fusion.8), channel_id=1, source_target_pairs={{0,8},{8,0},{16,24},{24,16},{1,9},{9,1},{17,25},{25,17},{2,10},{10... | collective-permute-start | bytes 786440 | tf_op jit(solution)/shard_map/ppermute | solution.py:54
  56.6 6.1 %collective-permute-start.5 = (bf16[8,4096]{1,0:T(8,128)(2,1)S(1)}, bf16[8,4096]{1,0:T(8,128)(2,1)S(1)}, u32[]{:S(2)}, u32[]{:S(2)}) collective-permute-start(bf16[8,4096]{1,0:T(8,128)(2,1)S(1)} %get-tuple-element.60), channel_id=1, source_target_pairs={{0,6},{2,0},{4,2},{6,4},{1,7},{3,1},{5,3},{7,5},{8,14},{10,8},{12,... | collective-permute-start | bytes 196616 | tf_op jit(solution)/shard_map/ppermute | solution.py:50
  60.0 8.1 %collective-permute-start.6 = (bf16[8,4096]{1,0:T(8,128)(2,1)S(1)}, bf16[8,4096]{1,0:T(8,128)(2,1)S(1)}, u32[]{:S(2)}, u32[]{:S(2)}) collective-permute-start(bf16[8,4096]{1,0:T(8,128)(2,1)S(1)} %get-tuple-element.62), channel_id=1, source_target_pairs={{0,4},{2,6},{4,0},{6,2},{1,5},{3,7},{5,1},{7,3},{8,12},{10,14},{12... | collective-permute-start | bytes 196616 | tf_op jit(solution)/shard_map/ppermute | solution.py:50
  61.5 6.7 %collective-permute-start.7 = (bf16[8,4096]{1,0:T(8,128)(2,1)S(1)}, bf16[8,4096]{1,0:T(8,128)(2,1)S(1)}, u32[]{:S(2)}, u32[]{:S(2)}) collective-permute-start(bf16[8,4096]{1,0:T(8,128)(2,1)S(1)} %get-tuple-element.61), channel_id=1, source_target_pairs={{0,2},{2,4},{4,6},{6,0},{1,3},{3,5},{5,7},{7,1},{8,10},{10,12},{12... | collective-permute-start | bytes 196616 | tf_op jit(solution)/shard_map/ppermute | solution.py:50
  68.2 4.3 %collective-permute-start.8 = (bf16[8,4096]{1,0:T(8,128)(2,1)S(1)}, bf16[8,4096]{1,0:T(8,128)(2,1)S(1)}, u32[]{:S(2)}, u32[]{:S(2)}) collective-permute-start(bf16[8,4096]{1,0:T(8,128)(2,1)S(1)} %fusion.12), channel_id=1, source_target_pairs={{0,1},{1,0},{2,3},{3,2},{4,5},{5,4},{6,7},{7,6},{8,9},{9,8},{10,11... | collective-permute-start | bytes 196616 | tf_op jit(solution)/shard_map/ppermute | solution.py:50
  69.7 4.5 %collective-permute-start.10 = (bf16[2,96,1536]{2,1,0:T(8,128)(2,1)S(1)}, bf16[2,96,1536]{2,1,0:T(8,128)(2,1)S(1)}, u32[]{:S(2)}, u32[]{:S(2)}) collective-permute-start(bf16[2,96,1536]{2,1,0:T(8,128)(2,1)S(1)} %pad_maximum_fusion), channel_id=1, source_target_pairs={{0,8},{8,0},{16,24},{24,16},{1,9},{9,1},{17,25},{25,17},{2,10},{10... | collective-permute-start | bytes 1769480 | tf_op jit(solution)/shard_map/ppermute | solution.py:54
  74.4 7.2 %copy-start.1 = (bf16[256,4096]{1,0:T(8,128)(2,1)S(1)}, bf16[256,4096]{1,0:T(8,128)(2,1)}, u32[]{:S(2)}) copy-start(bf16[256,4096]{1,0:T(8,128)(2,1)} %param.7) | copy-start | bytes 6291460

commit v15 on v11

--- a/solution.py
+++ b/solution.py
@@ -295,9 +295,13 @@
     )
     partial_features = partial_features.astype(jnp.bfloat16)
     feature_grad = partial_features[:MAXACT].astype(jnp.float32)
-    for k in range(1, shards):
+    for k in range(shards):
         piece = partial_features[k * MAXACT : (k + 1) * MAXACT]
-        feature_grad = feature_grad + shifted(piece, "seq", (shards,), (-k,)).astype(jnp.float32)
+        for step in range(parts):
+            if k == 0 and step == 0:
+                continue
+            arrived = shifted(piece, ("seq", "fsdp"), (shards, parts), (-k, step))
+            feature_grad = feature_grad + arrived.astype(jnp.float32)
     every_gate = jnp.concatenate([f[:window] for f in every_factors], axis=0)
     every_up = jnp.concatenate([f[window : 2 * window] for f in every_factors], axis=0)
     every_hidden = jnp.concatenate([f[2 * window :] for f in every_factors], axis=0)
@@ -306,9 +310,6 @@
     gate_grad, up_grad, down_grad = weight_grads(
         normed_cols, every_gate, every_up, every_hidden, masked_cols
     )
-    seq_sum = feature_grad.astype(jnp.bfloat16)
-    for step in range(1, parts):
-        feature_grad = feature_grad + shifted(seq_sum, "fsdp", (parts,), (step,)).astype(jnp.float32)
     _, pullback = jax.vjp(partial(normalize, norm_gain=norm_gain), source)
     slot_grad = pullback(feature_grad)[0].astype(jnp.bfloat16)
     own_columns = lax.dynamic_slice_in_dim(picker, place * own_rows, own_rows, 1)

time: 73.3 us -> 80.7 us (1.10)
  starting transfers between devices: 16.4 us -> 21.7 us
  waiting for transfers between devices: 16.1 us -> 19.2 us
  other arithmetic: 4.79 us -> 3.8 us
    ppermute x7 -> x10, starting transfers between devices: 13.6 us -> 19.5 us  [shifted(): return lax.ppermute(value, axes, pairs)]
    ppermute x4, waiting for transfers between devices: 1.59 us -> 5.37 us  [swapped(): return lax.ppermute(value, axis, [(i, i ^ distance) for i in range(size)])]
    another operation x2, other arithmetic: 1.06 us -> 0.08 us  [rep_exchange(): jnp.stack([gathered[o] for o in origins])]
    ppermute x7 -> x10, waiting for transfers between devices: 14.5 us -> 13.9 us  [shifted(): return lax.ppermute(value, axes, pairs)]
  transfers between devices with their start and end apart: 11 -> 14, of which waited for: 6 -> 8; matrix products, arithmetic and copies ran while one was open for 7% -> 4% of each run, Pallas kernels for 31% -> 0%
where the time goes in v15:
time: 80.7 us; the launch traced here: 80.5 us
  Pallas kernels  29.8 us (37%)
  starting transfers between devices  21.7 us (27%)
  waiting for transfers between devices  19.2 us (24%)
  other arithmetic  3.8 us (5%)
  local copies, waits for them, and re-layouts  2.73 us (3%)
  matrix products  2.34 us (3%)
  between operations  0.96 us (1%)
    pallas_call x1, Pallas kernels, weight_pass(): pl.pallas_call(weight_pass_kernel, grid=(units // chunk,), in_specs=[pl.B...  22.6 us
    ppermute x10, starting transfers between devices, shifted(): return lax.ppermute(value, axes, pairs)  19.5 us
    ppermute x10, waiting for transfers between devices, shifted(): return lax.ppermute(value, axes, pairs)  13.9 us
    pallas_call x1, Pallas kernels, weight_grads(): pl.pallas_call(grads_kernel, grid=(steps,), in_specs=[pl.BlockSpec((rows,...  7.15 us
    ppermute x4, waiting for transfers between devices, swapped(): return lax.ppermute(value, axis, [(i, i ^ distance) for i in range(size)])  5.37 us
    ppermute x4, starting transfers between devices, swapped(): return lax.ppermute(value, axis, [(i, i ^ distance) for i in range(size)])  2.23 us
  transfers between devices with their start and end apart: 14, of which 8 were waited for; matrix products, arithmetic and copies ran while one was open for 4% of the time, Pallas kernels for 0%

profile of v15, /device:TPU:0, one launch (start us, length us, event | category | flops | bytes accessed | tf_op | source)
XLA Modules:
  0.0 80.5 jit_solution(13570765921540125295)
XLA Ops:
  0.6 0.8 %convert_bitcast_fusion = (s32[2,128]{1,0:T(2,128)S(1)}, pred[256]{0:T(512)(128)(4,1)S(1)}) fusion(s32[256]{0:T(256)} %param.13), kind=kLoop, calls=%fused_computation.59 | loop fusion | flops 512 | bytes 2304 | tf_op jit(solution)/shard_map/convert
  1.5 0.3 reduce-window.9
  2.2 0.5 multiply_reduce_fusion.1
  2.8 0.8 %copy-done.2 = bf16[256,4096]{1,0:T(8,128)(2,1)S(1)} copy-done((bf16[256,4096]{1,0:T(8,128)(2,1)S(1)}, bf16[256,4096]{1,0:T(8,128)(2,1)}, u32[]{:S(2)}) %copy-start.2) | copy-done | bytes 2097176
  3.6 0.4 convolution_convert_fusion.1
  4.1 3.1 %collective-permute-start = (bf16[16,4096]{1,0:T(8,128)(2,1)S(1)}, bf16[16,4096]{1,0:T(8,128)(2,1)S(1)}, u32[]{:S(2)}, u32[]{:S(2)}) collective-permute-start(bf16[16,4096]{1,0:T(8,128)(2,1)S(1)} %pad_maximum_fusion.11), channel_id=1, source_target_pairs={{0,2},{2,4},{4,6},{6,0},{1,3},{3,5},{5,7},{7,1},{8,10},{10,12},{12... | collective-permute-start | bytes 393224 | tf_op jit(solution)/shard_map/ppermute | solution.py:50
  7.2 2.6 %collective-permute-start.1 = (bf16[16,4096]{1,0:T(8,128)(2,1)S(1)}, bf16[16,4096]{1,0:T(8,128)(2,1)S(1)}, u32[]{:S(2)}, u32[]{:S(2)}) collective-permute-start(bf16[16,4096]{1,0:T(8,128)(2,1)S(1)} %pad_maximum_fusion.11), channel_id=1, source_target_pairs={{0,4},{2,6},{4,0},{6,2},{1,5},{3,7},{5,1},{7,3},{8,12},{10,14},{12... | collective-permute-start | bytes 393224 | tf_op jit(solution)/shard_map/ppermute | solution.py:50
  9.7 1.3 %collective-permute-start.2 = (bf16[16,4096]{1,0:T(8,128)(2,1)S(1)}, bf16[16,4096]{1,0:T(8,128)(2,1)S(1)}, u32[]{:S(2)}, u32[]{:S(2)}) collective-permute-start(bf16[16,4096]{1,0:T(8,128)(2,1)S(1)} %pad_maximum_fusion.11), channel_id=1, source_target_pairs={{0,6},{2,0},{4,2},{6,4},{1,7},{3,1},{5,3},{7,5},{8,14},{10,8},{12,... | collective-permute-start | bytes 393224 | tf_op jit(solution)/shard_map/ppermute | solution.py:50
  11.1 2.5 %collective-permute-done = bf16[16,4096]{1,0:T(8,128)(2,1)S(1)} collective-permute-done((bf16[16,4096]{1,0:T(8,128)(2,1)S(1)}, bf16[16,4096]{1,0:T(8,128)(2,1)S(1)}, u32[]{:S(2)}, u32[]{:S(2)}) %collective-permute-start) | collective-permute-done | bytes 131104 | tf_op jit(solution)/shard_map/ppermute | solution.py:50
  13.6 4.8 %collective-permute-done.1 = bf16[16,4096]{1,0:T(8,128)(2,1)S(1)} collective-permute-done((bf16[16,4096]{1,0:T(8,128)(2,1)S(1)}, bf16[16,4096]{1,0:T(8,128)(2,1)S(1)}, u32[]{:S(2)}, u32[]{:S(2)}) %collective-permute-start.1) | collective-permute-done | bytes 131104 | tf_op jit(solution)/shard_map/ppermute | solution.py:50
  18.5 0.8 %pad_maximum_fusion.5 = (bf16[32,4096]{1,0:T(8,128)(2,1)}, bf16[32,4096]{1,0:T(8,128)(2,1)}) fusion(bf16[8,4096]{1,0:T(8,128)(2,1)S(1)} %get-tuple-element.54, bf16[8,4096]{1,0:T(8,128)(2,1)S(1)} %get-tuple-element.57, bf16[8,4096]{1,0:T(8,128)(2,1)S(1)} %get-tuple-element.60, bf16[8,4096]{1,0:T(8,128)(2,1)S(1)} %get-tuple-element.19, ...), kind=kLoop, calls=%fused_computation.8 | loop fusion | flops 2097152 | bytes 1048576 | tf_op jit(solution)/shard_map/concatenate | solution.py:282
  19.3 22.6 %shard_map.102 = (bf16[32,1536]{1,0:T(8,128)(2,1)}, bf16[32,1536]{1,0:T(8,128)(2,1)}, bf16[32,1536]{1,0:T(8,128)(2,1)}, f32[32,4096]{1,0:T(8,128)}) custom-call(bf16[32,4096]{1,0:T(8,128)(2,1)} %get-tuple-element.63.normed_ref, bf16[32,4096]{1,0:T(8,128)(2,1)} %get-tuple-element.64.masked_ref, bf16[4096,1536]{1,0:T(8,128)(2,1)} %gate_w_ref.1, ...), custom_call_target="tpu_custom_call" | custom-call | flops 2013265920 | bytes 38797312 | tf_op jit(solution)/shard_map/pallas_call | solution.py:190
  42.0 1.1 %convert_element_type.43 = bf16[32,4096]{1,0:T(8,128)(2,1)S(1)} convert(f32[32,4096]{1,0:T(8,128)} %get-tuple-element.11) | non-fusion elementwise | flops 131072 | bytes 786432 | tf_op jit(solution)/shard_map/convert_element_type | solution.py:296
  43.1 4.4 %collective-permute-start.4 = (bf16[8,4096]{1,0:T(8,128)(2,1)S(1)}, bf16[8,4096]{1,0:T(8,128)(2,1)S(1)}, u32[]{:S(2)}, u32[]{:S(2)}) collective-permute-start(bf16[8,4096]{1,0:T(8,128)(2,1)S(1)} %get-tuple-element.51), channel_id=1, source_target_pairs={{0,6},{1,7},{2,0},{3,1},{4,2},{5,3},{6,4},{7,5},{8,14},{9,15},{10,... | collective-permute-start | bytes 196616 | tf_op jit(solution)/shard_map/ppermute | solution.py:50
  47.5 1.0 %collective-permute-start.5 = (bf16[8,4096]{1,0:T(8,128)(2,1)S(1)}, bf16[8,4096]{1,0:T(8,128)(2,1)S(1)}, u32[]{:S(2)}, u32[]{:S(2)}) collective-permute-start(bf16[8,4096]{1,0:T(8,128)(2,1)S(1)} %get-tuple-element.51), channel_id=1, source_target_pairs={{0,7},{1,6},{2,1},{3,0},{4,3},{5,2},{6,5},{7,4},{8,15},{9,14},{10,... | collective-permute-start | bytes 196616 | tf_op jit(solution)/shard_map/ppermute | solution.py:50
  48.4 0.4 collective-permute-start.6
  48.8 2.5 %collective-permute-start.7 = (bf16[8,4096]{1,0:T(8,128)(2,1)S(1)}, bf16[8,4096]{1,0:T(8,128)(2,1)S(1)}, u32[]{:S(2)}, u32[]{:S(2)}) collective-permute-start(bf16[8,4096]{1,0:T(8,128)(2,1)S(1)} %get-tuple-element.50), channel_id=1, source_target_pairs={{0,5},{1,4},{2,7},{3,6},{4,1},{5,0},{6,3},{7,2},{8,13},{9,12},{10,... | collective-permute-start | bytes 196616 | tf_op jit(solution)/shard_map/ppermute | solution.py:50
  51.3 0.4 reshape.75
  51.8 0.8 fusion.11
  52.5 1.6 %collective-permute-start.3 = (bf16[8,4096]{1,0:T(8,128)(2,1)S(1)}, bf16[8,4096]{1,0:T(8,128)(2,1)S(1)}, u32[]{:S(2)}, u32[]{:S(2)}) collective-permute-start(bf16[8,4096]{1,0:T(8,128)(2,1)S(1)} %get-tuple-element.48), channel_id=1, source_target_pairs={{0,1},{1,0},{2,3},{3,2},{4,5},{5,4},{6,7},{7,6},{8,9},{9,8},{10,11... | collective-permute-start | bytes 196616 | tf_op jit(solution)/shard_map/ppermute | solution.py:50
  54.5 2.7 %collective-permute-done.3 = bf16[8,4096]{1,0:T(8,128)(2,1)S(1)} collective-permute-done((bf16[8,4096]{1,0:T(8,128)(2,1)S(1)}, bf16[8,4096]{1,0:T(8,128)(2,1)S(1)}, u32[]{:S(2)}, u32[]{:S(2)}) %collective-permute-start.3) | collective-permute-done | bytes 65568 | tf_op jit(solution)/shard_map/ppermute | solution.py:50
  57.1 1.7 %collective-permute-start.8 = (bf16[8,4096]{1,0:T(8,128)(2,1)S(1)}, bf16[8,4096]{1,0:T(8,128)(2,1)S(1)}, u32[]{:S(2)}, u32[]{:S(2)}) collective-permute-start(bf16[8,4096]{1,0:T(8,128)(2,1)S(1)} %get-tuple-element.49), channel_id=1, source_target_pairs={{0,2},{1,3},{2,4},{3,5},{4,6},{5,7},{6,0},{7,1},{8,10},{9,11},{10,... | collective-permute-start | bytes 196616 | tf_op jit(solution)/shard_map/ppermute | solution.py:50
  58.8 0.9 %collective-permute-start.9 = (bf16[8,4096]{1,0:T(8,128)(2,1)S(1)}, bf16[8,4096]{1,0:T(8,128)(2,1)S(1)}, u32[]{:S(2)}, u32[]{:S(2)}) collective-permute-start(bf16[8,4096]{1,0:T(8,128)(2,1)S(1)} %get-tuple-element.49), channel_id=1, source_target_pairs={{0,3},{1,2},{2,5},{3,4},{4,7},{5,6},{6,1},{7,0},{8,11},{9,10},{10,... | collective-permute-start | bytes 196616 | tf_op jit(solution)/shard_map/ppermute | solution.py:50
  59.8 1.6 %collective-permute-start.10 = (bf16[2,64,1024]{2,1,0:T(8,128)(2,1)S(1)}, bf16[2,64,1024]{2,1,0:T(8,128)(2,1)S(1)}, u32[]{:S(2)}, u32[]{:S(2)}) collective-permute-start(bf16[2,64,1024]{2,1,0:T(8,128)(2,1)S(1)} %pad_maximum_fusion.7), channel_id=1, source_target_pairs={{0,16},{8,24},{16,0},{24,8},{1,17},{9,25},{17,1},{25,9},{2,18},{10... | collective-permute-start | bytes 786440 | tf_op jit(solution)/shard_map/ppermute | solution.py:54
  61.4 0.5 collective-permute-start.12
  61.9 1.3 %collective-permute-done.8 = bf16[8,4096]{1,0:T(8,128)(2,1)S(1)} collective-permute-done((bf16[8,4096]{1,0:T(8,128)(2,1)S(1)}, bf16[8,4096]{1,0:T(8,128)(2,1)S(1)}, u32[]{:S(2)}, u32[]{:S(2)}) %collective-permute-start.8) | collective-permute-done | bytes 65568 | tf_op jit(solution)/shard_map/ppermute | solution.py:50
  63.2 2.6 %collective-permute-done.9 = bf16[8,4096]{1,0:T(8,128)(2,1)S(1)} collective-permute-done((bf16[8,4096]{1,0:T(8,128)(2,1)S(1)}, bf16[8,4096]{1,0:T(8,128)(2,1)S(1)}, u32[]{:S(2)}, u32[]{:S(2)}) %collective-permute-start.9) | collective-permute-done | bytes 65568 | tf_op jit(solution)/shard_map/ppermute | solution.py:50
  66.0 1.5 %convolution_convert_fusion = bf16[128,4096]{1,0:T(8,128)(2,1)} fusion(f32[8,4096]{1,0:T(8,128)S(1)} %get-tuple-element.62, f32[8,4096]{1,0:T(8,128)S(1)} %get-tuple-element.21, f32[8]{0:T(128)S(1)} %multiply_multiply_fusion, f32[8]{0:T(128)S(1)} %fusion.7, pred[8,256]{1,0:T(8,128)(4,1)S(1)} %fusion.4, s32[]{:T(128)S(6)} %select_n.16), kind=kOutput, calls=%fused_computation | convolution fusion | flops 9076736 | bytes 1312772 | tf_op jit(solution)/shard_map/dot_general | solution.py:23
  67.4 0.5 collective-permute-done.10
  68.1 3.0 %collective-permute-done.12 = bf16[1,96,1536]{2,1,0:T(8,128)(2,1)S(1)} collective-permute-done((bf16[1,96,1536]{2,1,0:T(8,128)(2,1)S(1)}, bf16[1,96,1536]{2,1,0:T(8,128)(2,1)S(1)}, u32[]{:S(2)}, u32[]{:S(2)}) %collective-permute-start.12) | collective-permute-done | bytes 294944 | tf_op jit(solution)/shard_map/ppermute | solution.py:54
  71.3 1.9 %collective-permute-done.13 = bf16[2,96,1536]{2,1,0:T(8,128)(2,1)S(1)} collective-permute-done((bf16[2,96,1536]{2,1,0:T(8,128)(2,1)S(1)}, bf16[2,96,1536]{2,1,0:T(8,128)(2,1)S(1)}, u32[]{:S(2)}, u32[]{:S(2)}) %collective-permute-start.13) | collective-permute-done | bytes 589856 | tf_op jit(solution)/shard_map/ppermute | solution.py:54
  73.4 7.1 %shard_map.103 = (f32[1024,1536]{1,0:T(8,128)}, f32[1024,1536]{1,0:T(8,128)}, f32[1536,1024]{1,0:T(8,128)}) custom-call(bf16[128,1024]{1,0:T(8,128)(2,1)S(1)} %pad_maximum_fusion.9.normed_ref, bf16[128,1536]{1,0:T(8,128)(2,1)S(1)} %pad_maximum_fusion.2.gate_ref, bf16[128,1536]{1,0:T(8,128)(2,1)S(1)} %pad_maximum_fusion.3.up_ref, ...), custom_call_target="tpu_custom_call" | custom-call | flops 1207959552 | bytes 20578304 | tf_op jit(solution)/shard_map/pallas_call | solution.py:234
  (58 shorter events, 1.7 us)
Async XLA Ops:
  0.6 1.6 %copy-start = (bf16[256,4096]{1,0:T(8,128)(2,1)S(1)}, bf16[256,4096]{1,0:T(8,128)(2,1)}, u32[]{:S(2)}) copy-start(bf16[256,4096]{1,0:T(8,128)(2,1)} %param.7) | copy-start | bytes 6291460
  1.9 1.7 %copy-start.2 = (bf16[256,4096]{1,0:T(8,128)(2,1)S(1)}, bf16[256,4096]{1,0:T(8,128)(2,1)}, u32[]{:S(2)}) copy-start(bf16[256,4096]{1,0:T(8,128)(2,1)} %param.8) | copy-start | bytes 6291460
  2.2 1.7 %copy-start.6 = (f32[4096]{0:T(1024)S(1)}, f32[4096]{0:T(1024)}, u32[]{:S(2)}) copy-start(f32[4096]{0:T(1024)} %param.9) | copy-start | bytes 49156
  4.1 9.5 %collective-permute-start = (bf16[16,4096]{1,0:T(8,128)(2,1)S(1)}, bf16[16,4096]{1,0:T(8,128)(2,1)S(1)}, u32[]{:S(2)}, u32[]{:S(2)}) collective-permute-start(bf16[16,4096]{1,0:T(8,128)(2,1)S(1)} %pad_maximum_fusion.11), channel_id=1, source_target_pairs={{0,2},{2,4},{4,6},{6,0},{1,3},{3,5},{5,7},{7,1},{8,10},{10,12},{12... | collective-permute-start | bytes 393224 | tf_op jit(solution)/shard_map/ppermute | solution.py:50
  7.2 11.2 %collective-permute-start.1 = (bf16[16,4096]{1,0:T(8,128)(2,1)S(1)}, bf16[16,4096]{1,0:T(8,128)(2,1)S(1)}, u32[]{:S(2)}, u32[]{:S(2)}) collective-permute-start(bf16[16,4096]{1,0:T(8,128)(2,1)S(1)} %pad_maximum_fusion.11), channel_id=1, source_target_pairs={{0,4},{2,6},{4,0},{6,2},{1,5},{3,7},{5,1},{7,3},{8,12},{10,14},{12... | collective-permute-start | bytes 393224 | tf_op jit(solution)/shard_map/ppermute | solution.py:50
  9.7 8.7 %collective-permute-start.2 = (bf16[16,4096]{1,0:T(8,128)(2,1)S(1)}, bf16[16,4096]{1,0:T(8,128)(2,1)S(1)}, u32[]{:S(2)}, u32[]{:S(2)}) collective-permute-start(bf16[16,4096]{1,0:T(8,128)(2,1)S(1)} %pad_maximum_fusion.11), channel_id=1, source_target_pairs={{0,6},{2,0},{4,2},{6,4},{1,7},{3,1},{5,3},{7,5},{8,14},{10,8},{12,... | collective-permute-start | bytes 393224 | tf_op jit(solution)/shard_map/ppermute | solution.py:50
  43.1 15.8 %collective-permute-start.4 = (bf16[8,4096]{1,0:T(8,128)(2,1)S(1)}, bf16[8,4096]{1,0:T(8,128)(2,1)S(1)}, u32[]{:S(2)}, u32[]{:S(2)}) collective-permute-start(bf16[8,4096]{1,0:T(8,128)(2,1)S(1)} %get-tuple-element.51), channel_id=1, source_target_pairs={{0,6},{1,7},{2,0},{3,1},{4,2},{5,3},{6,4},{7,5},{8,14},{9,15},{10,... | collective-permute-start | bytes 196616 | tf_op jit(solution)/shard_map/ppermute | solution.py:50
  47.5 12.3 %collective-permute-start.5 = (bf16[8,4096]{1,0:T(8,128)(2,1)S(1)}, bf16[8,4096]{1,0:T(8,128)(2,1)S(1)}, u32[]{:S(2)}, u32[]{:S(2)}) collective-permute-start(bf16[8,4096]{1,0:T(8,128)(2,1)S(1)} %get-tuple-element.51), channel_id=1, source_target_pairs={{0,7},{1,6},{2,1},{3,0},{4,3},{5,2},{6,5},{7,4},{8,15},{9,14},{10,... | collective-permute-start | bytes 196616 | tf_op jit(solution)/shard_map/ppermute | solution.py:50
  48.4 12.9 %collective-permute-start.6 = (bf16[8,4096]{1,0:T(8,128)(2,1)S(1)}, bf16[8,4096]{1,0:T(8,128)(2,1)S(1)}, u32[]{:S(2)}, u32[]{:S(2)}) collective-permute-start(bf16[8,4096]{1,0:T(8,128)(2,1)S(1)} %get-tuple-element.50), channel_id=1, source_target_pairs={{0,4},{1,5},{2,6},{3,7},{4,0},{5,1},{6,2},{7,3},{8,12},{9,13},{10,... | collective-permute-start | bytes 196616 | tf_op jit(solution)/shard_map/ppermute | solution.py:50
  48.8 13.0 %collective-permute-start.7 = (bf16[8,4096]{1,0:T(8,128)(2,1)S(1)}, bf16[8,4096]{1,0:T(8,128)(2,1)S(1)}, u32[]{:S(2)}, u32[]{:S(2)}) collective-permute-start(bf16[8,4096]{1,0:T(8,128)(2,1)S(1)} %get-tuple-element.50), channel_id=1, source_target_pairs={{0,5},{1,4},{2,7},{3,6},{4,1},{5,0},{6,3},{7,2},{8,13},{9,12},{10,... | collective-permute-start | bytes 196616 | tf_op jit(solution)/shard_map/ppermute | solution.py:50
  51.7 2.5 %copy-start.3 = (bf16[32,1536]{1,0:T(8,128)(2,1)S(1)}, bf16[32,1536]{1,0:T(8,128)(2,1)}, u32[]{:S(2)}) copy-start(bf16[32,1536]{1,0:T(8,128)(2,1)} %get-tuple-element.12) | copy-start | bytes 294916
  51.7 2.5 %copy-start.4 = (bf16[32,1536]{1,0:T(8,128)(2,1)S(1)}, bf16[32,1536]{1,0:T(8,128)(2,1)}, u32[]{:S(2)}) copy-start(bf16[32,1536]{1,0:T(8,128)(2,1)} %get-tuple-element.13) | copy-start | bytes 294916
  51.7 2.5 %copy-start.5 = (bf16[32,1536]{1,0:T(8,128)(2,1)S(1)}, bf16[32,1536]{1,0:T(8,128)(2,1)}, u32[]{:S(2)}) copy-start(bf16[32,1536]{1,0:T(8,128)(2,1)} %get-tuple-element.14) | copy-start | bytes 294916
  52.5 4.6 %collective-permute-start.3 = (bf16[8,4096]{1,0:T(8,128)(2,1)S(1)}, bf16[8,4096]{1,0:T(8,128)(2,1)S(1)}, u32[]{:S(2)}, u32[]{:S(2)}) collective-permute-start(bf16[8,4096]{1,0:T(8,128)(2,1)S(1)} %get-tuple-element.48), channel_id=1, source_target_pairs={{0,1},{1,0},{2,3},{3,2},{4,5},{5,4},{6,7},{7,6},{8,9},{9,8},{10,11... | collective-permute-start | bytes 196616 | tf_op jit(solution)/shard_map/ppermute | solution.py:50
  57.1 6.1 %collective-permute-start.8 = (bf16[8,4096]{1,0:T(8,128)(2,1)S(1)}, bf16[8,4096]{1,0:T(8,128)(2,1)S(1)}, u32[]{:S(2)}, u32[]{:S(2)}) collective-permute-start(bf16[8,4096]{1,0:T(8,128)(2,1)S(1)} %get-tuple-element.49), channel_id=1, source_target_pairs={{0,2},{1,3},{2,4},{3,5},{4,6},{5,7},{6,0},{7,1},{8,10},{9,11},{10,... | collective-permute-start | bytes 196616 | tf_op jit(solution)/shard_map/ppermute | solution.py:50
  58.8 7.0 %collective-permute-start.9 = (bf16[8,4096]{1,0:T(8,128)(2,1)S(1)}, bf16[8,4096]{1,0:T(8,128)(2,1)S(1)}, u32[]{:S(2)}, u32[]{:S(2)}) collective-permute-start(bf16[8,4096]{1,0:T(8,128)(2,1)S(1)} %get-tuple-element.49), channel_id=1, source_target_pairs={{0,3},{1,2},{2,5},{3,4},{4,7},{5,6},{6,1},{7,0},{8,11},{9,10},{10,... | collective-permute-start | bytes 196616 | tf_op jit(solution)/shard_map/ppermute | solution.py:50
  59.8 8.2 %collective-permute-start.10 = (bf16[2,64,1024]{2,1,0:T(8,128)(2,1)S(1)}, bf16[2,64,1024]{2,1,0:T(8,128)(2,1)S(1)}, u32[]{:S(2)}, u32[]{:S(2)}) collective-permute-start(bf16[2,64,1024]{2,1,0:T(8,128)(2,1)S(1)} %pad_maximum_fusion.7), channel_id=1, source_target_pairs={{0,16},{8,24},{16,0},{24,8},{1,17},{9,25},{17,1},{25,9},{2,18},{10... | collective-permute-start | bytes 786440 | tf_op jit(solution)/shard_map/ppermute | solution.py:54
  61.4 9.7 %collective-permute-start.12 = (bf16[1,96,1536]{2,1,0:T(8,128)(2,1)S(1)}, bf16[1,96,1536]{2,1,0:T(8,128)(2,1)S(1)}, u32[]{:S(2)}, u32[]{:S(2)}) collective-permute-start(bf16[1,96,1536]{2,1,0:T(8,128)(2,1)S(1)} %maximum_bitcast_fusion), channel_id=1, source_target_pairs={{0,16},{8,24},{16,0},{24,8},{1,17},{9,25},{17,1},{25,9},{2,18},{10... | collective-permute-start | bytes 884744 | tf_op jit(solution)/shard_map/ppermute | solution.py:54
  68.0 3.3 %collective-permute-start.11 = (bf16[2,64,1024]{2,1,0:T(8,128)(2,1)S(1)}, bf16[2,64,1024]{2,1,0:T(8,128)(2,1)S(1)}, u32[]{:S(2)}, u32[]{:S(2)}) collective-permute-start(bf16[2,64,1024]{2,1,0:T(8,128)(2,1)S(1)} %pad_maximum_fusion.8), channel_id=1, source_target_pairs={{0,8},{8,0},{16,24},{24,16},{1,9},{9,1},{17,25},{25,17},{2,10},{10... | collective-permute-start | bytes 786440 | tf_op jit(solution)/shard_map/ppermute | solution.py:54
  71.1 2.1 %collective-permute-start.13 = (bf16[2,96,1536]{2,1,0:T(8,128)(2,1)S(1)}, bf16[2,96,1536]{2,1,0:T(8,128)(2,1)S(1)}, u32[]{:S(2)}, u32[]{:S(2)}) collective-permute-start(bf16[2,96,1536]{2,1,0:T(8,128)(2,1)S(1)} %pad_maximum_fusion), channel_id=1, source_target_pairs={{0,8},{8,0},{16,24},{24,16},{1,9},{9,1},{17,25},{25,17},{2,10},{10... | collective-permute-start | bytes 1769480 | tf_op jit(solution)/shard_map/ppermute | solution.py:54
  73.3 7.2 %copy-start.1 = (bf16[256,4096]{1,0:T(8,128)(2,1)S(1)}, bf16[256,4096]{1,0:T(8,128)(2,1)}, u32[]{:S(2)}) copy-start(bf16[256,4096]{1,0:T(8,128)(2,1)} %param.7) | copy-start | bytes 6291460

commit v16 on v11

--- a/solution.py
+++ b/solution.py
@@ -154,7 +154,7 @@
 
 
 def weight_pass_kernel(normed_ref, masked_ref, gate_w_ref, up_w_ref, down_w_ref,
-                       gate_rows_ref, up_rows_ref, hidden_ref, features_ref):
+                       gate_rows_ref, up_rows_ref, hidden_ref, features_ref, total_ref):
     step = pl.program_id(0)
     normed = normed_ref[...]
     gate_w = gate_w_ref[...]
@@ -175,11 +175,15 @@
 
     @pl.when(step == 0)
     def _():
-        features_ref[...] = partial_features
+        total_ref[...] = partial_features
 
     @pl.when(step > 0)
     def _():
-        features_ref[...] += partial_features
+        total_ref[...] += partial_features
+
+    @pl.when(step == pl.num_programs(0) - 1)
+    def _():
+        features_ref[...] = total_ref[...].astype(features_ref.dtype)
 
 
 def weight_pass(window_normed, window_masked, gate_weight, up_weight, down_weight):
@@ -207,8 +211,9 @@
             factor_shape,
             factor_shape,
             factor_shape,
-            jax.ShapeDtypeStruct((rows, features), jnp.float32),
-        ],
+            jax.ShapeDtypeStruct((rows, features), jnp.bfloat16),
+        ],
+        scratch_shapes=[pltpu.VMEM((rows, features), jnp.float32)],
         compiler_params=pltpu.CompilerParams(vmem_limit_bytes=56 * 1024 * 1024),
         cost_estimate=pl.CostEstimate(
             flops=10 * rows * features * units,
@@ -293,7 +298,6 @@
         "rep",
         replicas,
     )
-    partial_features = partial_features.astype(jnp.bfloat16)
     feature_grad = partial_features[:MAXACT].astype(jnp.float32)
     for k in range(1, shards):
         piece = partial_features[k * MAXACT : (k + 1) * MAXACT]

time: 73.3 us -> 75.7 us (1.033)
  local copies, waits for them, and re-layouts: 2.73 us -> 3.63 us
  matrix products: 2.34 us -> 3.18 us
    convert_element_type x1 -> x0, other arithmetic: 1.07 us -> none  [local(): partial_features = partial_features.astype(jnp.bfloat16)]
    slice x1, local copies, waits for them, and re-layouts: 0.02 us -> 0.92 us  [local(): piece = partial_features[k * MAXACT:(k + 1) * MAXACT]]
    convert_element_type x1, other arithmetic: 0.04 us -> 0.88 us  [local(): seq_sum = feature_grad.astype(jnp.bfloat16)]
    reduce_sum x1, other arithmetic: 0.17 us -> 1.01 us  [normalize(): return widened * factor * norm_gain]
    dot_general x1, matrix products: 1.46 us -> 2.3 us  [contract_first(): lax.dot_general(left, right, (((0,), (0,)), ((), ())), preferred_element_...]
  transfers between devices with their start and end apart: 11 -> 11, of which waited for: 6 -> 6; matrix products, arithmetic and copies ran while one was open for 7% -> 10% of each run, Pallas kernels for 31% -> 30%
where the time goes in v16:
time: 75.7 us; the launch traced here: 75.3 us
  Pallas kernels  29.7 us (39%)
  starting transfers between devices  16.4 us (22%)
  waiting for transfers between devices  16.1 us (21%)
  other arithmetic  5.4 us (7%)
  local copies, waits for them, and re-layouts  3.63 us (5%)
  matrix products  3.18 us (4%)
  between operations  0.94 us (1%)
    pallas_call x1, Pallas kernels, weight_pass(): pl.pallas_call(weight_pass_kernel, grid=(units // chunk,), in_specs=[pl.B...  22.5 us
    ppermute x7, waiting for transfers between devices, shifted(): return lax.ppermute(value, axes, pairs)  14.5 us
    ppermute x7, starting transfers between devices, shifted(): return lax.ppermute(value, axes, pairs)  13.6 us
    pallas_call x1, Pallas kernels, weight_grads(): pl.pallas_call(grads_kernel, grid=(steps,), in_specs=[pl.BlockSpec((rows,...  7.15 us
    ppermute x4, starting transfers between devices, swapped(): return lax.ppermute(value, axis, [(i, i ^ distance) for i in range(size)])  2.78 us
    dot_general x1, matrix products, contract_first(): lax.dot_general(left, right, (((0,), (0,)), ((), ())), preferred_element_...  2.3 us
    ppermute x4, waiting for transfers between devices, swapped(): return lax.ppermute(value, axis, [(i, i ^ distance) for i in range(size)])  1.59 us
  transfers between devices with their start and end apart: 11, of which 6 were waited for; matrix products, arithmetic and copies ran while one was open for 10% of the time, Pallas kernels for 30%

profile of v16, /device:TPU:0, one launch (start us, length us, event | category | flops | bytes accessed | tf_op | source)
XLA Modules:
  0.0 75.3 jit_solution(10685171545081872203)
XLA Ops:
  0.6 0.8 %convert_bitcast_fusion = (s32[2,128]{1,0:T(2,128)S(1)}, pred[256]{0:T(512)(128)(4,1)S(1)}) fusion(s32[256]{0:T(256)} %param.13), kind=kLoop, calls=%fused_computation.61 | loop fusion | flops 512 | bytes 2304 | tf_op jit(solution)/shard_map/convert
  1.5 0.3 reduce-window.9
  2.1 0.2 copy-done
  2.2 0.5 multiply_reduce_fusion.1
  2.8 0.8 %copy-done.2 = bf16[256,4096]{1,0:T(8,128)(2,1)S(1)} copy-done((bf16[256,4096]{1,0:T(8,128)(2,1)S(1)}, bf16[256,4096]{1,0:T(8,128)(2,1)}, u32[]{:S(2)}) %copy-start.2) | copy-done | bytes 2097176
  3.6 0.4 convolution_convert_fusion.1
  4.1 3.1 %collective-permute-start = (bf16[16,4096]{1,0:T(8,128)(2,1)S(1)}, bf16[16,4096]{1,0:T(8,128)(2,1)S(1)}, u32[]{:S(2)}, u32[]{:S(2)}) collective-permute-start(bf16[16,4096]{1,0:T(8,128)(2,1)S(1)} %pad_maximum_fusion.11), channel_id=1, source_target_pairs={{0,2},{2,4},{4,6},{6,0},{1,3},{3,5},{5,7},{7,1},{8,10},{10,12},{12... | collective-permute-start | bytes 393224 | tf_op jit(solution)/shard_map/ppermute | solution.py:50
  7.2 2.6 %collective-permute-start.1 = (bf16[16,4096]{1,0:T(8,128)(2,1)S(1)}, bf16[16,4096]{1,0:T(8,128)(2,1)S(1)}, u32[]{:S(2)}, u32[]{:S(2)}) collective-permute-start(bf16[16,4096]{1,0:T(8,128)(2,1)S(1)} %pad_maximum_fusion.11), channel_id=1, source_target_pairs={{0,4},{2,6},{4,0},{6,2},{1,5},{3,7},{5,1},{7,3},{8,12},{10,14},{12... | collective-permute-start | bytes 393224 | tf_op jit(solution)/shard_map/ppermute | solution.py:50
  9.7 1.3 %collective-permute-start.2 = (bf16[16,4096]{1,0:T(8,128)(2,1)S(1)}, bf16[16,4096]{1,0:T(8,128)(2,1)S(1)}, u32[]{:S(2)}, u32[]{:S(2)}) collective-permute-start(bf16[16,4096]{1,0:T(8,128)(2,1)S(1)} %pad_maximum_fusion.11), channel_id=1, source_target_pairs={{0,6},{2,0},{4,2},{6,4},{1,7},{3,1},{5,3},{7,5},{8,14},{10,8},{12,... | collective-permute-start | bytes 393224 | tf_op jit(solution)/shard_map/ppermute | solution.py:50
  11.1 2.5 %collective-permute-done = bf16[16,4096]{1,0:T(8,128)(2,1)S(1)} collective-permute-done((bf16[16,4096]{1,0:T(8,128)(2,1)S(1)}, bf16[16,4096]{1,0:T(8,128)(2,1)S(1)}, u32[]{:S(2)}, u32[]{:S(2)}) %collective-permute-start) | collective-permute-done | bytes 131104 | tf_op jit(solution)/shard_map/ppermute | solution.py:50
  13.6 4.8 %collective-permute-done.1 = bf16[16,4096]{1,0:T(8,128)(2,1)S(1)} collective-permute-done((bf16[16,4096]{1,0:T(8,128)(2,1)S(1)}, bf16[16,4096]{1,0:T(8,128)(2,1)S(1)}, u32[]{:S(2)}, u32[]{:S(2)}) %collective-permute-start.1) | collective-permute-done | bytes 131104 | tf_op jit(solution)/shard_map/ppermute | solution.py:50
  18.5 0.4 reshape.75
  18.9 0.8 %fusion.13 = (bf16[64,1,1024]{2,1,0:T(2,128)(2,1)S(1)}, bf16[64,1,1024]{2,1,0:T(2,128)(2,1)S(1)}, bf16[64,1,1024]{2,1,0:T(2,128)(2,1)S(1)}, bf16[64,1,1024]{2,1,0:T(2,128)(2,1)S(1)}) fusion(bf16[64,4,1024]{2,1,0:T(4,128)(2,1)S(1)} %reshape.75), kind=kLoop, calls=%fused_computation.70 | loop fusion | bytes 1048576 | tf_op jit(solution)/shard_map/slice | solution.py:297
  20.0 1.6 %collective-permute-start.7 = (bf16[2,64,1024]{2,1,0:T(8,128)(2,1)S(1)}, bf16[2,64,1024]{2,1,0:T(8,128)(2,1)S(1)}, u32[]{:S(2)}, u32[]{:S(2)}) collective-permute-start(bf16[2,64,1024]{2,1,0:T(8,128)(2,1)S(1)} %pad_maximum_fusion.7), channel_id=1, source_target_pairs={{0,16},{8,24},{16,0},{24,8},{1,17},{9,25},{17,1},{25,9},{2,18},{10... | collective-permute-start | bytes 786440 | tf_op jit(solution)/shard_map/ppermute | solution.py:54
  21.6 0.8 %pad_maximum_fusion.5 = (bf16[32,4096]{1,0:T(8,128)(2,1)}, bf16[32,4096]{1,0:T(8,128)(2,1)}) fusion(bf16[8,4096]{1,0:T(8,128)(2,1)S(1)} %get-tuple-element.51, bf16[8,4096]{1,0:T(8,128)(2,1)S(1)} %get-tuple-element.54, bf16[8,4096]{1,0:T(8,128)(2,1)S(1)} %get-tuple-element.57, bf16[8,4096]{1,0:T(8,128)(2,1)S(1)} %get-tuple-element.19, ...), kind=kLoop, calls=%fused_computation.8 | loop fusion | flops 2097152 | bytes 1048576 | tf_op jit(solution)/shard_map/concatenate | solution.py:287
  22.4 22.5 %shard_map.102 = (bf16[32,1536]{1,0:T(8,128)(2,1)}, bf16[32,1536]{1,0:T(8,128)(2,1)}, bf16[32,1536]{1,0:T(8,128)(2,1)}, bf16[32,4096]{1,0:T(8,128)(2,1)}) custom-call(bf16[32,4096]{1,0:T(8,128)(2,1)} %get-tuple-element.60.normed_ref, bf16[32,4096]{1,0:T(8,128)(2,1)} %get-tuple-element.61.masked_ref, bf16[4096,1536]{1,0:T(8,128)(2,1)} %gate_w_ref.1, ...), custom_call_target="tpu_custom_call" | custom-call | flops 2013265920 | bytes 38797312 | tf_op jit(solution)/shard_map/pallas_call | solution.py:194
  44.9 0.9 %fusion.14 = (bf16[8,4096]{1,0:T(8,128)(2,1)S(1)}, bf16[8,4096]{1,0:T(8,128)(2,1)S(1)}, bf16[8,4096]{1,0:T(8,128)(2,1)S(1)}) fusion(bf16[32,4096]{1,0:T(8,128)(2,1)} %get-tuple-element.11), kind=kLoop, calls=%fused_computation.71 | loop fusion | bytes 393216 | tf_op jit(solution)/shard_map/slice | solution.py:303
  45.8 4.4 %collective-permute-start.3 = (bf16[8,4096]{1,0:T(8,128)(2,1)S(1)}, bf16[8,4096]{1,0:T(8,128)(2,1)S(1)}, u32[]{:S(2)}, u32[]{:S(2)}) collective-permute-start(bf16[8,4096]{1,0:T(8,128)(2,1)S(1)} %get-tuple-element.46), channel_id=1, source_target_pairs={{0,6},{2,0},{4,2},{6,4},{1,7},{3,1},{5,3},{7,5},{8,14},{10,8},{12,... | collective-permute-start | bytes 196616 | tf_op jit(solution)/shard_map/ppermute | solution.py:50
  50.2 0.4 collective-permute-start.4
  50.6 0.3 collective-permute-start.5
  50.9 1.0 %maximum_bitcast_fusion = bf16[1,96,1536]{2,1,0:T(8,128)(2,1)S(1)} fusion(bf16[32,1536]{1,0:T(8,128)(2,1)} %get-tuple-element.14, bf16[32,1536]{1,0:T(8,128)(2,1)} %get-tuple-element.13, bf16[32,1536]{1,0:T(8,128)(2,1)} %get-tuple-element.12), kind=kLoop, calls=%fused_computation.7 | loop fusion | flops 884736 | bytes 589824 | tf_op jit(solution)/shard_map/stack | solution.py:137
  51.9 0.6 collective-permute-start.9
  52.5 4.5 %collective-permute-done.4 = bf16[8,4096]{1,0:T(8,128)(2,1)S(1)} collective-permute-done((bf16[8,4096]{1,0:T(8,128)(2,1)S(1)}, bf16[8,4096]{1,0:T(8,128)(2,1)S(1)}, u32[]{:S(2)}, u32[]{:S(2)}) %collective-permute-start.4) | collective-permute-done | bytes 65568 | tf_op jit(solution)/shard_map/ppermute | solution.py:50
  56.9 0.9 %fusion.12 = bf16[8,4096]{1,0:T(8,128)(2,1)S(1)} fusion(bf16[8,4096]{1,0:T(8,128)(2,1)S(1)} %collective-permute-done.5, bf16[8,4096]{1,0:T(8,128)(2,1)S(1)} %collective-permute-done.4, bf16[8,4096]{1,0:T(8,128)(2,1)S(1)} %collective-permute-done.3, bf16[32,4096]{1,0:T(8,128)(2,1)} %get-tuple-element.11), kind=kLoop, calls=%fused_computation.69 | loop fusion | flops 262144 | bytes 327680 | tf_op jit(solution)/shard_map/convert_element_type | solution.py:313
  57.8 1.6 %collective-permute-start.6 = (bf16[8,4096]{1,0:T(8,128)(2,1)S(1)}, bf16[8,4096]{1,0:T(8,128)(2,1)S(1)}, u32[]{:S(2)}, u32[]{:S(2)}) collective-permute-start(bf16[8,4096]{1,0:T(8,128)(2,1)S(1)} %fusion.12), channel_id=1, source_target_pairs={{0,1},{1,0},{2,3},{3,2},{4,5},{5,4},{6,7},{7,6},{8,9},{9,8},{10,11... | collective-permute-start | bytes 196616 | tf_op jit(solution)/shard_map/ppermute | solution.py:50
  59.4 2.8 %collective-permute-done.6 = bf16[8,4096]{1,0:T(8,128)(2,1)S(1)} collective-permute-done((bf16[8,4096]{1,0:T(8,128)(2,1)S(1)}, bf16[8,4096]{1,0:T(8,128)(2,1)S(1)}, u32[]{:S(2)}, u32[]{:S(2)}) %collective-permute-start.6) | collective-permute-done | bytes 65568 | tf_op jit(solution)/shard_map/ppermute | solution.py:50
  62.1 1.0 %multiply_reduce_fusion = f32[8]{0:T(128)S(1)} fusion(f32[8,4096]{1,0:T(8,128)S(1)} %get-tuple-element.59, bf16[8,4096]{1,0:T(8,128)(2,1)S(1)} %collective-permute-done.6, f32[4096]{0:T(1024)S(1)} %copy-done.6, bf16[8,4096]{1,0:T(8,128)(2,1)S(1)} %collective-permute-done.5, bf16[8,4096]{1,0:T(8,128)(2,1)S(1)} %collective-permute-done.4, ...), kind=kLoop, calls=%fused_computation.21 | loop fusion | flops 393208 | bytes 475168 | tf_op jit(solution)/shard_map/transpose(jvp())/reduce_sum | solution.py:19
  63.2 2.3 %convolution_convert_fusion = bf16[128,4096]{1,0:T(8,128)(2,1)} fusion(f32[8,4096]{1,0:T(8,128)S(1)} %get-tuple-element.59, bf16[8,4096]{1,0:T(8,128)(2,1)S(1)} %collective-permute-done.6, f32[8]{0:T(128)S(1)} %multiply_multiply_fusion, f32[4096]{0:T(1024)S(1)} %copy-done.6, f32[8]{0:T(128)S(1)} %fusion.8, pred[8,256]{1,0:T(8,128)(4,1)S(1)} %fusion.5, ...), kind=kOutput, calls=%fused_computation | convolution fusion | flops 9404416 | bytes 1525764 | tf_op jit(solution)/shard_map/dot_general | solution.py:23
  65.7 0.6 collective-permute-start.10
  66.3 0.8 %collective-permute-done.8 = bf16[2,64,1024]{2,1,0:T(8,128)(2,1)S(1)} collective-permute-done((bf16[2,64,1024]{2,1,0:T(8,128)(2,1)S(1)}, bf16[2,64,1024]{2,1,0:T(8,128)(2,1)S(1)}, u32[]{:S(2)}, u32[]{:S(2)}) %collective-permute-start.8) | collective-permute-done | bytes 262176 | tf_op jit(solution)/shard_map/ppermute | solution.py:54
  67.2 0.8 %collective-permute-done.10 = bf16[2,96,1536]{2,1,0:T(8,128)(2,1)S(1)} collective-permute-done((bf16[2,96,1536]{2,1,0:T(8,128)(2,1)S(1)}, bf16[2,96,1536]{2,1,0:T(8,128)(2,1)S(1)}, u32[]{:S(2)}, u32[]{:S(2)}) %collective-permute-start.10) | collective-permute-done | bytes 589856 | tf_op jit(solution)/shard_map/ppermute | solution.py:54
  68.2 7.2 %shard_map.103 = (f32[1024,1536]{1,0:T(8,128)}, f32[1024,1536]{1,0:T(8,128)}, f32[1536,1024]{1,0:T(8,128)}) custom-call(bf16[128,1024]{1,0:T(8,128)(2,1)S(1)} %pad_maximum_fusion.9.normed_ref, bf16[128,1536]{1,0:T(8,128)(2,1)S(1)} %pad_maximum_fusion.2.gate_ref, bf16[128,1536]{1,0:T(8,128)(2,1)S(1)} %pad_maximum_fusion.3.up_ref, ...), custom_call_target="tpu_custom_call" | custom-call | flops 1207959552 | bytes 20578304 | tf_op jit(solution)/shard_map/pallas_call | solution.py:239
  (52 shorter events, 1.2 us)
Async XLA Ops:
  0.6 1.6 %copy-start = (bf16[256,4096]{1,0:T(8,128)(2,1)S(1)}, bf16[256,4096]{1,0:T(8,128)(2,1)}, u32[]{:S(2)}) copy-start(bf16[256,4096]{1,0:T(8,128)(2,1)} %param.7) | copy-start | bytes 6291460
  1.9 1.7 %copy-start.2 = (bf16[256,4096]{1,0:T(8,128)(2,1)S(1)}, bf16[256,4096]{1,0:T(8,128)(2,1)}, u32[]{:S(2)}) copy-start(bf16[256,4096]{1,0:T(8,128)(2,1)} %param.8) | copy-start | bytes 6291460
  2.2 1.7 %copy-start.6 = (f32[4096]{0:T(1024)S(1)}, f32[4096]{0:T(1024)}, u32[]{:S(2)}) copy-start(f32[4096]{0:T(1024)} %param.9) | copy-start | bytes 49156
  4.1 9.5 %collective-permute-start = (bf16[16,4096]{1,0:T(8,128)(2,1)S(1)}, bf16[16,4096]{1,0:T(8,128)(2,1)S(1)}, u32[]{:S(2)}, u32[]{:S(2)}) collective-permute-start(bf16[16,4096]{1,0:T(8,128)(2,1)S(1)} %pad_maximum_fusion.11), channel_id=1, source_target_pairs={{0,2},{2,4},{4,6},{6,0},{1,3},{3,5},{5,7},{7,1},{8,10},{10,12},{12... | collective-permute-start | bytes 393224 | tf_op jit(solution)/shard_map/ppermute | solution.py:50
  7.2 11.2 %collective-permute-start.1 = (bf16[16,4096]{1,0:T(8,128)(2,1)S(1)}, bf16[16,4096]{1,0:T(8,128)(2,1)S(1)}, u32[]{:S(2)}, u32[]{:S(2)}) collective-permute-start(bf16[16,4096]{1,0:T(8,128)(2,1)S(1)} %pad_maximum_fusion.11), channel_id=1, source_target_pairs={{0,4},{2,6},{4,0},{6,2},{1,5},{3,7},{5,1},{7,3},{8,12},{10,14},{12... | collective-permute-start | bytes 393224 | tf_op jit(solution)/shard_map/ppermute | solution.py:50
  9.7 8.7 %collective-permute-start.2 = (bf16[16,4096]{1,0:T(8,128)(2,1)S(1)}, bf16[16,4096]{1,0:T(8,128)(2,1)S(1)}, u32[]{:S(2)}, u32[]{:S(2)}) collective-permute-start(bf16[16,4096]{1,0:T(8,128)(2,1)S(1)} %pad_maximum_fusion.11), channel_id=1, source_target_pairs={{0,6},{2,0},{4,2},{6,4},{1,7},{3,1},{5,3},{7,5},{8,14},{10,8},{12,... | collective-permute-start | bytes 393224 | tf_op jit(solution)/shard_map/ppermute | solution.py:50
  20.0 45.5 %collective-permute-start.7 = (bf16[2,64,1024]{2,1,0:T(8,128)(2,1)S(1)}, bf16[2,64,1024]{2,1,0:T(8,128)(2,1)S(1)}, u32[]{:S(2)}, u32[]{:S(2)}) collective-permute-start(bf16[2,64,1024]{2,1,0:T(8,128)(2,1)S(1)} %pad_maximum_fusion.7), channel_id=1, source_target_pairs={{0,16},{8,24},{16,0},{24,8},{1,17},{9,25},{17,1},{25,9},{2,18},{10... | collective-permute-start | bytes 786440 | tf_op jit(solution)/shard_map/ppermute | solution.py:54
  45.8 6.6 %collective-permute-start.3 = (bf16[8,4096]{1,0:T(8,128)(2,1)S(1)}, bf16[8,4096]{1,0:T(8,128)(2,1)S(1)}, u32[]{:S(2)}, u32[]{:S(2)}) collective-permute-start(bf16[8,4096]{1,0:T(8,128)(2,1)S(1)} %get-tuple-element.46), channel_id=1, source_target_pairs={{0,6},{2,0},{4,2},{6,4},{1,7},{3,1},{5,3},{7,5},{8,14},{10,8},{12,... | collective-permute-start | bytes 196616 | tf_op jit(solution)/shard_map/ppermute | solution.py:50
  50.2 6.7 %collective-permute-start.4 = (bf16[8,4096]{1,0:T(8,128)(2,1)S(1)}, bf16[8,4096]{1,0:T(8,128)(2,1)S(1)}, u32[]{:S(2)}, u32[]{:S(2)}) collective-permute-start(bf16[8,4096]{1,0:T(8,128)(2,1)S(1)} %get-tuple-element.48), channel_id=1, source_target_pairs={{0,4},{2,6},{4,0},{6,2},{1,5},{3,7},{5,1},{7,3},{8,12},{10,14},{12... | collective-permute-start | bytes 196616 | tf_op jit(solution)/shard_map/ppermute | solution.py:50
  50.6 6.3 %collective-permute-start.5 = (bf16[8,4096]{1,0:T(8,128)(2,1)S(1)}, bf16[8,4096]{1,0:T(8,128)(2,1)S(1)}, u32[]{:S(2)}, u32[]{:S(2)}) collective-permute-start(bf16[8,4096]{1,0:T(8,128)(2,1)S(1)} %get-tuple-element.47), channel_id=1, source_target_pairs={{0,2},{2,4},{4,6},{6,0},{1,3},{3,5},{5,7},{7,1},{8,10},{10,12},{12... | collective-permute-start | bytes 196616 | tf_op jit(solution)/shard_map/ppermute | solution.py:50
  51.9 13.7 %collective-permute-start.9 = (bf16[1,96,1536]{2,1,0:T(8,128)(2,1)S(1)}, bf16[1,96,1536]{2,1,0:T(8,128)(2,1)S(1)}, u32[]{:S(2)}, u32[]{:S(2)}) collective-permute-start(bf16[1,96,1536]{2,1,0:T(8,128)(2,1)S(1)} %maximum_bitcast_fusion), channel_id=1, source_target_pairs={{0,16},{8,24},{16,0},{24,8},{1,17},{9,25},{17,1},{25,9},{2,18},{10... | collective-permute-start | bytes 884744 | tf_op jit(solution)/shard_map/ppermute | solution.py:54
  57.8 4.3 %collective-permute-start.6 = (bf16[8,4096]{1,0:T(8,128)(2,1)S(1)}, bf16[8,4096]{1,0:T(8,128)(2,1)S(1)}, u32[]{:S(2)}, u32[]{:S(2)}) collective-permute-start(bf16[8,4096]{1,0:T(8,128)(2,1)S(1)} %fusion.12), channel_id=1, source_target_pairs={{0,1},{1,0},{2,3},{3,2},{4,5},{5,4},{6,7},{7,6},{8,9},{9,8},{10,11... | collective-permute-start | bytes 196616 | tf_op jit(solution)/shard_map/ppermute | solution.py:50
  65.5 1.6 %collective-permute-start.8 = (bf16[2,64,1024]{2,1,0:T(8,128)(2,1)S(1)}, bf16[2,64,1024]{2,1,0:T(8,128)(2,1)S(1)}, u32[]{:S(2)}, u32[]{:S(2)}) collective-permute-start(bf16[2,64,1024]{2,1,0:T(8,128)(2,1)S(1)} %pad_maximum_fusion.8), channel_id=1, source_target_pairs={{0,8},{8,0},{16,24},{24,16},{1,9},{9,1},{17,25},{25,17},{2,10},{10... | collective-permute-start | bytes 786440 | tf_op jit(solution)/shard_map/ppermute | solution.py:54
  65.6 2.4 %copy-start.5 = (bf16[32,1536]{1,0:T(8,128)(2,1)S(1)}, bf16[32,1536]{1,0:T(8,128)(2,1)}, u32[]{:S(2)}) copy-start(bf16[32,1536]{1,0:T(8,128)(2,1)} %get-tuple-element.14) | copy-start | bytes 294916
  65.7 2.4 %copy-start.4 = (bf16[32,1536]{1,0:T(8,128)(2,1)S(1)}, bf16[32,1536]{1,0:T(8,128)(2,1)}, u32[]{:S(2)}) copy-start(bf16[32,1536]{1,0:T(8,128)(2,1)} %get-tuple-element.13) | copy-start | bytes 294916
  65.7 2.3 %collective-permute-start.10 = (bf16[2,96,1536]{2,1,0:T(8,128)(2,1)S(1)}, bf16[2,96,1536]{2,1,0:T(8,128)(2,1)S(1)}, u32[]{:S(2)}, u32[]{:S(2)}) collective-permute-start(bf16[2,96,1536]{2,1,0:T(8,128)(2,1)S(1)} %pad_maximum_fusion), channel_id=1, source_target_pairs={{0,8},{8,0},{16,24},{24,16},{1,9},{9,1},{17,25},{25,17},{2,10},{10... | collective-permute-start | bytes 1769480 | tf_op jit(solution)/shard_map/ppermute | solution.py:54
  66.3 1.8 %copy-start.3 = (bf16[32,1536]{1,0:T(8,128)(2,1)S(1)}, bf16[32,1536]{1,0:T(8,128)(2,1)}, u32[]{:S(2)}) copy-start(bf16[32,1536]{1,0:T(8,128)(2,1)} %get-tuple-element.12) | copy-start | bytes 294916
  68.1 7.2 %copy-start.1 = (bf16[256,4096]{1,0:T(8,128)(2,1)S(1)}, bf16[256,4096]{1,0:T(8,128)(2,1)}, u32[]{:S(2)}) copy-start(bf16[256,4096]{1,0:T(8,128)(2,1)} %param.7) | copy-start | bytes 6291460

commit v17 on v11

--- a/solution.py
+++ b/solution.py
@@ -129,21 +129,19 @@
     index = lax.axis_index(axis)
     stacked = jnp.stack(column_blocks)
     if power_of_two(size):
+        columns = {0: lax.dynamic_index_in_dim(stacked, index, 0, keepdims=False)}
+        for k in range(1, size):
+            outgoing = lax.dynamic_index_in_dim(stacked, index ^ k, 0, keepdims=False)
+            columns[k] = swapped(outgoing, axis, size, k)
         gathered = {0: factors}
-        held = {(0, k): lax.dynamic_index_in_dim(stacked, index ^ k, 0, keepdims=False) for k in range(size)}
         distance = size // 2
         while distance >= 1:
             origins = sorted(gathered)
             arrived = swapped(jnp.stack([gathered[o] for o in origins]), axis, size, distance)
             for position, origin in enumerate(origins):
                 gathered[origin ^ distance] = arrived[position]
-            leaving = sorted(key for key in held if key[1] & distance)
-            arrived = swapped(jnp.stack([held[key] for key in leaving]), axis, size, distance)
-            held = {key: v for key, v in held.items() if not key[1] & distance}
-            for position, (origin, target) in enumerate(leaving):
-                held[(origin ^ distance, target ^ distance)] = arrived[position]
             distance //= 2
-        return [gathered[o] for o in range(size)], [held[(o, 0)] for o in range(size)]
+        return [gathered[o] for o in range(size)], [columns[o] for o in range(size)]
     every_factors = [factors]
     every_columns = [lax.dynamic_index_in_dim(stacked, index, 0, keepdims=False)]
     for k in range(1, size):

time: 73.3 us -> 75 us (1.023)
  waiting for transfers between devices: 16.1 us -> 18.4 us
    ppermute x4 -> x5, waiting for transfers between devices: 1.59 us -> 3.25 us  [swapped(): return lax.ppermute(value, axis, [(i, i ^ distance) for i in range(size)])]
    ppermute x4 -> x5, starting transfers between devices: 2.78 us -> 2.23 us  [swapped(): return lax.ppermute(value, axis, [(i, i ^ distance) for i in range(size)])]
  transfers between devices with their start and end apart: 11 -> 12, of which waited for: 6 -> 7; matrix products, arithmetic and copies ran while one was open for 7% -> 6% of each run, Pallas kernels for 31% -> 30%
where the time goes in v17:
time: 75 us; the launch traced here: 74.8 us
  Pallas kernels  29.8 us (40%)
  waiting for transfers between devices  18.4 us (25%)
  starting transfers between devices  15.8 us (21%)
  other arithmetic  4.73 us (6%)
  local copies, waits for them, and re-layouts  2.73 us (4%)
  matrix products  2.34 us (3%)
  between operations  0.95 us (1%)
    pallas_call x1, Pallas kernels, weight_pass(): pl.pallas_call(weight_pass_kernel, grid=(units // chunk,), in_specs=[pl.B...  22.6 us
    ppermute x7, waiting for transfers between devices, shifted(): return lax.ppermute(value, axes, pairs)  15.1 us
    ppermute x7, starting transfers between devices, shifted(): return lax.ppermute(value, axes, pairs)  13.6 us
    pallas_call x1, Pallas kernels, weight_grads(): pl.pallas_call(grads_kernel, grid=(steps,), in_specs=[pl.BlockSpec((rows,...  7.15 us
    ppermute x5, waiting for transfers between devices, swapped(): return lax.ppermute(value, axis, [(i, i ^ distance) for i in range(size)])  3.25 us
    ppermute x5, starting transfers between devices, swapped(): return lax.ppermute(value, axis, [(i, i ^ distance) for i in range(size)])  2.23 us
  transfers between devices with their start and end apart: 12, of which 7 were waited for; matrix products, arithmetic and copies ran while one was open for 6% of the time, Pallas kernels for 30%

profile of v17, /device:TPU:0, one launch (start us, length us, event | category | flops | bytes accessed | tf_op | source)
XLA Modules:
  0.0 74.8 jit_solution(12180347301427548129)
XLA Ops:
  0.6 0.8 %convert_bitcast_fusion = (s32[2,128]{1,0:T(2,128)S(1)}, pred[256]{0:T(512)(128)(4,1)S(1)}) fusion(s32[256]{0:T(256)} %param.13), kind=kLoop, calls=%fused_computation.53 | loop fusion | flops 512 | bytes 2304 | tf_op jit(solution)/shard_map/convert
  1.5 0.3 reduce-window.9
  1.9 0.1 slice_reduce_fusion
  2.1 0.2 copy-done
  2.2 0.5 multiply_reduce_fusion.1
  2.8 0.8 %copy-done.2 = bf16[256,4096]{1,0:T(8,128)(2,1)S(1)} copy-done((bf16[256,4096]{1,0:T(8,128)(2,1)S(1)}, bf16[256,4096]{1,0:T(8,128)(2,1)}, u32[]{:S(2)}) %copy-start.2) | copy-done | bytes 2097176
  3.6 0.4 convolution_convert_fusion.1
  4.1 3.1 %collective-permute-start = (bf16[16,4096]{1,0:T(8,128)(2,1)S(1)}, bf16[16,4096]{1,0:T(8,128)(2,1)S(1)}, u32[]{:S(2)}, u32[]{:S(2)}) collective-permute-start(bf16[16,4096]{1,0:T(8,128)(2,1)S(1)} %pad_maximum_fusion.9), channel_id=1, source_target_pairs={{0,2},{2,4},{4,6},{6,0},{1,3},{3,5},{5,7},{7,1},{8,10},{10,12},{12... | collective-permute-start | bytes 393224 | tf_op jit(solution)/shard_map/ppermute | solution.py:50
  7.2 2.6 %collective-permute-start.1 = (bf16[16,4096]{1,0:T(8,128)(2,1)S(1)}, bf16[16,4096]{1,0:T(8,128)(2,1)S(1)}, u32[]{:S(2)}, u32[]{:S(2)}) collective-permute-start(bf16[16,4096]{1,0:T(8,128)(2,1)S(1)} %pad_maximum_fusion.9), channel_id=1, source_target_pairs={{0,4},{2,6},{4,0},{6,2},{1,5},{3,7},{5,1},{7,3},{8,12},{10,14},{12... | collective-permute-start | bytes 393224 | tf_op jit(solution)/shard_map/ppermute | solution.py:50
  9.7 1.3 %collective-permute-start.2 = (bf16[16,4096]{1,0:T(8,128)(2,1)S(1)}, bf16[16,4096]{1,0:T(8,128)(2,1)S(1)}, u32[]{:S(2)}, u32[]{:S(2)}) collective-permute-start(bf16[16,4096]{1,0:T(8,128)(2,1)S(1)} %pad_maximum_fusion.9), channel_id=1, source_target_pairs={{0,6},{2,0},{4,2},{6,4},{1,7},{3,1},{5,3},{7,5},{8,14},{10,8},{12,... | collective-permute-start | bytes 393224 | tf_op jit(solution)/shard_map/ppermute | solution.py:50
  11.1 2.5 %collective-permute-done = bf16[16,4096]{1,0:T(8,128)(2,1)S(1)} collective-permute-done((bf16[16,4096]{1,0:T(8,128)(2,1)S(1)}, bf16[16,4096]{1,0:T(8,128)(2,1)S(1)}, u32[]{:S(2)}, u32[]{:S(2)}) %collective-permute-start) | collective-permute-done | bytes 131104 | tf_op jit(solution)/shard_map/ppermute | solution.py:50
  13.6 4.8 %collective-permute-done.1 = bf16[16,4096]{1,0:T(8,128)(2,1)S(1)} collective-permute-done((bf16[16,4096]{1,0:T(8,128)(2,1)S(1)}, bf16[16,4096]{1,0:T(8,128)(2,1)S(1)}, u32[]{:S(2)}, u32[]{:S(2)}) %collective-permute-start.1) | collective-permute-done | bytes 131104 | tf_op jit(solution)/shard_map/ppermute | solution.py:50
  18.5 0.4 reshape.69
  18.9 0.8 %fusion.13 = (bf16[64,1,1024]{2,1,0:T(2,128)(2,1)S(1)}, bf16[64,1,1024]{2,1,0:T(2,128)(2,1)S(1)}, bf16[64,1,1024]{2,1,0:T(2,128)(2,1)S(1)}, bf16[64,1,1024]{2,1,0:T(2,128)(2,1)S(1)}) fusion(bf16[64,4,1024]{2,1,0:T(4,128)(2,1)S(1)} %reshape.69), kind=kLoop, calls=%fused_computation.62 | loop fusion | bytes 1048576 | tf_op jit(solution)/shard_map/slice | solution.py:290
  20.0 1.6 %collective-permute-start.8 = (bf16[64,1024]{1,0:T(8,128)(2,1)S(1)}, bf16[64,1024]{1,0:T(8,128)(2,1)S(1)}, u32[]{:S(2)}, u32[]{:S(2)}) collective-permute-start(bf16[64,1024]{1,0:T(8,128)(2,1)S(1)} %get-tuple-element.32), channel_id=1, source_target_pairs={{0,16},{8,24},{16,0},{24,8},{1,17},{9,25},{17,1},{25,9},{2,18},{10... | collective-permute-start | bytes 393224 | tf_op jit(solution)/shard_map/ppermute | solution.py:54
  21.6 0.8 %pad_maximum_fusion.5 = (bf16[32,4096]{1,0:T(8,128)(2,1)}, bf16[32,4096]{1,0:T(8,128)(2,1)}) fusion(bf16[8,4096]{1,0:T(8,128)(2,1)S(1)} %get-tuple-element.51, bf16[8,4096]{1,0:T(8,128)(2,1)S(1)} %get-tuple-element.54, bf16[8,4096]{1,0:T(8,128)(2,1)S(1)} %get-tuple-element.57, bf16[8,4096]{1,0:T(8,128)(2,1)S(1)} %get-tuple-element.19, ...), kind=kLoop, calls=%fused_computation.8 | loop fusion | flops 2097152 | bytes 1048576 | tf_op jit(solution)/shard_map/concatenate | solution.py:280
  22.4 22.6 %shard_map.102 = (bf16[32,1536]{1,0:T(8,128)(2,1)}, bf16[32,1536]{1,0:T(8,128)(2,1)}, bf16[32,1536]{1,0:T(8,128)(2,1)}, f32[32,4096]{1,0:T(8,128)}) custom-call(bf16[32,4096]{1,0:T(8,128)(2,1)} %get-tuple-element.60.normed_ref, bf16[32,4096]{1,0:T(8,128)(2,1)} %get-tuple-element.61.masked_ref, bf16[4096,1536]{1,0:T(8,128)(2,1)} %gate_w_ref.1, ...), custom_call_target="tpu_custom_call" | custom-call | flops 2013265920 | bytes 38797312 | tf_op jit(solution)/shard_map/pallas_call | solution.py:188
  45.1 1.1 %convert_element_type.37 = bf16[32,4096]{1,0:T(8,128)(2,1)S(1)} convert(f32[32,4096]{1,0:T(8,128)} %get-tuple-element.11) | non-fusion elementwise | flops 131072 | bytes 786432 | tf_op jit(solution)/shard_map/convert_element_type | solution.py:294
  46.2 4.4 %collective-permute-start.3 = (bf16[8,4096]{1,0:T(8,128)(2,1)S(1)}, bf16[8,4096]{1,0:T(8,128)(2,1)S(1)}, u32[]{:S(2)}, u32[]{:S(2)}) collective-permute-start(bf16[8,4096]{1,0:T(8,128)(2,1)S(1)} %get-tuple-element.40), channel_id=1, source_target_pairs={{0,6},{2,0},{4,2},{6,4},{1,7},{3,1},{5,3},{7,5},{8,14},{10,8},{12,... | collective-permute-start | bytes 196616 | tf_op jit(solution)/shard_map/ppermute | solution.py:50
  50.6 0.4 collective-permute-start.4
  50.9 0.3 collective-permute-start.5
  51.2 1.0 %maximum_bitcast_fusion = bf16[1,96,1536]{2,1,0:T(8,128)(2,1)S(1)} fusion(bf16[32,1536]{1,0:T(8,128)(2,1)} %get-tuple-element.14, bf16[32,1536]{1,0:T(8,128)(2,1)} %get-tuple-element.13, bf16[32,1536]{1,0:T(8,128)(2,1)} %get-tuple-element.12), kind=kLoop, calls=%fused_computation.7 | loop fusion | flops 884736 | bytes 589824 | tf_op jit(solution)/shard_map/stack | solution.py:140
  52.2 0.8 %collective-permute-done.3 = bf16[8,4096]{1,0:T(8,128)(2,1)S(1)} collective-permute-done((bf16[8,4096]{1,0:T(8,128)(2,1)S(1)}, bf16[8,4096]{1,0:T(8,128)(2,1)S(1)}, u32[]{:S(2)}, u32[]{:S(2)}) %collective-permute-start.3) | collective-permute-done | bytes 65568 | tf_op jit(solution)/shard_map/ppermute | solution.py:50
  53.1 4.3 %collective-permute-done.4 = bf16[8,4096]{1,0:T(8,128)(2,1)S(1)} collective-permute-done((bf16[8,4096]{1,0:T(8,128)(2,1)S(1)}, bf16[8,4096]{1,0:T(8,128)(2,1)S(1)}, u32[]{:S(2)}, u32[]{:S(2)}) %collective-permute-start.4) | collective-permute-done | bytes 65568 | tf_op jit(solution)/shard_map/ppermute | solution.py:50
  57.4 0.5 collective-permute-start.10
  57.9 1.6 %collective-permute-start.6 = (bf16[8,4096]{1,0:T(8,128)(2,1)S(1)}, bf16[8,4096]{1,0:T(8,128)(2,1)S(1)}, u32[]{:S(2)}, u32[]{:S(2)}) collective-permute-start(bf16[8,4096]{1,0:T(8,128)(2,1)S(1)} %fusion.12), channel_id=1, source_target_pairs={{0,1},{1,0},{2,3},{3,2},{4,5},{5,4},{6,7},{7,6},{8,9},{9,8},{10,11... | collective-permute-start | bytes 196616 | tf_op jit(solution)/shard_map/ppermute | solution.py:50
  59.6 2.7 %collective-permute-done.6 = bf16[8,4096]{1,0:T(8,128)(2,1)S(1)} collective-permute-done((bf16[8,4096]{1,0:T(8,128)(2,1)S(1)}, bf16[8,4096]{1,0:T(8,128)(2,1)S(1)}, u32[]{:S(2)}, u32[]{:S(2)}) %collective-permute-start.6) | collective-permute-done | bytes 65568 | tf_op jit(solution)/shard_map/ppermute | solution.py:50
  62.3 0.2 multiply_reduce_fusion
  62.4 1.5 %convolution_convert_fusion = bf16[128,4096]{1,0:T(8,128)(2,1)} fusion(f32[8,4096]{1,0:T(8,128)S(1)} %get-tuple-element.59, bf16[8,4096]{1,0:T(8,128)(2,1)S(1)} %collective-permute-done.6, f32[8]{0:T(128)S(1)} %multiply_multiply_fusion, f32[4096]{0:T(1024)S(1)} %copy-done.6, f32[8]{0:T(128)S(1)} %fusion.8, pred[8,256]{1,0:T(8,128)(4,1)S(1)} %fusion.5, ...), kind=kOutput, calls=%fused_computation | convolution fusion | flops 9404416 | bytes 1525764 | tf_op jit(solution)/shard_map/dot_general | solution.py:23
  63.9 1.3 %collective-permute-done.10 = bf16[1,96,1536]{2,1,0:T(8,128)(2,1)S(1)} collective-permute-done((bf16[1,96,1536]{2,1,0:T(8,128)(2,1)S(1)}, bf16[1,96,1536]{2,1,0:T(8,128)(2,1)S(1)}, u32[]{:S(2)}, u32[]{:S(2)}) %collective-permute-start.10) | collective-permute-done | bytes 294944 | tf_op jit(solution)/shard_map/ppermute | solution.py:54
  65.5 1.9 %collective-permute-done.11 = bf16[2,96,1536]{2,1,0:T(8,128)(2,1)S(1)} collective-permute-done((bf16[2,96,1536]{2,1,0:T(8,128)(2,1)S(1)}, bf16[2,96,1536]{2,1,0:T(8,128)(2,1)S(1)}, u32[]{:S(2)}, u32[]{:S(2)}) %collective-permute-start.11) | collective-permute-done | bytes 589856 | tf_op jit(solution)/shard_map/ppermute | solution.py:54
  67.6 7.2 %shard_map.103 = (f32[1024,1536]{1,0:T(8,128)}, f32[1024,1536]{1,0:T(8,128)}, f32[1536,1024]{1,0:T(8,128)}) custom-call(bf16[128,1024]{1,0:T(8,128)(2,1)S(1)} %pad_maximum_fusion.7.normed_ref, bf16[128,1536]{1,0:T(8,128)(2,1)S(1)} %pad_maximum_fusion.2.gate_ref, bf16[128,1536]{1,0:T(8,128)(2,1)S(1)} %pad_maximum_fusion.3.up_ref, ...), custom_call_target="tpu_custom_call" | custom-call | flops 1207959552 | bytes 20578304 | tf_op jit(solution)/shard_map/pallas_call | solution.py:232
  (53 shorter events, 1.2 us)
Async XLA Ops:
  0.6 1.6 %copy-start = (bf16[256,4096]{1,0:T(8,128)(2,1)S(1)}, bf16[256,4096]{1,0:T(8,128)(2,1)}, u32[]{:S(2)}) copy-start(bf16[256,4096]{1,0:T(8,128)(2,1)} %param.7) | copy-start | bytes 6291460
  1.9 1.7 %copy-start.2 = (bf16[256,4096]{1,0:T(8,128)(2,1)S(1)}, bf16[256,4096]{1,0:T(8,128)(2,1)}, u32[]{:S(2)}) copy-start(bf16[256,4096]{1,0:T(8,128)(2,1)} %param.8) | copy-start | bytes 6291460
  2.2 1.7 %copy-start.6 = (f32[4096]{0:T(1024)S(1)}, f32[4096]{0:T(1024)}, u32[]{:S(2)}) copy-start(f32[4096]{0:T(1024)} %param.9) | copy-start | bytes 49156
  4.1 9.5 %collective-permute-start = (bf16[16,4096]{1,0:T(8,128)(2,1)S(1)}, bf16[16,4096]{1,0:T(8,128)(2,1)S(1)}, u32[]{:S(2)}, u32[]{:S(2)}) collective-permute-start(bf16[16,4096]{1,0:T(8,128)(2,1)S(1)} %pad_maximum_fusion.9), channel_id=1, source_target_pairs={{0,2},{2,4},{4,6},{6,0},{1,3},{3,5},{5,7},{7,1},{8,10},{10,12},{12... | collective-permute-start | bytes 393224 | tf_op jit(solution)/shard_map/ppermute | solution.py:50
  7.2 11.2 %collective-permute-start.1 = (bf16[16,4096]{1,0:T(8,128)(2,1)S(1)}, bf16[16,4096]{1,0:T(8,128)(2,1)S(1)}, u32[]{:S(2)}, u32[]{:S(2)}) collective-permute-start(bf16[16,4096]{1,0:T(8,128)(2,1)S(1)} %pad_maximum_fusion.9), channel_id=1, source_target_pairs={{0,4},{2,6},{4,0},{6,2},{1,5},{3,7},{5,1},{7,3},{8,12},{10,14},{12... | collective-permute-start | bytes 393224 | tf_op jit(solution)/shard_map/ppermute | solution.py:50
  9.7 8.7 %collective-permute-start.2 = (bf16[16,4096]{1,0:T(8,128)(2,1)S(1)}, bf16[16,4096]{1,0:T(8,128)(2,1)S(1)}, u32[]{:S(2)}, u32[]{:S(2)}) collective-permute-start(bf16[16,4096]{1,0:T(8,128)(2,1)S(1)} %pad_maximum_fusion.9), channel_id=1, source_target_pairs={{0,6},{2,0},{4,2},{6,4},{1,7},{3,1},{5,3},{7,5},{8,14},{10,8},{12,... | collective-permute-start | bytes 393224 | tf_op jit(solution)/shard_map/ppermute | solution.py:50
  19.9 39.6 %collective-permute-start.7 = (bf16[64,1024]{1,0:T(8,128)(2,1)S(1)}, bf16[64,1024]{1,0:T(8,128)(2,1)S(1)}, u32[]{:S(2)}, u32[]{:S(2)}) collective-permute-start(bf16[64,1024]{1,0:T(8,128)(2,1)S(1)} %get-tuple-element.30), channel_id=1, source_target_pairs={{0,8},{8,0},{16,24},{24,16},{1,9},{9,1},{17,25},{25,17},{2,10},{10... | collective-permute-start | bytes 393224 | tf_op jit(solution)/shard_map/ppermute | solution.py:54
  20.0 39.5 %collective-permute-start.8 = (bf16[64,1024]{1,0:T(8,128)(2,1)S(1)}, bf16[64,1024]{1,0:T(8,128)(2,1)S(1)}, u32[]{:S(2)}, u32[]{:S(2)}) collective-permute-start(bf16[64,1024]{1,0:T(8,128)(2,1)S(1)} %get-tuple-element.32), channel_id=1, source_target_pairs={{0,16},{8,24},{16,0},{24,8},{1,17},{9,25},{17,1},{25,9},{2,18},{10... | collective-permute-start | bytes 393224 | tf_op jit(solution)/shard_map/ppermute | solution.py:54
  46.2 6.9 %collective-permute-start.3 = (bf16[8,4096]{1,0:T(8,128)(2,1)S(1)}, bf16[8,4096]{1,0:T(8,128)(2,1)S(1)}, u32[]{:S(2)}, u32[]{:S(2)}) collective-permute-start(bf16[8,4096]{1,0:T(8,128)(2,1)S(1)} %get-tuple-element.40), channel_id=1, source_target_pairs={{0,6},{2,0},{4,2},{6,4},{1,7},{3,1},{5,3},{7,5},{8,14},{10,8},{12,... | collective-permute-start | bytes 196616 | tf_op jit(solution)/shard_map/ppermute | solution.py:50
  50.6 6.8 %collective-permute-start.4 = (bf16[8,4096]{1,0:T(8,128)(2,1)S(1)}, bf16[8,4096]{1,0:T(8,128)(2,1)S(1)}, u32[]{:S(2)}, u32[]{:S(2)}) collective-permute-start(bf16[8,4096]{1,0:T(8,128)(2,1)S(1)} %get-tuple-element.42), channel_id=1, source_target_pairs={{0,4},{2,6},{4,0},{6,2},{1,5},{3,7},{5,1},{7,3},{8,12},{10,14},{12... | collective-permute-start | bytes 196616 | tf_op jit(solution)/shard_map/ppermute | solution.py:50
  50.9 7.0 %collective-permute-start.5 = (bf16[8,4096]{1,0:T(8,128)(2,1)S(1)}, bf16[8,4096]{1,0:T(8,128)(2,1)S(1)}, u32[]{:S(2)}, u32[]{:S(2)}) collective-permute-start(bf16[8,4096]{1,0:T(8,128)(2,1)S(1)} %get-tuple-element.41), channel_id=1, source_target_pairs={{0,2},{2,4},{4,6},{6,0},{1,3},{3,5},{5,7},{7,1},{8,10},{10,12},{12... | collective-permute-start | bytes 196616 | tf_op jit(solution)/shard_map/ppermute | solution.py:50
  53.1 6.5 %collective-permute-start.9 = (bf16[64,1024]{1,0:T(8,128)(2,1)S(1)}, bf16[64,1024]{1,0:T(8,128)(2,1)S(1)}, u32[]{:S(2)}, u32[]{:S(2)}) collective-permute-start(bf16[64,1024]{1,0:T(8,128)(2,1)S(1)} %get-tuple-element.31), channel_id=1, source_target_pairs={{0,24},{8,16},{16,8},{24,0},{1,25},{9,17},{17,9},{25,1},{2,26},{10... | collective-permute-start | bytes 393224 | tf_op jit(solution)/shard_map/ppermute | solution.py:54
  57.4 7.9 %collective-permute-start.10 = (bf16[1,96,1536]{2,1,0:T(8,128)(2,1)S(1)}, bf16[1,96,1536]{2,1,0:T(8,128)(2,1)S(1)}, u32[]{:S(2)}, u32[]{:S(2)}) collective-permute-start(bf16[1,96,1536]{2,1,0:T(8,128)(2,1)S(1)} %maximum_bitcast_fusion), channel_id=1, source_target_pairs={{0,16},{8,24},{16,0},{24,8},{1,17},{9,25},{17,1},{25,9},{2,18},{10... | collective-permute-start | bytes 884744 | tf_op jit(solution)/shard_map/ppermute | solution.py:54
  57.9 4.3 %collective-permute-start.6 = (bf16[8,4096]{1,0:T(8,128)(2,1)S(1)}, bf16[8,4096]{1,0:T(8,128)(2,1)S(1)}, u32[]{:S(2)}, u32[]{:S(2)}) collective-permute-start(bf16[8,4096]{1,0:T(8,128)(2,1)S(1)} %fusion.12), channel_id=1, source_target_pairs={{0,1},{1,0},{2,3},{3,2},{4,5},{5,4},{6,7},{7,6},{8,9},{9,8},{10,11... | collective-permute-start | bytes 196616 | tf_op jit(solution)/shard_map/ppermute | solution.py:50
  63.9 3.5 %copy-start.5 = (bf16[32,1536]{1,0:T(8,128)(2,1)S(1)}, bf16[32,1536]{1,0:T(8,128)(2,1)}, u32[]{:S(2)}) copy-start(bf16[32,1536]{1,0:T(8,128)(2,1)} %get-tuple-element.14) | copy-start | bytes 294916
  65.3 2.2 %copy-start.4 = (bf16[32,1536]{1,0:T(8,128)(2,1)S(1)}, bf16[32,1536]{1,0:T(8,128)(2,1)}, u32[]{:S(2)}) copy-start(bf16[32,1536]{1,0:T(8,128)(2,1)} %get-tuple-element.13) | copy-start | bytes 294916
  65.3 2.1 %collective-permute-start.11 = (bf16[2,96,1536]{2,1,0:T(8,128)(2,1)S(1)}, bf16[2,96,1536]{2,1,0:T(8,128)(2,1)S(1)}, u32[]{:S(2)}, u32[]{:S(2)}) collective-permute-start(bf16[2,96,1536]{2,1,0:T(8,128)(2,1)S(1)} %pad_maximum_fusion), channel_id=1, source_target_pairs={{0,8},{8,0},{16,24},{24,16},{1,9},{9,1},{17,25},{25,17},{2,10},{10... | collective-permute-start | bytes 1769480 | tf_op jit(solution)/shard_map/ppermute | solution.py:54
  65.4 2.1 %copy-start.3 = (bf16[32,1536]{1,0:T(8,128)(2,1)S(1)}, bf16[32,1536]{1,0:T(8,128)(2,1)}, u32[]{:S(2)}) copy-start(bf16[32,1536]{1,0:T(8,128)(2,1)} %get-tuple-element.12) | copy-start | bytes 294916
  67.5 7.2 %copy-start.1 = (bf16[256,4096]{1,0:T(8,128)(2,1)S(1)}, bf16[256,4096]{1,0:T(8,128)(2,1)}, u32[]{:S(2)}) copy-start(bf16[256,4096]{1,0:T(8,128)(2,1)} %param.7) | copy-start | bytes 6291460

commit v18 on v11

--- a/solution.py
+++ b/solution.py
@@ -185,7 +185,7 @@
 def weight_pass(window_normed, window_masked, gate_weight, up_weight, down_weight):
     rows, features = window_normed.shape
     units = gate_weight.shape[1]
-    chunk = next((size for size in (512, 256, 128) if units % size == 0), units)
+    chunk = next((size for size in (384, 512, 256, 128) if units % size == 0), units)
     factor_shape = jax.ShapeDtypeStruct((rows, units), jnp.bfloat16)
     return pl.pallas_call(
         weight_pass_kernel,

time: 73.3 us -> 72.8 us (level)
  no operation moved by 1% of the time
where the time goes in v18:
time: 72.8 us; the launch traced here: 72.6 us
  Pallas kernels  29.3 us (40%)
  starting transfers between devices  16.4 us (23%)
  waiting for transfers between devices  16.1 us (22%)
  other arithmetic  4.79 us (7%)
  local copies, waits for them, and re-layouts  2.73 us (4%)
  matrix products  2.34 us (3%)
  between operations  0.95 us (1%)
    pallas_call x1, Pallas kernels, weight_pass(): pl.pallas_call(weight_pass_kernel, grid=(units // chunk,), in_specs=[pl.B...  22.1 us
    ppermute x7, waiting for transfers between devices, shifted(): return lax.ppermute(value, axes, pairs)  14.5 us
    ppermute x7, starting transfers between devices, shifted(): return lax.ppermute(value, axes, pairs)  13.6 us
    pallas_call x1, Pallas kernels, weight_grads(): pl.pallas_call(grads_kernel, grid=(steps,), in_specs=[pl.BlockSpec((rows,...  7.15 us
    ppermute x4, starting transfers between devices, swapped(): return lax.ppermute(value, axis, [(i, i ^ distance) for i in range(size)])  2.78 us
    ppermute x4, waiting for transfers between devices, swapped(): return lax.ppermute(value, axis, [(i, i ^ distance) for i in range(size)])  1.59 us
    dot_general x1, matrix products, contract_first(): lax.dot_general(left, right, (((0,), (0,)), ((), ())), preferred_element_...  1.46 us
  transfers between devices with their start and end apart: 11, of which 6 were waited for; matrix products, arithmetic and copies ran while one was open for 7% of the time, Pallas kernels for 31%

profile of v18, /device:TPU:0, one launch (start us, length us, event | category | flops | bytes accessed | tf_op | source)
XLA Modules:
  0.0 72.6 jit_solution(10915402104218664199)
XLA Ops:
  0.6 0.8 %convert_bitcast_fusion = (s32[2,128]{1,0:T(2,128)S(1)}, pred[256]{0:T(512)(128)(4,1)S(1)}) fusion(s32[256]{0:T(256)} %param.13), kind=kLoop, calls=%fused_computation.61 | loop fusion | flops 512 | bytes 2304 | tf_op jit(solution)/shard_map/convert
  1.5 0.3 reduce-window.9
  1.9 0.1 slice_reduce_fusion
  2.1 0.2 copy-done
  2.2 0.5 multiply_reduce_fusion.1
  2.8 0.8 %copy-done.2 = bf16[256,4096]{1,0:T(8,128)(2,1)S(1)} copy-done((bf16[256,4096]{1,0:T(8,128)(2,1)S(1)}, bf16[256,4096]{1,0:T(8,128)(2,1)}, u32[]{:S(2)}) %copy-start.2) | copy-done | bytes 2097176
  3.6 0.4 convolution_convert_fusion.1
  4.1 3.1 %collective-permute-start = (bf16[16,4096]{1,0:T(8,128)(2,1)S(1)}, bf16[16,4096]{1,0:T(8,128)(2,1)S(1)}, u32[]{:S(2)}, u32[]{:S(2)}) collective-permute-start(bf16[16,4096]{1,0:T(8,128)(2,1)S(1)} %pad_maximum_fusion.11), channel_id=1, source_target_pairs={{0,2},{2,4},{4,6},{6,0},{1,3},{3,5},{5,7},{7,1},{8,10},{10,12},{12... | collective-permute-start | bytes 393224 | tf_op jit(solution)/shard_map/ppermute | solution.py:50
  7.2 2.6 %collective-permute-start.1 = (bf16[16,4096]{1,0:T(8,128)(2,1)S(1)}, bf16[16,4096]{1,0:T(8,128)(2,1)S(1)}, u32[]{:S(2)}, u32[]{:S(2)}) collective-permute-start(bf16[16,4096]{1,0:T(8,128)(2,1)S(1)} %pad_maximum_fusion.11), channel_id=1, source_target_pairs={{0,4},{2,6},{4,0},{6,2},{1,5},{3,7},{5,1},{7,3},{8,12},{10,14},{12... | collective-permute-start | bytes 393224 | tf_op jit(solution)/shard_map/ppermute | solution.py:50
  9.7 1.3 %collective-permute-start.2 = (bf16[16,4096]{1,0:T(8,128)(2,1)S(1)}, bf16[16,4096]{1,0:T(8,128)(2,1)S(1)}, u32[]{:S(2)}, u32[]{:S(2)}) collective-permute-start(bf16[16,4096]{1,0:T(8,128)(2,1)S(1)} %pad_maximum_fusion.11), channel_id=1, source_target_pairs={{0,6},{2,0},{4,2},{6,4},{1,7},{3,1},{5,3},{7,5},{8,14},{10,8},{12,... | collective-permute-start | bytes 393224 | tf_op jit(solution)/shard_map/ppermute | solution.py:50
  11.1 2.5 %collective-permute-done = bf16[16,4096]{1,0:T(8,128)(2,1)S(1)} collective-permute-done((bf16[16,4096]{1,0:T(8,128)(2,1)S(1)}, bf16[16,4096]{1,0:T(8,128)(2,1)S(1)}, u32[]{:S(2)}, u32[]{:S(2)}) %collective-permute-start) | collective-permute-done | bytes 131104 | tf_op jit(solution)/shard_map/ppermute | solution.py:50
  13.6 4.8 %collective-permute-done.1 = bf16[16,4096]{1,0:T(8,128)(2,1)S(1)} collective-permute-done((bf16[16,4096]{1,0:T(8,128)(2,1)S(1)}, bf16[16,4096]{1,0:T(8,128)(2,1)S(1)}, u32[]{:S(2)}, u32[]{:S(2)}) %collective-permute-start.1) | collective-permute-done | bytes 131104 | tf_op jit(solution)/shard_map/ppermute | solution.py:50
  18.5 0.4 reshape.75
  18.9 0.8 %fusion.13 = (bf16[64,1,1024]{2,1,0:T(2,128)(2,1)S(1)}, bf16[64,1,1024]{2,1,0:T(2,128)(2,1)S(1)}, bf16[64,1,1024]{2,1,0:T(2,128)(2,1)S(1)}, bf16[64,1,1024]{2,1,0:T(2,128)(2,1)S(1)}) fusion(bf16[64,4,1024]{2,1,0:T(4,128)(2,1)S(1)} %reshape.75), kind=kLoop, calls=%fused_computation.70 | loop fusion | bytes 1048576 | tf_op jit(solution)/shard_map/slice | solution.py:292
  20.0 1.6 %collective-permute-start.7 = (bf16[2,64,1024]{2,1,0:T(8,128)(2,1)S(1)}, bf16[2,64,1024]{2,1,0:T(8,128)(2,1)S(1)}, u32[]{:S(2)}, u32[]{:S(2)}) collective-permute-start(bf16[2,64,1024]{2,1,0:T(8,128)(2,1)S(1)} %pad_maximum_fusion.7), channel_id=1, source_target_pairs={{0,16},{8,24},{16,0},{24,8},{1,17},{9,25},{17,1},{25,9},{2,18},{10... | collective-permute-start | bytes 786440 | tf_op jit(solution)/shard_map/ppermute | solution.py:54
  21.6 0.8 %pad_maximum_fusion.5 = (bf16[32,4096]{1,0:T(8,128)(2,1)}, bf16[32,4096]{1,0:T(8,128)(2,1)}) fusion(bf16[8,4096]{1,0:T(8,128)(2,1)S(1)} %get-tuple-element.51, bf16[8,4096]{1,0:T(8,128)(2,1)S(1)} %get-tuple-element.54, bf16[8,4096]{1,0:T(8,128)(2,1)S(1)} %get-tuple-element.57, bf16[8,4096]{1,0:T(8,128)(2,1)S(1)} %get-tuple-element.19, ...), kind=kLoop, calls=%fused_computation.8 | loop fusion | flops 2097152 | bytes 1048576 | tf_op jit(solution)/shard_map/concatenate | solution.py:282
  22.4 22.1 %shard_map.102 = (bf16[32,1536]{1,0:T(8,128)(2,1)}, bf16[32,1536]{1,0:T(8,128)(2,1)}, bf16[32,1536]{1,0:T(8,128)(2,1)}, f32[32,4096]{1,0:T(8,128)}) custom-call(bf16[32,4096]{1,0:T(8,128)(2,1)} %get-tuple-element.60.normed_ref, bf16[32,4096]{1,0:T(8,128)(2,1)} %get-tuple-element.61.masked_ref, bf16[4096,1536]{1,0:T(8,128)(2,1)} %gate_w_ref.1, ...), custom_call_target="tpu_custom_call" | custom-call | flops 2013265920 | bytes 38797312 | tf_op jit(solution)/shard_map/pallas_call | solution.py:190
  44.5 1.1 %convert_element_type.37 = bf16[32,4096]{1,0:T(8,128)(2,1)S(1)} convert(f32[32,4096]{1,0:T(8,128)} %get-tuple-element.11) | non-fusion elementwise | flops 131072 | bytes 786432 | tf_op jit(solution)/shard_map/convert_element_type | solution.py:296
  45.6 4.4 %collective-permute-start.3 = (bf16[8,4096]{1,0:T(8,128)(2,1)S(1)}, bf16[8,4096]{1,0:T(8,128)(2,1)S(1)}, u32[]{:S(2)}, u32[]{:S(2)}) collective-permute-start(bf16[8,4096]{1,0:T(8,128)(2,1)S(1)} %get-tuple-element.46), channel_id=1, source_target_pairs={{0,6},{2,0},{4,2},{6,4},{1,7},{3,1},{5,3},{7,5},{8,14},{10,8},{12,... | collective-permute-start | bytes 196616 | tf_op jit(solution)/shard_map/ppermute | solution.py:50
  50.0 0.4 collective-permute-start.4
  50.4 0.3 collective-permute-start.5
  50.7 1.0 %maximum_bitcast_fusion = bf16[1,96,1536]{2,1,0:T(8,128)(2,1)S(1)} fusion(bf16[32,1536]{1,0:T(8,128)(2,1)} %get-tuple-element.14, bf16[32,1536]{1,0:T(8,128)(2,1)} %get-tuple-element.13, bf16[32,1536]{1,0:T(8,128)(2,1)} %get-tuple-element.12), kind=kLoop, calls=%fused_computation.7 | loop fusion | flops 884736 | bytes 589824 | tf_op jit(solution)/shard_map/stack | solution.py:137
  51.7 0.6 collective-permute-start.9
  52.3 4.5 %collective-permute-done.4 = bf16[8,4096]{1,0:T(8,128)(2,1)S(1)} collective-permute-done((bf16[8,4096]{1,0:T(8,128)(2,1)S(1)}, bf16[8,4096]{1,0:T(8,128)(2,1)S(1)}, u32[]{:S(2)}, u32[]{:S(2)}) %collective-permute-start.4) | collective-permute-done | bytes 65568 | tf_op jit(solution)/shard_map/ppermute | solution.py:50
  56.8 1.6 %collective-permute-start.6 = (bf16[8,4096]{1,0:T(8,128)(2,1)S(1)}, bf16[8,4096]{1,0:T(8,128)(2,1)S(1)}, u32[]{:S(2)}, u32[]{:S(2)}) collective-permute-start(bf16[8,4096]{1,0:T(8,128)(2,1)S(1)} %fusion.12), channel_id=1, source_target_pairs={{0,1},{1,0},{2,3},{3,2},{4,5},{5,4},{6,7},{7,6},{8,9},{9,8},{10,11... | collective-permute-start | bytes 196616 | tf_op jit(solution)/shard_map/ppermute | solution.py:50
  58.3 2.8 %collective-permute-done.6 = bf16[8,4096]{1,0:T(8,128)(2,1)S(1)} collective-permute-done((bf16[8,4096]{1,0:T(8,128)(2,1)S(1)}, bf16[8,4096]{1,0:T(8,128)(2,1)S(1)}, u32[]{:S(2)}, u32[]{:S(2)}) %collective-permute-start.6) | collective-permute-done | bytes 65568 | tf_op jit(solution)/shard_map/ppermute | solution.py:50
  61.1 0.2 multiply_reduce_fusion
  61.3 1.5 %convolution_convert_fusion = bf16[128,4096]{1,0:T(8,128)(2,1)} fusion(f32[8,4096]{1,0:T(8,128)S(1)} %get-tuple-element.59, bf16[8,4096]{1,0:T(8,128)(2,1)S(1)} %collective-permute-done.6, f32[8]{0:T(128)S(1)} %multiply_multiply_fusion, f32[4096]{0:T(1024)S(1)} %copy-done.6, f32[8]{0:T(128)S(1)} %fusion.8, pred[8,256]{1,0:T(8,128)(4,1)S(1)} %fusion.5, ...), kind=kOutput, calls=%fused_computation | convolution fusion | flops 9404416 | bytes 1525764 | tf_op jit(solution)/shard_map/dot_general | solution.py:23
  63.0 0.6 collective-permute-start.10
  63.6 0.8 %collective-permute-done.8 = bf16[2,64,1024]{2,1,0:T(8,128)(2,1)S(1)} collective-permute-done((bf16[2,64,1024]{2,1,0:T(8,128)(2,1)S(1)}, bf16[2,64,1024]{2,1,0:T(8,128)(2,1)S(1)}, u32[]{:S(2)}, u32[]{:S(2)}) %collective-permute-start.8) | collective-permute-done | bytes 262176 | tf_op jit(solution)/shard_map/ppermute | solution.py:54
  64.5 0.8 %collective-permute-done.10 = bf16[2,96,1536]{2,1,0:T(8,128)(2,1)S(1)} collective-permute-done((bf16[2,96,1536]{2,1,0:T(8,128)(2,1)S(1)}, bf16[2,96,1536]{2,1,0:T(8,128)(2,1)S(1)}, u32[]{:S(2)}, u32[]{:S(2)}) %collective-permute-start.10) | collective-permute-done | bytes 589856 | tf_op jit(solution)/shard_map/ppermute | solution.py:54
  65.4 7.1 %shard_map.103 = (f32[1024,1536]{1,0:T(8,128)}, f32[1024,1536]{1,0:T(8,128)}, f32[1536,1024]{1,0:T(8,128)}) custom-call(bf16[128,1024]{1,0:T(8,128)(2,1)S(1)} %pad_maximum_fusion.9.normed_ref, bf16[128,1536]{1,0:T(8,128)(2,1)S(1)} %pad_maximum_fusion.2.gate_ref, bf16[128,1536]{1,0:T(8,128)(2,1)S(1)} %pad_maximum_fusion.3.up_ref, ...), custom_call_target="tpu_custom_call" | custom-call | flops 1207959552 | bytes 20578304 | tf_op jit(solution)/shard_map/pallas_call | solution.py:234
  (53 shorter events, 1.2 us)
Async XLA Ops:
  0.6 1.6 %copy-start = (bf16[256,4096]{1,0:T(8,128)(2,1)S(1)}, bf16[256,4096]{1,0:T(8,128)(2,1)}, u32[]{:S(2)}) copy-start(bf16[256,4096]{1,0:T(8,128)(2,1)} %param.7) | copy-start | bytes 6291460
  1.9 1.7 %copy-start.2 = (bf16[256,4096]{1,0:T(8,128)(2,1)S(1)}, bf16[256,4096]{1,0:T(8,128)(2,1)}, u32[]{:S(2)}) copy-start(bf16[256,4096]{1,0:T(8,128)(2,1)} %param.8) | copy-start | bytes 6291460
  2.2 1.7 %copy-start.6 = (f32[4096]{0:T(1024)S(1)}, f32[4096]{0:T(1024)}, u32[]{:S(2)}) copy-start(f32[4096]{0:T(1024)} %param.9) | copy-start | bytes 49156
  4.1 9.5 %collective-permute-start = (bf16[16,4096]{1,0:T(8,128)(2,1)S(1)}, bf16[16,4096]{1,0:T(8,128)(2,1)S(1)}, u32[]{:S(2)}, u32[]{:S(2)}) collective-permute-start(bf16[16,4096]{1,0:T(8,128)(2,1)S(1)} %pad_maximum_fusion.11), channel_id=1, source_target_pairs={{0,2},{2,4},{4,6},{6,0},{1,3},{3,5},{5,7},{7,1},{8,10},{10,12},{12... | collective-permute-start | bytes 393224 | tf_op jit(solution)/shard_map/ppermute | solution.py:50
  7.2 11.2 %collective-permute-start.1 = (bf16[16,4096]{1,0:T(8,128)(2,1)S(1)}, bf16[16,4096]{1,0:T(8,128)(2,1)S(1)}, u32[]{:S(2)}, u32[]{:S(2)}) collective-permute-start(bf16[16,4096]{1,0:T(8,128)(2,1)S(1)} %pad_maximum_fusion.11), channel_id=1, source_target_pairs={{0,4},{2,6},{4,0},{6,2},{1,5},{3,7},{5,1},{7,3},{8,12},{10,14},{12... | collective-permute-start | bytes 393224 | tf_op jit(solution)/shard_map/ppermute | solution.py:50
  9.7 8.7 %collective-permute-start.2 = (bf16[16,4096]{1,0:T(8,128)(2,1)S(1)}, bf16[16,4096]{1,0:T(8,128)(2,1)S(1)}, u32[]{:S(2)}, u32[]{:S(2)}) collective-permute-start(bf16[16,4096]{1,0:T(8,128)(2,1)S(1)} %pad_maximum_fusion.11), channel_id=1, source_target_pairs={{0,6},{2,0},{4,2},{6,4},{1,7},{3,1},{5,3},{7,5},{8,14},{10,8},{12,... | collective-permute-start | bytes 393224 | tf_op jit(solution)/shard_map/ppermute | solution.py:50
  20.0 42.8 %collective-permute-start.7 = (bf16[2,64,1024]{2,1,0:T(8,128)(2,1)S(1)}, bf16[2,64,1024]{2,1,0:T(8,128)(2,1)S(1)}, u32[]{:S(2)}, u32[]{:S(2)}) collective-permute-start(bf16[2,64,1024]{2,1,0:T(8,128)(2,1)S(1)} %pad_maximum_fusion.7), channel_id=1, source_target_pairs={{0,16},{8,24},{16,0},{24,8},{1,17},{9,25},{17,1},{25,9},{2,18},{10... | collective-permute-start | bytes 786440 | tf_op jit(solution)/shard_map/ppermute | solution.py:54
  45.6 6.6 %collective-permute-start.3 = (bf16[8,4096]{1,0:T(8,128)(2,1)S(1)}, bf16[8,4096]{1,0:T(8,128)(2,1)S(1)}, u32[]{:S(2)}, u32[]{:S(2)}) collective-permute-start(bf16[8,4096]{1,0:T(8,128)(2,1)S(1)} %get-tuple-element.46), channel_id=1, source_target_pairs={{0,6},{2,0},{4,2},{6,4},{1,7},{3,1},{5,3},{7,5},{8,14},{10,8},{12,... | collective-permute-start | bytes 196616 | tf_op jit(solution)/shard_map/ppermute | solution.py:50
  50.0 6.7 %collective-permute-start.4 = (bf16[8,4096]{1,0:T(8,128)(2,1)S(1)}, bf16[8,4096]{1,0:T(8,128)(2,1)S(1)}, u32[]{:S(2)}, u32[]{:S(2)}) collective-permute-start(bf16[8,4096]{1,0:T(8,128)(2,1)S(1)} %get-tuple-element.48), channel_id=1, source_target_pairs={{0,4},{2,6},{4,0},{6,2},{1,5},{3,7},{5,1},{7,3},{8,12},{10,14},{12... | collective-permute-start | bytes 196616 | tf_op jit(solution)/shard_map/ppermute | solution.py:50
  50.4 6.3 %collective-permute-start.5 = (bf16[8,4096]{1,0:T(8,128)(2,1)S(1)}, bf16[8,4096]{1,0:T(8,128)(2,1)S(1)}, u32[]{:S(2)}, u32[]{:S(2)}) collective-permute-start(bf16[8,4096]{1,0:T(8,128)(2,1)S(1)} %get-tuple-element.47), channel_id=1, source_target_pairs={{0,2},{2,4},{4,6},{6,0},{1,3},{3,5},{5,7},{7,1},{8,10},{10,12},{12... | collective-permute-start | bytes 196616 | tf_op jit(solution)/shard_map/ppermute | solution.py:50
  51.7 11.2 %collective-permute-start.9 = (bf16[1,96,1536]{2,1,0:T(8,128)(2,1)S(1)}, bf16[1,96,1536]{2,1,0:T(8,128)(2,1)S(1)}, u32[]{:S(2)}, u32[]{:S(2)}) collective-permute-start(bf16[1,96,1536]{2,1,0:T(8,128)(2,1)S(1)} %maximum_bitcast_fusion), channel_id=1, source_target_pairs={{0,16},{8,24},{16,0},{24,8},{1,17},{9,25},{17,1},{25,9},{2,18},{10... | collective-permute-start | bytes 884744 | tf_op jit(solution)/shard_map/ppermute | solution.py:54
  56.8 4.3 %collective-permute-start.6 = (bf16[8,4096]{1,0:T(8,128)(2,1)S(1)}, bf16[8,4096]{1,0:T(8,128)(2,1)S(1)}, u32[]{:S(2)}, u32[]{:S(2)}) collective-permute-start(bf16[8,4096]{1,0:T(8,128)(2,1)S(1)} %fusion.12), channel_id=1, source_target_pairs={{0,1},{1,0},{2,3},{3,2},{4,5},{5,4},{6,7},{7,6},{8,9},{9,8},{10,11... | collective-permute-start | bytes 196616 | tf_op jit(solution)/shard_map/ppermute | solution.py:50
  62.8 1.6 %collective-permute-start.8 = (bf16[2,64,1024]{2,1,0:T(8,128)(2,1)S(1)}, bf16[2,64,1024]{2,1,0:T(8,128)(2,1)S(1)}, u32[]{:S(2)}, u32[]{:S(2)}) collective-permute-start(bf16[2,64,1024]{2,1,0:T(8,128)(2,1)S(1)} %pad_maximum_fusion.8), channel_id=1, source_target_pairs={{0,8},{8,0},{16,24},{24,16},{1,9},{9,1},{17,25},{25,17},{2,10},{10... | collective-permute-start | bytes 786440 | tf_op jit(solution)/shard_map/ppermute | solution.py:54
  62.9 2.4 %copy-start.5 = (bf16[32,1536]{1,0:T(8,128)(2,1)S(1)}, bf16[32,1536]{1,0:T(8,128)(2,1)}, u32[]{:S(2)}) copy-start(bf16[32,1536]{1,0:T(8,128)(2,1)} %get-tuple-element.14) | copy-start | bytes 294916
  63.0 2.4 %copy-start.4 = (bf16[32,1536]{1,0:T(8,128)(2,1)S(1)}, bf16[32,1536]{1,0:T(8,128)(2,1)}, u32[]{:S(2)}) copy-start(bf16[32,1536]{1,0:T(8,128)(2,1)} %get-tuple-element.13) | copy-start | bytes 294916
  63.0 2.3 %collective-permute-start.10 = (bf16[2,96,1536]{2,1,0:T(8,128)(2,1)S(1)}, bf16[2,96,1536]{2,1,0:T(8,128)(2,1)S(1)}, u32[]{:S(2)}, u32[]{:S(2)}) collective-permute-start(bf16[2,96,1536]{2,1,0:T(8,128)(2,1)S(1)} %pad_maximum_fusion), channel_id=1, source_target_pairs={{0,8},{8,0},{16,24},{24,16},{1,9},{9,1},{17,25},{25,17},{2,10},{10... | collective-permute-start | bytes 1769480 | tf_op jit(solution)/shard_map/ppermute | solution.py:54
  63.6 1.8 %copy-start.3 = (bf16[32,1536]{1,0:T(8,128)(2,1)S(1)}, bf16[32,1536]{1,0:T(8,128)(2,1)}, u32[]{:S(2)}) copy-start(bf16[32,1536]{1,0:T(8,128)(2,1)} %get-tuple-element.12) | copy-start | bytes 294916
  65.4 7.2 %copy-start.1 = (bf16[256,4096]{1,0:T(8,128)(2,1)S(1)}, bf16[256,4096]{1,0:T(8,128)(2,1)}, u32[]{:S(2)}) copy-start(bf16[256,4096]{1,0:T(8,128)(2,1)} %param.7) | copy-start | bytes 6291460

commit v19 on v18

--- a/solution.py
+++ b/solution.py
@@ -229,7 +229,7 @@
 def weight_grads(normed_cols, every_gate, every_up, every_hidden, masked_cols):
     rows, share = normed_cols.shape
     units = every_gate.shape[1]
-    steps = 4 if share % 512 == 0 and units % 512 == 0 else 1
+    steps = 2 if share % 256 == 0 and units % 256 == 0 else 1
     share_block, unit_block = share // steps, units // steps
     return pl.pallas_call(
         grads_kernel,

time: 72.8 us -> 73.3 us (level)
  transfers between devices with their start and end apart: 11 -> 11, of which waited for: 6 -> 6; matrix products, arithmetic and copies ran while one was open for 7% -> 7% of each run, Pallas kernels for 31% -> 30%
where the time goes in v19:
time: 73.3 us; the launch traced here: 73.1 us
  Pallas kernels  29.8 us (41%)
  starting transfers between devices  16.4 us (22%)
  waiting for transfers between devices  16.1 us (22%)
  other arithmetic  4.79 us (7%)
  local copies, waits for them, and re-layouts  2.73 us (4%)
  matrix products  2.34 us (3%)
  between operations  0.95 us (1%)
    pallas_call x1, Pallas kernels, weight_pass(): pl.pallas_call(weight_pass_kernel, grid=(units // chunk,), in_specs=[pl.B...  22.1 us
    ppermute x7, waiting for transfers between devices, shifted(): return lax.ppermute(value, axes, pairs)  14.5 us
    ppermute x7, starting transfers between devices, shifted(): return lax.ppermute(value, axes, pairs)  13.6 us
    pallas_call x1, Pallas kernels, weight_grads(): pl.pallas_call(grads_kernel, grid=(steps,), in_specs=[pl.BlockSpec((rows,...  7.66 us
    ppermute x4, starting transfers between devices, swapped(): return lax.ppermute(value, axis, [(i, i ^ distance) for i in range(size)])  2.78 us
    ppermute x4, waiting for transfers between devices, swapped(): return lax.ppermute(value, axis, [(i, i ^ distance) for i in range(size)])  1.59 us
  transfers between devices with their start and end apart: 11, of which 6 were waited for; matrix products, arithmetic and copies ran while one was open for 7% of the time, Pallas kernels for 30%

profile of v19, /device:TPU:0, one launch (start us, length us, event | category | flops | bytes accessed | tf_op | source)
XLA Modules:
  0.0 73.1 jit_solution(10994698441894202533)
XLA Ops:
  0.6 0.8 %convert_bitcast_fusion = (s32[2,128]{1,0:T(2,128)S(1)}, pred[256]{0:T(512)(128)(4,1)S(1)}) fusion(s32[256]{0:T(256)} %param.13), kind=kLoop, calls=%fused_computation.61 | loop fusion | flops 512 | bytes 2304 | tf_op jit(solution)/shard_map/convert
  1.5 0.3 reduce-window.9
  1.9 0.1 slice_reduce_fusion
  2.1 0.2 copy-done
  2.2 0.5 multiply_reduce_fusion.1
  2.8 0.8 %copy-done.2 = bf16[256,4096]{1,0:T(8,128)(2,1)S(1)} copy-done((bf16[256,4096]{1,0:T(8,128)(2,1)S(1)}, bf16[256,4096]{1,0:T(8,128)(2,1)}, u32[]{:S(2)}) %copy-start.2) | copy-done | bytes 2097176
  3.6 0.4 convolution_convert_fusion.1
  4.1 3.1 %collective-permute-start = (bf16[16,4096]{1,0:T(8,128)(2,1)S(1)}, bf16[16,4096]{1,0:T(8,128)(2,1)S(1)}, u32[]{:S(2)}, u32[]{:S(2)}) collective-permute-start(bf16[16,4096]{1,0:T(8,128)(2,1)S(1)} %pad_maximum_fusion.11), channel_id=1, source_target_pairs={{0,2},{2,4},{4,6},{6,0},{1,3},{3,5},{5,7},{7,1},{8,10},{10,12},{12... | collective-permute-start | bytes 393224 | tf_op jit(solution)/shard_map/ppermute | solution.py:50
  7.2 2.6 %collective-permute-start.1 = (bf16[16,4096]{1,0:T(8,128)(2,1)S(1)}, bf16[16,4096]{1,0:T(8,128)(2,1)S(1)}, u32[]{:S(2)}, u32[]{:S(2)}) collective-permute-start(bf16[16,4096]{1,0:T(8,128)(2,1)S(1)} %pad_maximum_fusion.11), channel_id=1, source_target_pairs={{0,4},{2,6},{4,0},{6,2},{1,5},{3,7},{5,1},{7,3},{8,12},{10,14},{12... | collective-permute-start | bytes 393224 | tf_op jit(solution)/shard_map/ppermute | solution.py:50
  9.7 1.3 %collective-permute-start.2 = (bf16[16,4096]{1,0:T(8,128)(2,1)S(1)}, bf16[16,4096]{1,0:T(8,128)(2,1)S(1)}, u32[]{:S(2)}, u32[]{:S(2)}) collective-permute-start(bf16[16,4096]{1,0:T(8,128)(2,1)S(1)} %pad_maximum_fusion.11), channel_id=1, source_target_pairs={{0,6},{2,0},{4,2},{6,4},{1,7},{3,1},{5,3},{7,5},{8,14},{10,8},{12,... | collective-permute-start | bytes 393224 | tf_op jit(solution)/shard_map/ppermute | solution.py:50
  11.1 2.5 %collective-permute-done = bf16[16,4096]{1,0:T(8,128)(2,1)S(1)} collective-permute-done((bf16[16,4096]{1,0:T(8,128)(2,1)S(1)}, bf16[16,4096]{1,0:T(8,128)(2,1)S(1)}, u32[]{:S(2)}, u32[]{:S(2)}) %collective-permute-start) | collective-permute-done | bytes 131104 | tf_op jit(solution)/shard_map/ppermute | solution.py:50
  13.6 4.8 %collective-permute-done.1 = bf16[16,4096]{1,0:T(8,128)(2,1)S(1)} collective-permute-done((bf16[16,4096]{1,0:T(8,128)(2,1)S(1)}, bf16[16,4096]{1,0:T(8,128)(2,1)S(1)}, u32[]{:S(2)}, u32[]{:S(2)}) %collective-permute-start.1) | collective-permute-done | bytes 131104 | tf_op jit(solution)/shard_map/ppermute | solution.py:50
  18.5 0.4 reshape.75
  18.9 0.8 %fusion.13 = (bf16[64,1,1024]{2,1,0:T(2,128)(2,1)S(1)}, bf16[64,1,1024]{2,1,0:T(2,128)(2,1)S(1)}, bf16[64,1,1024]{2,1,0:T(2,128)(2,1)S(1)}, bf16[64,1,1024]{2,1,0:T(2,128)(2,1)S(1)}) fusion(bf16[64,4,1024]{2,1,0:T(4,128)(2,1)S(1)} %reshape.75), kind=kLoop, calls=%fused_computation.70 | loop fusion | bytes 1048576 | tf_op jit(solution)/shard_map/slice | solution.py:292
  20.0 1.6 %collective-permute-start.7 = (bf16[2,64,1024]{2,1,0:T(8,128)(2,1)S(1)}, bf16[2,64,1024]{2,1,0:T(8,128)(2,1)S(1)}, u32[]{:S(2)}, u32[]{:S(2)}) collective-permute-start(bf16[2,64,1024]{2,1,0:T(8,128)(2,1)S(1)} %pad_maximum_fusion.7), channel_id=1, source_target_pairs={{0,16},{8,24},{16,0},{24,8},{1,17},{9,25},{17,1},{25,9},{2,18},{10... | collective-permute-start | bytes 786440 | tf_op jit(solution)/shard_map/ppermute | solution.py:54
  21.6 0.8 %pad_maximum_fusion.5 = (bf16[32,4096]{1,0:T(8,128)(2,1)}, bf16[32,4096]{1,0:T(8,128)(2,1)}) fusion(bf16[8,4096]{1,0:T(8,128)(2,1)S(1)} %get-tuple-element.51, bf16[8,4096]{1,0:T(8,128)(2,1)S(1)} %get-tuple-element.54, bf16[8,4096]{1,0:T(8,128)(2,1)S(1)} %get-tuple-element.57, bf16[8,4096]{1,0:T(8,128)(2,1)S(1)} %get-tuple-element.19, ...), kind=kLoop, calls=%fused_computation.8 | loop fusion | flops 2097152 | bytes 1048576 | tf_op jit(solution)/shard_map/concatenate | solution.py:282
  22.4 22.1 %shard_map.102 = (bf16[32,1536]{1,0:T(8,128)(2,1)}, bf16[32,1536]{1,0:T(8,128)(2,1)}, bf16[32,1536]{1,0:T(8,128)(2,1)}, f32[32,4096]{1,0:T(8,128)}) custom-call(bf16[32,4096]{1,0:T(8,128)(2,1)} %get-tuple-element.60.normed_ref, bf16[32,4096]{1,0:T(8,128)(2,1)} %get-tuple-element.61.masked_ref, bf16[4096,1536]{1,0:T(8,128)(2,1)} %gate_w_ref.1, ...), custom_call_target="tpu_custom_call" | custom-call | flops 2013265920 | bytes 38797312 | tf_op jit(solution)/shard_map/pallas_call | solution.py:190
  44.5 1.1 %convert_element_type.37 = bf16[32,4096]{1,0:T(8,128)(2,1)S(1)} convert(f32[32,4096]{1,0:T(8,128)} %get-tuple-element.11) | non-fusion elementwise | flops 131072 | bytes 786432 | tf_op jit(solution)/shard_map/convert_element_type | solution.py:296
  45.6 4.4 %collective-permute-start.3 = (bf16[8,4096]{1,0:T(8,128)(2,1)S(1)}, bf16[8,4096]{1,0:T(8,128)(2,1)S(1)}, u32[]{:S(2)}, u32[]{:S(2)}) collective-permute-start(bf16[8,4096]{1,0:T(8,128)(2,1)S(1)} %get-tuple-element.46), channel_id=1, source_target_pairs={{0,6},{2,0},{4,2},{6,4},{1,7},{3,1},{5,3},{7,5},{8,14},{10,8},{12,... | collective-permute-start | bytes 196616 | tf_op jit(solution)/shard_map/ppermute | solution.py:50
  50.0 0.4 collective-permute-start.4
  50.4 0.3 collective-permute-start.5
  50.7 1.0 %maximum_bitcast_fusion = bf16[1,96,1536]{2,1,0:T(8,128)(2,1)S(1)} fusion(bf16[32,1536]{1,0:T(8,128)(2,1)} %get-tuple-element.14, bf16[32,1536]{1,0:T(8,128)(2,1)} %get-tuple-element.13, bf16[32,1536]{1,0:T(8,128)(2,1)} %get-tuple-element.12), kind=kLoop, calls=%fused_computation.7 | loop fusion | flops 884736 | bytes 589824 | tf_op jit(solution)/shard_map/stack | solution.py:137
  51.7 0.6 collective-permute-start.9
  52.3 4.5 %collective-permute-done.4 = bf16[8,4096]{1,0:T(8,128)(2,1)S(1)} collective-permute-done((bf16[8,4096]{1,0:T(8,128)(2,1)S(1)}, bf16[8,4096]{1,0:T(8,128)(2,1)S(1)}, u32[]{:S(2)}, u32[]{:S(2)}) %collective-permute-start.4) | collective-permute-done | bytes 65568 | tf_op jit(solution)/shard_map/ppermute | solution.py:50
  56.8 1.6 %collective-permute-start.6 = (bf16[8,4096]{1,0:T(8,128)(2,1)S(1)}, bf16[8,4096]{1,0:T(8,128)(2,1)S(1)}, u32[]{:S(2)}, u32[]{:S(2)}) collective-permute-start(bf16[8,4096]{1,0:T(8,128)(2,1)S(1)} %fusion.12), channel_id=1, source_target_pairs={{0,1},{1,0},{2,3},{3,2},{4,5},{5,4},{6,7},{7,6},{8,9},{9,8},{10,11... | collective-permute-start | bytes 196616 | tf_op jit(solution)/shard_map/ppermute | solution.py:50
  58.3 2.8 %collective-permute-done.6 = bf16[8,4096]{1,0:T(8,128)(2,1)S(1)} collective-permute-done((bf16[8,4096]{1,0:T(8,128)(2,1)S(1)}, bf16[8,4096]{1,0:T(8,128)(2,1)S(1)}, u32[]{:S(2)}, u32[]{:S(2)}) %collective-permute-start.6) | collective-permute-done | bytes 65568 | tf_op jit(solution)/shard_map/ppermute | solution.py:50
  61.1 0.2 multiply_reduce_fusion
  61.3 1.5 %convolution_convert_fusion = bf16[128,4096]{1,0:T(8,128)(2,1)} fusion(f32[8,4096]{1,0:T(8,128)S(1)} %get-tuple-element.59, bf16[8,4096]{1,0:T(8,128)(2,1)S(1)} %collective-permute-done.6, f32[8]{0:T(128)S(1)} %multiply_multiply_fusion, f32[4096]{0:T(1024)S(1)} %copy-done.6, f32[8]{0:T(128)S(1)} %fusion.8, pred[8,256]{1,0:T(8,128)(4,1)S(1)} %fusion.5, ...), kind=kOutput, calls=%fused_computation | convolution fusion | flops 9404416 | bytes 1525764 | tf_op jit(solution)/shard_map/dot_general | solution.py:23
  63.0 0.6 collective-permute-start.10
  63.6 0.8 %collective-permute-done.8 = bf16[2,64,1024]{2,1,0:T(8,128)(2,1)S(1)} collective-permute-done((bf16[2,64,1024]{2,1,0:T(8,128)(2,1)S(1)}, bf16[2,64,1024]{2,1,0:T(8,128)(2,1)S(1)}, u32[]{:S(2)}, u32[]{:S(2)}) %collective-permute-start.8) | collective-permute-done | bytes 262176 | tf_op jit(solution)/shard_map/ppermute | solution.py:54
  64.5 0.8 %collective-permute-done.10 = bf16[2,96,1536]{2,1,0:T(8,128)(2,1)S(1)} collective-permute-done((bf16[2,96,1536]{2,1,0:T(8,128)(2,1)S(1)}, bf16[2,96,1536]{2,1,0:T(8,128)(2,1)S(1)}, u32[]{:S(2)}, u32[]{:S(2)}) %collective-permute-start.10) | collective-permute-done | bytes 589856 | tf_op jit(solution)/shard_map/ppermute | solution.py:54
  65.4 7.7 %shard_map.103 = (f32[1024,1536]{1,0:T(8,128)}, f32[1024,1536]{1,0:T(8,128)}, f32[1536,1024]{1,0:T(8,128)}) custom-call(bf16[128,1024]{1,0:T(8,128)(2,1)S(1)} %pad_maximum_fusion.9.normed_ref, bf16[128,1536]{1,0:T(8,128)(2,1)S(1)} %pad_maximum_fusion.2.gate_ref, bf16[128,1536]{1,0:T(8,128)(2,1)S(1)} %pad_maximum_fusion.3.up_ref, ...), custom_call_target="tpu_custom_call" | custom-call | flops 1207959552 | bytes 20578304 | tf_op jit(solution)/shard_map/pallas_call | solution.py:234
  (53 shorter events, 1.2 us)
Async XLA Ops:
  0.6 1.6 %copy-start = (bf16[256,4096]{1,0:T(8,128)(2,1)S(1)}, bf16[256,4096]{1,0:T(8,128)(2,1)}, u32[]{:S(2)}) copy-start(bf16[256,4096]{1,0:T(8,128)(2,1)} %param.7) | copy-start | bytes 6291460
  1.9 1.7 %copy-start.2 = (bf16[256,4096]{1,0:T(8,128)(2,1)S(1)}, bf16[256,4096]{1,0:T(8,128)(2,1)}, u32[]{:S(2)}) copy-start(bf16[256,4096]{1,0:T(8,128)(2,1)} %param.8) | copy-start | bytes 6291460
  2.2 1.7 %copy-start.6 = (f32[4096]{0:T(1024)S(1)}, f32[4096]{0:T(1024)}, u32[]{:S(2)}) copy-start(f32[4096]{0:T(1024)} %param.9) | copy-start | bytes 49156
  4.1 9.5 %collective-permute-start = (bf16[16,4096]{1,0:T(8,128)(2,1)S(1)}, bf16[16,4096]{1,0:T(8,128)(2,1)S(1)}, u32[]{:S(2)}, u32[]{:S(2)}) collective-permute-start(bf16[16,4096]{1,0:T(8,128)(2,1)S(1)} %pad_maximum_fusion.11), channel_id=1, source_target_pairs={{0,2},{2,4},{4,6},{6,0},{1,3},{3,5},{5,7},{7,1},{8,10},{10,12},{12... | collective-permute-start | bytes 393224 | tf_op jit(solution)/shard_map/ppermute | solution.py:50
  7.2 11.2 %collective-permute-start.1 = (bf16[16,4096]{1,0:T(8,128)(2,1)S(1)}, bf16[16,4096]{1,0:T(8,128)(2,1)S(1)}, u32[]{:S(2)}, u32[]{:S(2)}) collective-permute-start(bf16[16,4096]{1,0:T(8,128)(2,1)S(1)} %pad_maximum_fusion.11), channel_id=1, source_target_pairs={{0,4},{2,6},{4,0},{6,2},{1,5},{3,7},{5,1},{7,3},{8,12},{10,14},{12... | collective-permute-start | bytes 393224 | tf_op jit(solution)/shard_map/ppermute | solution.py:50
  9.7 8.7 %collective-permute-start.2 = (bf16[16,4096]{1,0:T(8,128)(2,1)S(1)}, bf16[16,4096]{1,0:T(8,128)(2,1)S(1)}, u32[]{:S(2)}, u32[]{:S(2)}) collective-permute-start(bf16[16,4096]{1,0:T(8,128)(2,1)S(1)} %pad_maximum_fusion.11), channel_id=1, source_target_pairs={{0,6},{2,0},{4,2},{6,4},{1,7},{3,1},{5,3},{7,5},{8,14},{10,8},{12,... | collective-permute-start | bytes 393224 | tf_op jit(solution)/shard_map/ppermute | solution.py:50
  20.0 42.8 %collective-permute-start.7 = (bf16[2,64,1024]{2,1,0:T(8,128)(2,1)S(1)}, bf16[2,64,1024]{2,1,0:T(8,128)(2,1)S(1)}, u32[]{:S(2)}, u32[]{:S(2)}) collective-permute-start(bf16[2,64,1024]{2,1,0:T(8,128)(2,1)S(1)} %pad_maximum_fusion.7), channel_id=1, source_target_pairs={{0,16},{8,24},{16,0},{24,8},{1,17},{9,25},{17,1},{25,9},{2,18},{10... | collective-permute-start | bytes 786440 | tf_op jit(solution)/shard_map/ppermute | solution.py:54
  45.6 6.6 %collective-permute-start.3 = (bf16[8,4096]{1,0:T(8,128)(2,1)S(1)}, bf16[8,4096]{1,0:T(8,128)(2,1)S(1)}, u32[]{:S(2)}, u32[]{:S(2)}) collective-permute-start(bf16[8,4096]{1,0:T(8,128)(2,1)S(1)} %get-tuple-element.46), channel_id=1, source_target_pairs={{0,6},{2,0},{4,2},{6,4},{1,7},{3,1},{5,3},{7,5},{8,14},{10,8},{12,... | collective-permute-start | bytes 196616 | tf_op jit(solution)/shard_map/ppermute | solution.py:50
  50.0 6.7 %collective-permute-start.4 = (bf16[8,4096]{1,0:T(8,128)(2,1)S(1)}, bf16[8,4096]{1,0:T(8,128)(2,1)S(1)}, u32[]{:S(2)}, u32[]{:S(2)}) collective-permute-start(bf16[8,4096]{1,0:T(8,128)(2,1)S(1)} %get-tuple-element.48), channel_id=1, source_target_pairs={{0,4},{2,6},{4,0},{6,2},{1,5},{3,7},{5,1},{7,3},{8,12},{10,14},{12... | collective-permute-start | bytes 196616 | tf_op jit(solution)/shard_map/ppermute | solution.py:50
  50.4 6.3 %collective-permute-start.5 = (bf16[8,4096]{1,0:T(8,128)(2,1)S(1)}, bf16[8,4096]{1,0:T(8,128)(2,1)S(1)}, u32[]{:S(2)}, u32[]{:S(2)}) collective-permute-start(bf16[8,4096]{1,0:T(8,128)(2,1)S(1)} %get-tuple-element.47), channel_id=1, source_target_pairs={{0,2},{2,4},{4,6},{6,0},{1,3},{3,5},{5,7},{7,1},{8,10},{10,12},{12... | collective-permute-start | bytes 196616 | tf_op jit(solution)/shard_map/ppermute | solution.py:50
  51.7 11.2 %collective-permute-start.9 = (bf16[1,96,1536]{2,1,0:T(8,128)(2,1)S(1)}, bf16[1,96,1536]{2,1,0:T(8,128)(2,1)S(1)}, u32[]{:S(2)}, u32[]{:S(2)}) collective-permute-start(bf16[1,96,1536]{2,1,0:T(8,128)(2,1)S(1)} %maximum_bitcast_fusion), channel_id=1, source_target_pairs={{0,16},{8,24},{16,0},{24,8},{1,17},{9,25},{17,1},{25,9},{2,18},{10... | collective-permute-start | bytes 884744 | tf_op jit(solution)/shard_map/ppermute | solution.py:54
  56.8 4.3 %collective-permute-start.6 = (bf16[8,4096]{1,0:T(8,128)(2,1)S(1)}, bf16[8,4096]{1,0:T(8,128)(2,1)S(1)}, u32[]{:S(2)}, u32[]{:S(2)}) collective-permute-start(bf16[8,4096]{1,0:T(8,128)(2,1)S(1)} %fusion.12), channel_id=1, source_target_pairs={{0,1},{1,0},{2,3},{3,2},{4,5},{5,4},{6,7},{7,6},{8,9},{9,8},{10,11... | collective-permute-start | bytes 196616 | tf_op jit(solution)/shard_map/ppermute | solution.py:50
  62.8 1.6 %collective-permute-start.8 = (bf16[2,64,1024]{2,1,0:T(8,128)(2,1)S(1)}, bf16[2,64,1024]{2,1,0:T(8,128)(2,1)S(1)}, u32[]{:S(2)}, u32[]{:S(2)}) collective-permute-start(bf16[2,64,1024]{2,1,0:T(8,128)(2,1)S(1)} %pad_maximum_fusion.8), channel_id=1, source_target_pairs={{0,8},{8,0},{16,24},{24,16},{1,9},{9,1},{17,25},{25,17},{2,10},{10... | collective-permute-start | bytes 786440 | tf_op jit(solution)/shard_map/ppermute | solution.py:54
  62.9 2.4 %copy-start.5 = (bf16[32,1536]{1,0:T(8,128)(2,1)S(1)}, bf16[32,1536]{1,0:T(8,128)(2,1)}, u32[]{:S(2)}) copy-start(bf16[32,1536]{1,0:T(8,128)(2,1)} %get-tuple-element.14) | copy-start | bytes 294916
  63.0 2.4 %copy-start.4 = (bf16[32,1536]{1,0:T(8,128)(2,1)S(1)}, bf16[32,1536]{1,0:T(8,128)(2,1)}, u32[]{:S(2)}) copy-start(bf16[32,1536]{1,0:T(8,128)(2,1)} %get-tuple-element.13) | copy-start | bytes 294916
  63.0 2.3 %collective-permute-start.10 = (bf16[2,96,1536]{2,1,0:T(8,128)(2,1)S(1)}, bf16[2,96,1536]{2,1,0:T(8,128)(2,1)S(1)}, u32[]{:S(2)}, u32[]{:S(2)}) collective-permute-start(bf16[2,96,1536]{2,1,0:T(8,128)(2,1)S(1)} %pad_maximum_fusion), channel_id=1, source_target_pairs={{0,8},{8,0},{16,24},{24,16},{1,9},{9,1},{17,25},{25,17},{2,10},{10... | collective-permute-start | bytes 1769480 | tf_op jit(solution)/shard_map/ppermute | solution.py:54
  63.6 1.8 %copy-start.3 = (bf16[32,1536]{1,0:T(8,128)(2,1)S(1)}, bf16[32,1536]{1,0:T(8,128)(2,1)}, u32[]{:S(2)}) copy-start(bf16[32,1536]{1,0:T(8,128)(2,1)} %get-tuple-element.12) | copy-start | bytes 294916
  65.4 7.7 %copy-start.1 = (bf16[256,4096]{1,0:T(8,128)(2,1)S(1)}, bf16[256,4096]{1,0:T(8,128)(2,1)}, u32[]{:S(2)}) copy-start(bf16[256,4096]{1,0:T(8,128)(2,1)} %param.7) | copy-start | bytes 6291460
